TPU v7x, 32 devices: a whole 2x2x4 slice. The times are simulated.
32 devices in a mesh: cap: 4 (over z), lat: 4 (over x, core), rad: 2 (over y).
Axes of the slice: x: 2, y: 2, z: 4, core: 2. Of those that a mesh axis runs over, the one named last changes fastest.
Arguments:
- adjoint_temp: float32 [64, 128, 1024], P('rad', 'cap', 'lat'), may hold values from -6 to 6
- velocity: bfloat16 [2, 64, 128, 1024], P(None, 'rad', 'cap', 'lat'), may hold values from -6 to 6
- visc_flow: bfloat16 [64, 128, 1024], P('rad', 'cap', 'lat'), may hold values from 0.099609375 to 1
- visc_yield: bfloat16 [64, 128, 1024], P('rad', 'cap', 'lat'), may hold values from 0.049804688 to 1
- yield_mask: int32 [64, 128, 1024], P('rad', 'cap', 'lat'), may hold values 0 or 1
- radial_inverse: float32 [64, 64], replicated
- marker_rows: bfloat16 [64, 32768], P('rad', ('cap', 'lat')), may hold values from -6 to 6
- recv_cells: int32 [32768], P(('cap', 'lat')), may hold values from 0 to 8191
- recv_counts: int32 [64], P(('cap', 'lat')), may hold values from 64 to 512, as said below
Outputs:
- adjoint_prev: float32 [64, 128, 1024], P(None, ('cap', 'rad'), 'lat')
Inputs may be any that keep to these rules, and one draw needn't show every extreme that they name: `recv_counts`: some bucket holds exactly 512 live slots and some exactly 64 in every draw.
All inputs are finite; a program needn't handle non-finite values. No bound on the sum of `yield_mask` on one device may be relied on, other than what follows from the above.
Results may differ from a plain program's by a relative error of at most 0.0003.
Values may be sent and summed in bfloat16 or wider, within the bound.
No kernel may reach another device: no remote copies, remote signals or barrier semaphores. Data moves between devices by JAX's collectives and lax.ppermute only.
A program may use at most 64 MiB of HBM per device.

v0:
```python
import math

import jax
import jax.numpy as jnp
from jax import lax
from jax.sharding import PartitionSpec as P

PICARD = 3


relax_coef = 0.25
advect_coef = 0.1


def extended(x, sides, width):
    for axis, dim in sides:
        devices, length = (lax.axis_size(axis), x.shape[dim])
        up = [(i, (i + 1) % devices) for i in range(devices - 1)]
        down = [(j, i) for i, j in up]
        last = lax.slice_in_dim(x, length - width, length, axis=dim)
        first = lax.slice_in_dim(x, 0, width, axis=dim)
        before = lax.ppermute(last, axis, up)
        after = lax.ppermute(first, axis, down)
        x = jnp.concatenate([before, x, after], axis=dim)
    return x


def viscous(w_pad, eta_pad, w_mid, eta_mid):
    total = jnp.zeros_like(w_mid)
    for neigh_w, neigh_e in (
        (w_pad[:, 2:, 1:-1], eta_pad[:, 2:, 1:-1]),
        (w_pad[:, :-2, 1:-1], eta_pad[:, :-2, 1:-1]),
        (w_pad[:, 1:-1, 2:], eta_pad[:, 1:-1, 2:]),
        (w_pad[:, 1:-1, :-2], eta_pad[:, 1:-1, :-2]),
    ):
        total = total + 0.5 * (eta_mid + neigh_e) * (neigh_w - w_mid)
    return total


def per_device(
    adjoint_temp,
    velocity,
    visc_flow,
    visc_yield,
    yield_mask,
    radial_inverse,
    marker_rows,
    recv_cells,
    recv_counts,
):
    layers, first_len, second_len = adjoint_temp.shape
    flow = visc_flow.astype(jnp.float32)
    plast = visc_yield.astype(jnp.float32)
    eta = jnp.where(yield_mask == 1, flow * plast / (flow + plast), flow)
    iterate = adjoint_temp
    lam_pad = None
    for sweep in range(PICARD):
        padded = extended(jnp.stack([iterate, eta]), (("cap", 2), ("lat", 3)), 1)
        if sweep == 0:
            lam_pad = padded[0]
        iterate = adjoint_temp + relax_coef * viscous(padded[0], padded[1], iterate, eta)
    advect = velocity[0] * (lam_pad[:, 2:, 1:-1] - lam_pad[:, :-2, 1:-1]) + velocity[1] * (
        lam_pad[:, 1:-1, 2:] - lam_pad[:, 1:-1, :-2]
    )
    received = lax.all_to_all(marker_rows, "lat", split_axis=1, concat_axis=1, tiled=True)
    senders = lax.axis_size("lat")
    slot_total = received.shape[1]
    per_sender = slot_total // senders
    live = (jnp.arange(per_sender, dtype=jnp.int32)[None, :] < recv_counts[:, None]).reshape(-1)
    target = jnp.where(live, recv_cells, -1)
    block = math.gcd(slot_total, 512)
    blocks = slot_total // block
    cell_count = first_len * second_len
    rows_blocks = received.reshape(layers, blocks, block).transpose(1, 0, 2)
    target_blocks = target.reshape(blocks, block)
    cell_ids = jnp.arange(cell_count, dtype=jnp.int32)

    def deposit_block(total, item):
        rows_part, target_part = item
        onehot = (target_part[:, None] == cell_ids[None, :]).astype(jnp.bfloat16)
        return (total + jnp.dot(rows_part, onehot, preferred_element_type=jnp.float32), None)

    deposit, unused = lax.scan(
        deposit_block, jnp.zeros((layers, cell_count), jnp.float32), (rows_blocks, target_blocks)
    )
    deposit = deposit.reshape(layers, first_len, second_len)
    rhs = iterate + advect_coef * advect + deposit
    full_layers = radial_inverse.shape[0]
    columns = lax.all_to_all(rhs, "rad", split_axis=1, concat_axis=0, tiled=True)
    result = jnp.dot(
        radial_inverse, columns.reshape(full_layers, -1), precision=lax.Precision.HIGHEST
    )
    return result.reshape(columns.shape)


def solution(mesh):
    in_specs = (
        P("rad", "cap", "lat"),
        P(None, "rad", "cap", "lat"),
        P("rad", "cap", "lat"),
        P("rad", "cap", "lat"),
        P("rad", "cap", "lat"),
        P(),
        P("rad", ("cap", "lat")),
        P(("cap", "lat")),
        P(("cap", "lat")),
    )
    out_specs = P(None, ("cap", "rad"), "lat")
    return jax.shard_map(
        per_device, mesh=mesh, in_specs=in_specs, out_specs=out_specs, check_vma=False
    )
```

profile of v0, /device:TPU:0, one launch (start us, length us, event | category | flops | bytes accessed | tf_op | source)
XLA Modules:
  0.0 150.8 jit_solution(331933865882135294)
XLA Ops:
  0.0 1.9 %convert_select_fusion = f32[32,32,256]{2,1,0:T(8,128)S(1)} fusion(bf16[32,32,256]{2,1,0:T(8,128)(2,1)} %param.13, bf16[32,32,256]{2,1,0:T(8,128)(2,1)} %param.14, s32[32,32,256]{2,1,0:T(8,128)} %param.15), kind=kLoop, calls=%fused_computation.43 | loop fusion | flops 1835008 | bytes 3145728 | tf_op jit(solution)/shard_map/jit(_where)/select_n | solution.py:54
  2.1 4.9 %collective-permute-start = (f32[2,32,1,256]{3,2,1,0:T(1,128)S(1)}, f32[2,32,1,256]{3,2,1,0:T(1,128)S(1)}, u32[]{:S(2)}, u32[]{:S(2)}) collective-permute-start(f32[2,32,1,256]{3,2,1,0:T(1,128)S(1)} %get-tuple-element.62), channel_id=1, source_target_pairs={{0,8},{8,16},{16,24},{1,9},{9,17},{17,25},{2,10},{10,18},{18,26},{... | collective-permute-start | bytes 196616 | tf_op jit(solution)/shard_map/ppermute | solution.py:22
  7.0 1.3 collective-permute-start.1
  8.3 0.6 collective-permute-done
  8.9 4.3 %collective-permute-done.1 = f32[2,32,1,256]{3,2,1,0:T(1,128)S(1)} collective-permute-done((f32[2,32,1,256]{3,2,1,0:T(1,128)S(1)}, f32[2,32,1,256]{3,2,1,0:T(1,128)S(1)}, u32[]{:S(2)}, u32[]{:S(2)}) %collective-permute-start.1) | collective-permute-done | bytes 65568 | tf_op jit(solution)/shard_map/ppermute | solution.py:23
  13.2 0.4 fusion.21
  13.6 1.9 %fusion.75 = (f32[2,32,34,1]{3,2,1,0:T(8,128)}, f32[2,32,34,1]{3,2,1,0:T(8,128)}) fusion(f32[2,32,34,256]{3,2,1,0:T(8,128)S(1)} %fusion.21), kind=kLoop, calls=%fused_computation.124 | loop fusion | bytes 34816 | tf_op jit(solution)/shard_map/slice | solution.py:20
  15.5 1.9 %copy.28 = f32[2,32,34,1]{2,1,3,0:T(8,128)S(1)} copy(f32[2,32,34,1]{3,2,1,0:T(8,128)} %get-tuple-element.76) | data formatting | bytes 17408 | tf_op jit(solution)/shard_map/slice | solution.py:20
  17.4 1.3 collective-permute-start.2
  18.7 1.9 %copy.29 = f32[2,32,34,1]{2,1,3,0:T(8,128)S(1)} copy(f32[2,32,34,1]{3,2,1,0:T(8,128)} %get-tuple-element.77) | data formatting | bytes 17408 | tf_op jit(solution)/shard_map/slice | solution.py:21
  20.5 1.3 collective-permute-start.3
  21.8 1.6 %copy.30 = f32[2,32,34,1]{3,2,1,0:T(8,128)} copy(f32[2,32,34,1]{2,1,3,0:T(8,128)S(1)} %collective-permute-done.2) | data formatting | bytes 17408 | tf_op jit(solution)/shard_map/ppermute | solution.py:22
  23.5 1.9 %collective-permute-done.3 = f32[2,32,34,1]{2,1,3,0:T(8,128)S(1)} collective-permute-done((f32[2,32,34,1]{2,1,3,0:T(8,128)S(1)}, f32[2,32,34,1]{2,1,3,0:T(8,128)S(1)}, u32[]{:S(2)}, u32[]{:S(2)}) %collective-permute-start.3) | collective-permute-done | bytes 8736 | tf_op jit(solution)/shard_map/ppermute | solution.py:23
  25.3 1.6 %copy.31 = f32[2,32,34,1]{3,2,1,0:T(8,128)} copy(f32[2,32,34,1]{2,1,3,0:T(8,128)S(1)} %collective-permute-done.3) | data formatting | bytes 17408 | tf_op jit(solution)/shard_map/ppermute | solution.py:23
  27.0 4.3 %fusion.11 = f32[2,32,34,258]{3,2,1,0:T(8,128)S(1)} fusion(f32[1,32,32,256]{3,2,1,0:T(8,128)S(1)} %bitcast.53, f32[2,32,34,1]{3,2,1,0:T(8,128)} %copy.31, f32[2,32,1,256]{3,2,1,0:T(1,128)S(1)} %collective-permute-done.1, f32[1,32,32,256]{3,2,1,0:T(8,128)S(1)} %bitcast.60, f32[2,32,1,256]{3,2,1,0:T(1,128)S(1)} %collective-permute-done, f32[2,32,34,1]{3,2,1,0:T(8,128)} %copy.30), kind=kLoop, calls=%fused_computation.15 | loop fusion | flops 2807040 | bytes 4491264 | tf_op jit(solution)/shard_map/concatenate | solution.py:24
  31.5 1.0 copy-done.2
  32.5 2.0 %fusion.58 = f32[32,32,256]{2,1,0:T(8,128)S(1)} fusion(f32[32,32,256]{2,1,0:T(8,128)S(1)} %copy-done.2, f32[32,32,256]{2,1,0:T(8,128)S(1)} %convert_select_fusion, f32[32,34,258]{2,1,0:T(8,128)S(1)} %get-tuple-element.71, f32[32,34,258]{2,1,0:T(8,128)S(1)} %get-tuple-element.70), kind=kLoop, calls=%fused_computation.96 | loop fusion | flops 5505024 | bytes 11534336 | tf_op jit(solution)/shard_map/add | solution.py:61
  34.5 1.0 copy-done.7
  35.5 0.7 fusion.70
  36.2 3.5 %collective-permute-start.4 = (f32[2,32,1,256]{3,2,1,0:T(1,128)}, f32[2,32,1,256]{3,2,1,0:T(1,128)S(1)}, u32[]{:S(2)}, u32[]{:S(2)}) collective-permute-start(f32[2,32,1,256]{3,2,1,0:T(1,128)} %get-tuple-element.80), channel_id=1, source_target_pairs={{0,8},{8,16},{16,24},{1,9},{9,17},{17,25},{2,10},{10,18},{18,26},{... | collective-permute-start | bytes 196616 | tf_op jit(solution)/shard_map/ppermute | solution.py:22
  39.7 1.3 collective-permute-start.5
  41.0 0.6 copy.49
  41.6 3.9 %all-to-all-start = ((bf16[32,4,512]{2,0,1:T(8,128)(2,1)}), bf16[32,4,512]{2,0,1:T(8,128)(2,1)S(1)}, u32[]{:S(2)}, u32[]{:S(2)}) async-start(bf16[32,4,512]{2,0,1:T(8,128)(2,1)} %bitcast.46), calls=%async_computation | async-start | bytes 262144 | tf_op jit(solution)/shard_map/all_to_all | solution.py:65
  45.5 0.3 collective-permute-done.5
  45.8 1.6 %fusion.23 = f32[2,32,34,256]{3,2,1,0:T(8,128)S(1)} fusion(f32[1,32,32,256]{3,2,1,0:T(8,128)S(1)} %bitcast.54, f32[2,32,1,256]{3,2,1,0:T(1,128)S(1)} %collective-permute-done.5, f32[1,32,32,256]{3,2,1,0:T(8,128)} %bitcast.65, f32[2,32,1,256]{3,2,1,0:T(1,128)S(1)} %collective-permute-done.4), kind=kLoop, calls=%fused_computation.30 | loop fusion | flops 1671168 | bytes 4456448 | tf_op jit(solution)/shard_map/concatenate | solution.py:24
  47.4 1.9 %fusion.74 = (f32[2,32,34,1]{3,2,1,0:T(8,128)}, f32[2,32,34,1]{3,2,1,0:T(8,128)}) fusion(f32[2,32,34,256]{3,2,1,0:T(8,128)S(1)} %fusion.23), kind=kLoop, calls=%fused_computation.123 | loop fusion | bytes 34816 | tf_op jit(solution)/shard_map/slice | solution.py:20
  49.3 1.9 %copy.32 = f32[2,32,34,1]{2,1,3,0:T(8,128)S(1)} copy(f32[2,32,34,1]{3,2,1,0:T(8,128)} %get-tuple-element.74) | data formatting | bytes 17408 | tf_op jit(solution)/shard_map/slice | solution.py:20
  51.2 3.4 %collective-permute-start.6 = (f32[2,32,34,1]{2,1,3,0:T(8,128)S(1)}, f32[2,32,34,1]{2,1,3,0:T(8,128)S(1)}, u32[]{:S(2)}, u32[]{:S(2)}) collective-permute-start(f32[2,32,34,1]{2,1,3,0:T(8,128)S(1)} %copy.32), channel_id=1, source_target_pairs={{0,2},{2,4},{4,6},{1,3},{3,5},{5,7},{8,10},{10,12},{12,14},{9,11},... | collective-permute-start | bytes 26120 | tf_op jit(solution)/shard_map/ppermute | solution.py:22
  54.6 1.9 %copy.33 = f32[2,32,34,1]{2,1,3,0:T(8,128)S(1)} copy(f32[2,32,34,1]{3,2,1,0:T(8,128)} %get-tuple-element.75) | data formatting | bytes 17408 | tf_op jit(solution)/shard_map/slice | solution.py:21
  56.4 1.5 collective-permute-start.7
  58.0 1.6 %copy.34 = f32[2,32,34,1]{3,2,1,0:T(8,128)} copy(f32[2,32,34,1]{2,1,3,0:T(8,128)S(1)} %collective-permute-done.6) | data formatting | bytes 17408 | tf_op jit(solution)/shard_map/ppermute | solution.py:22
  59.7 0.7 collective-permute-done.7
  60.4 2.4 %copy.35 = f32[2,32,34,1]{3,2,1,0:T(8,128)} copy(f32[2,32,34,1]{2,1,3,0:T(8,128)} %collective-permute-done.7) | data formatting | bytes 17408 | tf_op jit(solution)/shard_map/ppermute | solution.py:23
  62.8 4.4 %fusion.15 = f32[2,32,34,258]{3,2,1,0:T(8,128)S(1)} fusion(f32[1,32,32,256]{3,2,1,0:T(8,128)S(1)} %bitcast.55, f32[2,32,34,1]{3,2,1,0:T(8,128)} %copy.35, f32[2,32,1,256]{3,2,1,0:T(1,128)S(1)} %collective-permute-done.5, f32[1,32,32,256]{3,2,1,0:T(8,128)} %bitcast.66, f32[2,32,1,256]{3,2,1,0:T(1,128)S(1)} %collective-permute-done.4, f32[2,32,34,1]{3,2,1,0:T(8,128)} %copy.34), kind=kLoop, calls=%fused_computation.19 | loop fusion | flops 2807040 | bytes 4491264 | tf_op jit(solution)/shard_map/concatenate | solution.py:24
  67.5 0.9 copy-done.3
  68.8 1.9 %fusion.44 = f32[32,32,256]{2,1,0:T(8,128)S(1)} fusion(f32[32,32,256]{2,1,0:T(8,128)S(1)} %copy-done.3, f32[32,32,256]{2,1,0:T(8,128)S(1)} %copy-done.8, f32[32,34,258]{2,1,0:T(8,128)S(1)} %get-tuple-element.69, f32[32,32,256]{2,1,0:T(8,128)S(1)} %convert_select_fusion, f32[32,34,258]{2,1,0:T(8,128)S(1)} %get-tuple-element.68), kind=kLoop, calls=%fused_computation.74 | loop fusion | flops 5505024 | bytes 12582912 | tf_op jit(solution)/shard_map/add | solution.py:61
  70.7 1.0 copy-done.5
  71.8 3.7 %collective-permute-start.8 = (f32[2,32,1,256]{3,2,1,0:T(1,128)S(1)}, f32[2,32,1,256]{3,2,1,0:T(1,128)S(1)}, u32[]{:S(2)}, u32[]{:S(2)}) collective-permute-start(f32[2,32,1,256]{3,2,1,0:T(1,128)S(1)} %get-tuple-element.78), channel_id=1, source_target_pairs={{0,8},{8,16},{16,24},{1,9},{9,17},{17,25},{2,10},{10,18},{18,26},{... | collective-permute-start | bytes 196616 | tf_op jit(solution)/shard_map/ppermute | solution.py:22
  75.5 1.3 collective-permute-start.9
  76.8 0.5 collective-permute-done.8
  77.3 4.3 %collective-permute-done.9 = f32[2,32,1,256]{3,2,1,0:T(1,128)S(1)} collective-permute-done((f32[2,32,1,256]{3,2,1,0:T(1,128)S(1)}, f32[2,32,1,256]{3,2,1,0:T(1,128)S(1)}, u32[]{:S(2)}, u32[]{:S(2)}) %collective-permute-start.9) | collective-permute-done | bytes 65568 | tf_op jit(solution)/shard_map/ppermute | solution.py:23
  81.6 1.6 %fusion.25 = f32[2,32,34,256]{3,2,1,0:T(8,128)S(1)} fusion(f32[1,32,32,256]{3,2,1,0:T(8,128)S(1)} %bitcast.56, f32[2,32,1,256]{3,2,1,0:T(1,128)S(1)} %collective-permute-done.9, f32[1,32,32,256]{3,2,1,0:T(8,128)} %bitcast.62, f32[2,32,1,256]{3,2,1,0:T(1,128)S(1)} %collective-permute-done.8), kind=kLoop, calls=%fused_computation.32 | loop fusion | flops 1671168 | bytes 4456448 | tf_op jit(solution)/shard_map/concatenate | solution.py:24
  83.2 1.9 %fusion.73 = (f32[2,32,34,1]{3,2,1,0:T(8,128)}, f32[2,32,34,1]{3,2,1,0:T(8,128)}) fusion(f32[2,32,34,256]{3,2,1,0:T(8,128)S(1)} %fusion.25), kind=kLoop, calls=%fused_computation.122 | loop fusion | bytes 34816 | tf_op jit(solution)/shard_map/slice | solution.py:20
  85.1 1.9 %copy.36 = f32[2,32,34,1]{2,1,3,0:T(8,128)S(1)} copy(f32[2,32,34,1]{3,2,1,0:T(8,128)} %get-tuple-element.72) | data formatting | bytes 17408 | tf_op jit(solution)/shard_map/slice | solution.py:20
  86.9 3.1 %collective-permute-start.10 = (f32[2,32,34,1]{2,1,3,0:T(8,128)S(1)}, f32[2,32,34,1]{2,1,3,0:T(8,128)S(1)}, u32[]{:S(2)}, u32[]{:S(2)}) collective-permute-start(f32[2,32,34,1]{2,1,3,0:T(8,128)S(1)} %copy.36), channel_id=1, source_target_pairs={{0,2},{2,4},{4,6},{1,3},{3,5},{5,7},{8,10},{10,12},{12,14},{9,11},... | collective-permute-start | bytes 26120 | tf_op jit(solution)/shard_map/ppermute | solution.py:22
  90.0 1.9 %copy.37 = f32[2,32,34,1]{2,1,3,0:T(8,128)S(1)} copy(f32[2,32,34,1]{3,2,1,0:T(8,128)} %get-tuple-element.73) | data formatting | bytes 17408 | tf_op jit(solution)/shard_map/slice | solution.py:21
  91.9 1.5 %collective-permute-start.11 = (f32[2,32,34,1]{2,1,3,0:T(8,128)S(1)}, f32[2,32,34,1]{2,1,3,0:T(8,128)S(1)}, u32[]{:S(2)}, u32[]{:S(2)}) collective-permute-start(f32[2,32,34,1]{2,1,3,0:T(8,128)S(1)} %copy.37), channel_id=1, source_target_pairs={{2,0},{4,2},{6,4},{3,1},{5,3},{7,5},{10,8},{12,10},{14,12},{11,9},... | collective-permute-start | bytes 26120 | tf_op jit(solution)/shard_map/ppermute | solution.py:23
  93.4 21.3 %while.11 = (s32[]{:T(128)}, f32[32,8192]{1,0:T(8,128)}, bf16[4,32,512]{2,1,0:T(8,128)(2,1)S(1)}, s32[4,512]{1,0:T(4,128)S(1)}, s32[]{:T(128)}, /*index=5*/s32[]{:T(128)}) while((s32[]{:T(128)}, f32[32,8192]{1,0:T(8,128)}, bf16[4,32,512]{2,1,0:T(8,128)(2,1)S(1)}, s32[4,512]{1,0:T(4,128)S(1)}, s32[]{:T(128)}, ...), condition=%wide.region_1.2_spmd.clone, body=%wide.region_0.1_spmd.clone.sunk | while | flops 273154048 | bytes 2136151 | solution.py:83
  93.4 4.4 %fusion.82 = f32[32,8192]{1,0:T(8,128)} fusion(s32[512]{0:T(512)S(1)} %bitcast.74, f32[32,8192]{1,0:T(8,128)} %get-tuple-element.116, pred[]{:T(512)S(6)} %compare.3, bf16[4,32,512]{2,1,0:T(8,128)(2,1)S(1)} %get-tuple-element.123, s32[]{:T(128)} %get-tuple-element.115), kind=kOutput, calls=%fused_computation.3.clone.1 | convolution fusion | flops 273154048 | bytes 2131973 | tf_op jit(solution)/shard_map/while/body/eval_jaxpr/dot_general | solution.py:81
  97.9 5.6 %fusion.82 = f32[32,8192]{1,0:T(8,128)} fusion(s32[512]{0:T(512)S(1)} %bitcast.74, f32[32,8192]{1,0:T(8,128)} %get-tuple-element.116, pred[]{:T(512)S(6)} %compare.3, bf16[4,32,512]{2,1,0:T(8,128)(2,1)S(1)} %get-tuple-element.123, s32[]{:T(128)} %get-tuple-element.115), kind=kOutput, calls=%fused_computation.3.clone.1 | convolution fusion | flops 273154048 | bytes 2131973 | tf_op jit(solution)/shard_map/while/body/eval_jaxpr/dot_general | solution.py:81
  103.5 5.6 %fusion.82 = f32[32,8192]{1,0:T(8,128)} fusion(s32[512]{0:T(512)S(1)} %bitcast.74, f32[32,8192]{1,0:T(8,128)} %get-tuple-element.116, pred[]{:T(512)S(6)} %compare.3, bf16[4,32,512]{2,1,0:T(8,128)(2,1)S(1)} %get-tuple-element.123, s32[]{:T(128)} %get-tuple-element.115), kind=kOutput, calls=%fused_computation.3.clone.1 | convolution fusion | flops 273154048 | bytes 2131973 | tf_op jit(solution)/shard_map/while/body/eval_jaxpr/dot_general | solution.py:81
  109.1 5.6 %fusion.82 = f32[32,8192]{1,0:T(8,128)} fusion(s32[512]{0:T(512)S(1)} %bitcast.74, f32[32,8192]{1,0:T(8,128)} %get-tuple-element.116, pred[]{:T(512)S(6)} %compare.3, bf16[4,32,512]{2,1,0:T(8,128)(2,1)S(1)} %get-tuple-element.123, s32[]{:T(128)} %get-tuple-element.115), kind=kOutput, calls=%fused_computation.3.clone.1 | convolution fusion | flops 273154048 | bytes 2131973 | tf_op jit(solution)/shard_map/while/body/eval_jaxpr/dot_general | solution.py:81
  114.8 2.5 %copy.45 = f32[4,8,32,256]{3,2,1,0:T(8,128)} copy(f32[4,8,32,256]{3,1,2,0:T(8,128)} %bitcast.71) | data formatting | bytes 2097152
  117.3 1.6 %copy.38 = f32[2,32,34,1]{3,2,1,0:T(8,128)} copy(f32[2,32,34,1]{2,1,3,0:T(8,128)S(1)} %collective-permute-done.10) | data formatting | bytes 17408 | tf_op jit(solution)/shard_map/ppermute | solution.py:22
  118.9 1.6 %copy.39 = f32[2,32,34,1]{3,2,1,0:T(8,128)} copy(f32[2,32,34,1]{2,1,3,0:T(8,128)S(1)} %collective-permute-done.11) | data formatting | bytes 17408 | tf_op jit(solution)/shard_map/ppermute | solution.py:23
  120.6 4.4 %fusion.19 = f32[2,32,34,258]{3,2,1,0:T(8,128)S(1)} fusion(f32[1,32,32,256]{3,2,1,0:T(8,128)S(1)} %bitcast.57, f32[2,32,34,1]{3,2,1,0:T(8,128)} %copy.39, f32[2,32,1,256]{3,2,1,0:T(1,128)S(1)} %collective-permute-done.9, f32[1,32,32,256]{3,2,1,0:T(8,128)} %bitcast.63, f32[2,32,1,256]{3,2,1,0:T(1,128)S(1)} %collective-permute-done.8, f32[2,32,34,1]{3,2,1,0:T(8,128)} %copy.38), kind=kLoop, calls=%fused_computation.23 | loop fusion | flops 2807040 | bytes 4491264 | tf_op jit(solution)/shard_map/concatenate | solution.py:24
  125.3 0.9 copy-done.4
  127.2 3.0 %bitcast_add_fusion = f32[32,32,256]{2,1,0:T(8,128)S(1)} fusion(f32[4,8,32,256]{3,2,1,0:T(8,128)S(1)} %copy-done.9, f32[32,32,256]{2,1,0:T(8,128)S(1)} %copy-done.4, f32[32,32,256]{2,1,0:T(8,128)S(1)} %copy-done.6, f32[32,34,258]{2,1,0:T(8,128)S(1)} %get-tuple-element.67, f32[32,32,256]{2,1,0:T(8,128)S(1)} %convert_select_fusion, ...), kind=kLoop, calls=%fused_computation.47 | loop fusion | flops 8126464 | bytes 18874368 | tf_op jit(solution)/shard_map/add | solution.py:87
  130.2 0.6 copy.41
  130.8 16.4 %all_to_all.24 = f32[32,32,256]{2,0,1:T(8,128)S(1)} all-to-all(f32[32,32,256]{2,0,1:T(8,128)S(1)} %copy.41), channel_id=1, replica_groups=mesh['cap'=4,'lat'=4,'rad'=2] {'rad'}, dimensions={1} | all-to-all | bytes 2097152 | tf_op jit(solution)/shard_map/all_to_all | solution.py:89
  147.1 0.6 copy.42
  147.8 0.6 copy.46
  148.4 1.1 fusion.76
  149.5 1.3 copy.47
  (43 shorter events, 2.5 us)
Async XLA Ops:
  0.0 148.4 %copy-start = (f32[64,64]{1,0:T(8,128)S(1)}, f32[64,64]{1,0:T(8,128)}, u32[]{:S(2)}) copy-start(f32[64,64]{1,0:T(8,128)} %param.16) | copy-start | bytes 49156
  0.0 1.9 %copy-start.1 = (f32[32,32,256]{2,1,0:T(8,128)S(1)}, f32[32,32,256]{2,1,0:T(8,128)}, u32[]{:S(2)}) copy-start(f32[32,32,256]{2,1,0:T(8,128)} %param.11) | copy-start | bytes 3145732
  2.1 6.8 %collective-permute-start = (f32[2,32,1,256]{3,2,1,0:T(1,128)S(1)}, f32[2,32,1,256]{3,2,1,0:T(1,128)S(1)}, u32[]{:S(2)}, u32[]{:S(2)}) collective-permute-start(f32[2,32,1,256]{3,2,1,0:T(1,128)S(1)} %get-tuple-element.62), channel_id=1, source_target_pairs={{0,8},{8,16},{16,24},{1,9},{9,17},{17,25},{2,10},{10,18},{18,26},{... | collective-permute-start | bytes 196616 | tf_op jit(solution)/shard_map/ppermute | solution.py:22
  7.0 6.2 %collective-permute-start.1 = (f32[2,32,1,256]{3,2,1,0:T(1,128)S(1)}, f32[2,32,1,256]{3,2,1,0:T(1,128)S(1)}, u32[]{:S(2)}, u32[]{:S(2)}) collective-permute-start(f32[2,32,1,256]{3,2,1,0:T(1,128)S(1)} %get-tuple-element.82), channel_id=1, source_target_pairs={{8,0},{16,8},{24,16},{9,1},{17,9},{25,17},{10,2},{18,10},{26,18},{... | collective-permute-start | bytes 196616 | tf_op jit(solution)/shard_map/ppermute | solution.py:23
  17.4 4.4 %collective-permute-start.2 = (f32[2,32,34,1]{2,1,3,0:T(8,128)S(1)}, f32[2,32,34,1]{2,1,3,0:T(8,128)S(1)}, u32[]{:S(2)}, u32[]{:S(2)}) collective-permute-start(f32[2,32,34,1]{2,1,3,0:T(8,128)S(1)} %copy.28), channel_id=1, source_target_pairs={{0,2},{2,4},{4,6},{1,3},{3,5},{5,7},{8,10},{10,12},{12,14},{9,11},... | collective-permute-start | bytes 26120 | tf_op jit(solution)/shard_map/ppermute | solution.py:22
  20.5 4.8 %collective-permute-start.3 = (f32[2,32,34,1]{2,1,3,0:T(8,128)S(1)}, f32[2,32,34,1]{2,1,3,0:T(8,128)S(1)}, u32[]{:S(2)}, u32[]{:S(2)}) collective-permute-start(f32[2,32,34,1]{2,1,3,0:T(8,128)S(1)} %copy.29), channel_id=1, source_target_pairs={{2,0},{4,2},{6,4},{3,1},{5,3},{7,5},{10,8},{12,10},{14,12},{11,9},... | collective-permute-start | bytes 26120 | tf_op jit(solution)/shard_map/ppermute | solution.py:23
  31.3 1.2 copy-start.2
  32.5 8.5 %copy-start.11 = (bf16[32,2048]{1,0:T(8,128)(2,1)S(1)}, bf16[32,2048]{1,0:T(8,128)(2,1)}, u32[]{:S(2)}) copy-start(bf16[32,2048]{1,0:T(8,128)(2,1)} %param.17) | copy-start | bytes 393220
  34.5 1.0 copy-start.7
  36.2 9.3 %collective-permute-start.4 = (f32[2,32,1,256]{3,2,1,0:T(1,128)}, f32[2,32,1,256]{3,2,1,0:T(1,128)S(1)}, u32[]{:S(2)}, u32[]{:S(2)}) collective-permute-start(f32[2,32,1,256]{3,2,1,0:T(1,128)} %get-tuple-element.80), channel_id=1, source_target_pairs={{0,8},{8,16},{16,24},{1,9},{9,17},{17,25},{2,10},{10,18},{18,26},{... | collective-permute-start | bytes 196616 | tf_op jit(solution)/shard_map/ppermute | solution.py:22
  39.7 6.2 %collective-permute-start.5 = (f32[2,32,1,256]{3,2,1,0:T(1,128)S(1)}, f32[2,32,1,256]{3,2,1,0:T(1,128)S(1)}, u32[]{:S(2)}, u32[]{:S(2)}) collective-permute-start(f32[2,32,1,256]{3,2,1,0:T(1,128)S(1)} %get-tuple-element.81), channel_id=1, source_target_pairs={{8,0},{16,8},{24,16},{9,1},{17,9},{25,17},{10,2},{18,10},{26,18},{... | collective-permute-start | bytes 196616 | tf_op jit(solution)/shard_map/ppermute | solution.py:23
  41.6 51.8 %all-to-all-start = ((bf16[32,4,512]{2,0,1:T(8,128)(2,1)}), bf16[32,4,512]{2,0,1:T(8,128)(2,1)S(1)}, u32[]{:S(2)}, u32[]{:S(2)}) async-start(bf16[32,4,512]{2,0,1:T(8,128)(2,1)} %bitcast.46), calls=%async_computation | async-start | bytes 262144 | tf_op jit(solution)/shard_map/all_to_all | solution.py:65
  49.3 8.6 %copy-start.13 = (s32[4]{0:T(128)S(1)}, s32[4]{0:T(128)}, u32[]{:S(2)}) copy-start(s32[4]{0:T(128)} %param.19) | copy-start | bytes 52
  51.2 6.8 %collective-permute-start.6 = (f32[2,32,34,1]{2,1,3,0:T(8,128)S(1)}, f32[2,32,34,1]{2,1,3,0:T(8,128)S(1)}, u32[]{:S(2)}, u32[]{:S(2)}) collective-permute-start(f32[2,32,34,1]{2,1,3,0:T(8,128)S(1)} %copy.32), channel_id=1, source_target_pairs={{0,2},{2,4},{4,6},{1,3},{3,5},{5,7},{8,10},{10,12},{12,14},{9,11},... | collective-permute-start | bytes 26120 | tf_op jit(solution)/shard_map/ppermute | solution.py:22
  56.4 4.0 %collective-permute-start.7 = (f32[2,32,34,1]{2,1,3,0:T(8,128)S(1)}, f32[2,32,34,1]{2,1,3,0:T(8,128)}, u32[]{:S(2)}, u32[]{:S(2)}) collective-permute-start(f32[2,32,34,1]{2,1,3,0:T(8,128)S(1)} %copy.33), channel_id=1, source_target_pairs={{2,0},{4,2},{6,4},{3,1},{5,3},{7,5},{10,8},{12,10},{14,12},{11,9},... | collective-permute-start | bytes 26120 | tf_op jit(solution)/shard_map/ppermute | solution.py:23
  67.2 1.2 copy-start.3
  67.2 1.5 %copy-start.8 = (f32[32,32,256]{2,1,0:T(8,128)S(1)}, f32[32,32,256]{2,1,0:T(8,128)}, u32[]{:S(2)}) copy-start(f32[32,32,256]{2,1,0:T(8,128)} %copy-done.7) | copy-start | bytes 3145732
  68.8 8.0 %copy-start.12 = (s32[2048]{0:T(1024)S(1)}, s32[2048]{0:T(1024)}, u32[]{:S(2)}) copy-start(s32[2048]{0:T(1024)} %param.18) | copy-start | bytes 24580
  70.6 1.0 copy-start.5
  71.8 5.6 %collective-permute-start.8 = (f32[2,32,1,256]{3,2,1,0:T(1,128)S(1)}, f32[2,32,1,256]{3,2,1,0:T(1,128)S(1)}, u32[]{:S(2)}, u32[]{:S(2)}) collective-permute-start(f32[2,32,1,256]{3,2,1,0:T(1,128)S(1)} %get-tuple-element.78), channel_id=1, source_target_pairs={{0,8},{8,16},{16,24},{1,9},{9,17},{17,25},{2,10},{10,18},{18,26},{... | collective-permute-start | bytes 196616 | tf_op jit(solution)/shard_map/ppermute | solution.py:22
  75.5 6.2 %collective-permute-start.9 = (f32[2,32,1,256]{3,2,1,0:T(1,128)S(1)}, f32[2,32,1,256]{3,2,1,0:T(1,128)S(1)}, u32[]{:S(2)}, u32[]{:S(2)}) collective-permute-start(f32[2,32,1,256]{3,2,1,0:T(1,128)S(1)} %get-tuple-element.79), channel_id=1, source_target_pairs={{8,0},{16,8},{24,16},{9,1},{17,9},{25,17},{10,2},{18,10},{26,18},{... | collective-permute-start | bytes 196616 | tf_op jit(solution)/shard_map/ppermute | solution.py:23
  86.9 30.3 %collective-permute-start.10 = (f32[2,32,34,1]{2,1,3,0:T(8,128)S(1)}, f32[2,32,34,1]{2,1,3,0:T(8,128)S(1)}, u32[]{:S(2)}, u32[]{:S(2)}) collective-permute-start(f32[2,32,34,1]{2,1,3,0:T(8,128)S(1)} %copy.36), channel_id=1, source_target_pairs={{0,2},{2,4},{4,6},{1,3},{3,5},{5,7},{8,10},{10,12},{12,14},{9,11},... | collective-permute-start | bytes 26120 | tf_op jit(solution)/shard_map/ppermute | solution.py:22
  91.9 27.0 %collective-permute-start.11 = (f32[2,32,34,1]{2,1,3,0:T(8,128)S(1)}, f32[2,32,34,1]{2,1,3,0:T(8,128)S(1)}, u32[]{:S(2)}, u32[]{:S(2)}) collective-permute-start(f32[2,32,34,1]{2,1,3,0:T(8,128)S(1)} %copy.37), channel_id=1, source_target_pairs={{2,0},{4,2},{6,4},{3,1},{5,3},{7,5},{10,8},{12,10},{14,12},{11,9},... | collective-permute-start | bytes 26120 | tf_op jit(solution)/shard_map/ppermute | solution.py:23
  125.0 1.2 copy-start.4
  125.0 1.5 %copy-start.6 = (f32[32,32,256]{2,1,0:T(8,128)S(1)}, f32[32,32,256]{2,1,0:T(8,128)}, u32[]{:S(2)}) copy-start(f32[32,32,256]{2,1,0:T(8,128)} %copy-done.5) | copy-start | bytes 3145732
  125.0 1.8 %copy-start.9 = (f32[4,8,32,256]{3,2,1,0:T(8,128)S(1)}, f32[4,8,32,256]{3,2,1,0:T(8,128)}, u32[]{:S(2)}) copy-start(f32[4,8,32,256]{3,2,1,0:T(8,128)} %copy.45) | copy-start | bytes 3145732
  125.0 2.1 %copy-start.10 = (bf16[2,32,32,256]{3,2,1,0:T(8,128)(2,1)S(1)}, bf16[2,32,32,256]{3,2,1,0:T(8,128)(2,1)}, u32[]{:S(2)}) copy-start(bf16[2,32,32,256]{3,2,1,0:T(8,128)(2,1)} %param.12) | copy-start | bytes 3145732
where the time goes:
time: 153 us; the launch traced here: 151 us
  local copies, waits for them, and re-layouts  40.6 us (27%)
  starting transfers between devices  31.9 us (21%)
  other arithmetic  26.6 us (17%)
  matrix products  22.4 us (15%)
  blocking collectives  16.4 us (11%)
  waiting for transfers between devices  12.6 us (8%)
    dot_general x4, matrix products, deposit_block(): jnp.dot(rows_part, onehot, preferred_element_type=jnp.float32)  21.3 us
    ppermute x6, starting transfers between devices, extended(): before = lax.ppermute(last, axis, up)  19.9 us
    concatenate x6, other arithmetic, extended(): x = jnp.concatenate([before, x, after], axis=dim)  16.7 us
    all_to_all x1, blocking collectives, per_device(): lax.all_to_all(rhs, 'rad', split_axis=1, concat_axis=0, tiled=True)  16.4 us
    ppermute x6, waiting for transfers between devices, extended(): after = lax.ppermute(first, axis, down)  11.5 us
    slice x6, local copies, waits for them, and re-layouts, extended(): last = lax.slice_in_dim(x, length - width, length, axis=dim)  11.2 us
    unnamed x32, local copies, waits for them, and re-layouts  10.5 us
    ppermute x6, starting transfers between devices, extended(): after = lax.ppermute(first, axis, down)  8.14 us
  transfers between devices with their start and end apart: 13, of which 7 were waited for; matrix products, arithmetic and copies ran while one was open for 36% of the time, Pallas kernels for 0%

commit v1 on v0

v1 whole, which is shorter than its diff:
```python
import functools

import jax
import jax.numpy as jnp
from jax import lax
from jax.experimental import pallas as pl
from jax.experimental.pallas import tpu as pltpu
from jax.sharding import PartitionSpec as P

PICARD = 3
GHOST = 3

relax_coef = 0.25
advect_coef = 0.1


def _shift_pairs(n_rows, n_cols, dr, dc):
    pairs = []
    for r in range(n_rows):
        for c in range(n_cols):
            rr, cc = r + dr, c + dc
            if 0 <= rr < n_rows and 0 <= cc < n_cols:
                pairs.append((r * n_cols + c, rr * n_cols + cc))
    return pairs


def _halo(x, n_cap, n_lat):
    g = GHOST
    rows, cols = x.shape[2], x.shape[3]
    top_src = x[:, :, rows - g:, :]
    bot_src = x[:, :, :g, :]
    left_src = x[:, :, :, cols - g:]
    right_src = x[:, :, :, :g]
    both = ("cap", "lat")
    top = lax.ppermute(top_src, "cap", _shift_pairs(n_cap, 1, 1, 0))
    bot = lax.ppermute(bot_src, "cap", _shift_pairs(n_cap, 1, -1, 0))
    left = lax.ppermute(left_src, "lat", _shift_pairs(1, n_lat, 0, 1))
    right = lax.ppermute(right_src, "lat", _shift_pairs(1, n_lat, 0, -1))
    tl = lax.ppermute(x[:, :, rows - g:, cols - g:], both, _shift_pairs(n_cap, n_lat, 1, 1))
    tr = lax.ppermute(x[:, :, rows - g:, :g], both, _shift_pairs(n_cap, n_lat, 1, -1))
    bl = lax.ppermute(x[:, :, :g, cols - g:], both, _shift_pairs(n_cap, n_lat, -1, 1))
    br = lax.ppermute(x[:, :, :g, :g], both, _shift_pairs(n_cap, n_lat, -1, -1))
    return top, bot, left, right, tl, tr, bl, br


def _extend(main, top, bot, left, right, tl, tr, bl, br, ext_rows, ext_cols):
    g = GHOST
    layers, rows, cols = main.shape
    zc = ext_cols - cols - 2 * g
    zr = ext_rows - rows - 2 * g

    def row_band(mid, rgt, lft, n):
        z = jnp.zeros((layers, n, zc), main.dtype)
        return jnp.concatenate([mid, rgt, z, lft], axis=2)

    band_main = row_band(main, right, left, rows)
    band_bot = row_band(bot, br, bl, g)
    band_top = row_band(top, tr, tl, g)
    zero_rows = jnp.zeros((layers, zr, ext_cols), main.dtype)
    return jnp.concatenate([band_main, band_bot, zero_rows, band_top], axis=1)


def _inside_mask(rows, cols, ext_rows, ext_cols, c, d, n_cap, n_lat):
    g = GHOST
    i = jnp.arange(ext_rows, dtype=jnp.int32)
    j = jnp.arange(ext_cols, dtype=jnp.int32)
    local_r = jnp.where(i < rows + g, i, jnp.where(i >= ext_rows - g, i - ext_rows, -10**6))
    local_c = jnp.where(j < cols + g, j, jnp.where(j >= ext_cols - g, j - ext_cols, -10**6))
    glob_r = c * rows + local_r
    glob_c = d * cols + local_c
    ok_r = (local_r > -10**5) & (glob_r >= 0) & (glob_r < n_cap * rows)
    ok_c = (local_c > -10**5) & (glob_c >= 0) & (glob_c < n_lat * cols)
    return (ok_r[:, None] & ok_c[None, :]).astype(jnp.float32)


def _sweep_kernel(rad_ref, lam_ref, eta_ref, mask_ref, vel_ref, dep_ref, send_ref, keep_ref):
    lam = lam_ref[...]
    eta = eta_ref[...]
    m = mask_ref[...][None] > 0.5
    n_r, n_c = lam.shape[1], lam.shape[2]
    rows, cols = dep_ref.shape[1], dep_ref.shape[2]

    def up(x):
        return pltpu.roll(x, n_r - 1, 1)

    def dn(x):
        return pltpu.roll(x, 1, 1)

    def rt(x):
        return pltpu.roll(x, n_c - 1, 2)

    def lf(x):
        return pltpu.roll(x, 1, 2)

    ca = 0.5 * (eta + up(eta))
    cd = dn(ca)
    cb = 0.5 * (eta + rt(eta))
    cl = lf(cb)
    w = lam
    for _ in range(PICARD):
        total = ca * (up(w) - w)
        total = total + cd * (dn(w) - w)
        total = total + cb * (rt(w) - w)
        total = total + cl * (lf(w) - w)
        w = jnp.where(m, lam + relax_coef * total, 0.0)
    v0 = vel_ref[0].astype(jnp.float32)
    v1 = vel_ref[1].astype(jnp.float32)
    da = (up(lam) - dn(lam))[:, :rows, :cols]
    db = (rt(lam) - lf(lam))[:, :rows, :cols]
    adv = v0 * da + v1 * db
    rhs = w[:, :rows, :cols] + advect_coef * adv + dep_ref[...]
    half = rows // 2
    lo = rhs[:, :half, :]
    hi = rhs[:, half:, :]
    is_zero = rad_ref[0] == 0
    send_ref[...] = jnp.where(is_zero, hi, lo)
    keep_ref[...] = jnp.where(is_zero, lo, hi)


def _sweeps(rad_idx, lam_ext, eta_ext, mask, vel, dep, block_layers):
    layers, ext_r, ext_c = lam_ext.shape
    rows, cols = dep.shape[1], dep.shape[2]
    half = rows // 2
    grid = (layers // block_layers,)
    out_shape = [jax.ShapeDtypeStruct((layers, half, cols), jnp.float32)] * 2
    return pl.pallas_call(
        _sweep_kernel,
        out_shape=out_shape,
        grid=grid,
        in_specs=[
            pl.BlockSpec(memory_space=pltpu.SMEM),
            pl.BlockSpec((block_layers, ext_r, ext_c), lambda i: (i, 0, 0)),
            pl.BlockSpec((block_layers, ext_r, ext_c), lambda i: (i, 0, 0)),
            pl.BlockSpec((ext_r, ext_c), lambda i: (0, 0)),
            pl.BlockSpec((2, block_layers, rows, cols), lambda i: (0, i, 0, 0)),
            pl.BlockSpec((block_layers, rows, cols), lambda i: (i, 0, 0)),
        ],
        out_specs=[
            pl.BlockSpec((block_layers, half, cols), lambda i: (i, 0, 0)),
            pl.BlockSpec((block_layers, half, cols), lambda i: (i, 0, 0)),
        ],
    )(rad_idx, lam_ext, eta_ext, mask, vel, dep)


def per_device(
    adjoint_temp,
    velocity,
    visc_flow,
    visc_yield,
    yield_mask,
    radial_inverse,
    marker_rows,
    recv_cells,
    recv_counts,
):
    layers, rows, cols = adjoint_temp.shape
    n_cap = lax.axis_size("cap")
    n_lat = lax.axis_size("lat")
    n_rad = lax.axis_size("rad")
    c = lax.axis_index("cap")
    d = lax.axis_index("lat")
    r = lax.axis_index("rad")

    received = lax.all_to_all(marker_rows, "lat", split_axis=1, concat_axis=1, tiled=True)

    flow = visc_flow.astype(jnp.float32)
    plast = visc_yield.astype(jnp.float32)
    eta = jnp.where(yield_mask == 1, flow * plast / (flow + plast), flow)

    stacked = jnp.stack([adjoint_temp, eta])
    pieces = _halo(stacked, n_cap, n_lat)
    ext_rows = ((rows + 2 * GHOST + 7) // 8) * 8
    ext_cols = ((cols + 2 * GHOST + 127) // 128) * 128
    lam_ext = _extend(adjoint_temp, *[p[0] for p in pieces], ext_rows, ext_cols)
    eta_ext = _extend(eta, *[p[1] for p in pieces], ext_rows, ext_cols)
    mask = _inside_mask(rows, cols, ext_rows, ext_cols, c, d, n_cap, n_lat)

    senders = n_lat
    slot_total = received.shape[1]
    per_sender = slot_total // senders
    live = (jnp.arange(per_sender, dtype=jnp.int32)[None, :] < recv_counts[:, None]).reshape(-1)
    cell_a = recv_cells // cols
    cell_b = recv_cells % cols
    hit_a = (cell_a[None, :] == jnp.arange(rows, dtype=jnp.int32)[:, None]) & live[None, :]
    xa = jnp.where(hit_a[None], received[:, None, :], jnp.zeros((), received.dtype))
    onehot_b = (cell_b[:, None] == jnp.arange(cols, dtype=jnp.int32)[None, :]).astype(received.dtype)
    deposit = jnp.einsum("las,sb->lab", xa, onehot_b, preferred_element_type=jnp.float32)

    rad_idx = r.astype(jnp.int32).reshape(1)
    n_chunks = 2
    chunk = layers // n_chunks
    block_layers = 4
    keeps = []
    recvs = []
    for k in range(n_chunks):
        sl = slice(k * chunk, (k + 1) * chunk)
        send, keep = _sweeps(
            rad_idx, lam_ext[sl], eta_ext[sl], mask, velocity[:, sl], deposit[sl], block_layers
        )
        recvs.append(lax.ppermute(send, "rad", _shift_pairs(1, n_rad, 0, 1) + _shift_pairs(1, n_rad, 0, -1)))
        keeps.append(keep)

    full_layers = radial_inverse.shape[0]
    mine = jnp.concatenate(keeps, axis=0)
    theirs = jnp.concatenate(recvs, axis=0)
    columns = jnp.concatenate([mine, theirs], axis=0)
    my_cols = lax.dynamic_slice_in_dim(radial_inverse, r * layers, layers, axis=1)
    peer_cols = lax.dynamic_slice_in_dim(radial_inverse, (1 - r) * layers, layers, axis=1)
    r_perm = jnp.concatenate([my_cols, peer_cols], axis=1)
    result = jnp.dot(
        r_perm, columns.reshape(full_layers, -1), precision=lax.Precision.HIGHEST
    )
    return result.reshape(columns.shape)


def solution(mesh):
    in_specs = (
        P("rad", "cap", "lat"),
        P(None, "rad", "cap", "lat"),
        P("rad", "cap", "lat"),
        P("rad", "cap", "lat"),
        P("rad", "cap", "lat"),
        P(),
        P("rad", ("cap", "lat")),
        P(("cap", "lat")),
        P(("cap", "lat")),
    )
    out_specs = P(None, ("cap", "rad"), "lat")
    return jax.shard_map(
        per_device, mesh=mesh, in_specs=in_specs, out_specs=out_specs, check_vma=False
    )
```

time: 153 us -> 89 us (0.58)
  matrix products: 22.4 us -> 3.8 us
  other arithmetic: 26.6 us -> 8.52 us
  blocking collectives: 16.4 us -> 0 us
  local copies, waits for them, and re-layouts: 40.6 us -> 24.3 us
  Pallas kernels: 0 us -> 11.3 us
  waiting for transfers between devices: 12.6 us -> 8.65 us
    dot_general x5 -> x2, matrix products: 22.4 us -> 3.8 us  [the longest x1 2.21 us: per_device(): jnp.einsum('las,sb->lab', xa, onehot_b, preferred_element_type=jnp.float32)]
    all_to_all x1 -> x0, blocking collectives: 16.4 us -> none  [per_device(): lax.all_to_all(rhs, 'rad', split_axis=1, concat_axis=0, tiled=True)]
    concatenate x6 -> x3, other arithmetic: 16.7 us -> 1.92 us  [the longest x1 1.02 us: per_device(): columns = jnp.concatenate([mine, theirs], axis=0)]
    pallas_call x0 -> x2, Pallas kernels: none -> 11.3 us  [_sweeps(): pl.pallas_call(_sweep_kernel, out_shape=out_shape, grid=grid, in_specs=[p...]
    ppermute x6 -> x0, local copies, waits for them, and re-layouts: 10.6 us -> none  [the longest x3 5.69 us: extended(): after = lax.ppermute(first, axis, down)]
    add x3 -> x0, other arithmetic: 6.86 us -> none  [the longest x2 3.87 us: per_device(): adjoint_temp + relax_coef * viscous(padded[0], padded[1], iterate, eta)]
    squeeze x3 -> x6, local copies, waits for them, and re-layouts: 0.77 us -> 7.55 us  [per_device(): eta_ext = _extend(eta, *[p[1] for p in pieces], ext_rows, ext_cols)]
    unnamed x32 -> x31, local copies, waits for them, and re-layouts: 10.5 us -> 3.91 us
  transfers between devices with their start and end apart: 13 -> 11, of which waited for: 7 -> 2; matrix products, arithmetic and copies ran while one was open for 36% -> 29% of each run, Pallas kernels for 0% -> 6%
where the time goes in v1:
time: 89 us; the launch traced here: 87.9 us
  starting transfers between devices  31.1 us (35%)
  local copies, waits for them, and re-layouts  24.3 us (27%)
  Pallas kernels  11.3 us (13%)
  waiting for transfers between devices  8.65 us (10%)
  other arithmetic  8.52 us (10%)
  matrix products  3.8 us (4%)
    pallas_call x2, Pallas kernels, _sweeps(): pl.pallas_call(_sweep_kernel, out_shape=out_shape, grid=grid, in_specs=[p...  11.3 us
    ppermute x1, starting transfers between devices, _halo(): lax.ppermute(x[:, :, rows - g:, cols - g:], both, _shift_pairs(n_cap, n_l...  9.4 us
    ppermute x2, waiting for transfers between devices, per_device(): lax.ppermute(send, 'rad', _shift_pairs(1, n_rad, 0, 1) + _shift_pairs(1,...  8.62 us
    squeeze x6, local copies, waits for them, and re-layouts, per_device(): eta_ext = _extend(eta, *[p[1] for p in pieces], ext_rows, ext_cols)  7.55 us
    all_to_all x1, starting transfers between devices, per_device(): lax.all_to_all(marker_rows, 'lat', split_axis=1, concat_axis=1, tiled=True)  5.45 us
    ppermute x1, starting transfers between devices, _halo(): top = lax.ppermute(top_src, 'cap', _shift_pairs(n_cap, 1, 1, 0))  5.27 us
    unnamed x31, local copies, waits for them, and re-layouts  3.91 us
    another operation x3, other arithmetic, per_device(): stacked = jnp.stack([adjoint_temp, eta])  3.2 us
  transfers between devices with their start and end apart: 11, of which 2 were waited for; matrix products, arithmetic and copies ran while one was open for 29% of the time, Pallas kernels for 6%

profile of v1, /device:TPU:0, one launch (start us, length us, event | category | flops | bytes accessed | tf_op | source)
XLA Modules:
  0.0 87.9 jit_solution(13704328526555571378)
XLA Ops:
  0.0 1.9 %convert_select_fusion = f32[32,32,256]{2,1,0:T(8,128)S(1)} fusion(bf16[32,32,256]{2,1,0:T(8,128)(2,1)} %param.11, bf16[32,32,256]{2,1,0:T(8,128)(2,1)} %param.12, s32[32,32,256]{2,1,0:T(8,128)} %param.13), kind=kLoop, calls=%fused_computation.35 | loop fusion | flops 1835008 | bytes 3145728 | tf_op jit(solution)/shard_map/jit(_where)/select_n | solution.py:168
  1.9 0.9 %fusion.28 = (f32[2,32,3,3]{3,2,1,0:T(4,128)}, f32[2,32,3,3]{3,2,1,0:T(4,128)}, f32[2,32,3,3]{3,2,1,0:T(4,128)S(1)}, f32[2,32,3,3]{3,2,1,0:T(4,128)}) fusion(f32[1,32,32,256]{3,2,1,0:T(8,128)S(1)} %bitcast.60, f32[1,32,32,256]{3,2,1,0:T(8,128)S(1)} %bitcast.57), kind=kLoop, calls=%fused_computation.51 | loop fusion | flops 2304 | bytes 2106368 | tf_op jit(solution)/shard_map/stack | solution.py:170
  2.9 1.3 %collective-permute-start.3 = (f32[2,32,3,3]{3,2,1,0:T(4,128)}, f32[2,32,3,3]{3,2,1,0:T(4,128)}, u32[]{:S(2)}, u32[]{:S(2)}) collective-permute-start(f32[2,32,3,3]{3,2,1,0:T(4,128)} %get-tuple-element.17), channel_id=1, source_target_pairs={{10,0},{12,2},{14,4},{18,8},{20,10},{22,12},{26,16},{28,18},{30,20... | collective-permute-start | bytes 6920 | tf_op jit(solution)/shard_map/ppermute | solution.py:42
  4.2 1.3 %collective-permute-start.4 = (f32[2,32,3,3]{3,2,1,0:T(4,128)}, f32[2,32,3,3]{3,2,1,0:T(4,128)}, u32[]{:S(2)}, u32[]{:S(2)}) collective-permute-start(f32[2,32,3,3]{3,2,1,0:T(4,128)} %get-tuple-element.18), channel_id=1, source_target_pairs={{8,2},{10,4},{12,6},{16,10},{18,12},{20,14},{24,18},{26,20},{28,22... | collective-permute-start | bytes 6920 | tf_op jit(solution)/shard_map/ppermute | solution.py:41
  5.5 1.3 %collective-permute-start.6 = (f32[2,32,3,3]{3,2,1,0:T(4,128)}, f32[2,32,3,3]{3,2,1,0:T(4,128)}, u32[]{:S(2)}, u32[]{:S(2)}) collective-permute-start(f32[2,32,3,3]{3,2,1,0:T(4,128)} %get-tuple-element.20), channel_id=1, source_target_pairs={{2,8},{4,10},{6,12},{10,16},{12,18},{14,20},{18,24},{20,26},{22,28... | collective-permute-start | bytes 6920 | tf_op jit(solution)/shard_map/ppermute | solution.py:40
  6.8 9.4 %collective-permute-start.7 = (f32[2,32,3,3]{3,2,1,0:T(4,128)S(1)}, f32[2,32,3,3]{3,2,1,0:T(4,128)}, u32[]{:S(2)}, u32[]{:S(2)}) collective-permute-start(f32[2,32,3,3]{3,2,1,0:T(4,128)S(1)} %get-tuple-element.19), channel_id=1, source_target_pairs={{0,10},{2,12},{4,14},{8,18},{10,20},{12,22},{16,26},{18,28},{20,30... | collective-permute-start | bytes 6920 | tf_op jit(solution)/shard_map/ppermute | solution.py:39
  16.2 1.3 %fusion.18 = (f32[2,32,32,3]{3,2,1,0:T(8,128)}, f32[2,32,32,3]{3,2,1,0:T(8,128)S(1)}) fusion(f32[1,32,32,256]{3,2,1,0:T(8,128)S(1)} %bitcast.61, f32[1,32,32,256]{3,2,1,0:T(8,128)S(1)} %bitcast.58), kind=kLoop, calls=%fused_computation.39 | loop fusion | flops 12288 | bytes 2146304 | tf_op jit(solution)/shard_map/stack | solution.py:170
  17.5 2.3 %copy.21 = f32[2,32,32,3]{2,1,3,0:T(8,128)} copy(f32[2,32,32,3]{3,2,1,0:T(8,128)} %get-tuple-element.13) | data formatting | bytes 49152 | tf_op jit(solution)/shard_map/slice | solution.py:33
  19.9 1.3 %collective-permute-start = (f32[2,32,32,3]{2,1,3,0:T(8,128)}, f32[2,32,32,3]{2,1,3,0:T(8,128)}, u32[]{:S(2)}, u32[]{:S(2)}) collective-permute-start(f32[2,32,32,3]{2,1,3,0:T(8,128)} %copy.21), channel_id=1, source_target_pairs={{2,0},{4,2},{6,4},{3,1},{5,3},{7,5},{10,8},{12,10},{14,12},{11,9},... | collective-permute-start | bytes 73736 | tf_op jit(solution)/shard_map/ppermute | solution.py:38
  21.2 0.0 copy-done.9
  21.2 0.7 copy.48
  21.8 5.4 %all-to-all-start = ((bf16[32,4,512]{2,0,1:T(8,128)(2,1)}), bf16[32,4,512]{2,0,1:T(8,128)(2,1)S(1)}, u32[]{:S(2)}, u32[]{:S(2)}) async-start(bf16[32,4,512]{2,0,1:T(8,128)(2,1)} %bitcast.56), calls=%async_computation | async-start | bytes 262144 | tf_op jit(solution)/shard_map/all_to_all | solution.py:164
  27.4 0.1 fusion.33
  27.4 2.2 %fusion.41 = (bf16[2,16,32,256]{3,2,1,0:T(8,128)(2,1)}, bf16[2,16,32,256]{3,2,1,0:T(8,128)(2,1)}) fusion(bf16[2,32,32,256]{3,2,1,0:T(8,128)(2,1)} %param.10), kind=kLoop, calls=%fused_computation.97 | loop fusion | bytes 2097152 | tf_op jit(solution)/shard_map/slice | solution.py:198
  29.7 0.7 and_convert_fusion.mask_ref
  30.4 0.7 fusion.26
  31.1 0.9 %fusion.24 = (f32[2,32,3,256]{3,2,1,0:T(4,128)}, f32[2,32,3,256]{3,2,1,0:T(4,128)}) fusion(f32[1,32,32,256]{3,2,1,0:T(8,128)S(1)} %bitcast.62, f32[1,32,32,256]{3,2,1,0:T(8,128)S(1)} %bitcast.59), kind=kLoop, calls=%fused_computation.46 | loop fusion | flops 98304 | bytes 2490368 | tf_op jit(solution)/shard_map/stack | solution.py:170
  32.0 1.1 %copy.23 = f32[2,32,32,3]{2,1,3,0:T(8,128)} copy(f32[2,32,32,3]{3,2,1,0:T(8,128)S(1)} %get-tuple-element.14) | data formatting | bytes 49152 | tf_op jit(solution)/shard_map/slice | solution.py:32
  33.1 0.1 pad.19.clone
  33.2 0.1 pad.25.clone
  33.3 0.0 collective-permute-done.3
  33.3 2.4 %collective-permute-start.1 = (f32[2,32,32,3]{2,1,3,0:T(8,128)}, f32[2,32,32,3]{2,1,3,0:T(8,128)S(1)}, u32[]{:S(2)}, u32[]{:S(2)}) collective-permute-start(f32[2,32,32,3]{2,1,3,0:T(8,128)} %copy.23), channel_id=1, source_target_pairs={{0,2},{2,4},{4,6},{1,3},{3,5},{5,7},{8,10},{10,12},{12,14},{9,11},... | collective-permute-start | bytes 73736 | tf_op jit(solution)/shard_map/ppermute | solution.py:37
  35.7 0.9 %slice_bitcast_fusion.7 = (f32[32,3,3]{2,1,0:T(4,128)S(1)}, f32[32,3,3]{2,1,0:T(4,128)S(1)}) fusion(f32[2,32,3,3]{3,2,1,0:T(4,128)} %collective-permute-done.3), kind=kLoop, calls=%fused_computation.62 | loop fusion | bytes 4608 | tf_op jit(solution)/shard_map/squeeze | solution.py:175
  36.6 0.0 collective-permute-done.4
  36.6 1.3 %collective-permute-start.2 = (f32[2,32,3,256]{3,2,1,0:T(4,128)}, f32[2,32,3,256]{3,2,1,0:T(4,128)}, u32[]{:S(2)}, u32[]{:S(2)}) collective-permute-start(f32[2,32,3,256]{3,2,1,0:T(4,128)} %get-tuple-element.15), channel_id=1, source_target_pairs={{8,0},{16,8},{24,16},{9,1},{17,9},{25,17},{10,2},{18,10},{26,18},{... | collective-permute-start | bytes 589832 | tf_op jit(solution)/shard_map/ppermute | solution.py:36
  37.9 1.5 %slice_bitcast_fusion.6 = (f32[32,3,3]{2,1,0:T(4,128)}, f32[32,3,3]{2,1,0:T(4,128)S(1)}) fusion(f32[2,32,3,3]{3,2,1,0:T(4,128)} %collective-permute-done.4), kind=kLoop, calls=%fused_computation.61 | loop fusion | bytes 4608 | tf_op jit(solution)/shard_map/squeeze | solution.py:175
  39.4 0.0 collective-permute-done.6
  39.4 5.3 %collective-permute-start.5 = (f32[2,32,3,256]{3,2,1,0:T(4,128)}, f32[2,32,3,256]{3,2,1,0:T(4,128)}, u32[]{:S(2)}, u32[]{:S(2)}) collective-permute-start(f32[2,32,3,256]{3,2,1,0:T(4,128)} %get-tuple-element.16), channel_id=1, source_target_pairs={{0,8},{8,16},{16,24},{1,9},{9,17},{17,25},{2,10},{10,18},{18,26},{... | collective-permute-start | bytes 589832 | tf_op jit(solution)/shard_map/ppermute | solution.py:35
  44.7 1.6 %slice_bitcast_fusion.5 = (f32[32,3,3]{2,1,0:T(4,128)}, f32[32,3,3]{2,1,0:T(4,128)}) fusion(f32[2,32,3,3]{3,2,1,0:T(4,128)} %collective-permute-done.6), kind=kLoop, calls=%fused_computation.60 | loop fusion | bytes 4608 | tf_op jit(solution)/shard_map/squeeze | solution.py:175
  46.2 0.0 collective-permute-done.7
  46.2 1.6 %slice_bitcast_fusion.4 = (f32[32,3,3]{2,1,0:T(4,128)}, f32[32,3,3]{2,1,0:T(4,128)}) fusion(f32[2,32,3,3]{3,2,1,0:T(4,128)} %collective-permute-done.7), kind=kLoop, calls=%fused_computation.59 | loop fusion | bytes 4608 | tf_op jit(solution)/shard_map/squeeze | solution.py:175
  47.8 0.0 collective-permute-done
  47.8 0.8 fusion.42
  48.6 0.0 collective-permute-done.1
  48.6 0.6 fusion.43
  49.3 1.1 %copy.33 = f32[1,32,32,3]{3,2,1,0:T(8,128)} copy(f32[1,32,32,3]{2,1,3,0:T(8,128)S(1)} %get-tuple-element.41) | data formatting | bytes 24576
  50.3 1.1 %copy.34 = f32[1,32,32,3]{3,2,1,0:T(8,128)} copy(f32[1,32,32,3]{2,1,3,0:T(8,128)S(1)} %get-tuple-element.43) | data formatting | bytes 24576
  51.4 0.3 copy.31
  51.6 1.1 %copy.32 = f32[1,32,32,3]{3,2,1,0:T(8,128)S(1)} copy(f32[1,32,32,3]{2,1,3,0:T(8,128)} %get-tuple-element.44) | data formatting | bytes 24576
  52.7 0.0 all-to-all-done
  52.7 2.2 %fusion = f32[32,32,256]{2,1,0:T(8,128)S(1)} fusion(pred[32,2048]{1,0:T(8,128)(4,1)} %fusion.26, bf16[32,2048]{1,0:T(8,128)(2,1)S(1)} %bitcast.70, s32[2048]{0:T(1024)S(1)} %get-tuple-element.47), kind=kOutput, calls=%fused_computation.14 | convolution fusion | flops 1076363264 | bytes 1253376 | tf_op jit(solution)/shard_map/las,sb->lab/dot_general | solution.py:187
  55.0 0.0 copy-start.2
  55.0 0.0 copy-start.4
  55.0 0.0 copy-start.6
  55.0 1.1 %fusion.40 = (f32[16,32,256]{2,1,0:T(8,128)}, f32[16,32,256]{2,1,0:T(8,128)}) fusion(f32[32,32,256]{2,1,0:T(8,128)S(1)} %fusion), kind=kLoop, calls=%fused_computation.96 | loop fusion | bytes 2097152 | tf_op jit(solution)/shard_map/slice | solution.py:198
  56.1 0.0 collective-permute-done.2
  56.1 1.0 %slice_bitcast_fusion.1 = (f32[32,3,256]{2,1,0:T(4,128)S(1)}, f32[32,3,256]{2,1,0:T(4,128)S(1)}) fusion(f32[2,32,3,256]{3,2,1,0:T(4,128)} %collective-permute-done.2), kind=kLoop, calls=%fused_computation.55 | loop fusion | bytes 393216 | tf_op jit(solution)/shard_map/squeeze | solution.py:175
  57.2 0.0 collective-permute-done.5
  57.2 1.0 %slice_bitcast_fusion = (f32[32,3,256]{2,1,0:T(4,128)S(1)}, f32[32,3,256]{2,1,0:T(4,128)S(1)}) fusion(f32[2,32,3,256]{3,2,1,0:T(4,128)} %collective-permute-done.5), kind=kLoop, calls=%fused_computation.54 | loop fusion | bytes 393216 | tf_op jit(solution)/shard_map/squeeze | solution.py:175
  58.3 0.5 fusion.14
  58.7 0.4 copy-done.3
  59.1 0.0 copy-done.5
  59.1 0.5 fusion.10
  59.6 2.0 %fusion.38 = (f32[16,40,384]{2,1,0:T(8,128)}, f32[16,40,384]{2,1,0:T(8,128)}, f32[16,40,384]{2,1,0:T(8,128)}, f32[16,40,384]{2,1,0:T(8,128)}) fusion(f32[32,40,384]{2,1,0:T(8,128)S(1)} %fusion.14, f32[32,40,384]{2,1,0:T(8,128)S(1)} %fusion.10), kind=kLoop, calls=%fused_computation.94 | loop fusion | bytes 7864320 | tf_op jit(solution)/shard_map/slice | solution.py:198
  61.6 5.7 %shard_map.91 = (f32[16,16,256]{2,1,0:T(8,128)}, f32[16,16,256]{2,1,0:T(8,128)}) custom-call(s32[1]{0:T(128)} %bitcast.1.rad_ref, f32[16,40,384]{2,1,0:T(8,128)} %get-tuple-element.50.lam_ref, f32[16,40,384]{2,1,0:T(8,128)} %get-tuple-element.21.eta_ref, f32[40,384]{1,0:T(8,128)} %and_convert_fusion.mask_ref, ...), custom_call_target="tpu_custom_call" | custom-call | tf_op jit(solution)/shard_map/pallas_call | solution.py:126
  67.3 1.6 %collective-permute-start.8 = (f32[16,16,256]{2,1,0:T(8,128)}, f32[16,16,256]{2,1,0:T(8,128)S(1)}, u32[]{:S(2)}, u32[]{:S(2)}) collective-permute-start(f32[16,16,256]{2,1,0:T(8,128)} %get-tuple-element.11), channel_id=1, source_target_pairs={{0,1},{1,0},{2,3},{3,2},{4,5},{5,4},{6,7},{7,6},{8,9},{9,8},{10,11... | collective-permute-start | bytes 786440 | tf_op jit(solution)/shard_map/ppermute | solution.py:200
  68.8 5.6 %shard_map.92 = (f32[16,16,256]{2,1,0:T(8,128)}, f32[16,16,256]{2,1,0:T(8,128)}) custom-call(s32[1]{0:T(128)} %bitcast.1.rad_ref, f32[16,40,384]{2,1,0:T(8,128)} %get-tuple-element.49.lam_ref, f32[16,40,384]{2,1,0:T(8,128)} %get-tuple-element.22.eta_ref, f32[40,384]{1,0:T(8,128)} %and_convert_fusion.mask_ref, ...), custom_call_target="tpu_custom_call" | custom-call | tf_op jit(solution)/shard_map/pallas_call | solution.py:126
  74.5 0.5 collective-permute-start.9
  75.0 0.1 constant_dynamic-slice_fusion.1
  75.1 1.5 %collective-permute-done.8 = f32[16,16,256]{2,1,0:T(8,128)S(1)} collective-permute-done((f32[16,16,256]{2,1,0:T(8,128)}, f32[16,16,256]{2,1,0:T(8,128)S(1)}, u32[]{:S(2)}, u32[]{:S(2)}) %collective-permute-start.8) | collective-permute-done | bytes 262176 | tf_op jit(solution)/shard_map/ppermute | solution.py:200
  76.6 7.1 %collective-permute-done.9 = f32[16,16,256]{2,1,0:T(8,128)S(1)} collective-permute-done((f32[16,16,256]{2,1,0:T(8,128)}, f32[16,16,256]{2,1,0:T(8,128)S(1)}, u32[]{:S(2)}, u32[]{:S(2)}) %collective-permute-start.9) | collective-permute-done | bytes 262176 | tf_op jit(solution)/shard_map/ppermute | solution.py:200
  83.7 1.0 %pad_maximum_fusion.4 = f32[64,16,256]{2,1,0:T(8,128)S(1)} fusion(f32[16,16,256]{2,1,0:T(8,128)S(1)} %collective-permute-done.9, f32[16,16,256]{2,1,0:T(8,128)S(1)} %collective-permute-done.8, f32[16,16,256]{2,1,0:T(8,128)} %get-tuple-element.10, f32[16,16,256]{2,1,0:T(8,128)S(1)} %copy-done.8), kind=kLoop, calls=%fused_computation.44 | loop fusion | flops 786432 | bytes 2097152 | tf_op jit(solution)/shard_map/concatenate | solution.py:206
  84.7 1.6 %fusion.20 = f32[64,16,256]{2,0,1:T(8,128)S(1)} fusion(f32[64,32]{1,0:T(8,128)S(1)} %get-tuple-element.46, f32[64,32]{1,0:T(8,128)S(1)} %get-tuple-element.45, f32[8,8,16,256]{3,2,1,0:T(8,128)S(1)} %bitcast.63), kind=kOutput, calls=%fused_computation.41 | convolution fusion | flops 201330688 | bytes 2113536 | tf_op jit(solution)/shard_map/dot_general | solution.py:210
  86.3 1.6 %copy.30 = f32[64,16,256]{2,1,0:T(8,128)} copy(f32[64,16,256]{2,0,1:T(8,128)S(1)} %fusion.20) | data formatting | bytes 2097152 | tf_op jit(solution)/shard_map/dot_general | solution.py:210
  (28 shorter events, 0.1 us)
Async XLA Ops:
  0.0 1.9 %copy-start = (f32[32,32,256]{2,1,0:T(8,128)S(1)}, f32[32,32,256]{2,1,0:T(8,128)}, u32[]{:S(2)}) copy-start(f32[32,32,256]{2,1,0:T(8,128)} %param.9) | copy-start | bytes 3145732
  2.9 30.4 %collective-permute-start.3 = (f32[2,32,3,3]{3,2,1,0:T(4,128)}, f32[2,32,3,3]{3,2,1,0:T(4,128)}, u32[]{:S(2)}, u32[]{:S(2)}) collective-permute-start(f32[2,32,3,3]{3,2,1,0:T(4,128)} %get-tuple-element.17), channel_id=1, source_target_pairs={{10,0},{12,2},{14,4},{18,8},{20,10},{22,12},{26,16},{28,18},{30,20... | collective-permute-start | bytes 6920 | tf_op jit(solution)/shard_map/ppermute | solution.py:42
  4.2 32.4 %collective-permute-start.4 = (f32[2,32,3,3]{3,2,1,0:T(4,128)}, f32[2,32,3,3]{3,2,1,0:T(4,128)}, u32[]{:S(2)}, u32[]{:S(2)}) collective-permute-start(f32[2,32,3,3]{3,2,1,0:T(4,128)} %get-tuple-element.18), channel_id=1, source_target_pairs={{8,2},{10,4},{12,6},{16,10},{18,12},{20,14},{24,18},{26,20},{28,22... | collective-permute-start | bytes 6920 | tf_op jit(solution)/shard_map/ppermute | solution.py:41
  5.5 33.9 %collective-permute-start.6 = (f32[2,32,3,3]{3,2,1,0:T(4,128)}, f32[2,32,3,3]{3,2,1,0:T(4,128)}, u32[]{:S(2)}, u32[]{:S(2)}) collective-permute-start(f32[2,32,3,3]{3,2,1,0:T(4,128)} %get-tuple-element.20), channel_id=1, source_target_pairs={{2,8},{4,10},{6,12},{10,16},{12,18},{14,20},{18,24},{20,26},{22,28... | collective-permute-start | bytes 6920 | tf_op jit(solution)/shard_map/ppermute | solution.py:40
  6.8 14.4 %copy-start.9 = (bf16[32,2048]{1,0:T(8,128)(2,1)S(1)}, bf16[32,2048]{1,0:T(8,128)(2,1)}, u32[]{:S(2)}) copy-start(bf16[32,2048]{1,0:T(8,128)(2,1)} %param.15) | copy-start | bytes 393220
  6.8 20.5 %copy-start.11 = (s32[2048]{0:T(1024)S(1)}, s32[2048]{0:T(1024)}, u32[]{:S(2)}) copy-start(s32[2048]{0:T(1024)} %param.16) | copy-start | bytes 24580
  6.8 20.6 %copy-start.12 = (s32[4]{0:T(128)S(1)}, s32[4]{0:T(128)}, u32[]{:S(2)}) copy-start(s32[4]{0:T(128)} %param.17) | copy-start | bytes 52
  6.8 39.4 %collective-permute-start.7 = (f32[2,32,3,3]{3,2,1,0:T(4,128)S(1)}, f32[2,32,3,3]{3,2,1,0:T(4,128)}, u32[]{:S(2)}, u32[]{:S(2)}) collective-permute-start(f32[2,32,3,3]{3,2,1,0:T(4,128)S(1)} %get-tuple-element.19), channel_id=1, source_target_pairs={{0,10},{2,12},{4,14},{8,18},{10,20},{12,22},{16,26},{18,28},{20,30... | collective-permute-start | bytes 6920 | tf_op jit(solution)/shard_map/ppermute | solution.py:39
  19.9 27.9 %collective-permute-start = (f32[2,32,32,3]{2,1,3,0:T(8,128)}, f32[2,32,32,3]{2,1,3,0:T(8,128)}, u32[]{:S(2)}, u32[]{:S(2)}) collective-permute-start(f32[2,32,32,3]{2,1,3,0:T(8,128)} %copy.21), channel_id=1, source_target_pairs={{2,0},{4,2},{6,4},{3,1},{5,3},{7,5},{10,8},{12,10},{14,12},{11,9},... | collective-permute-start | bytes 73736 | tf_op jit(solution)/shard_map/ppermute | solution.py:38
  21.8 30.9 %all-to-all-start = ((bf16[32,4,512]{2,0,1:T(8,128)(2,1)}), bf16[32,4,512]{2,0,1:T(8,128)(2,1)S(1)}, u32[]{:S(2)}, u32[]{:S(2)}) async-start(bf16[32,4,512]{2,0,1:T(8,128)(2,1)} %bitcast.56), calls=%async_computation | async-start | bytes 262144 | tf_op jit(solution)/shard_map/all_to_all | solution.py:164
  33.3 15.4 %collective-permute-start.1 = (f32[2,32,32,3]{2,1,3,0:T(8,128)}, f32[2,32,32,3]{2,1,3,0:T(8,128)S(1)}, u32[]{:S(2)}, u32[]{:S(2)}) collective-permute-start(f32[2,32,32,3]{2,1,3,0:T(8,128)} %copy.23), channel_id=1, source_target_pairs={{0,2},{2,4},{4,6},{1,3},{3,5},{5,7},{8,10},{10,12},{12,14},{9,11},... | collective-permute-start | bytes 73736 | tf_op jit(solution)/shard_map/ppermute | solution.py:37
  36.6 19.6 %collective-permute-start.2 = (f32[2,32,3,256]{3,2,1,0:T(4,128)}, f32[2,32,3,256]{3,2,1,0:T(4,128)}, u32[]{:S(2)}, u32[]{:S(2)}) collective-permute-start(f32[2,32,3,256]{3,2,1,0:T(4,128)} %get-tuple-element.15), channel_id=1, source_target_pairs={{8,0},{16,8},{24,16},{9,1},{17,9},{25,17},{10,2},{18,10},{26,18},{... | collective-permute-start | bytes 589832 | tf_op jit(solution)/shard_map/ppermute | solution.py:36
  39.4 17.8 %collective-permute-start.5 = (f32[2,32,3,256]{3,2,1,0:T(4,128)}, f32[2,32,3,256]{3,2,1,0:T(4,128)}, u32[]{:S(2)}, u32[]{:S(2)}) collective-permute-start(f32[2,32,3,256]{3,2,1,0:T(4,128)} %get-tuple-element.16), channel_id=1, source_target_pairs={{0,8},{8,16},{16,24},{1,9},{9,17},{17,25},{2,10},{10,18},{18,26},{... | collective-permute-start | bytes 589832 | tf_op jit(solution)/shard_map/ppermute | solution.py:35
  54.9 3.3 %copy-start.1 = (f32[1,32,32,3]{3,2,1,0:T(8,128)S(1)}, f32[1,32,32,3]{3,2,1,0:T(8,128)}, u32[]{:S(2)}) copy-start(f32[1,32,32,3]{3,2,1,0:T(8,128)} %copy.33) | copy-start | bytes 36868
  55.0 3.3 %copy-start.2 = (f32[1,32,32,3]{3,2,1,0:T(8,128)S(1)}, f32[1,32,32,3]{3,2,1,0:T(8,128)}, u32[]{:S(2)}) copy-start(f32[1,32,32,3]{3,2,1,0:T(8,128)} %copy.34) | copy-start | bytes 36868
  55.0 3.3 %copy-start.4 = (f32[32,3,3]{2,1,0:T(4,128)S(1)}, f32[32,3,3]{2,1,0:T(4,128)}, u32[]{:S(2)}) copy-start(f32[32,3,3]{2,1,0:T(4,128)} %get-tuple-element.35) | copy-start | bytes 3460
  55.0 3.3 %copy-start.6 = (f32[32,3,3]{2,1,0:T(4,128)S(1)}, f32[32,3,3]{2,1,0:T(4,128)}, u32[]{:S(2)}) copy-start(f32[32,3,3]{2,1,0:T(4,128)} %get-tuple-element.37) | copy-start | bytes 3460
  55.0 3.3 %copy-start.7 = (f32[32,3,3]{2,1,0:T(4,128)S(1)}, f32[32,3,3]{2,1,0:T(4,128)}, u32[]{:S(2)}) copy-start(f32[32,3,3]{2,1,0:T(4,128)} %get-tuple-element.39) | copy-start | bytes 3460
  58.3 0.8 copy-start.3
  58.3 0.9 copy-start.5
  67.3 7.8 %copy-start.10 = (f32[64,64]{1,0:T(8,128)S(1)}, f32[64,64]{1,0:T(8,128)}, u32[]{:S(2)}) copy-start(f32[64,64]{1,0:T(8,128)} %param.14) | copy-start | bytes 49156
  67.3 16.5 %copy-start.8 = (f32[16,16,256]{2,1,0:T(8,128)S(1)}, f32[16,16,256]{2,1,0:T(8,128)}, u32[]{:S(2)}) copy-start(f32[16,16,256]{2,1,0:T(8,128)} %get-tuple-element.9) | copy-start | bytes 786436
  67.3 9.4 %collective-permute-start.8 = (f32[16,16,256]{2,1,0:T(8,128)}, f32[16,16,256]{2,1,0:T(8,128)S(1)}, u32[]{:S(2)}, u32[]{:S(2)}) collective-permute-start(f32[16,16,256]{2,1,0:T(8,128)} %get-tuple-element.11), channel_id=1, source_target_pairs={{0,1},{1,0},{2,3},{3,2},{4,5},{5,4},{6,7},{7,6},{8,9},{9,8},{10,11... | collective-permute-start | bytes 786440 | tf_op jit(solution)/shard_map/ppermute | solution.py:200
  74.5 9.2 %collective-permute-start.9 = (f32[16,16,256]{2,1,0:T(8,128)}, f32[16,16,256]{2,1,0:T(8,128)S(1)}, u32[]{:S(2)}, u32[]{:S(2)}) collective-permute-start(f32[16,16,256]{2,1,0:T(8,128)} %get-tuple-element.12), channel_id=1, source_target_pairs={{0,1},{1,0},{2,3},{3,2},{4,5},{5,4},{6,7},{7,6},{8,9},{9,8},{10,11... | collective-permute-start | bytes 786440 | tf_op jit(solution)/shard_map/ppermute | solution.py:200

commit v2 on v1

v2 whole, which is shorter than its diff:
```python
import jax
import jax.numpy as jnp
from jax import lax
from jax.experimental import pallas as pl
from jax.experimental.pallas import tpu as pltpu
from jax.sharding import PartitionSpec as P

PICARD = 3
GHOST = 3

relax_coef = 0.25
advect_coef = 0.1


def _inside_mask(rows, cols, ext_rows, ext_cols, c, d, n_cap, n_lat):
    g = GHOST
    far = -(1 << 20)
    i = jnp.arange(ext_rows, dtype=jnp.int32)
    j = jnp.arange(ext_cols, dtype=jnp.int32)
    local_r = jnp.where(i < rows + g, i, jnp.where(i >= ext_rows - g, i - ext_rows, far))
    local_c = jnp.where(j < cols + g, j, jnp.where(j >= ext_cols - g, j - ext_cols, far))
    glob_r = c * rows + local_r
    glob_c = d * cols + local_c
    ok_r = (local_r > far) & (glob_r >= 0) & (glob_r < n_cap * rows)
    ok_c = (local_c > far) & (glob_c >= 0) & (glob_c < n_lat * cols)
    return (ok_r[:, None] & ok_c[None, :]).astype(jnp.float32)


def _pairs(n, step):
    return [(i, i + step) for i in range(n) if 0 <= i + step < n]


def _sweep_kernel(rad_ref, lam_ref, eta_ref, rowh_ref, colh_ref, mask_ref, vel_ref, dep_ref,
                  send_ref, keep_ref, lam_x, eta_x):
    layers, rows, cols = lam_ref.shape
    n_r, n_c = lam_x.shape[1], lam_x.shape[2]
    for ref, src, k in ((lam_x, lam_ref, 0), (eta_x, eta_ref, 1)):
        ref[:, :rows, :cols] = src[...]
        ref[:, rows:, :cols] = rowh_ref[k]
        ref[:, :, cols:] = colh_ref[k]
    lam = lam_x[...]
    eta = eta_x[...]
    m = mask_ref[...][None]

    def up(x):
        return pltpu.roll(x, n_r - 1, 1)

    def dn(x):
        return pltpu.roll(x, 1, 1)

    def rt(x):
        return pltpu.roll(x, n_c - 1, 2)

    def lf(x):
        return pltpu.roll(x, 1, 2)

    ca_raw = 0.5 * (eta + up(eta))
    cb_raw = 0.5 * (eta + rt(eta))
    mq = relax_coef * m
    ca = ca_raw * mq
    cd = dn(ca_raw) * mq
    cb = cb_raw * mq
    cl = lf(cb_raw) * mq
    w = lam
    for _ in range(PICARD - 1):
        total = ca * (up(w) - w)
        total = total + cd * (dn(w) - w)
        total = total + cb * (rt(w) - w)
        total = total + cl * (lf(w) - w)
        w = lam + total

    def main(x):
        return x[:, :rows, :cols]

    wm = main(w)
    total = main(ca) * (main(up(w)) - wm)
    total = total + main(cd) * (main(dn(w)) - wm)
    total = total + main(cb) * (main(rt(w)) - wm)
    total = total + main(cl) * (main(lf(w)) - wm)
    w3 = main(lam) + total
    v0 = vel_ref[0].astype(jnp.float32)
    v1 = vel_ref[1].astype(jnp.float32)
    adv = v0 * main(up(lam) - dn(lam)) + v1 * main(rt(lam) - lf(lam))
    rhs = w3 + advect_coef * adv + dep_ref[...]
    half = rows // 2
    lo = rhs[:, :half, :]
    hi = rhs[:, half:, :]
    is_zero = rad_ref[0] == 0
    send_ref[...] = jnp.where(is_zero, hi, lo)
    keep_ref[...] = jnp.where(is_zero, lo, hi)


def _sweeps(rad_idx, lam, eta, rowh, colh, mask, vel, dep, first_layer, n_layers, block_layers):
    _, rows, cols = lam.shape
    ext_r, ext_c = mask.shape
    half = rows // 2
    off = first_layer // block_layers
    bl = block_layers
    grid = (n_layers // bl,)
    out_shape = [jax.ShapeDtypeStruct((n_layers, half, cols), jnp.float32)] * 2
    return pl.pallas_call(
        _sweep_kernel,
        out_shape=out_shape,
        grid=grid,
        in_specs=[
            pl.BlockSpec(memory_space=pltpu.SMEM),
            pl.BlockSpec((bl, rows, cols), lambda i: (i + off, 0, 0)),
            pl.BlockSpec((bl, rows, cols), lambda i: (i + off, 0, 0)),
            pl.BlockSpec((2, bl, ext_r - rows, cols), lambda i: (0, i + off, 0, 0)),
            pl.BlockSpec((2, bl, ext_r, ext_c - cols), lambda i: (0, i + off, 0, 0)),
            pl.BlockSpec((ext_r, ext_c), lambda i: (0, 0)),
            pl.BlockSpec((2, bl, rows, cols), lambda i: (0, i + off, 0, 0)),
            pl.BlockSpec((bl, rows, cols), lambda i: (i + off, 0, 0)),
        ],
        out_specs=[
            pl.BlockSpec((bl, half, cols), lambda i: (i, 0, 0)),
            pl.BlockSpec((bl, half, cols), lambda i: (i, 0, 0)),
        ],
        scratch_shapes=[
            pltpu.VMEM((bl, ext_r, ext_c), jnp.float32),
            pltpu.VMEM((bl, ext_r, ext_c), jnp.float32),
        ],
    )(rad_idx, lam, eta, rowh, colh, mask, vel, dep)


def per_device(
    adjoint_temp,
    velocity,
    visc_flow,
    visc_yield,
    yield_mask,
    radial_inverse,
    marker_rows,
    recv_cells,
    recv_counts,
):
    layers, rows, cols = adjoint_temp.shape
    n_cap = lax.axis_size("cap")
    n_lat = lax.axis_size("lat")
    n_rad = lax.axis_size("rad")
    c = lax.axis_index("cap")
    d = lax.axis_index("lat")
    r = lax.axis_index("rad")

    received = lax.all_to_all(marker_rows, "lat", split_axis=1, concat_axis=1, tiled=True)

    flow = visc_flow.astype(jnp.float32)
    plast = visc_yield.astype(jnp.float32)
    eta = jnp.where(yield_mask == 1, flow * plast / (flow + plast), flow)

    g = GHOST
    ext_rows = ((rows + 2 * g + 7) // 8) * 8
    ext_cols = ((cols + 2 * g + 127) // 128) * 128
    top_send = jnp.concatenate([adjoint_temp[:, rows - g:], eta[:, rows - g:]], axis=1)
    bot_send = jnp.concatenate([adjoint_temp[:, :g], eta[:, :g]], axis=1)
    top = lax.ppermute(top_send, "cap", _pairs(n_cap, 1))
    bot = lax.ppermute(bot_send, "cap", _pairs(n_cap, -1))
    zr = jnp.zeros((layers, ext_rows - rows - 2 * g, cols), jnp.float32)
    rowh = jnp.stack([
        jnp.concatenate([bot[:, :g], zr, top[:, :g]], axis=1),
        jnp.concatenate([bot[:, g:], zr, top[:, g:]], axis=1),
    ])

    def col_piece(sl):
        parts = []
        for k, src in enumerate((adjoint_temp, eta)):
            parts.append(jnp.concatenate([src[:, :, sl], rowh[k][:, :, sl]], axis=1))
        return jnp.stack(parts)

    left_send = col_piece(slice(0, g)).reshape(-1)
    right_send = col_piece(slice(cols - g, cols)).reshape(-1)
    from_right = lax.ppermute(left_send, "lat", _pairs(n_lat, -1)).reshape(2, layers, ext_rows, g)
    from_left = lax.ppermute(right_send, "lat", _pairs(n_lat, 1)).reshape(2, layers, ext_rows, g)
    zc = jnp.zeros((2, layers, ext_rows, ext_cols - cols - 2 * g), jnp.float32)
    colh = jnp.concatenate([from_right, zc, from_left], axis=3)
    mask = _inside_mask(rows, cols, ext_rows, ext_cols, c, d, n_cap, n_lat)

    senders = n_lat
    slot_total = received.shape[1]
    per_sender = slot_total // senders
    live = (jnp.arange(per_sender, dtype=jnp.int32)[None, :] < recv_counts[:, None]).reshape(-1)
    cell_a = recv_cells // cols
    cell_b = recv_cells % cols
    hit_a = (cell_a[None, :] == jnp.arange(rows, dtype=jnp.int32)[:, None]) & live[None, :]
    xa = jnp.where(hit_a[None], received[:, None, :], jnp.zeros((), received.dtype))
    onehot_b = (cell_b[:, None] == jnp.arange(cols, dtype=jnp.int32)[None, :]).astype(received.dtype)
    deposit = jnp.einsum("las,sb->lab", xa, onehot_b, preferred_element_type=jnp.float32)

    rad_idx = r.astype(jnp.int32).reshape(1)
    n_chunks = 4
    chunk = layers // n_chunks
    block_layers = 4
    keeps = []
    recvs = []
    for k in range(n_chunks):
        send, keep = _sweeps(
            rad_idx, adjoint_temp, eta, rowh, colh, mask, velocity, deposit,
            k * chunk, chunk, block_layers,
        )
        recvs.append(lax.ppermute(send, "rad", _pairs(n_rad, 1) + _pairs(n_rad, -1)))
        keeps.append(keep)

    full_layers = radial_inverse.shape[0]
    mine = jnp.concatenate(keeps, axis=0)
    theirs = jnp.concatenate(recvs, axis=0)
    columns = jnp.concatenate([mine, theirs], axis=0)
    my_cols = lax.dynamic_slice_in_dim(radial_inverse, r * layers, layers, axis=1)
    peer_cols = lax.dynamic_slice_in_dim(radial_inverse, (1 - r) * layers, layers, axis=1)
    r_perm = jnp.concatenate([my_cols, peer_cols], axis=1)
    result = jnp.dot(
        r_perm, columns.reshape(full_layers, -1), precision=lax.Precision.HIGHEST
    )
    return result.reshape(columns.shape)


def solution(mesh):
    in_specs = (
        P("rad", "cap", "lat"),
        P(None, "rad", "cap", "lat"),
        P("rad", "cap", "lat"),
        P("rad", "cap", "lat"),
        P("rad", "cap", "lat"),
        P(),
        P("rad", ("cap", "lat")),
        P(("cap", "lat")),
        P(("cap", "lat")),
    )
    out_specs = P(None, ("cap", "rad"), "lat")
    return jax.shard_map(
        per_device, mesh=mesh, in_specs=in_specs, out_specs=out_specs, check_vma=False
    )
```

time: 89 us -> 71.1 us (0.80)
  starting transfers between devices: 31.1 us -> 19.5 us
  local copies, waits for them, and re-layouts: 24.3 us -> 12.8 us
  waiting for transfers between devices: 8.65 us -> 12.6 us
  Pallas kernels: 11.3 us -> 14.3 us
  other arithmetic: 8.52 us -> 7.11 us
    ppermute x10 -> x8, starting transfers between devices: 25.6 us -> 16.2 us  [the longest x1 6.25 us: per_device(): top = lax.ppermute(top_send, 'cap', _pairs(n_cap, 1))]
    squeeze x6 -> x0, local copies, waits for them, and re-layouts: 7.55 us -> none  [per_device(): eta_ext = _extend(eta, *[p[1] for p in pieces], ext_rows, ext_cols)]
    slice x7 -> x13, local copies, waits for them, and re-layouts: 10.3 us -> 3.5 us  [the longest x10 2.26 us: col_piece(): parts.append(jnp.concatenate([src[:, :, sl], rowh[k][:, :, sl]], axis=1))]
    reshape x0 -> x4, local copies, waits for them, and re-layouts: none -> 4.13 us  [the longest x1 1.18 us: per_device(): lax.ppermute(left_send, 'lat', _pairs(n_lat, -1))]
    pallas_call x2 -> x4, Pallas kernels: 11.3 us -> 14.3 us  [_sweeps(): pl.pallas_call(_sweep_kernel, out_shape=out_shape, grid=grid, in_specs=[p...]
    unnamed x31 -> x34, local copies, waits for them, and re-layouts: 3.91 us -> 1.61 us
    ppermute x10 -> x8, waiting for transfers between devices: 8.64 us -> 10.8 us  [the longest x4 10.8 us: per_device(): lax.ppermute(send, 'rad', _pairs(n_rad, 1) + _pairs(n_rad, -1))]
    all_to_all x1, starting transfers between devices: 5.45 us -> 3.32 us  [per_device(): lax.all_to_all(marker_rows, 'lat', split_axis=1, concat_axis=1, tiled=True)]
  transfers between devices with their start and end apart: 11 -> 9, of which waited for: 2 -> 5; matrix products, arithmetic and copies ran while one was open for 29% -> 15% of each run, Pallas kernels for 6% -> 0%
where the time goes in v2:
time: 71.1 us; the launch traced here: 70.7 us
  starting transfers between devices  19.5 us (27%)
  Pallas kernels  14.3 us (20%)
  local copies, waits for them, and re-layouts  12.8 us (18%)
  waiting for transfers between devices  12.6 us (18%)
  other arithmetic  7.11 us (10%)
  matrix products  3.95 us (6%)
    pallas_call x4, Pallas kernels, _sweeps(): pl.pallas_call(_sweep_kernel, out_shape=out_shape, grid=grid, in_specs=[p...  14.3 us
    ppermute x4, waiting for transfers between devices, per_device(): lax.ppermute(send, 'rad', _pairs(n_rad, 1) + _pairs(n_rad, -1))  10.8 us
    ppermute x1, starting transfers between devices, per_device(): top = lax.ppermute(top_send, 'cap', _pairs(n_cap, 1))  6.25 us
    ppermute x4, starting transfers between devices, per_device(): lax.ppermute(send, 'rad', _pairs(n_rad, 1) + _pairs(n_rad, -1))  4.13 us
    all_to_all x1, starting transfers between devices, per_device(): lax.all_to_all(marker_rows, 'lat', split_axis=1, concat_axis=1, tiled=True)  3.32 us
    ppermute x1, starting transfers between devices, per_device(): lax.ppermute(right_send, 'lat', _pairs(n_lat, 1))  3.21 us
    dot_general x1, matrix products, per_device(): jnp.einsum('las,sb->lab', xa, onehot_b, preferred_element_type=jnp.float32)  2.36 us
    slice x10, local copies, waits for them, and re-layouts, col_piece(): parts.append(jnp.concatenate([src[:, :, sl], rowh[k][:, :, sl]], axis=1))  2.26 us
  transfers between devices with their start and end apart: 9, of which 5 were waited for; matrix products, arithmetic and copies ran while one was open for 15% of the time, Pallas kernels for 0%

profile of v2, /device:TPU:0, one launch (start us, length us, event | category | flops | bytes accessed | tf_op | source)
XLA Modules:
  0.0 70.7 jit_solution(14568212064747906653)
XLA Ops:
  0.0 1.9 %convert_select_fusion.eta_ref = f32[32,32,256]{2,1,0:T(8,128)S(1)} fusion(bf16[32,32,256]{2,1,0:T(8,128)(2,1)} %param.11, bf16[32,32,256]{2,1,0:T(8,128)(2,1)} %param.12, s32[32,32,256]{2,1,0:T(8,128)} %param.13), kind=kLoop, calls=%fused_computation.7 | loop fusion | flops 1835008 | bytes 3145728 | tf_op jit(solution)/shard_map/jit(_where)/select_n | solution.py:149
  1.9 0.0 copy-start
  1.9 0.0 copy-start.2
  2.0 0.1 fusion.23
  2.1 0.8 %pad_maximum_fusion.2 = f32[32,6,256]{2,1,0:T(8,128)} fusion(f32[32,3,256]{2,1,0:T(4,128)S(1)} %get-tuple-element.44, f32[32,3,256]{2,1,0:T(4,128)S(1)} %get-tuple-element.25), kind=kLoop, calls=%fused_computation.17 | loop fusion | flops 49152 | bytes 393216 | tf_op jit(solution)/shard_map/concatenate | solution.py:155
  2.8 1.3 %collective-permute-start = (f32[32,6,256]{2,1,0:T(8,128)}, f32[32,6,256]{2,1,0:T(8,128)S(1)}, u32[]{:S(2)}, u32[]{:S(2)}) collective-permute-start(f32[32,6,256]{2,1,0:T(8,128)} %pad_maximum_fusion.2), channel_id=1, source_target_pairs={{8,0},{16,8},{24,16},{9,1},{17,9},{25,17},{10,2},{18,10},{26,18},{... | collective-permute-start | bytes 589832 | tf_op jit(solution)/shard_map/ppermute | solution.py:157
  4.1 0.7 %pad_maximum_fusion.3 = f32[32,6,256]{2,1,0:T(8,128)} fusion(f32[32,3,256]{2,1,0:T(4,128)S(1)} %get-tuple-element.43, f32[32,3,256]{2,1,0:T(4,128)S(1)} %get-tuple-element.26), kind=kLoop, calls=%fused_computation.18 | loop fusion | flops 49152 | bytes 393216 | tf_op jit(solution)/shard_map/concatenate | solution.py:154
  4.9 6.2 %collective-permute-start.1 = (f32[32,6,256]{2,1,0:T(8,128)}, f32[32,6,256]{2,1,0:T(8,128)}, u32[]{:S(2)}, u32[]{:S(2)}) collective-permute-start(f32[32,6,256]{2,1,0:T(8,128)} %pad_maximum_fusion.3), channel_id=1, source_target_pairs={{0,8},{8,16},{16,24},{1,9},{9,17},{17,25},{2,10},{10,18},{18,26},{... | collective-permute-start | bytes 589832 | tf_op jit(solution)/shard_map/ppermute | solution.py:156
  11.1 0.7 copy.54
  11.8 3.3 %all-to-all-start = ((bf16[32,4,512]{2,0,1:T(8,128)(2,1)}), bf16[32,4,512]{2,0,1:T(8,128)(2,1)S(1)}, u32[]{:S(2)}, u32[]{:S(2)}) async-start(bf16[32,4,512]{2,0,1:T(8,128)(2,1)} %bitcast.40), calls=%async_computation | async-start | bytes 262144 | tf_op jit(solution)/shard_map/all_to_all | solution.py:145
  15.1 0.2 fusion.22
  15.3 0.2 fusion.21
  15.5 0.0 copy-start.7
  15.6 0.0 copy-start.8
  15.6 0.3 copy.27
  15.9 0.3 copy.39
  16.1 0.3 copy.32
  16.4 0.3 copy.40
  16.7 0.1 pad.21.clone
  16.8 0.1 pad.1.clone
  16.9 0.1 fusion.16
  17.0 0.7 and_convert_fusion.mask_ref
  17.7 0.1 fusion.12
  17.8 0.1 constant_dynamic-slice_fusion.1
  17.9 1.8 %all-to-all-done = bf16[32,4,512]{2,0,1:T(8,128)(2,1)S(1)} async-done(((bf16[32,4,512]{2,0,1:T(8,128)(2,1)}), bf16[32,4,512]{2,0,1:T(8,128)(2,1)S(1)}, u32[]{:S(2)}, u32[]{:S(2)}) %all-to-all-start) | async-done | bytes 131104 | tf_op jit(solution)/shard_map/all_to_all | solution.py:145
  19.7 2.4 %fusion.dep_ref = f32[32,32,256]{2,1,0:T(8,128)} fusion(pred[32,2048]{1,0:T(8,128)(4,1)S(1)} %fusion.12, bf16[32,2048]{1,0:T(8,128)(2,1)S(1)} %bitcast.46, s32[2048]{0:T(1024)S(1)} %get-tuple-element.39), kind=kOutput, calls=%fused_computation | convolution fusion | flops 1076363264 | bytes 1253376 | tf_op jit(solution)/shard_map/las,sb->lab/dot_general | solution.py:187
  22.1 0.1 fusion.27
  22.1 1.1 %fusion.28 = (f32[32,3,256]{2,1,0:T(4,128)S(1)}, f32[32,3,256]{2,1,0:T(4,128)S(1)}) fusion(f32[32,6,256]{2,1,0:T(8,128)} %collective-permute-done.1), kind=kLoop, calls=%fused_computation.72 | loop fusion | bytes 393216 | tf_op jit(solution)/shard_map/slice | solution.py:160
  23.2 0.1 pad_maximum_fusion.4
  23.4 0.1 fusion.26
  23.5 0.3 copy.28
  23.7 0.1 fusion.25
  23.9 0.3 copy.26
  24.1 0.1 maximum_bitcast_fusion.1
  24.2 0.1 maximum_bitcast_fusion
  24.3 0.5 copy.29
  24.9 0.9 %reshape.111 = f32[7680]{0:T(1024)S(1)} reshape(f32[2,32,40,3]{3,2,1,0:T(8,128)S(1)} %copy.29) | data formatting | bytes 61440 | tf_op jit(solution)/shard_map/reshape | solution.py:170
  25.7 1.3 %collective-permute-start.2 = (f32[7680]{0:T(1024)S(1)}, f32[7680]{0:T(1024)S(1)}, u32[]{:S(2)}, u32[]{:S(2)}) collective-permute-start(f32[7680]{0:T(1024)S(1)} %reshape.111), channel_id=1, source_target_pairs={{2,0},{4,2},{6,4},{3,1},{5,3},{7,5},{10,8},{12,10},{14,12},{11,9},... | collective-permute-start | bytes 92168 | tf_op jit(solution)/shard_map/ppermute | solution.py:172
  27.0 0.3 copy.33
  27.3 0.3 copy.31
  27.6 0.1 maximum_bitcast_fusion.3
  27.7 0.1 maximum_bitcast_fusion.2
  27.8 0.5 copy.34
  28.3 0.9 %reshape.113 = f32[7680]{0:T(1024)S(1)} reshape(f32[2,32,40,3]{3,2,1,0:T(8,128)S(1)} %copy.34) | data formatting | bytes 61440 | tf_op jit(solution)/shard_map/reshape | solution.py:171
  29.2 3.2 %collective-permute-start.3 = (f32[7680]{0:T(1024)S(1)}, f32[7680]{0:T(1024)S(1)}, u32[]{:S(2)}, u32[]{:S(2)}) collective-permute-start(f32[7680]{0:T(1024)S(1)} %reshape.113), channel_id=1, source_target_pairs={{0,2},{2,4},{4,6},{1,3},{3,5},{5,7},{8,10},{10,12},{12,14},{9,11},... | collective-permute-start | bytes 92168 | tf_op jit(solution)/shard_map/ppermute | solution.py:173
  32.4 0.8 %pad_maximum_fusion.1.rowh_ref = f32[2,32,8,256]{3,2,1,0:T(8,128)} fusion(f32[1,32,8,256]{3,2,1,0:T(8,128)S(1)} %bitcast.42, f32[1,32,8,256]{3,2,1,0:T(8,128)S(1)} %bitcast.41), kind=kLoop, calls=%fused_computation.16 | loop fusion | flops 131072 | bytes 1048576 | tf_op jit(solution)/shard_map/stack | solution.py:159
  33.3 1.2 %reshape.112 = f32[2,32,40,3]{3,2,1,0:T(8,128)S(1)} reshape(f32[7680]{0:T(1024)S(1)} %collective-permute-done.2) | data formatting | bytes 61440 | tf_op jit(solution)/shard_map/reshape | solution.py:172
  34.5 1.2 %reshape.114 = f32[2,32,40,3]{3,2,1,0:T(8,128)S(1)} reshape(f32[7680]{0:T(1024)S(1)} %collective-permute-done.3) | data formatting | bytes 61440 | tf_op jit(solution)/shard_map/reshape | solution.py:173
  35.6 1.5 %pad_maximum_fusion.colh_ref = f32[2,32,40,128]{3,2,1,0:T(8,128)} fusion(f32[2,32,40,3]{3,2,1,0:T(8,128)S(1)} %reshape.114, f32[2,32,40,3]{3,2,1,0:T(8,128)S(1)} %reshape.112, f32[128]{0:T(128)S(1)} %pad.1.clone), kind=kLoop, calls=%fused_computation.10 | loop fusion | flops 655360 | bytes 1372672 | tf_op jit(solution)/shard_map/concatenate | solution.py:175
  37.1 3.5 %shard_map.94 = (f32[8,16,256]{2,1,0:T(8,128)}, f32[8,16,256]{2,1,0:T(8,128)}) custom-call(s32[1]{0:T(128)} %bitcast.1.rad_ref, f32[32,32,256]{2,1,0:T(8,128)} %lam_ref.7, f32[32,32,256]{2,1,0:T(8,128)} %copy-done, f32[2,32,8,256]{3,2,1,0:T(8,128)} %pad_maximum_fusion.1.rowh_ref, f32[2,32,40,128]{3,2,1,0:T(8,128)} %pad_maximum_fusion.colh_ref, ...), custom_call_target="tpu_custom_call" | custom-call | tf_op jit(solution)/shard_map/pallas_call | solution.py:101
  40.7 3.6 %shard_map.93 = (f32[8,16,256]{2,1,0:T(8,128)}, f32[8,16,256]{2,1,0:T(8,128)}) custom-call(s32[1]{0:T(128)} %bitcast.1.rad_ref, f32[32,32,256]{2,1,0:T(8,128)} %lam_ref.7, f32[32,32,256]{2,1,0:T(8,128)} %copy-done, f32[2,32,8,256]{3,2,1,0:T(8,128)} %pad_maximum_fusion.1.rowh_ref, f32[2,32,40,128]{3,2,1,0:T(8,128)} %pad_maximum_fusion.colh_ref, ...), custom_call_target="tpu_custom_call" | custom-call | tf_op jit(solution)/shard_map/pallas_call | solution.py:101
  44.2 3.6 %shard_map.92 = (f32[8,16,256]{2,1,0:T(8,128)}, f32[8,16,256]{2,1,0:T(8,128)}) custom-call(s32[1]{0:T(128)} %bitcast.1.rad_ref, f32[32,32,256]{2,1,0:T(8,128)} %lam_ref.7, f32[32,32,256]{2,1,0:T(8,128)} %copy-done, f32[2,32,8,256]{3,2,1,0:T(8,128)} %pad_maximum_fusion.1.rowh_ref, f32[2,32,40,128]{3,2,1,0:T(8,128)} %pad_maximum_fusion.colh_ref, ...), custom_call_target="tpu_custom_call" | custom-call | tf_op jit(solution)/shard_map/pallas_call | solution.py:101
  47.9 3.7 %shard_map.91 = (f32[8,16,256]{2,1,0:T(8,128)}, f32[8,16,256]{2,1,0:T(8,128)}) custom-call(s32[1]{0:T(128)} %bitcast.1.rad_ref, f32[32,32,256]{2,1,0:T(8,128)} %lam_ref.7, f32[32,32,256]{2,1,0:T(8,128)} %copy-done, f32[2,32,8,256]{3,2,1,0:T(8,128)} %pad_maximum_fusion.1.rowh_ref, f32[2,32,40,128]{3,2,1,0:T(8,128)} %pad_maximum_fusion.colh_ref, ...), custom_call_target="tpu_custom_call" | custom-call | tf_op jit(solution)/shard_map/pallas_call | solution.py:101
  51.5 0.9 %constant_dynamic-update-slice_fusion.7 = f32[64,16,256]{2,1,0:T(8,128)S(1)} fusion(f32[8,16,256]{2,1,0:T(8,128)} %get-tuple-element.13), kind=kLoop, calls=%fused_computation.41 | loop fusion | bytes 262144
  52.5 2.0 %collective-permute-start.4 = (f32[8,16,256]{2,1,0:T(8,128)}, f32[8,16,256]{2,1,0:T(8,128)S(1)}, u32[]{:S(2)}, u32[]{:S(2)}) collective-permute-start(f32[8,16,256]{2,1,0:T(8,128)} %get-tuple-element.17), channel_id=1, source_target_pairs={{0,1},{1,0},{2,3},{3,2},{4,5},{5,4},{6,7},{7,6},{8,9},{9,8},{10,11... | collective-permute-start | bytes 393224 | tf_op jit(solution)/shard_map/ppermute | solution.py:200
  54.5 0.1 collective-permute-start.5
  54.6 1.9 %collective-permute-start.6 = (f32[8,16,256]{2,1,0:T(8,128)S(1)}, f32[8,16,256]{2,1,0:T(8,128)S(1)}, u32[]{:S(2)}, u32[]{:S(2)}) collective-permute-start(f32[8,16,256]{2,1,0:T(8,128)S(1)} %copy-done.10), channel_id=1, source_target_pairs={{0,1},{1,0},{2,3},{3,2},{4,5},{5,4},{6,7},{7,6},{8,9},{9,8},{10,11... | collective-permute-start | bytes 393224 | tf_op jit(solution)/shard_map/ppermute | solution.py:200
  56.5 0.1 collective-permute-start.7
  56.7 2.4 %collective-permute-done.4 = f32[8,16,256]{2,1,0:T(8,128)S(1)} collective-permute-done((f32[8,16,256]{2,1,0:T(8,128)}, f32[8,16,256]{2,1,0:T(8,128)S(1)}, u32[]{:S(2)}, u32[]{:S(2)}) %collective-permute-start.4) | collective-permute-done | bytes 131104 | tf_op jit(solution)/shard_map/ppermute | solution.py:200
  59.1 2.8 %collective-permute-done.5 = f32[8,16,256]{2,1,0:T(8,128)S(1)} collective-permute-done((f32[8,16,256]{2,1,0:T(8,128)S(1)}, f32[8,16,256]{2,1,0:T(8,128)S(1)}, u32[]{:S(2)}, u32[]{:S(2)}) %collective-permute-start.5) | collective-permute-done | bytes 131104 | tf_op jit(solution)/shard_map/ppermute | solution.py:200
  61.9 2.8 %collective-permute-done.6 = f32[8,16,256]{2,1,0:T(8,128)S(1)} collective-permute-done((f32[8,16,256]{2,1,0:T(8,128)S(1)}, f32[8,16,256]{2,1,0:T(8,128)S(1)}, u32[]{:S(2)}, u32[]{:S(2)}) %collective-permute-start.6) | collective-permute-done | bytes 131104 | tf_op jit(solution)/shard_map/ppermute | solution.py:200
  64.7 2.8 %collective-permute-done.7 = f32[8,16,256]{2,1,0:T(8,128)S(1)} collective-permute-done((f32[8,16,256]{2,1,0:T(8,128)S(1)}, f32[8,16,256]{2,1,0:T(8,128)S(1)}, u32[]{:S(2)}, u32[]{:S(2)}) %collective-permute-start.7) | collective-permute-done | bytes 131104 | tf_op jit(solution)/shard_map/ppermute | solution.py:200
  67.5 1.6 %fusion.8 = f32[64,16,256]{2,0,1:T(8,128)S(1)} fusion(f32[64,32]{1,0:T(8,128)S(1)} %get-tuple-element.38, f32[64,32]{1,0:T(8,128)S(1)} %get-tuple-element.37, f32[8,8,16,256]{3,2,1,0:T(8,128)S(1)} %bitcast.43), kind=kOutput, calls=%fused_computation.12 | convolution fusion | flops 201330688 | bytes 2113536 | tf_op jit(solution)/shard_map/dot_general | solution.py:210
  69.1 1.6 %copy.38 = f32[64,16,256]{2,1,0:T(8,128)} copy(f32[64,16,256]{2,0,1:T(8,128)S(1)} %fusion.8) | data formatting | bytes 2097152 | tf_op jit(solution)/shard_map/dot_general | solution.py:210
  (40 shorter events, 0.2 us)
Async XLA Ops:
  0.0 1.9 %copy-start.1 = (f32[32,32,256]{2,1,0:T(8,128)S(1)}, f32[32,32,256]{2,1,0:T(8,128)}, u32[]{:S(2)}) copy-start(f32[32,32,256]{2,1,0:T(8,128)} %lam_ref.7) | copy-start | bytes 3145732
  1.9 13.2 %copy-start = (f32[32,32,256]{2,1,0:T(8,128)}, f32[32,32,256]{2,1,0:T(8,128)S(1)}, u32[]{:S(2)}) copy-start(f32[32,32,256]{2,1,0:T(8,128)S(1)} %convert_select_fusion.eta_ref) | copy-start | bytes 3145732
  1.9 9.2 %copy-start.2 = (bf16[32,2048]{1,0:T(8,128)(2,1)S(1)}, bf16[32,2048]{1,0:T(8,128)(2,1)}, u32[]{:S(2)}) copy-start(bf16[32,2048]{1,0:T(8,128)(2,1)} %param.15) | copy-start | bytes 393220
  2.8 19.3 %collective-permute-start = (f32[32,6,256]{2,1,0:T(8,128)}, f32[32,6,256]{2,1,0:T(8,128)S(1)}, u32[]{:S(2)}, u32[]{:S(2)}) collective-permute-start(f32[32,6,256]{2,1,0:T(8,128)} %pad_maximum_fusion.2), channel_id=1, source_target_pairs={{8,0},{16,8},{24,16},{9,1},{17,9},{25,17},{10,2},{18,10},{26,18},{... | collective-permute-start | bytes 589832 | tf_op jit(solution)/shard_map/ppermute | solution.py:157
  4.9 17.3 %collective-permute-start.1 = (f32[32,6,256]{2,1,0:T(8,128)}, f32[32,6,256]{2,1,0:T(8,128)}, u32[]{:S(2)}, u32[]{:S(2)}) collective-permute-start(f32[32,6,256]{2,1,0:T(8,128)} %pad_maximum_fusion.3), channel_id=1, source_target_pairs={{0,8},{8,16},{16,24},{1,9},{9,17},{17,25},{2,10},{10,18},{18,26},{... | collective-permute-start | bytes 589832 | tf_op jit(solution)/shard_map/ppermute | solution.py:156
  11.8 7.9 %all-to-all-start = ((bf16[32,4,512]{2,0,1:T(8,128)(2,1)}), bf16[32,4,512]{2,0,1:T(8,128)(2,1)S(1)}, u32[]{:S(2)}, u32[]{:S(2)}) async-start(bf16[32,4,512]{2,0,1:T(8,128)(2,1)} %bitcast.40), calls=%async_computation | async-start | bytes 262144 | tf_op jit(solution)/shard_map/all_to_all | solution.py:145
  15.5 1.4 %copy-start.7 = (s32[2048]{0:T(1024)S(1)}, s32[2048]{0:T(1024)}, u32[]{:S(2)}) copy-start(s32[2048]{0:T(1024)} %param.16) | copy-start | bytes 24580
  15.6 1.4 %copy-start.8 = (s32[4]{0:T(128)S(1)}, s32[4]{0:T(128)}, u32[]{:S(2)}) copy-start(s32[4]{0:T(128)} %param.17) | copy-start | bytes 52
  15.6 2.2 %copy-start.6 = (f32[64,64]{1,0:T(8,128)S(1)}, f32[64,64]{1,0:T(8,128)}, u32[]{:S(2)}) copy-start(f32[64,64]{1,0:T(8,128)} %param.14) | copy-start | bytes 49156
  25.7 7.5 %collective-permute-start.2 = (f32[7680]{0:T(1024)S(1)}, f32[7680]{0:T(1024)S(1)}, u32[]{:S(2)}, u32[]{:S(2)}) collective-permute-start(f32[7680]{0:T(1024)S(1)} %reshape.111), channel_id=1, source_target_pairs={{2,0},{4,2},{6,4},{3,1},{5,3},{7,5},{10,8},{12,10},{14,12},{11,9},... | collective-permute-start | bytes 92168 | tf_op jit(solution)/shard_map/ppermute | solution.py:172
  29.2 5.2 %collective-permute-start.3 = (f32[7680]{0:T(1024)S(1)}, f32[7680]{0:T(1024)S(1)}, u32[]{:S(2)}, u32[]{:S(2)}) collective-permute-start(f32[7680]{0:T(1024)S(1)} %reshape.113), channel_id=1, source_target_pairs={{0,2},{2,4},{4,6},{1,3},{3,5},{5,7},{8,10},{10,12},{12,14},{9,11},... | collective-permute-start | bytes 92168 | tf_op jit(solution)/shard_map/ppermute | solution.py:173
  47.8 6.7 %copy-start.11 = (f32[8,16,256]{2,1,0:T(8,128)S(1)}, f32[8,16,256]{2,1,0:T(8,128)}, u32[]{:S(2)}) copy-start(f32[8,16,256]{2,1,0:T(8,128)} %get-tuple-element.18) | copy-start | bytes 393220
  47.8 6.7 %copy-start.10 = (f32[8,16,256]{2,1,0:T(8,128)S(1)}, f32[8,16,256]{2,1,0:T(8,128)}, u32[]{:S(2)}) copy-start(f32[8,16,256]{2,1,0:T(8,128)} %get-tuple-element.19) | copy-start | bytes 393220
  47.8 8.7 %copy-start.9 = (f32[8,16,256]{2,1,0:T(8,128)S(1)}, f32[8,16,256]{2,1,0:T(8,128)}, u32[]{:S(2)}) copy-start(f32[8,16,256]{2,1,0:T(8,128)} %get-tuple-element.20) | copy-start | bytes 393220
  47.9 8.7 %copy-start.5 = (f32[8,16,256]{2,1,0:T(8,128)S(1)}, f32[8,16,256]{2,1,0:T(8,128)}, u32[]{:S(2)}) copy-start(f32[8,16,256]{2,1,0:T(8,128)} %get-tuple-element.14) | copy-start | bytes 393220
  47.9 8.8 %copy-start.4 = (f32[8,16,256]{2,1,0:T(8,128)S(1)}, f32[8,16,256]{2,1,0:T(8,128)}, u32[]{:S(2)}) copy-start(f32[8,16,256]{2,1,0:T(8,128)} %get-tuple-element.15) | copy-start | bytes 393220
  47.9 8.8 %copy-start.3 = (f32[8,16,256]{2,1,0:T(8,128)S(1)}, f32[8,16,256]{2,1,0:T(8,128)}, u32[]{:S(2)}) copy-start(f32[8,16,256]{2,1,0:T(8,128)} %get-tuple-element.16) | copy-start | bytes 393220
  52.5 6.6 %collective-permute-start.4 = (f32[8,16,256]{2,1,0:T(8,128)}, f32[8,16,256]{2,1,0:T(8,128)S(1)}, u32[]{:S(2)}, u32[]{:S(2)}) collective-permute-start(f32[8,16,256]{2,1,0:T(8,128)} %get-tuple-element.17), channel_id=1, source_target_pairs={{0,1},{1,0},{2,3},{3,2},{4,5},{5,4},{6,7},{7,6},{8,9},{9,8},{10,11... | collective-permute-start | bytes 393224 | tf_op jit(solution)/shard_map/ppermute | solution.py:200
  54.5 7.4 %collective-permute-start.5 = (f32[8,16,256]{2,1,0:T(8,128)S(1)}, f32[8,16,256]{2,1,0:T(8,128)S(1)}, u32[]{:S(2)}, u32[]{:S(2)}) collective-permute-start(f32[8,16,256]{2,1,0:T(8,128)S(1)} %copy-done.11), channel_id=1, source_target_pairs={{0,1},{1,0},{2,3},{3,2},{4,5},{5,4},{6,7},{7,6},{8,9},{9,8},{10,11... | collective-permute-start | bytes 393224 | tf_op jit(solution)/shard_map/ppermute | solution.py:200
  54.6 10.2 %collective-permute-start.6 = (f32[8,16,256]{2,1,0:T(8,128)S(1)}, f32[8,16,256]{2,1,0:T(8,128)S(1)}, u32[]{:S(2)}, u32[]{:S(2)}) collective-permute-start(f32[8,16,256]{2,1,0:T(8,128)S(1)} %copy-done.10), channel_id=1, source_target_pairs={{0,1},{1,0},{2,3},{3,2},{4,5},{5,4},{6,7},{7,6},{8,9},{9,8},{10,11... | collective-permute-start | bytes 393224 | tf_op jit(solution)/shard_map/ppermute | solution.py:200
  56.5 11.0 %collective-permute-start.7 = (f32[8,16,256]{2,1,0:T(8,128)S(1)}, f32[8,16,256]{2,1,0:T(8,128)S(1)}, u32[]{:S(2)}, u32[]{:S(2)}) collective-permute-start(f32[8,16,256]{2,1,0:T(8,128)S(1)} %copy-done.9), channel_id=1, source_target_pairs={{0,1},{1,0},{2,3},{3,2},{4,5},{5,4},{6,7},{7,6},{8,9},{9,8},{10,11... | collective-permute-start | bytes 393224 | tf_op jit(solution)/shard_map/ppermute | solution.py:200

commit v3 on v2

--- a/solution.py
+++ b/solution.py
@@ -31,7 +31,7 @@
 
 
 def _sweep_kernel(rad_ref, lam_ref, eta_ref, rowh_ref, colh_ref, mask_ref, vel_ref, dep_ref,
-                  send_ref, keep_ref, lam_x, eta_x):
+                  after_ref, recv_ref, send_ref, keep_ref, lam_x, eta_x):
     layers, rows, cols = lam_ref.shape
     n_r, n_c = lam_x.shape[1], lam_x.shape[2]
     for ref, src, k in ((lam_x, lam_ref, 0), (eta_x, eta_ref, 1)):
@@ -90,7 +90,8 @@
     keep_ref[...] = jnp.where(is_zero, lo, hi)
 
 
-def _sweeps(rad_idx, lam, eta, rowh, colh, mask, vel, dep, first_layer, n_layers, block_layers):
+def _sweeps(rad_idx, lam, eta, rowh, colh, mask, vel, dep, after, recv, first_layer, n_layers,
+            block_layers):
     _, rows, cols = lam.shape
     ext_r, ext_c = mask.shape
     half = rows // 2
@@ -111,6 +112,8 @@
             pl.BlockSpec((ext_r, ext_c), lambda i: (0, 0)),
             pl.BlockSpec((2, bl, rows, cols), lambda i: (0, i + off, 0, 0)),
             pl.BlockSpec((bl, rows, cols), lambda i: (i + off, 0, 0)),
+            pl.BlockSpec(memory_space=pl.ANY),
+            pl.BlockSpec(memory_space=pl.ANY),
         ],
         out_specs=[
             pl.BlockSpec((bl, half, cols), lambda i: (i, 0, 0)),
@@ -120,7 +123,12 @@
             pltpu.VMEM((bl, ext_r, ext_c), jnp.float32),
             pltpu.VMEM((bl, ext_r, ext_c), jnp.float32),
         ],
-    )(rad_idx, lam, eta, rowh, colh, mask, vel, dep)
+        cost_estimate=pl.CostEstimate(
+            flops=n_layers * ext_r * ext_c * 60,
+            transcendentals=0,
+            bytes_accessed=n_layers * (2 * ext_r * ext_c * 4 + rows * cols * 12),
+        ),
+    )(rad_idx, lam, eta, rowh, colh, mask, vel, dep, after, recv)
 
 
 def per_device(
@@ -167,12 +175,13 @@
             parts.append(jnp.concatenate([src[:, :, sl], rowh[k][:, :, sl]], axis=1))
         return jnp.stack(parts)
 
-    left_send = col_piece(slice(0, g)).reshape(-1)
-    right_send = col_piece(slice(cols - g, cols)).reshape(-1)
-    from_right = lax.ppermute(left_send, "lat", _pairs(n_lat, -1)).reshape(2, layers, ext_rows, g)
-    from_left = lax.ppermute(right_send, "lat", _pairs(n_lat, 1)).reshape(2, layers, ext_rows, g)
+    flat = jnp.stack([col_piece(slice(0, g)), col_piece(slice(cols - g, cols))]).reshape(-1)
+    piece = flat.shape[0] // 2
+    from_right = lax.ppermute(flat[:piece], "lat", _pairs(n_lat, -1))
+    from_left = lax.ppermute(flat[piece:], "lat", _pairs(n_lat, 1))
+    got = jnp.concatenate([from_right, from_left]).reshape(2, 2, layers, ext_rows, g)
     zc = jnp.zeros((2, layers, ext_rows, ext_cols - cols - 2 * g), jnp.float32)
-    colh = jnp.concatenate([from_right, zc, from_left], axis=3)
+    colh = jnp.concatenate([got[0], zc, got[1]], axis=3)
     mask = _inside_mask(rows, cols, ext_rows, ext_cols, c, d, n_cap, n_lat)
 
     senders = n_lat
@@ -192,11 +201,14 @@
     block_layers = 4
     keeps = []
     recvs = []
+    after = rad_idx
     for k in range(n_chunks):
+        landed = recvs[k - 2] if k >= 2 else rad_idx
         send, keep = _sweeps(
-            rad_idx, adjoint_temp, eta, rowh, colh, mask, velocity, deposit,
+            rad_idx, adjoint_temp, eta, rowh, colh, mask, velocity, deposit, after, landed,
             k * chunk, chunk, block_layers,
         )
+        after = keep
         recvs.append(lax.ppermute(send, "rad", _pairs(n_rad, 1) + _pairs(n_rad, -1)))
         keeps.append(keep)
 

time: 71.1 us -> 68.7 us (0.966)
  waiting for transfers between devices: 12.6 us -> 5.35 us
  local copies, waits for them, and re-layouts: 12.8 us -> 17.7 us
    ppermute x4, waiting for transfers between devices: 10.8 us -> 3.52 us  [per_device(): lax.ppermute(send, 'rad', _pairs(n_rad, 1) + _pairs(n_rad, -1))]
    unnamed x34 -> x28, local copies, waits for them, and re-layouts: 1.61 us -> 6.51 us
    reshape x4 -> x0, local copies, waits for them, and re-layouts: 4.13 us -> none  [the longest x1 1.18 us: per_device(): lax.ppermute(left_send, 'lat', _pairs(n_lat, -1))]
    concatenate x1 -> x3, local copies, waits for them, and re-layouts: 0.08 us -> 2.44 us  [the longest x2 2.37 us: per_device(): jnp.concatenate([from_right, from_left]).reshape(2, 2, layers, ext_rows, g)]
    slice x0 -> x2, local copies, waits for them, and re-layouts: none -> 1.77 us  [the longest x1 0.88 us: per_device(): from_right = lax.ppermute(flat[:piece], 'lat', _pairs(n_lat, -1))]
  transfers between devices with their start and end apart: 9 -> 9, of which waited for: 5 -> 2; matrix products, arithmetic and copies ran while one was open for 15% -> 22% of each run, Pallas kernels for 0% -> 16%
where the time goes in v3:
time: 68.7 us; the launch traced here: 68.2 us
  starting transfers between devices  19.4 us (28%)
  local copies, waits for them, and re-layouts  17.7 us (26%)
  Pallas kernels  14.2 us (21%)
  other arithmetic  7.16 us (10%)
  waiting for transfers between devices  5.35 us (8%)
  matrix products  3.96 us (6%)
    pallas_call x4, Pallas kernels, _sweeps(): pl.pallas_call(_sweep_kernel, out_shape=out_shape, grid=grid, in_specs=[p...  14.2 us
    unnamed x28, local copies, waits for them, and re-layouts  6.51 us
    ppermute x1, starting transfers between devices, per_device(): top = lax.ppermute(top_send, 'cap', _pairs(n_cap, 1))  6.26 us
    ppermute x4, starting transfers between devices, per_device(): lax.ppermute(send, 'rad', _pairs(n_rad, 1) + _pairs(n_rad, -1))  4.07 us
    ppermute x4, waiting for transfers between devices, per_device(): lax.ppermute(send, 'rad', _pairs(n_rad, 1) + _pairs(n_rad, -1))  3.52 us
    all_to_all x1, starting transfers between devices, per_device(): lax.all_to_all(marker_rows, 'lat', split_axis=1, concat_axis=1, tiled=True)  3.32 us
    ppermute x1, starting transfers between devices, per_device(): from_left = lax.ppermute(flat[piece:], 'lat', _pairs(n_lat, 1))  3.21 us
    dot_general x1, matrix products, per_device(): jnp.einsum('las,sb->lab', xa, onehot_b, preferred_element_type=jnp.float32)  2.37 us
  transfers between devices with their start and end apart: 9, of which 2 were waited for; matrix products, arithmetic and copies ran while one was open for 22% of the time, Pallas kernels for 16%

profile of v3, /device:TPU:0, one launch (start us, length us, event | category | flops | bytes accessed | tf_op | source)
XLA Modules:
  0.0 68.2 jit_solution(14293510584466254716)
XLA Ops:
  0.0 1.9 %convert_select_fusion.eta_ref = f32[32,32,256]{2,1,0:T(8,128)S(1)} fusion(bf16[32,32,256]{2,1,0:T(8,128)(2,1)} %param.11, bf16[32,32,256]{2,1,0:T(8,128)(2,1)} %param.12, s32[32,32,256]{2,1,0:T(8,128)} %param.13), kind=kLoop, calls=%fused_computation.7 | loop fusion | flops 1835008 | bytes 3145728 | tf_op jit(solution)/shard_map/jit(_where)/select_n | solution.py:157
  1.9 0.0 copy-start
  2.0 0.1 fusion.23
  2.1 0.8 %pad_maximum_fusion.2 = f32[32,6,256]{2,1,0:T(8,128)} fusion(f32[32,3,256]{2,1,0:T(4,128)S(1)} %get-tuple-element.44, f32[32,3,256]{2,1,0:T(4,128)S(1)} %get-tuple-element.25), kind=kLoop, calls=%fused_computation.17 | loop fusion | flops 49152 | bytes 393216 | tf_op jit(solution)/shard_map/concatenate | solution.py:163
  2.8 1.3 %collective-permute-start = (f32[32,6,256]{2,1,0:T(8,128)}, f32[32,6,256]{2,1,0:T(8,128)S(1)}, u32[]{:S(2)}, u32[]{:S(2)}) collective-permute-start(f32[32,6,256]{2,1,0:T(8,128)} %pad_maximum_fusion.2), channel_id=1, source_target_pairs={{8,0},{16,8},{24,16},{9,1},{17,9},{25,17},{10,2},{18,10},{26,18},{... | collective-permute-start | bytes 589832 | tf_op jit(solution)/shard_map/ppermute | solution.py:165
  4.1 0.8 %pad_maximum_fusion.3 = f32[32,6,256]{2,1,0:T(8,128)} fusion(f32[32,3,256]{2,1,0:T(4,128)S(1)} %get-tuple-element.43, f32[32,3,256]{2,1,0:T(4,128)S(1)} %get-tuple-element.26), kind=kLoop, calls=%fused_computation.18 | loop fusion | flops 49152 | bytes 393216 | tf_op jit(solution)/shard_map/concatenate | solution.py:162
  4.9 6.3 %collective-permute-start.1 = (f32[32,6,256]{2,1,0:T(8,128)}, f32[32,6,256]{2,1,0:T(8,128)}, u32[]{:S(2)}, u32[]{:S(2)}) collective-permute-start(f32[32,6,256]{2,1,0:T(8,128)} %pad_maximum_fusion.3), channel_id=1, source_target_pairs={{0,8},{8,16},{16,24},{1,9},{9,17},{17,25},{2,10},{10,18},{18,26},{... | collective-permute-start | bytes 589832 | tf_op jit(solution)/shard_map/ppermute | solution.py:164
  11.1 0.7 copy.54
  11.8 3.3 %all-to-all-start = ((bf16[32,4,512]{2,0,1:T(8,128)(2,1)}), bf16[32,4,512]{2,0,1:T(8,128)(2,1)S(1)}, u32[]{:S(2)}, u32[]{:S(2)}) async-start(bf16[32,4,512]{2,0,1:T(8,128)(2,1)} %bitcast.40), calls=%async_computation | async-start | bytes 262144 | tf_op jit(solution)/shard_map/all_to_all | solution.py:153
  15.1 0.2 fusion.22
  15.3 0.2 fusion.21
  15.6 0.3 copy.27
  15.9 0.3 copy.39
  16.2 0.3 copy.32
  16.5 0.3 copy.40
  16.7 0.1 pad.21.clone
  16.8 0.1 pad.1.clone
  17.0 0.1 fusion.16
  17.1 0.7 %and_convert_fusion.mask_ref = f32[40,384]{1,0:T(8,128)} fusion(pred[384]{0:T(512)(128)(4,1)S(1)} %compare_and_fusion, pred[40]{0:T(512)(128)(4,1)S(1)} %compare_and_fusion.1), kind=kLoop, calls=%fused_computation.26 | loop fusion | flops 30720 | bytes 61864 | tf_op jit(solution)/shard_map/convert_element_type | solution.py:26
  17.8 0.1 fusion.12
  17.8 0.1 constant_dynamic-slice_fusion.1
  17.9 1.8 %all-to-all-done = bf16[32,4,512]{2,0,1:T(8,128)(2,1)S(1)} async-done(((bf16[32,4,512]{2,0,1:T(8,128)(2,1)}), bf16[32,4,512]{2,0,1:T(8,128)(2,1)S(1)}, u32[]{:S(2)}, u32[]{:S(2)}) %all-to-all-start) | async-done | bytes 131104 | tf_op jit(solution)/shard_map/all_to_all | solution.py:153
  19.7 2.4 %fusion.dep_ref = f32[32,32,256]{2,1,0:T(8,128)} fusion(pred[32,2048]{1,0:T(8,128)(4,1)S(1)} %fusion.12, bf16[32,2048]{1,0:T(8,128)(2,1)S(1)} %bitcast.46, s32[2048]{0:T(1024)S(1)} %get-tuple-element.39), kind=kOutput, calls=%fused_computation | convolution fusion | flops 1076363264 | bytes 1253376 | tf_op jit(solution)/shard_map/las,sb->lab/dot_general | solution.py:196
  22.1 0.1 fusion.27
  22.2 1.1 %fusion.28 = (f32[32,3,256]{2,1,0:T(4,128)S(1)}, f32[32,3,256]{2,1,0:T(4,128)S(1)}) fusion(f32[32,6,256]{2,1,0:T(8,128)} %collective-permute-done.1), kind=kLoop, calls=%fused_computation.72 | loop fusion | bytes 393216 | tf_op jit(solution)/shard_map/slice | solution.py:168
  23.3 0.1 pad_maximum_fusion.4
  23.4 0.1 fusion.26
  23.5 0.3 copy.28
  23.8 0.1 fusion.25
  23.9 0.3 copy.26
  24.2 0.1 maximum_bitcast_fusion.1
  24.3 0.1 maximum_bitcast_fusion
  24.4 0.5 copy.29
  24.9 0.9 %slice.74 = f32[7680]{0:T(1024)S(1)} reshape(f32[2,32,40,3]{3,2,1,0:T(8,128)S(1)} %copy.29) | data formatting | bytes 61440 | tf_op jit(solution)/shard_map/slice | solution.py:180
  25.8 1.3 %collective-permute-start.2 = (f32[7680]{0:T(1024)S(1)}, f32[7680]{0:T(1024)S(1)}, u32[]{:S(2)}, u32[]{:S(2)}) collective-permute-start(f32[7680]{0:T(1024)S(1)} %slice.74), channel_id=1, source_target_pairs={{2,0},{4,2},{6,4},{3,1},{5,3},{7,5},{10,8},{12,10},{14,12},{11,9},... | collective-permute-start | bytes 92168 | tf_op jit(solution)/shard_map/ppermute | solution.py:180
  27.1 0.3 copy.33
  27.3 0.3 copy.31
  27.6 0.1 maximum_bitcast_fusion.3
  27.7 0.1 maximum_bitcast_fusion.2
  27.8 0.5 copy.34
  28.4 0.9 %slice.79 = f32[7680]{0:T(1024)S(1)} reshape(f32[2,32,40,3]{3,2,1,0:T(8,128)S(1)} %copy.34) | data formatting | bytes 61440 | tf_op jit(solution)/shard_map/slice | solution.py:181
  29.2 3.2 %collective-permute-start.3 = (f32[7680]{0:T(1024)S(1)}, f32[7680]{0:T(1024)S(1)}, u32[]{:S(2)}, u32[]{:S(2)}) collective-permute-start(f32[7680]{0:T(1024)S(1)} %slice.79), channel_id=1, source_target_pairs={{0,2},{2,4},{4,6},{1,3},{3,5},{5,7},{8,10},{10,12},{12,14},{9,11},... | collective-permute-start | bytes 92168 | tf_op jit(solution)/shard_map/ppermute | solution.py:181
  32.5 0.8 %pad_maximum_fusion.1.rowh_ref = f32[2,32,8,256]{3,2,1,0:T(8,128)} fusion(f32[1,32,8,256]{3,2,1,0:T(8,128)S(1)} %bitcast.42, f32[1,32,8,256]{3,2,1,0:T(8,128)S(1)} %bitcast.41), kind=kLoop, calls=%fused_computation.16 | loop fusion | flops 131072 | bytes 1048576 | tf_op jit(solution)/shard_map/stack | solution.py:167
  33.3 1.2 %concatenate.47 = f32[2,32,40,3]{3,2,1,0:T(8,128)S(1)} reshape(f32[7680]{0:T(1024)S(1)} %collective-permute-done.2) | data formatting | bytes 61440 | tf_op jit(solution)/shard_map/concatenate | solution.py:182
  34.5 1.2 %concatenate.50 = f32[2,32,40,3]{3,2,1,0:T(8,128)S(1)} reshape(f32[7680]{0:T(1024)S(1)} %collective-permute-done.3) | data formatting | bytes 61440 | tf_op jit(solution)/shard_map/concatenate | solution.py:182
  35.7 1.5 %pad_maximum_fusion.colh_ref = f32[2,32,40,128]{3,2,1,0:T(8,128)} fusion(f32[2,32,40,3]{3,2,1,0:T(8,128)S(1)} %concatenate.50, f32[2,32,40,3]{3,2,1,0:T(8,128)S(1)} %concatenate.47, f32[128]{0:T(128)S(1)} %pad.1.clone), kind=kLoop, calls=%fused_computation.10 | loop fusion | flops 655360 | bytes 1372672 | tf_op jit(solution)/shard_map/concatenate | solution.py:184
  37.2 3.5 %shard_map.91 = (f32[8,16,256]{2,1,0:T(8,128)}, f32[8,16,256]{2,1,0:T(8,128)}) custom-call(s32[1]{0:T(128)} %bitcast.1.rad_ref.after_ref.recv_ref, f32[32,32,256]{2,1,0:T(8,128)} %lam_ref.7, f32[32,32,256]{2,1,0:T(8,128)} %copy-done, f32[2,32,8,256]{3,2,1,0:T(8,128)} %pad_maximum_fusion.1.rowh_ref, f32[2,32,40,128]{3,2,1,0:T(8,128)} %pad_maximum_fusion.colh_ref, ...), custom_call_target="tpu_custom_call" | custom-call | flops 7372800 | bytes 1769472 | tf_op jit(solution)/shard_map/pallas_call | solution.py:102
  40.7 2.0 %collective-permute-start.4 = (f32[8,16,256]{2,1,0:T(8,128)}, f32[8,16,256]{2,1,0:T(8,128)S(1)}, u32[]{:S(2)}, u32[]{:S(2)}) collective-permute-start(f32[8,16,256]{2,1,0:T(8,128)} %get-tuple-element.15), channel_id=1, source_target_pairs={{0,1},{1,0},{2,3},{3,2},{4,5},{5,4},{6,7},{7,6},{8,9},{9,8},{10,11... | collective-permute-start | bytes 393224 | tf_op jit(solution)/shard_map/ppermute | solution.py:212
  42.7 0.9 %constant_dynamic-update-slice_fusion.7 = f32[64,16,256]{2,1,0:T(8,128)S(1)} fusion(f32[8,16,256]{2,1,0:T(8,128)} %get-tuple-element.13.after_ref), kind=kLoop, calls=%fused_computation.41 | loop fusion | bytes 262144
  43.6 3.6 %shard_map.92 = (f32[8,16,256]{2,1,0:T(8,128)}, f32[8,16,256]{2,1,0:T(8,128)}) custom-call(s32[1]{0:T(128)} %bitcast.1.rad_ref.after_ref.recv_ref, f32[32,32,256]{2,1,0:T(8,128)} %lam_ref.7, f32[32,32,256]{2,1,0:T(8,128)} %copy-done, f32[2,32,8,256]{3,2,1,0:T(8,128)} %pad_maximum_fusion.1.rowh_ref, f32[2,32,40,128]{3,2,1,0:T(8,128)} %pad_maximum_fusion.colh_ref, ...), custom_call_target="tpu_custom_call" | custom-call | flops 7372800 | bytes 1769472 | tf_op jit(solution)/shard_map/pallas_call | solution.py:102
  47.2 0.1 collective-permute-start.5
  47.3 0.9 %constant_dynamic-update-slice_fusion.6 = f32[64,16,256]{2,1,0:T(8,128)S(1)} fusion(f32[64,16,256]{2,1,0:T(8,128)S(1)} %constant_dynamic-update-slice_fusion.7, f32[8,16,256]{2,1,0:T(8,128)} %get-tuple-element.14.after_ref), kind=kLoop, calls=%fused_computation.40 | loop fusion | bytes 262144
  48.2 0.7 copy-done.2
  48.8 3.5 %shard_map.93 = (f32[8,16,256]{2,1,0:T(8,128)}, f32[8,16,256]{2,1,0:T(8,128)}) custom-call(s32[1]{0:T(128)} %bitcast.1.rad_ref.after_ref.recv_ref, f32[32,32,256]{2,1,0:T(8,128)} %lam_ref.7, f32[32,32,256]{2,1,0:T(8,128)} %copy-done, f32[2,32,8,256]{3,2,1,0:T(8,128)} %pad_maximum_fusion.1.rowh_ref, f32[2,32,40,128]{3,2,1,0:T(8,128)} %pad_maximum_fusion.colh_ref, ...), custom_call_target="tpu_custom_call" | custom-call | flops 7372800 | bytes 1769472 | tf_op jit(solution)/shard_map/pallas_call | solution.py:102
  52.4 2.0 %collective-permute-start.6 = (f32[8,16,256]{2,1,0:T(8,128)}, f32[8,16,256]{2,1,0:T(8,128)S(1)}, u32[]{:S(2)}, u32[]{:S(2)}) collective-permute-start(f32[8,16,256]{2,1,0:T(8,128)} %get-tuple-element.19), channel_id=1, source_target_pairs={{0,1},{1,0},{2,3},{3,2},{4,5},{5,4},{6,7},{7,6},{8,9},{9,8},{10,11... | collective-permute-start | bytes 393224 | tf_op jit(solution)/shard_map/ppermute | solution.py:212
  54.4 0.9 %constant_dynamic-update-slice_fusion.5 = f32[64,16,256]{2,1,0:T(8,128)S(1)} fusion(f32[64,16,256]{2,1,0:T(8,128)S(1)} %constant_dynamic-update-slice_fusion.6, f32[8,16,256]{2,1,0:T(8,128)} %get-tuple-element.16.after_ref), kind=kLoop, calls=%fused_computation.39 | loop fusion | bytes 262144
  55.3 0.6 copy-done.4
  55.9 3.6 %shard_map.94 = (f32[8,16,256]{2,1,0:T(8,128)}, f32[8,16,256]{2,1,0:T(8,128)}) custom-call(s32[1]{0:T(128)} %bitcast.1.rad_ref.after_ref.recv_ref, f32[32,32,256]{2,1,0:T(8,128)} %lam_ref.7, f32[32,32,256]{2,1,0:T(8,128)} %copy-done, f32[2,32,8,256]{3,2,1,0:T(8,128)} %pad_maximum_fusion.1.rowh_ref, f32[2,32,40,128]{3,2,1,0:T(8,128)} %pad_maximum_fusion.colh_ref, ...), custom_call_target="tpu_custom_call" | custom-call | flops 7372800 | bytes 1769472 | tf_op jit(solution)/shard_map/pallas_call | solution.py:102
  59.5 0.1 collective-permute-start.7
  59.6 0.9 %constant_dynamic-update-slice_fusion.4 = f32[64,16,256]{2,1,0:T(8,128)S(1)} fusion(f32[64,16,256]{2,1,0:T(8,128)S(1)} %constant_dynamic-update-slice_fusion.5, f32[8,16,256]{2,1,0:T(8,128)} %get-tuple-element.18), kind=kLoop, calls=%fused_computation.38 | loop fusion | bytes 262144
  60.5 0.9 %constant_dynamic-update-slice_fusion.2 = f32[64,16,256]{2,1,0:T(8,128)S(1)} fusion(f32[64,16,256]{2,1,0:T(8,128)S(1)} %constant_dynamic-update-slice_fusion.3, f32[8,16,256]{2,1,0:T(8,128)} %copy-done.4), kind=kLoop, calls=%fused_computation.36 | loop fusion | bytes 262144
  61.5 3.5 %collective-permute-done.7 = f32[8,16,256]{2,1,0:T(8,128)S(1)} collective-permute-done((f32[8,16,256]{2,1,0:T(8,128)}, f32[8,16,256]{2,1,0:T(8,128)S(1)}, u32[]{:S(2)}, u32[]{:S(2)}) %collective-permute-start.7) | collective-permute-done | bytes 131104 | tf_op jit(solution)/shard_map/ppermute | solution.py:212
  65.0 1.6 %fusion.8 = f32[64,16,256]{2,0,1:T(8,128)S(1)} fusion(f32[64,32]{1,0:T(8,128)S(1)} %get-tuple-element.38, f32[64,32]{1,0:T(8,128)S(1)} %get-tuple-element.37, f32[8,8,16,256]{3,2,1,0:T(8,128)S(1)} %bitcast.43), kind=kOutput, calls=%fused_computation.12 | convolution fusion | flops 201330688 | bytes 2113536 | tf_op jit(solution)/shard_map/dot_general | solution.py:222
  66.6 1.6 %copy.38 = f32[64,16,256]{2,1,0:T(8,128)} copy(f32[64,16,256]{2,0,1:T(8,128)S(1)} %fusion.8) | data formatting | bytes 2097152 | tf_op jit(solution)/shard_map/dot_general | solution.py:222
  (34 shorter events, 0.2 us)
Async XLA Ops:
  0.0 1.9 %copy-start.1 = (f32[32,32,256]{2,1,0:T(8,128)S(1)}, f32[32,32,256]{2,1,0:T(8,128)}, u32[]{:S(2)}) copy-start(f32[32,32,256]{2,1,0:T(8,128)} %lam_ref.7) | copy-start | bytes 3145732
  1.9 13.2 %copy-start = (f32[32,32,256]{2,1,0:T(8,128)}, f32[32,32,256]{2,1,0:T(8,128)S(1)}, u32[]{:S(2)}) copy-start(f32[32,32,256]{2,1,0:T(8,128)S(1)} %convert_select_fusion.eta_ref) | copy-start | bytes 3145732
  1.9 9.2 %copy-start.5 = (bf16[32,2048]{1,0:T(8,128)(2,1)S(1)}, bf16[32,2048]{1,0:T(8,128)(2,1)}, u32[]{:S(2)}) copy-start(bf16[32,2048]{1,0:T(8,128)(2,1)} %param.15) | copy-start | bytes 393220
  2.8 19.3 %collective-permute-start = (f32[32,6,256]{2,1,0:T(8,128)}, f32[32,6,256]{2,1,0:T(8,128)S(1)}, u32[]{:S(2)}, u32[]{:S(2)}) collective-permute-start(f32[32,6,256]{2,1,0:T(8,128)} %pad_maximum_fusion.2), channel_id=1, source_target_pairs={{8,0},{16,8},{24,16},{9,1},{17,9},{25,17},{10,2},{18,10},{26,18},{... | collective-permute-start | bytes 589832 | tf_op jit(solution)/shard_map/ppermute | solution.py:165
  4.9 17.3 %collective-permute-start.1 = (f32[32,6,256]{2,1,0:T(8,128)}, f32[32,6,256]{2,1,0:T(8,128)}, u32[]{:S(2)}, u32[]{:S(2)}) collective-permute-start(f32[32,6,256]{2,1,0:T(8,128)} %pad_maximum_fusion.3), channel_id=1, source_target_pairs={{0,8},{8,16},{16,24},{1,9},{9,17},{17,25},{2,10},{10,18},{18,26},{... | collective-permute-start | bytes 589832 | tf_op jit(solution)/shard_map/ppermute | solution.py:164
  11.8 7.9 %all-to-all-start = ((bf16[32,4,512]{2,0,1:T(8,128)(2,1)}), bf16[32,4,512]{2,0,1:T(8,128)(2,1)S(1)}, u32[]{:S(2)}, u32[]{:S(2)}) async-start(bf16[32,4,512]{2,0,1:T(8,128)(2,1)} %bitcast.40), calls=%async_computation | async-start | bytes 262144 | tf_op jit(solution)/shard_map/all_to_all | solution.py:153
  15.6 1.4 %copy-start.7 = (s32[2048]{0:T(1024)S(1)}, s32[2048]{0:T(1024)}, u32[]{:S(2)}) copy-start(s32[2048]{0:T(1024)} %param.16) | copy-start | bytes 24580
  15.6 1.4 %copy-start.8 = (s32[4]{0:T(128)S(1)}, s32[4]{0:T(128)}, u32[]{:S(2)}) copy-start(s32[4]{0:T(128)} %param.17) | copy-start | bytes 52
  15.6 2.2 %copy-start.6 = (f32[64,64]{1,0:T(8,128)S(1)}, f32[64,64]{1,0:T(8,128)}, u32[]{:S(2)}) copy-start(f32[64,64]{1,0:T(8,128)} %param.14) | copy-start | bytes 49156
  25.8 7.5 %collective-permute-start.2 = (f32[7680]{0:T(1024)S(1)}, f32[7680]{0:T(1024)S(1)}, u32[]{:S(2)}, u32[]{:S(2)}) collective-permute-start(f32[7680]{0:T(1024)S(1)} %slice.74), channel_id=1, source_target_pairs={{2,0},{4,2},{6,4},{3,1},{5,3},{7,5},{10,8},{12,10},{14,12},{11,9},... | collective-permute-start | bytes 92168 | tf_op jit(solution)/shard_map/ppermute | solution.py:180
  29.2 5.3 %collective-permute-start.3 = (f32[7680]{0:T(1024)S(1)}, f32[7680]{0:T(1024)S(1)}, u32[]{:S(2)}, u32[]{:S(2)}) collective-permute-start(f32[7680]{0:T(1024)S(1)} %slice.79), channel_id=1, source_target_pairs={{0,2},{2,4},{4,6},{1,3},{3,5},{5,7},{8,10},{10,12},{12,14},{9,11},... | collective-permute-start | bytes 92168 | tf_op jit(solution)/shard_map/ppermute | solution.py:181
  40.7 7.4 %collective-permute-start.4 = (f32[8,16,256]{2,1,0:T(8,128)}, f32[8,16,256]{2,1,0:T(8,128)S(1)}, u32[]{:S(2)}, u32[]{:S(2)}) collective-permute-start(f32[8,16,256]{2,1,0:T(8,128)} %get-tuple-element.15), channel_id=1, source_target_pairs={{0,1},{1,0},{2,3},{3,2},{4,5},{5,4},{6,7},{7,6},{8,9},{9,8},{10,11... | collective-permute-start | bytes 393224 | tf_op jit(solution)/shard_map/ppermute | solution.py:212
  47.2 8.1 %collective-permute-start.5 = (f32[8,16,256]{2,1,0:T(8,128)}, f32[8,16,256]{2,1,0:T(8,128)S(1)}, u32[]{:S(2)}, u32[]{:S(2)}) collective-permute-start(f32[8,16,256]{2,1,0:T(8,128)} %get-tuple-element.17), channel_id=1, source_target_pairs={{0,1},{1,0},{2,3},{3,2},{4,5},{5,4},{6,7},{7,6},{8,9},{9,8},{10,11... | collective-permute-start | bytes 393224 | tf_op jit(solution)/shard_map/ppermute | solution.py:212
  48.2 0.7 copy-start.2
  52.4 9.0 %collective-permute-start.6 = (f32[8,16,256]{2,1,0:T(8,128)}, f32[8,16,256]{2,1,0:T(8,128)S(1)}, u32[]{:S(2)}, u32[]{:S(2)}) collective-permute-start(f32[8,16,256]{2,1,0:T(8,128)} %get-tuple-element.19), channel_id=1, source_target_pairs={{0,1},{1,0},{2,3},{3,2},{4,5},{5,4},{6,7},{7,6},{8,9},{9,8},{10,11... | collective-permute-start | bytes 393224 | tf_op jit(solution)/shard_map/ppermute | solution.py:212
  55.3 5.2 %copy-start.3 = (f32[8,16,256]{2,1,0:T(8,128)S(1)}, f32[8,16,256]{2,1,0:T(8,128)}, u32[]{:S(2)}) copy-start(f32[8,16,256]{2,1,0:T(8,128)} %copy-done.2) | copy-start | bytes 393220
  55.3 0.6 copy-start.4
  59.5 5.5 %collective-permute-start.7 = (f32[8,16,256]{2,1,0:T(8,128)}, f32[8,16,256]{2,1,0:T(8,128)S(1)}, u32[]{:S(2)}, u32[]{:S(2)}) collective-permute-start(f32[8,16,256]{2,1,0:T(8,128)} %get-tuple-element.20), channel_id=1, source_target_pairs={{0,1},{1,0},{2,3},{3,2},{4,5},{5,4},{6,7},{7,6},{8,9},{9,8},{10,11... | collective-permute-start | bytes 393224 | tf_op jit(solution)/shard_map/ppermute | solution.py:212

commit v4 on v3

--- a/solution.py
+++ b/solution.py
@@ -124,9 +124,9 @@
             pltpu.VMEM((bl, ext_r, ext_c), jnp.float32),
         ],
         cost_estimate=pl.CostEstimate(
-            flops=n_layers * ext_r * ext_c * 60,
+            flops=n_layers * ext_r * ext_c * 6000,
             transcendentals=0,
-            bytes_accessed=n_layers * (2 * ext_r * ext_c * 4 + rows * cols * 12),
+            bytes_accessed=n_layers * 1_600_000,
         ),
     )(rad_idx, lam, eta, rowh, colh, mask, vel, dep, after, recv)
 
@@ -212,17 +212,35 @@
         recvs.append(lax.ppermute(send, "rad", _pairs(n_rad, 1) + _pairs(n_rad, -1)))
         keeps.append(keep)
 
-    full_layers = radial_inverse.shape[0]
-    mine = jnp.concatenate(keeps, axis=0)
-    theirs = jnp.concatenate(recvs, axis=0)
-    columns = jnp.concatenate([mine, theirs], axis=0)
     my_cols = lax.dynamic_slice_in_dim(radial_inverse, r * layers, layers, axis=1)
     peer_cols = lax.dynamic_slice_in_dim(radial_inverse, (1 - r) * layers, layers, axis=1)
     r_perm = jnp.concatenate([my_cols, peer_cols], axis=1)
-    result = jnp.dot(
-        r_perm, columns.reshape(full_layers, -1), precision=lax.Precision.HIGHEST
-    )
-    return result.reshape(columns.shape)
+    return _radial(r_perm, keeps + recvs)
+
+
+def _radial_kernel(kr_ref, *refs):
+    pieces, out_ref = refs[:-1], refs[-1]
+    x = jnp.concatenate([p[...] for p in pieces], axis=0)
+    n_l, n_a, n_b = x.shape
+    tile = kr_ref.shape[0] // n_l
+    for t in range(n_a // tile):
+        xt = x[:, t * tile:(t + 1) * tile, :].reshape(n_l * tile, n_b)
+        yt = jnp.dot(kr_ref[...], xt, precision=lax.Precision.HIGHEST,
+                     preferred_element_type=jnp.float32)
+        out_ref[:, t * tile:(t + 1) * tile, :] = yt.reshape(n_l, tile, n_b)
+
+
+def _radial(r_perm, pieces):
+    tile = 8
+    n_l = r_perm.shape[0]
+    _, n_a, n_b = pieces[0].shape
+    kr = jnp.kron(r_perm, jnp.eye(tile, dtype=jnp.float32))
+    return pl.pallas_call(
+        _radial_kernel,
+        out_shape=jax.ShapeDtypeStruct((n_l, n_a, n_b), jnp.float32),
+        in_specs=[pl.BlockSpec(memory_space=pltpu.VMEM)] * (1 + len(pieces)),
+        out_specs=pl.BlockSpec(memory_space=pltpu.VMEM),
+    )(kr, *pieces)
 
 
 def solution(mesh):

time: 68.7 us -> 83 us (1.21)
  the two profiles are of different devices: /device:TPU:0 before, /device:TPU:26 now
where the time goes in v4:
time: 83 us; the launch traced here: 82.3 us
  local copies, waits for them, and re-layouts  25.6 us (31%)
  starting transfers between devices  20.2 us (24%)
  Pallas kernels  18.6 us (22%)
  other arithmetic  15.2 us (18%)
  matrix products  2.37 us (3%)
    pallas_call x4, Pallas kernels, _sweeps(): pl.pallas_call(_sweep_kernel, out_shape=out_shape, grid=grid, in_specs=[p...  14.2 us
    mul x1, local copies, waits for them, and re-layouts, _radial(): kr = jnp.kron(r_perm, jnp.eye(tile, dtype=jnp.float32))  13.4 us
    mul x1, other arithmetic, _radial(): kr = jnp.kron(r_perm, jnp.eye(tile, dtype=jnp.float32))  7.95 us
    ppermute x1, starting transfers between devices, per_device(): bot = lax.ppermute(bot_send, 'cap', _pairs(n_cap, -1))  5.26 us
    pallas_call x1, Pallas kernels, _radial(): pl.pallas_call(_radial_kernel, out_shape=jax.ShapeDtypeStruct((n_l, n_a,...  4.4 us
    ppermute x4, starting transfers between devices, per_device(): lax.ppermute(send, 'rad', _pairs(n_rad, 1) + _pairs(n_rad, -1))  4.05 us
    all_to_all x1, starting transfers between devices, per_device(): lax.all_to_all(marker_rows, 'lat', split_axis=1, concat_axis=1, tiled=True)  3.83 us
    ppermute x1, starting transfers between devices, per_device(): from_right = lax.ppermute(flat[:piece], 'lat', _pairs(n_lat, -1))  3.8 us
  transfers between devices with their start and end apart: 9, of which 1 were waited for; matrix products, arithmetic and copies ran while one was open for 39% of the time, Pallas kernels for 13%

profile of v4, /device:TPU:26, one launch (start us, length us, event | category | flops | bytes accessed | tf_op | source)
XLA Modules:
  0.0 82.3 jit_solution(9252684859359952221)
XLA Ops:
  0.0 1.9 %convert_select_fusion.eta_ref = f32[32,32,256]{2,1,0:T(8,128)S(1)} fusion(bf16[32,32,256]{2,1,0:T(8,128)(2,1)} %param.11, bf16[32,32,256]{2,1,0:T(8,128)(2,1)} %param.12, s32[32,32,256]{2,1,0:T(8,128)} %param.13), kind=kLoop, calls=%fused_computation.8 | loop fusion | flops 1835008 | bytes 3145728 | tf_op jit(solution)/shard_map/jit(_where)/select_n | solution.py:157
  1.9 0.0 copy-start
  1.9 0.0 copy-start.6
  2.0 0.1 fusion.18
  2.1 0.7 pad_maximum_fusion.3
  2.8 1.3 %collective-permute-start.1 = (f32[32,6,256]{2,1,0:T(8,128)}, f32[32,6,256]{2,1,0:T(8,128)S(1)}, u32[]{:S(2)}, u32[]{:S(2)}) collective-permute-start(f32[32,6,256]{2,1,0:T(8,128)} %pad_maximum_fusion.3), channel_id=1, source_target_pairs={{0,8},{8,16},{16,24},{1,9},{9,17},{17,25},{2,10},{10,18},{18,26},{... | collective-permute-start | bytes 589832 | tf_op jit(solution)/shard_map/ppermute | solution.py:164
  4.1 0.8 pad_maximum_fusion.2
  4.9 5.3 %collective-permute-start = (f32[32,6,256]{2,1,0:T(8,128)}, f32[32,6,256]{2,1,0:T(8,128)}, u32[]{:S(2)}, u32[]{:S(2)}) collective-permute-start(f32[32,6,256]{2,1,0:T(8,128)} %pad_maximum_fusion.2), channel_id=1, source_target_pairs={{8,0},{16,8},{24,16},{9,1},{17,9},{25,17},{10,2},{18,10},{26,18},{... | collective-permute-start | bytes 589832 | tf_op jit(solution)/shard_map/ppermute | solution.py:165
  10.1 0.7 copy.38
  10.8 3.8 %all-to-all-start = ((bf16[32,4,512]{2,0,1:T(8,128)(2,1)}), bf16[32,4,512]{2,0,1:T(8,128)(2,1)S(1)}, u32[]{:S(2)}, u32[]{:S(2)}) async-start(bf16[32,4,512]{2,0,1:T(8,128)(2,1)} %bitcast.28), calls=%async_computation | async-start | bytes 262144 | tf_op jit(solution)/shard_map/all_to_all | solution.py:153
  14.6 0.2 fusion.17
  14.8 0.2 fusion.16
  15.1 0.0 copy-start.9
  15.1 0.3 copy.27
  15.3 0.3 copy.33
  15.6 0.3 copy.22
  15.9 0.3 copy.32
  16.2 0.1 pad.21.clone
  16.3 0.1 pad.1.clone
  16.4 0.1 fusion.11
  16.5 0.7 and_convert_fusion.mask_ref
  17.2 0.1 fusion.9
  17.3 0.1 constant_dynamic-slice_fusion.1
  17.4 0.1 pad_maximum_fusion.8
  17.5 0.1 all-to-all-done
  17.6 2.4 %fusion.dep_ref = f32[32,32,256]{2,1,0:T(8,128)} fusion(pred[32,2048]{1,0:T(8,128)(4,1)S(1)} %fusion.9, bf16[32,2048]{1,0:T(8,128)(2,1)S(1)} %bitcast.33, s32[2048]{0:T(1024)S(1)} %get-tuple-element.39), kind=kOutput, calls=%fused_computation.1 | convolution fusion | flops 1076363264 | bytes 1253376 | tf_op jit(solution)/shard_map/las,sb->lab/dot_general | solution.py:196
  20.0 0.1 fusion.23
  20.0 1.1 %fusion.22 = (f32[32,3,256]{2,1,0:T(4,128)S(1)}, f32[32,3,256]{2,1,0:T(4,128)S(1)}) fusion(f32[32,6,256]{2,1,0:T(8,128)} %collective-permute-done), kind=kLoop, calls=%fused_computation.60 | loop fusion | bytes 393216 | tf_op jit(solution)/shard_map/slice | solution.py:168
  21.1 0.1 pad_maximum_fusion.4
  21.3 0.1 fusion.21
  21.4 0.3 copy.28
  21.6 0.1 fusion.20
  21.8 0.3 copy.26
  22.0 0.1 maximum_bitcast_fusion.3
  22.1 0.1 maximum_bitcast_fusion.2
  22.2 0.5 copy.29
  22.7 0.9 %slice.79 = f32[7680]{0:T(1024)S(1)} reshape(f32[2,32,40,3]{3,2,1,0:T(8,128)S(1)} %copy.29) | data formatting | bytes 61440 | tf_op jit(solution)/shard_map/slice | solution.py:181
  23.6 1.9 %collective-permute-start.3 = (f32[7680]{0:T(1024)S(1)}, f32[7680]{0:T(1024)S(1)}, u32[]{:S(2)}, u32[]{:S(2)}) collective-permute-start(f32[7680]{0:T(1024)S(1)} %slice.79), channel_id=1, source_target_pairs={{0,2},{2,4},{4,6},{1,3},{3,5},{5,7},{8,10},{10,12},{12,14},{9,11},... | collective-permute-start | bytes 92168 | tf_op jit(solution)/shard_map/ppermute | solution.py:181
  25.6 0.3 copy.23
  25.9 0.3 copy.21
  26.1 0.1 maximum_bitcast_fusion.1
  26.2 0.1 maximum_bitcast_fusion
  26.3 0.5 copy.24
  26.9 0.9 %slice.74 = f32[7680]{0:T(1024)S(1)} reshape(f32[2,32,40,3]{3,2,1,0:T(8,128)S(1)} %copy.24) | data formatting | bytes 61440 | tf_op jit(solution)/shard_map/slice | solution.py:180
  27.7 3.8 %collective-permute-start.2 = (f32[7680]{0:T(1024)S(1)}, f32[7680]{0:T(1024)S(1)}, u32[]{:S(2)}, u32[]{:S(2)}) collective-permute-start(f32[7680]{0:T(1024)S(1)} %slice.74), channel_id=1, source_target_pairs={{2,0},{4,2},{6,4},{3,1},{5,3},{7,5},{10,8},{12,10},{14,12},{11,9},... | collective-permute-start | bytes 92168 | tf_op jit(solution)/shard_map/ppermute | solution.py:180
  31.5 0.8 %pad_maximum_fusion.1.rowh_ref = f32[2,32,8,256]{3,2,1,0:T(8,128)} fusion(f32[1,32,8,256]{3,2,1,0:T(8,128)S(1)} %bitcast.30, f32[1,32,8,256]{3,2,1,0:T(8,128)S(1)} %bitcast.29), kind=kLoop, calls=%fused_computation.14 | loop fusion | flops 131072 | bytes 1048576 | tf_op jit(solution)/shard_map/stack | solution.py:167
  32.4 1.2 %concatenate.47 = f32[2,32,40,3]{3,2,1,0:T(8,128)S(1)} reshape(f32[7680]{0:T(1024)S(1)} %collective-permute-done.3) | data formatting | bytes 61440 | tf_op jit(solution)/shard_map/concatenate | solution.py:182
  33.6 1.2 %concatenate.44 = f32[2,32,40,3]{3,2,1,0:T(8,128)S(1)} reshape(f32[7680]{0:T(1024)S(1)} %collective-permute-done.2) | data formatting | bytes 61440 | tf_op jit(solution)/shard_map/concatenate | solution.py:182
  34.8 1.5 %pad_maximum_fusion.colh_ref = f32[2,32,40,128]{3,2,1,0:T(8,128)} fusion(f32[2,32,40,3]{3,2,1,0:T(8,128)S(1)} %concatenate.47, f32[2,32,40,3]{3,2,1,0:T(8,128)S(1)} %concatenate.44, f32[128]{0:T(128)S(1)} %pad.1.clone), kind=kLoop, calls=%fused_computation.11 | loop fusion | flops 655360 | bytes 1372672 | tf_op jit(solution)/shard_map/concatenate | solution.py:184
  36.3 3.5 %shard_map.91 = (f32[8,16,256]{2,1,0:T(8,128)}, f32[8,16,256]{2,1,0:T(8,128)}) custom-call(s32[1]{0:T(128)} %bitcast.rad_ref.after_ref.recv_ref, f32[32,32,256]{2,1,0:T(8,128)} %lam_ref.7, f32[32,32,256]{2,1,0:T(8,128)} %copy-done, f32[2,32,8,256]{3,2,1,0:T(8,128)} %pad_maximum_fusion.1.rowh_ref, f32[2,32,40,128]{3,2,1,0:T(8,128)} %pad_maximum_fusion.colh_ref, ...), custom_call_target="tpu_custom_call" | custom-call | flops 737280000 | bytes 12800000 | tf_op jit(solution)/shard_map/pallas_call | solution.py:102
  39.8 1.5 %collective-permute-start.4 = (f32[8,16,256]{2,1,0:T(8,128)}, f32[8,16,256]{2,1,0:T(8,128)S(1)}, u32[]{:S(2)}, u32[]{:S(2)}) collective-permute-start(f32[8,16,256]{2,1,0:T(8,128)} %get-tuple-element.15), channel_id=1, source_target_pairs={{0,1},{1,0},{2,3},{3,2},{4,5},{5,4},{6,7},{7,6},{8,9},{9,8},{10,11... | collective-permute-start | bytes 393224 | tf_op jit(solution)/shard_map/ppermute | solution.py:212
  41.3 3.5 %shard_map.92 = (f32[8,16,256]{2,1,0:T(8,128)}, f32[8,16,256]{2,1,0:T(8,128)}) custom-call(s32[1]{0:T(128)} %bitcast.rad_ref.after_ref.recv_ref, f32[32,32,256]{2,1,0:T(8,128)} %lam_ref.7, f32[32,32,256]{2,1,0:T(8,128)} %copy-done, f32[2,32,8,256]{3,2,1,0:T(8,128)} %pad_maximum_fusion.1.rowh_ref, f32[2,32,40,128]{3,2,1,0:T(8,128)} %pad_maximum_fusion.colh_ref, ...), custom_call_target="tpu_custom_call" | custom-call | flops 737280000 | bytes 12800000 | tf_op jit(solution)/shard_map/pallas_call | solution.py:102
  44.9 0.5 collective-permute-start.5
  45.4 0.7 copy-done.2
  46.1 3.5 %shard_map.93 = (f32[8,16,256]{2,1,0:T(8,128)}, f32[8,16,256]{2,1,0:T(8,128)}) custom-call(s32[1]{0:T(128)} %bitcast.rad_ref.after_ref.recv_ref, f32[32,32,256]{2,1,0:T(8,128)} %lam_ref.7, f32[32,32,256]{2,1,0:T(8,128)} %copy-done, f32[2,32,8,256]{3,2,1,0:T(8,128)} %pad_maximum_fusion.1.rowh_ref, f32[2,32,40,128]{3,2,1,0:T(8,128)} %pad_maximum_fusion.colh_ref, ...), custom_call_target="tpu_custom_call" | custom-call | flops 737280000 | bytes 12800000 | tf_op jit(solution)/shard_map/pallas_call | solution.py:102
  49.6 1.5 %collective-permute-start.6 = (f32[8,16,256]{2,1,0:T(8,128)}, f32[8,16,256]{2,1,0:T(8,128)S(1)}, u32[]{:S(2)}, u32[]{:S(2)}) collective-permute-start(f32[8,16,256]{2,1,0:T(8,128)} %get-tuple-element.19), channel_id=1, source_target_pairs={{0,1},{1,0},{2,3},{3,2},{4,5},{5,4},{6,7},{7,6},{8,9},{9,8},{10,11... | collective-permute-start | bytes 393224 | tf_op jit(solution)/shard_map/ppermute | solution.py:212
  51.1 0.6 copy-done.3
  51.8 3.5 %shard_map.94 = (f32[8,16,256]{2,1,0:T(8,128)}, f32[8,16,256]{2,1,0:T(8,128)}) custom-call(s32[1]{0:T(128)} %bitcast.rad_ref.after_ref.recv_ref, f32[32,32,256]{2,1,0:T(8,128)} %lam_ref.7, f32[32,32,256]{2,1,0:T(8,128)} %copy-done, f32[2,32,8,256]{3,2,1,0:T(8,128)} %pad_maximum_fusion.1.rowh_ref, f32[2,32,40,128]{3,2,1,0:T(8,128)} %pad_maximum_fusion.colh_ref, ...), custom_call_target="tpu_custom_call" | custom-call | flops 737280000 | bytes 12800000 | tf_op jit(solution)/shard_map/pallas_call | solution.py:102
  55.3 0.5 collective-permute-start.7
  55.8 8.0 %broadcast_multiply_fusion = f32[64,8,64,8]{3,2,1,0:T(8,128)} fusion(f32[8,8]{1,0:T(8,128)S(1)} %fusion.13, f32[64,64]{1,0:T(8,128)S(1)} %pad_maximum_fusion.8), kind=kLoop, calls=%fused_computation | loop fusion | flops 262144 | bytes 1065216 | tf_op jit(solution)/shard_map/jit(kron)/mul | solution.py:237
  63.8 13.4 %mul.44.kr_ref = f32[512,512]{1,0:T(8,128)} reshape(f32[64,8,64,8]{3,2,1,0:T(8,128)} %broadcast_multiply_fusion) | data formatting | bytes 2097152 | tf_op jit(solution)/shard_map/jit(kron)/mul | solution.py:237
  77.2 0.6 copy-done.4
  77.9 0.1 copy-done.5
  77.9 4.4 %shard_map.95 = f32[64,16,256]{2,1,0:T(8,128)} custom-call(f32[512,512]{1,0:T(8,128)} %mul.44.kr_ref, f32[8,16,256]{2,1,0:T(8,128)} %get-tuple-element.13.after_ref.refs_0_, f32[8,16,256]{2,1,0:T(8,128)} %get-tuple-element.14.after_ref.refs_1_, f32[8,16,256]{2,1,0:T(8,128)} %get-tuple-element.16.after_ref.refs_2_, f32[8,16,256]{2,1,0:T(8,128)} %get-tuple-element.18.refs_3_, ...), custom_call_target="tpu_custom_call" | custom-call | tf_op jit(solution)/shard_map/pallas_call | solution.py:238
  (31 shorter events, 0.1 us)
Async XLA Ops:
  0.0 1.9 %copy-start.1 = (f32[32,32,256]{2,1,0:T(8,128)S(1)}, f32[32,32,256]{2,1,0:T(8,128)}, u32[]{:S(2)}) copy-start(f32[32,32,256]{2,1,0:T(8,128)} %lam_ref.7) | copy-start | bytes 3145732
  1.9 12.7 %copy-start = (f32[32,32,256]{2,1,0:T(8,128)}, f32[32,32,256]{2,1,0:T(8,128)S(1)}, u32[]{:S(2)}) copy-start(f32[32,32,256]{2,1,0:T(8,128)S(1)} %convert_select_fusion.eta_ref) | copy-start | bytes 3145732
  1.9 8.2 %copy-start.6 = (bf16[32,2048]{1,0:T(8,128)(2,1)S(1)}, bf16[32,2048]{1,0:T(8,128)(2,1)}, u32[]{:S(2)}) copy-start(bf16[32,2048]{1,0:T(8,128)(2,1)} %param.15) | copy-start | bytes 393220
  2.8 17.2 %collective-permute-start.1 = (f32[32,6,256]{2,1,0:T(8,128)}, f32[32,6,256]{2,1,0:T(8,128)S(1)}, u32[]{:S(2)}, u32[]{:S(2)}) collective-permute-start(f32[32,6,256]{2,1,0:T(8,128)} %pad_maximum_fusion.3), channel_id=1, source_target_pairs={{0,8},{8,16},{16,24},{1,9},{9,17},{17,25},{2,10},{10,18},{18,26},{... | collective-permute-start | bytes 589832 | tf_op jit(solution)/shard_map/ppermute | solution.py:164
  4.9 15.2 %collective-permute-start = (f32[32,6,256]{2,1,0:T(8,128)}, f32[32,6,256]{2,1,0:T(8,128)}, u32[]{:S(2)}, u32[]{:S(2)}) collective-permute-start(f32[32,6,256]{2,1,0:T(8,128)} %pad_maximum_fusion.2), channel_id=1, source_target_pairs={{8,0},{16,8},{24,16},{9,1},{17,9},{25,17},{10,2},{18,10},{26,18},{... | collective-permute-start | bytes 589832 | tf_op jit(solution)/shard_map/ppermute | solution.py:165
  10.8 6.8 %all-to-all-start = ((bf16[32,4,512]{2,0,1:T(8,128)(2,1)}), bf16[32,4,512]{2,0,1:T(8,128)(2,1)S(1)}, u32[]{:S(2)}, u32[]{:S(2)}) async-start(bf16[32,4,512]{2,0,1:T(8,128)(2,1)} %bitcast.28), calls=%async_computation | async-start | bytes 262144 | tf_op jit(solution)/shard_map/all_to_all | solution.py:153
  15.0 1.4 %copy-start.8 = (s32[2048]{0:T(1024)S(1)}, s32[2048]{0:T(1024)}, u32[]{:S(2)}) copy-start(s32[2048]{0:T(1024)} %param.16) | copy-start | bytes 24580
  15.1 1.4 %copy-start.9 = (s32[4]{0:T(128)S(1)}, s32[4]{0:T(128)}, u32[]{:S(2)}) copy-start(s32[4]{0:T(128)} %param.17) | copy-start | bytes 52
  15.1 2.2 %copy-start.7 = (f32[64,64]{1,0:T(8,128)S(1)}, f32[64,64]{1,0:T(8,128)}, u32[]{:S(2)}) copy-start(f32[64,64]{1,0:T(8,128)} %param.14) | copy-start | bytes 49156
  23.6 8.8 %collective-permute-start.3 = (f32[7680]{0:T(1024)S(1)}, f32[7680]{0:T(1024)S(1)}, u32[]{:S(2)}, u32[]{:S(2)}) collective-permute-start(f32[7680]{0:T(1024)S(1)} %slice.79), channel_id=1, source_target_pairs={{0,2},{2,4},{4,6},{1,3},{3,5},{5,7},{8,10},{10,12},{12,14},{9,11},... | collective-permute-start | bytes 92168 | tf_op jit(solution)/shard_map/ppermute | solution.py:181
  27.7 5.8 %collective-permute-start.2 = (f32[7680]{0:T(1024)S(1)}, f32[7680]{0:T(1024)S(1)}, u32[]{:S(2)}, u32[]{:S(2)}) collective-permute-start(f32[7680]{0:T(1024)S(1)} %slice.74), channel_id=1, source_target_pairs={{2,0},{4,2},{6,4},{3,1},{5,3},{7,5},{10,8},{12,10},{14,12},{11,9},... | collective-permute-start | bytes 92168 | tf_op jit(solution)/shard_map/ppermute | solution.py:180
  39.8 5.6 %collective-permute-start.4 = (f32[8,16,256]{2,1,0:T(8,128)}, f32[8,16,256]{2,1,0:T(8,128)S(1)}, u32[]{:S(2)}, u32[]{:S(2)}) collective-permute-start(f32[8,16,256]{2,1,0:T(8,128)} %get-tuple-element.15), channel_id=1, source_target_pairs={{0,1},{1,0},{2,3},{3,2},{4,5},{5,4},{6,7},{7,6},{8,9},{9,8},{10,11... | collective-permute-start | bytes 393224 | tf_op jit(solution)/shard_map/ppermute | solution.py:212
  44.9 6.2 %collective-permute-start.5 = (f32[8,16,256]{2,1,0:T(8,128)}, f32[8,16,256]{2,1,0:T(8,128)S(1)}, u32[]{:S(2)}, u32[]{:S(2)}) collective-permute-start(f32[8,16,256]{2,1,0:T(8,128)} %get-tuple-element.17), channel_id=1, source_target_pairs={{0,1},{1,0},{2,3},{3,2},{4,5},{5,4},{6,7},{7,6},{8,9},{9,8},{10,11... | collective-permute-start | bytes 393224 | tf_op jit(solution)/shard_map/ppermute | solution.py:212
  45.4 0.7 copy-start.2
  49.6 27.6 %collective-permute-start.6 = (f32[8,16,256]{2,1,0:T(8,128)}, f32[8,16,256]{2,1,0:T(8,128)S(1)}, u32[]{:S(2)}, u32[]{:S(2)}) collective-permute-start(f32[8,16,256]{2,1,0:T(8,128)} %get-tuple-element.19), channel_id=1, source_target_pairs={{0,1},{1,0},{2,3},{3,2},{4,5},{5,4},{6,7},{7,6},{8,9},{9,8},{10,11... | collective-permute-start | bytes 393224 | tf_op jit(solution)/shard_map/ppermute | solution.py:212
  51.1 0.6 copy-start.3
  55.3 21.9 %collective-permute-start.7 = (f32[8,16,256]{2,1,0:T(8,128)}, f32[8,16,256]{2,1,0:T(8,128)S(1)}, u32[]{:S(2)}, u32[]{:S(2)}) collective-permute-start(f32[8,16,256]{2,1,0:T(8,128)} %get-tuple-element.20), channel_id=1, source_target_pairs={{0,1},{1,0},{2,3},{3,2},{4,5},{5,4},{6,7},{7,6},{8,9},{9,8},{10,11... | collective-permute-start | bytes 393224 | tf_op jit(solution)/shard_map/ppermute | solution.py:212
  77.2 0.7 copy-start.4
  77.2 0.7 copy-start.5

commit v5 on v3

--- a/solution.py
+++ b/solution.py
@@ -1,3 +1,5 @@
+import functools
+
 import jax
 import jax.numpy as jnp
 from jax import lax
@@ -124,9 +126,9 @@
             pltpu.VMEM((bl, ext_r, ext_c), jnp.float32),
         ],
         cost_estimate=pl.CostEstimate(
-            flops=n_layers * ext_r * ext_c * 60,
+            flops=n_layers * ext_r * ext_c * 6000,
             transcendentals=0,
-            bytes_accessed=n_layers * (2 * ext_r * ext_c * 4 + rows * cols * 12),
+            bytes_accessed=n_layers * 1_600_000,
         ),
     )(rad_idx, lam, eta, rowh, colh, mask, vel, dep, after, recv)
 
@@ -212,17 +214,47 @@
         recvs.append(lax.ppermute(send, "rad", _pairs(n_rad, 1) + _pairs(n_rad, -1)))
         keeps.append(keep)
 
-    full_layers = radial_inverse.shape[0]
-    mine = jnp.concatenate(keeps, axis=0)
-    theirs = jnp.concatenate(recvs, axis=0)
-    columns = jnp.concatenate([mine, theirs], axis=0)
     my_cols = lax.dynamic_slice_in_dim(radial_inverse, r * layers, layers, axis=1)
     peer_cols = lax.dynamic_slice_in_dim(radial_inverse, (1 - r) * layers, layers, axis=1)
     r_perm = jnp.concatenate([my_cols, peer_cols], axis=1)
-    result = jnp.dot(
-        r_perm, columns.reshape(full_layers, -1), precision=lax.Precision.HIGHEST
-    )
-    return result.reshape(columns.shape)
+    pieces = keeps + recvs
+    split = len(pieces) - 2
+    step = pieces[0].shape[0]
+    partial = _radial(r_perm[:, :split * step], pieces[:split], after=recvs[-2])
+    return _radial(r_perm[:, split * step:], pieces[split:], partial=partial)
+
+
+def _radial_kernel(n_pieces, has_partial, r_ref, *refs):
+    pieces = refs[:n_pieces]
+    rest = refs[n_pieces:]
+    partial_ref = rest[0] if has_partial else None
+    out_ref, xs = rest[-2], rest[-1]
+    step = pieces[0].shape[0]
+    for i, p in enumerate(pieces):
+        xs[i * step:(i + 1) * step] = p[...]
+    rmat = r_ref[...]
+    for a in range(xs.shape[1]):
+        y = jnp.dot(rmat, xs[:, a, :], precision=lax.Precision.HIGHEST,
+                    preferred_element_type=jnp.float32)
+        if has_partial:
+            y = partial_ref[:, a, :] + y
+        out_ref[:, a, :] = y
+
+
+def _radial(r_cols, pieces, partial=None, after=None):
+    n_k, n_l = r_cols.shape
+    _, n_a, n_b = pieces[0].shape
+    extra = [] if partial is None else [partial]
+    fake = [] if after is None else [after]
+    in_specs = [pl.BlockSpec(memory_space=pltpu.VMEM)] * (1 + len(pieces) + len(extra))
+    in_specs += [pl.BlockSpec(memory_space=pl.ANY)] * len(fake)
+    return pl.pallas_call(
+        functools.partial(_radial_kernel, len(pieces), partial is not None),
+        out_shape=jax.ShapeDtypeStruct((n_k, n_a, n_b), jnp.float32),
+        in_specs=in_specs,
+        out_specs=pl.BlockSpec(memory_space=pltpu.VMEM),
+        scratch_shapes=[pltpu.VMEM((n_l, n_a, n_b), jnp.float32)],
+    )(r_cols, *pieces, *extra, *fake)
 
 
 def solution(mesh):

time: 68.7 us -> 67.7 us (0.985)
  Pallas kernels: 14.2 us -> 21.1 us
  local copies, waits for them, and re-layouts: 17.7 us -> 13.9 us
  waiting for transfers between devices: 5.35 us -> 2.4 us
  matrix products: 3.96 us -> 2.37 us
    pallas_call x0 -> x2, Pallas kernels: none -> 6.88 us  [_radial(): pl.pallas_call(functools.partial(_radial_kernel, len(pieces), partial is...]
    unnamed x28 -> x23, local copies, waits for them, and re-layouts: 6.51 us -> 3.62 us
    ppermute x4, waiting for transfers between devices: 3.52 us -> 0.87 us  [per_device(): lax.ppermute(send, 'rad', _pairs(n_rad, 1) + _pairs(n_rad, -1))]
    dot_general x1 -> x0, matrix products: 1.59 us -> none  [per_device(): jnp.dot(r_perm, columns.reshape(full_layers, -1), precision=lax.Precision...]
    dot_general x1 -> x0, local copies, waits for them, and re-layouts: 1.58 us -> none  [per_device(): jnp.dot(r_perm, columns.reshape(full_layers, -1), precision=lax.Precision...]
    concatenate x0 -> x1, other arithmetic: none -> 0.69 us  [per_device(): r_perm = jnp.concatenate([my_cols, peer_cols], axis=1)]
  transfers between devices with their start and end apart: 9 -> 9, of which waited for: 2 -> 2; matrix products, arithmetic and copies ran while one was open for 22% -> 18% of each run, Pallas kernels for 16% -> 21%
where the time goes in v5:
time: 67.7 us; the launch traced here: 67.2 us
  Pallas kernels  21.1 us (31%)
  starting transfers between devices  19.4 us (29%)
  local copies, waits for them, and re-layouts  13.9 us (21%)
  other arithmetic  7.83 us (12%)
  waiting for transfers between devices  2.4 us (4%)
  matrix products  2.37 us (4%)
    pallas_call x4, Pallas kernels, _sweeps(): pl.pallas_call(_sweep_kernel, out_shape=out_shape, grid=grid, in_specs=[p...  14.2 us
    pallas_call x2, Pallas kernels, _radial(): pl.pallas_call(functools.partial(_radial_kernel, len(pieces), partial is...  6.88 us
    ppermute x1, starting transfers between devices, per_device(): top = lax.ppermute(top_send, 'cap', _pairs(n_cap, 1))  6.25 us
    ppermute x4, starting transfers between devices, per_device(): lax.ppermute(send, 'rad', _pairs(n_rad, 1) + _pairs(n_rad, -1))  4.05 us
    unnamed x23, local copies, waits for them, and re-layouts  3.62 us
    all_to_all x1, starting transfers between devices, per_device(): lax.all_to_all(marker_rows, 'lat', split_axis=1, concat_axis=1, tiled=True)  3.32 us
    ppermute x1, starting transfers between devices, per_device(): from_left = lax.ppermute(flat[piece:], 'lat', _pairs(n_lat, 1))  3.21 us
    concatenate x2, local copies, waits for them, and re-layouts, per_device(): jnp.concatenate([from_right, from_left]).reshape(2, 2, layers, ext_rows, g)  2.37 us
  transfers between devices with their start and end apart: 9, of which 2 were waited for; matrix products, arithmetic and copies ran while one was open for 18% of the time, Pallas kernels for 21%

profile of v5, /device:TPU:0, one launch (start us, length us, event | category | flops | bytes accessed | tf_op | source)
XLA Modules:
  0.0 67.2 jit_solution(8872495019198746265)
XLA Ops:
  0.0 1.9 %convert_select_fusion.eta_ref = f32[32,32,256]{2,1,0:T(8,128)S(1)} fusion(bf16[32,32,256]{2,1,0:T(8,128)(2,1)} %param.11, bf16[32,32,256]{2,1,0:T(8,128)(2,1)} %param.12, s32[32,32,256]{2,1,0:T(8,128)} %param.13), kind=kLoop, calls=%fused_computation.7 | loop fusion | flops 1835008 | bytes 3145728 | tf_op jit(solution)/shard_map/jit(_where)/select_n | solution.py:159
  1.9 0.0 copy-start.7
  2.0 0.1 fusion.17
  2.1 0.8 %pad_maximum_fusion.2 = f32[32,6,256]{2,1,0:T(8,128)} fusion(f32[32,3,256]{2,1,0:T(4,128)S(1)} %get-tuple-element.44, f32[32,3,256]{2,1,0:T(4,128)S(1)} %get-tuple-element.25), kind=kLoop, calls=%fused_computation.14 | loop fusion | flops 49152 | bytes 393216 | tf_op jit(solution)/shard_map/concatenate | solution.py:165
  2.8 1.3 %collective-permute-start = (f32[32,6,256]{2,1,0:T(8,128)}, f32[32,6,256]{2,1,0:T(8,128)S(1)}, u32[]{:S(2)}, u32[]{:S(2)}) collective-permute-start(f32[32,6,256]{2,1,0:T(8,128)} %pad_maximum_fusion.2), channel_id=1, source_target_pairs={{8,0},{16,8},{24,16},{9,1},{17,9},{25,17},{10,2},{18,10},{26,18},{... | collective-permute-start | bytes 589832 | tf_op jit(solution)/shard_map/ppermute | solution.py:167
  4.1 0.7 %pad_maximum_fusion.3 = f32[32,6,256]{2,1,0:T(8,128)} fusion(f32[32,3,256]{2,1,0:T(4,128)S(1)} %get-tuple-element.43, f32[32,3,256]{2,1,0:T(4,128)S(1)} %get-tuple-element.26), kind=kLoop, calls=%fused_computation.15 | loop fusion | flops 49152 | bytes 393216 | tf_op jit(solution)/shard_map/concatenate | solution.py:164
  4.9 6.3 %collective-permute-start.1 = (f32[32,6,256]{2,1,0:T(8,128)}, f32[32,6,256]{2,1,0:T(8,128)}, u32[]{:S(2)}, u32[]{:S(2)}) collective-permute-start(f32[32,6,256]{2,1,0:T(8,128)} %pad_maximum_fusion.3), channel_id=1, source_target_pairs={{0,8},{8,16},{16,24},{1,9},{9,17},{17,25},{2,10},{10,18},{18,26},{... | collective-permute-start | bytes 589832 | tf_op jit(solution)/shard_map/ppermute | solution.py:166
  11.1 0.7 copy.38
  11.8 3.3 %all-to-all-start = ((bf16[32,4,512]{2,0,1:T(8,128)(2,1)}), bf16[32,4,512]{2,0,1:T(8,128)(2,1)S(1)}, u32[]{:S(2)}, u32[]{:S(2)}) async-start(bf16[32,4,512]{2,0,1:T(8,128)(2,1)} %bitcast.26), calls=%async_computation | async-start | bytes 262144 | tf_op jit(solution)/shard_map/all_to_all | solution.py:155
  15.1 0.2 fusion.16
  15.4 0.2 fusion.15
  15.6 0.4 copy-done.8
  16.1 0.1 fusion.11
  16.2 0.1 fusion.9
  16.2 0.7 %and_convert_fusion.mask_ref = f32[40,384]{1,0:T(8,128)} fusion(pred[384]{0:T(512)(128)(4,1)S(1)} %compare_and_fusion, pred[40]{0:T(512)(128)(4,1)S(1)} %compare_and_fusion.1), kind=kLoop, calls=%fused_computation.23 | loop fusion | flops 30720 | bytes 61864 | tf_op jit(solution)/shard_map/convert_element_type | solution.py:28
  16.9 0.3 copy.22
  17.2 0.3 copy.32
  17.5 0.3 copy.27
  17.7 0.3 copy.33
  18.0 0.1 pad.23.clone
  18.1 0.1 pad.3.clone
  18.2 1.5 %all-to-all-done = bf16[32,4,512]{2,0,1:T(8,128)(2,1)S(1)} async-done(((bf16[32,4,512]{2,0,1:T(8,128)(2,1)}), bf16[32,4,512]{2,0,1:T(8,128)(2,1)S(1)}, u32[]{:S(2)}, u32[]{:S(2)}) %all-to-all-start) | async-done | bytes 131104 | tf_op jit(solution)/shard_map/all_to_all | solution.py:155
  19.7 2.4 %fusion.dep_ref = f32[32,32,256]{2,1,0:T(8,128)} fusion(pred[32,2048]{1,0:T(8,128)(4,1)S(1)} %fusion.9, bf16[32,2048]{1,0:T(8,128)(2,1)S(1)} %bitcast.31, s32[2048]{0:T(1024)S(1)} %get-tuple-element.39), kind=kOutput, calls=%fused_computation | convolution fusion | flops 1076363264 | bytes 1253376 | tf_op jit(solution)/shard_map/las,sb->lab/dot_general | solution.py:198
  22.1 0.1 fusion.21
  22.2 1.1 %fusion.22 = (f32[32,3,256]{2,1,0:T(4,128)S(1)}, f32[32,3,256]{2,1,0:T(4,128)S(1)}) fusion(f32[32,6,256]{2,1,0:T(8,128)} %collective-permute-done.1), kind=kLoop, calls=%fused_computation.59 | loop fusion | bytes 393216 | tf_op jit(solution)/shard_map/slice | solution.py:170
  23.3 0.1 pad_maximum_fusion.4
  23.4 0.1 fusion.20
  23.5 0.3 copy.23
  23.8 0.1 fusion.19
  23.9 0.3 copy.21
  24.2 0.1 maximum_bitcast_fusion.1
  24.3 0.1 maximum_bitcast_fusion
  24.4 0.5 copy.24
  24.9 0.9 %slice.81 = f32[7680]{0:T(1024)S(1)} reshape(f32[2,32,40,3]{3,2,1,0:T(8,128)S(1)} %copy.24) | data formatting | bytes 61440 | tf_op jit(solution)/shard_map/slice | solution.py:182
  25.8 1.3 %collective-permute-start.2 = (f32[7680]{0:T(1024)S(1)}, f32[7680]{0:T(1024)S(1)}, u32[]{:S(2)}, u32[]{:S(2)}) collective-permute-start(f32[7680]{0:T(1024)S(1)} %slice.81), channel_id=1, source_target_pairs={{2,0},{4,2},{6,4},{3,1},{5,3},{7,5},{10,8},{12,10},{14,12},{11,9},... | collective-permute-start | bytes 92168 | tf_op jit(solution)/shard_map/ppermute | solution.py:182
  27.1 0.3 copy.28
  27.3 0.3 copy.26
  27.6 0.1 maximum_bitcast_fusion.3
  27.7 0.1 maximum_bitcast_fusion.2
  27.8 0.5 copy.29
  28.3 0.9 %slice.86 = f32[7680]{0:T(1024)S(1)} reshape(f32[2,32,40,3]{3,2,1,0:T(8,128)S(1)} %copy.29) | data formatting | bytes 61440 | tf_op jit(solution)/shard_map/slice | solution.py:183
  29.2 3.2 %collective-permute-start.3 = (f32[7680]{0:T(1024)S(1)}, f32[7680]{0:T(1024)S(1)}, u32[]{:S(2)}, u32[]{:S(2)}) collective-permute-start(f32[7680]{0:T(1024)S(1)} %slice.86), channel_id=1, source_target_pairs={{0,2},{2,4},{4,6},{1,3},{3,5},{5,7},{8,10},{10,12},{12,14},{9,11},... | collective-permute-start | bytes 92168 | tf_op jit(solution)/shard_map/ppermute | solution.py:183
  32.5 0.8 %pad_maximum_fusion.1.rowh_ref = f32[2,32,8,256]{3,2,1,0:T(8,128)} fusion(f32[1,32,8,256]{3,2,1,0:T(8,128)S(1)} %bitcast.28, f32[1,32,8,256]{3,2,1,0:T(8,128)S(1)} %bitcast.27), kind=kLoop, calls=%fused_computation.13 | loop fusion | flops 131072 | bytes 1048576 | tf_op jit(solution)/shard_map/stack | solution.py:169
  33.3 1.2 %concatenate.43 = f32[2,32,40,3]{3,2,1,0:T(8,128)S(1)} reshape(f32[7680]{0:T(1024)S(1)} %collective-permute-done.2) | data formatting | bytes 61440 | tf_op jit(solution)/shard_map/concatenate | solution.py:184
  34.5 1.2 %concatenate.46 = f32[2,32,40,3]{3,2,1,0:T(8,128)S(1)} reshape(f32[7680]{0:T(1024)S(1)} %collective-permute-done.3) | data formatting | bytes 61440 | tf_op jit(solution)/shard_map/concatenate | solution.py:184
  35.7 1.5 %pad_maximum_fusion.colh_ref = f32[2,32,40,128]{3,2,1,0:T(8,128)} fusion(f32[2,32,40,3]{3,2,1,0:T(8,128)S(1)} %concatenate.46, f32[2,32,40,3]{3,2,1,0:T(8,128)S(1)} %concatenate.43, f32[128]{0:T(128)S(1)} %pad.3.clone), kind=kLoop, calls=%fused_computation.10 | loop fusion | flops 655360 | bytes 1372672 | tf_op jit(solution)/shard_map/concatenate | solution.py:186
  37.2 3.5 %shard_map.91 = (f32[8,16,256]{2,1,0:T(8,128)}, f32[8,16,256]{2,1,0:T(8,128)}) custom-call(s32[1]{0:T(128)} %bitcast.rad_ref.after_ref.recv_ref, f32[32,32,256]{2,1,0:T(8,128)} %lam_ref.7, f32[32,32,256]{2,1,0:T(8,128)} %copy-done, f32[2,32,8,256]{3,2,1,0:T(8,128)} %pad_maximum_fusion.1.rowh_ref, f32[2,32,40,128]{3,2,1,0:T(8,128)} %pad_maximum_fusion.colh_ref, ...), custom_call_target="tpu_custom_call" | custom-call | flops 737280000 | bytes 12800000 | tf_op jit(solution)/shard_map/pallas_call | solution.py:104
  40.7 2.0 %collective-permute-start.4 = (f32[8,16,256]{2,1,0:T(8,128)}, f32[8,16,256]{2,1,0:T(8,128)S(1)}, u32[]{:S(2)}, u32[]{:S(2)}) collective-permute-start(f32[8,16,256]{2,1,0:T(8,128)} %get-tuple-element.15), channel_id=1, source_target_pairs={{0,1},{1,0},{2,3},{3,2},{4,5},{5,4},{6,7},{7,6},{8,9},{9,8},{10,11... | collective-permute-start | bytes 393224 | tf_op jit(solution)/shard_map/ppermute | solution.py:214
  42.7 3.6 %shard_map.92 = (f32[8,16,256]{2,1,0:T(8,128)}, f32[8,16,256]{2,1,0:T(8,128)}) custom-call(s32[1]{0:T(128)} %bitcast.rad_ref.after_ref.recv_ref, f32[32,32,256]{2,1,0:T(8,128)} %lam_ref.7, f32[32,32,256]{2,1,0:T(8,128)} %copy-done, f32[2,32,8,256]{3,2,1,0:T(8,128)} %pad_maximum_fusion.1.rowh_ref, f32[2,32,40,128]{3,2,1,0:T(8,128)} %pad_maximum_fusion.colh_ref, ...), custom_call_target="tpu_custom_call" | custom-call | flops 737280000 | bytes 12800000 | tf_op jit(solution)/shard_map/pallas_call | solution.py:104
  46.2 0.1 collective-permute-start.6
  46.3 0.1 constant_dynamic-slice_fusion.1
  46.4 0.9 %collective-permute-done.4.recv_ref.refs_4_ = f32[8,16,256]{2,1,0:T(8,128)S(1)} collective-permute-done((f32[8,16,256]{2,1,0:T(8,128)}, f32[8,16,256]{2,1,0:T(8,128)S(1)}, u32[]{:S(2)}, u32[]{:S(2)}) %collective-permute-start.4) | collective-permute-done | bytes 131104 | tf_op jit(solution)/shard_map/ppermute | solution.py:214
  47.3 0.6 copy-done.2
  47.9 3.5 %shard_map.93 = (f32[8,16,256]{2,1,0:T(8,128)}, f32[8,16,256]{2,1,0:T(8,128)}) custom-call(s32[1]{0:T(128)} %bitcast.rad_ref.after_ref.recv_ref, f32[32,32,256]{2,1,0:T(8,128)} %lam_ref.7, f32[32,32,256]{2,1,0:T(8,128)} %copy-done, f32[2,32,8,256]{3,2,1,0:T(8,128)} %pad_maximum_fusion.1.rowh_ref, f32[2,32,40,128]{3,2,1,0:T(8,128)} %pad_maximum_fusion.colh_ref, ...), custom_call_target="tpu_custom_call" | custom-call | flops 737280000 | bytes 12800000 | tf_op jit(solution)/shard_map/pallas_call | solution.py:104
  51.4 1.7 %collective-permute-start.5 = (f32[8,16,256]{2,1,0:T(8,128)}, f32[8,16,256]{2,1,0:T(8,128)S(1)}, u32[]{:S(2)}, u32[]{:S(2)}) collective-permute-start(f32[8,16,256]{2,1,0:T(8,128)} %get-tuple-element.16), channel_id=1, source_target_pairs={{0,1},{1,0},{2,3},{3,2},{4,5},{5,4},{6,7},{7,6},{8,9},{9,8},{10,11... | collective-permute-start | bytes 393224 | tf_op jit(solution)/shard_map/ppermute | solution.py:214
  53.2 0.6 copy-done.3
  53.8 3.5 %shard_map.94 = (f32[8,16,256]{2,1,0:T(8,128)}, f32[8,16,256]{2,1,0:T(8,128)}) custom-call(s32[1]{0:T(128)} %bitcast.rad_ref.after_ref.recv_ref, f32[32,32,256]{2,1,0:T(8,128)} %lam_ref.7, f32[32,32,256]{2,1,0:T(8,128)} %copy-done, f32[2,32,8,256]{3,2,1,0:T(8,128)} %pad_maximum_fusion.1.rowh_ref, f32[2,32,40,128]{3,2,1,0:T(8,128)} %pad_maximum_fusion.colh_ref, ...), custom_call_target="tpu_custom_call" | custom-call | flops 737280000 | bytes 12800000 | tf_op jit(solution)/shard_map/pallas_call | solution.py:104
  57.4 0.3 collective-permute-start.7
  57.7 0.7 %constant_dynamic-slice_fusion.r_ref = f32[64,16]{1,0:T(8,128)} fusion(f32[64,64]{1,0:T(8,128)S(1)} %copy-done.5, s32[]{:T(128)S(6)} %add.54), kind=kLoop, calls=%fused_computation.48 | loop fusion | bytes 8196 | tf_op jit(solution)/shard_map/slice | solution.py:224
  58.3 0.7 %pad_maximum_fusion.8.r_ref = f32[64,48]{1,0:T(8,128)} fusion(f32[64,32]{1,0:T(8,128)S(1)} %get-tuple-element.38, f32[64,32]{1,0:T(8,128)S(1)} %get-tuple-element.37), kind=kLoop, calls=%fused_computation.28 | loop fusion | flops 3072 | bytes 28672 | tf_op jit(solution)/shard_map/concatenate | solution.py:219
  59.0 0.6 copy-done.4
  59.7 3.4 %shard_map.95.refs_2_ = f32[64,16,256]{2,1,0:T(8,128)} custom-call(f32[64,48]{1,0:T(8,128)} %pad_maximum_fusion.8.r_ref, f32[8,16,256]{2,1,0:T(8,128)} %get-tuple-element.13.after_ref.refs_0_, f32[8,16,256]{2,1,0:T(8,128)} %get-tuple-element.14.after_ref.refs_1_, f32[8,16,256]{2,1,0:T(8,128)} %get-tuple-element.17.after_ref.refs_2_, ...), custom_call_target="tpu_custom_call" | custom-call | tf_op jit(solution)/shard_map/pallas_call | solution.py:251
  63.1 0.7 copy-done.6
  63.8 3.5 %shard_map.96 = f32[64,16,256]{2,1,0:T(8,128)} custom-call(f32[64,16]{1,0:T(8,128)} %constant_dynamic-slice_fusion.r_ref, f32[8,16,256]{2,1,0:T(8,128)} %copy-done.4, f32[8,16,256]{2,1,0:T(8,128)} %copy-done.6, f32[64,16,256]{2,1,0:T(8,128)} %shard_map.95.refs_2_), custom_call_target="tpu_custom_call" | custom-call | tf_op jit(solution)/shard_map/pallas_call | solution.py:251
  (30 shorter events, 0.1 us)
Async XLA Ops:
  0.0 1.9 %copy-start.1 = (f32[32,32,256]{2,1,0:T(8,128)S(1)}, f32[32,32,256]{2,1,0:T(8,128)}, u32[]{:S(2)}) copy-start(f32[32,32,256]{2,1,0:T(8,128)} %lam_ref.7) | copy-start | bytes 3145732
  1.9 13.2 %copy-start = (f32[32,32,256]{2,1,0:T(8,128)}, f32[32,32,256]{2,1,0:T(8,128)S(1)}, u32[]{:S(2)}) copy-start(f32[32,32,256]{2,1,0:T(8,128)S(1)} %convert_select_fusion.eta_ref) | copy-start | bytes 3145732
  1.9 9.2 %copy-start.7 = (bf16[32,2048]{1,0:T(8,128)(2,1)S(1)}, bf16[32,2048]{1,0:T(8,128)(2,1)}, u32[]{:S(2)}) copy-start(bf16[32,2048]{1,0:T(8,128)(2,1)} %param.15) | copy-start | bytes 393220
  2.8 19.3 %collective-permute-start = (f32[32,6,256]{2,1,0:T(8,128)}, f32[32,6,256]{2,1,0:T(8,128)S(1)}, u32[]{:S(2)}, u32[]{:S(2)}) collective-permute-start(f32[32,6,256]{2,1,0:T(8,128)} %pad_maximum_fusion.2), channel_id=1, source_target_pairs={{8,0},{16,8},{24,16},{9,1},{17,9},{25,17},{10,2},{18,10},{26,18},{... | collective-permute-start | bytes 589832 | tf_op jit(solution)/shard_map/ppermute | solution.py:167
  4.9 17.3 %collective-permute-start.1 = (f32[32,6,256]{2,1,0:T(8,128)}, f32[32,6,256]{2,1,0:T(8,128)}, u32[]{:S(2)}, u32[]{:S(2)}) collective-permute-start(f32[32,6,256]{2,1,0:T(8,128)} %pad_maximum_fusion.3), channel_id=1, source_target_pairs={{0,8},{8,16},{16,24},{1,9},{9,17},{17,25},{2,10},{10,18},{18,26},{... | collective-permute-start | bytes 589832 | tf_op jit(solution)/shard_map/ppermute | solution.py:166
  11.8 7.9 %all-to-all-start = ((bf16[32,4,512]{2,0,1:T(8,128)(2,1)}), bf16[32,4,512]{2,0,1:T(8,128)(2,1)S(1)}, u32[]{:S(2)}, u32[]{:S(2)}) async-start(bf16[32,4,512]{2,0,1:T(8,128)(2,1)} %bitcast.26), calls=%async_computation | async-start | bytes 262144 | tf_op jit(solution)/shard_map/all_to_all | solution.py:155
  15.3 0.7 %copy-start.8 = (s32[2048]{0:T(1024)S(1)}, s32[2048]{0:T(1024)}, u32[]{:S(2)}) copy-start(s32[2048]{0:T(1024)} %param.16) | copy-start | bytes 24580
  15.4 0.7 %copy-start.9 = (s32[4]{0:T(128)S(1)}, s32[4]{0:T(128)}, u32[]{:S(2)}) copy-start(s32[4]{0:T(128)} %param.17) | copy-start | bytes 52
  25.8 7.5 %collective-permute-start.2 = (f32[7680]{0:T(1024)S(1)}, f32[7680]{0:T(1024)S(1)}, u32[]{:S(2)}, u32[]{:S(2)}) collective-permute-start(f32[7680]{0:T(1024)S(1)} %slice.81), channel_id=1, source_target_pairs={{2,0},{4,2},{6,4},{3,1},{5,3},{7,5},{10,8},{12,10},{14,12},{11,9},... | collective-permute-start | bytes 92168 | tf_op jit(solution)/shard_map/ppermute | solution.py:182
  29.2 5.3 %collective-permute-start.3 = (f32[7680]{0:T(1024)S(1)}, f32[7680]{0:T(1024)S(1)}, u32[]{:S(2)}, u32[]{:S(2)}) collective-permute-start(f32[7680]{0:T(1024)S(1)} %slice.86), channel_id=1, source_target_pairs={{0,2},{2,4},{4,6},{1,3},{3,5},{5,7},{8,10},{10,12},{12,14},{9,11},... | collective-permute-start | bytes 92168 | tf_op jit(solution)/shard_map/ppermute | solution.py:183
  40.7 6.5 %collective-permute-start.4 = (f32[8,16,256]{2,1,0:T(8,128)}, f32[8,16,256]{2,1,0:T(8,128)S(1)}, u32[]{:S(2)}, u32[]{:S(2)}) collective-permute-start(f32[8,16,256]{2,1,0:T(8,128)} %get-tuple-element.15), channel_id=1, source_target_pairs={{0,1},{1,0},{2,3},{3,2},{4,5},{5,4},{6,7},{7,6},{8,9},{9,8},{10,11... | collective-permute-start | bytes 393224 | tf_op jit(solution)/shard_map/ppermute | solution.py:214
  42.7 3.6 %copy-start.5 = (f32[64,64]{1,0:T(8,128)S(1)}, f32[64,64]{1,0:T(8,128)}, u32[]{:S(2)}) copy-start(f32[64,64]{1,0:T(8,128)} %param.14) | copy-start | bytes 49156
  46.2 6.9 %collective-permute-start.6 = (f32[8,16,256]{2,1,0:T(8,128)}, f32[8,16,256]{2,1,0:T(8,128)S(1)}, u32[]{:S(2)}, u32[]{:S(2)}) collective-permute-start(f32[8,16,256]{2,1,0:T(8,128)} %get-tuple-element.18), channel_id=1, source_target_pairs={{0,1},{1,0},{2,3},{3,2},{4,5},{5,4},{6,7},{7,6},{8,9},{9,8},{10,11... | collective-permute-start | bytes 393224 | tf_op jit(solution)/shard_map/ppermute | solution.py:214
  47.2 0.6 copy-start.2
  51.4 7.6 %collective-permute-start.5 = (f32[8,16,256]{2,1,0:T(8,128)}, f32[8,16,256]{2,1,0:T(8,128)S(1)}, u32[]{:S(2)}, u32[]{:S(2)}) collective-permute-start(f32[8,16,256]{2,1,0:T(8,128)} %get-tuple-element.16), channel_id=1, source_target_pairs={{0,1},{1,0},{2,3},{3,2},{4,5},{5,4},{6,7},{7,6},{8,9},{9,8},{10,11... | collective-permute-start | bytes 393224 | tf_op jit(solution)/shard_map/ppermute | solution.py:214
  53.2 0.6 copy-start.3
  57.4 5.7 %collective-permute-start.7 = (f32[8,16,256]{2,1,0:T(8,128)}, f32[8,16,256]{2,1,0:T(8,128)S(1)}, u32[]{:S(2)}, u32[]{:S(2)}) collective-permute-start(f32[8,16,256]{2,1,0:T(8,128)} %get-tuple-element.19), channel_id=1, source_target_pairs={{0,1},{1,0},{2,3},{3,2},{4,5},{5,4},{6,7},{7,6},{8,9},{9,8},{10,11... | collective-permute-start | bytes 393224 | tf_op jit(solution)/shard_map/ppermute | solution.py:214
  59.0 0.7 copy-start.4
  63.1 0.7 copy-start.6

commit v6 on v5

--- a/solution.py
+++ b/solution.py
@@ -234,7 +234,7 @@
         xs[i * step:(i + 1) * step] = p[...]
     rmat = r_ref[...]
     for a in range(xs.shape[1]):
-        y = jnp.dot(rmat, xs[:, a, :], precision=lax.Precision.HIGHEST,
+        y = jnp.dot(rmat, xs[:, a, :], precision=lax.Precision.HIGH,
                     preferred_element_type=jnp.float32)
         if has_partial:
             y = partial_ref[:, a, :] + y

time: 67.7 us -> 67.3 us (level)
  no operation moved by 1% of the time
where the time goes in v6:
time: 67.3 us; the launch traced here: 66.8 us
  Pallas kernels  20.6 us (31%)
  starting transfers between devices  19.4 us (29%)
  local copies, waits for them, and re-layouts  13.9 us (21%)
  other arithmetic  7.83 us (12%)
  waiting for transfers between devices  2.4 us (4%)
  matrix products  2.37 us (4%)
    pallas_call x4, Pallas kernels, _sweeps(): pl.pallas_call(_sweep_kernel, out_shape=out_shape, grid=grid, in_specs=[p...  14.2 us
    pallas_call x2, Pallas kernels, _radial(): pl.pallas_call(functools.partial(_radial_kernel, len(pieces), partial is...  6.42 us
    ppermute x1, starting transfers between devices, per_device(): top = lax.ppermute(top_send, 'cap', _pairs(n_cap, 1))  6.25 us
    ppermute x4, starting transfers between devices, per_device(): lax.ppermute(send, 'rad', _pairs(n_rad, 1) + _pairs(n_rad, -1))  4.05 us
    unnamed x23, local copies, waits for them, and re-layouts  3.62 us
    all_to_all x1, starting transfers between devices, per_device(): lax.all_to_all(marker_rows, 'lat', split_axis=1, concat_axis=1, tiled=True)  3.32 us
    ppermute x1, starting transfers between devices, per_device(): from_left = lax.ppermute(flat[piece:], 'lat', _pairs(n_lat, 1))  3.21 us
    concatenate x2, local copies, waits for them, and re-layouts, per_device(): jnp.concatenate([from_right, from_left]).reshape(2, 2, layers, ext_rows, g)  2.37 us
  transfers between devices with their start and end apart: 9, of which 2 were waited for; matrix products, arithmetic and copies ran while one was open for 18% of the time, Pallas kernels for 21%

profile of v6, /device:TPU:0, one launch (start us, length us, event | category | flops | bytes accessed | tf_op | source)
XLA Modules:
  0.0 66.8 jit_solution(15439606800298142498)
XLA Ops:
  0.0 1.9 %convert_select_fusion.eta_ref = f32[32,32,256]{2,1,0:T(8,128)S(1)} fusion(bf16[32,32,256]{2,1,0:T(8,128)(2,1)} %param.11, bf16[32,32,256]{2,1,0:T(8,128)(2,1)} %param.12, s32[32,32,256]{2,1,0:T(8,128)} %param.13), kind=kLoop, calls=%fused_computation.7 | loop fusion | flops 1835008 | bytes 3145728 | tf_op jit(solution)/shard_map/jit(_where)/select_n | solution.py:159
  1.9 0.0 copy-start
  2.0 0.1 fusion.17
  2.1 0.8 %pad_maximum_fusion.2 = f32[32,6,256]{2,1,0:T(8,128)} fusion(f32[32,3,256]{2,1,0:T(4,128)S(1)} %get-tuple-element.44, f32[32,3,256]{2,1,0:T(4,128)S(1)} %get-tuple-element.25), kind=kLoop, calls=%fused_computation.14 | loop fusion | flops 49152 | bytes 393216 | tf_op jit(solution)/shard_map/concatenate | solution.py:165
  2.8 1.3 %collective-permute-start = (f32[32,6,256]{2,1,0:T(8,128)}, f32[32,6,256]{2,1,0:T(8,128)S(1)}, u32[]{:S(2)}, u32[]{:S(2)}) collective-permute-start(f32[32,6,256]{2,1,0:T(8,128)} %pad_maximum_fusion.2), channel_id=1, source_target_pairs={{8,0},{16,8},{24,16},{9,1},{17,9},{25,17},{10,2},{18,10},{26,18},{... | collective-permute-start | bytes 589832 | tf_op jit(solution)/shard_map/ppermute | solution.py:167
  4.1 0.7 %pad_maximum_fusion.3 = f32[32,6,256]{2,1,0:T(8,128)} fusion(f32[32,3,256]{2,1,0:T(4,128)S(1)} %get-tuple-element.43, f32[32,3,256]{2,1,0:T(4,128)S(1)} %get-tuple-element.26), kind=kLoop, calls=%fused_computation.15 | loop fusion | flops 49152 | bytes 393216 | tf_op jit(solution)/shard_map/concatenate | solution.py:164
  4.9 6.3 %collective-permute-start.1 = (f32[32,6,256]{2,1,0:T(8,128)}, f32[32,6,256]{2,1,0:T(8,128)}, u32[]{:S(2)}, u32[]{:S(2)}) collective-permute-start(f32[32,6,256]{2,1,0:T(8,128)} %pad_maximum_fusion.3), channel_id=1, source_target_pairs={{0,8},{8,16},{16,24},{1,9},{9,17},{17,25},{2,10},{10,18},{18,26},{... | collective-permute-start | bytes 589832 | tf_op jit(solution)/shard_map/ppermute | solution.py:166
  11.1 0.7 copy.38
  11.8 3.3 %all-to-all-start = ((bf16[32,4,512]{2,0,1:T(8,128)(2,1)}), bf16[32,4,512]{2,0,1:T(8,128)(2,1)S(1)}, u32[]{:S(2)}, u32[]{:S(2)}) async-start(bf16[32,4,512]{2,0,1:T(8,128)(2,1)} %bitcast.26), calls=%async_computation | async-start | bytes 262144 | tf_op jit(solution)/shard_map/all_to_all | solution.py:155
  15.1 0.2 fusion.16
  15.4 0.2 fusion.15
  15.6 0.4 copy-done.8
  16.1 0.1 fusion.11
  16.2 0.1 fusion.9
  16.2 0.7 %and_convert_fusion.mask_ref = f32[40,384]{1,0:T(8,128)} fusion(pred[384]{0:T(512)(128)(4,1)S(1)} %compare_and_fusion, pred[40]{0:T(512)(128)(4,1)S(1)} %compare_and_fusion.1), kind=kLoop, calls=%fused_computation.23 | loop fusion | flops 30720 | bytes 61864 | tf_op jit(solution)/shard_map/convert_element_type | solution.py:28
  16.9 0.3 copy.22
  17.2 0.3 copy.32
  17.5 0.3 copy.27
  17.7 0.3 copy.33
  18.0 0.1 pad.23.clone
  18.1 0.1 pad.3.clone
  18.2 1.5 %all-to-all-done = bf16[32,4,512]{2,0,1:T(8,128)(2,1)S(1)} async-done(((bf16[32,4,512]{2,0,1:T(8,128)(2,1)}), bf16[32,4,512]{2,0,1:T(8,128)(2,1)S(1)}, u32[]{:S(2)}, u32[]{:S(2)}) %all-to-all-start) | async-done | bytes 131104 | tf_op jit(solution)/shard_map/all_to_all | solution.py:155
  19.7 2.4 %fusion.dep_ref = f32[32,32,256]{2,1,0:T(8,128)} fusion(pred[32,2048]{1,0:T(8,128)(4,1)S(1)} %fusion.9, bf16[32,2048]{1,0:T(8,128)(2,1)S(1)} %bitcast.31, s32[2048]{0:T(1024)S(1)} %get-tuple-element.39), kind=kOutput, calls=%fused_computation | convolution fusion | flops 1076363264 | bytes 1253376 | tf_op jit(solution)/shard_map/las,sb->lab/dot_general | solution.py:198
  22.1 0.1 fusion.21
  22.2 1.1 %fusion.22 = (f32[32,3,256]{2,1,0:T(4,128)S(1)}, f32[32,3,256]{2,1,0:T(4,128)S(1)}) fusion(f32[32,6,256]{2,1,0:T(8,128)} %collective-permute-done.1), kind=kLoop, calls=%fused_computation.59 | loop fusion | bytes 393216 | tf_op jit(solution)/shard_map/slice | solution.py:170
  23.3 0.1 pad_maximum_fusion.4
  23.4 0.1 fusion.20
  23.5 0.3 copy.23
  23.8 0.1 fusion.19
  23.9 0.3 copy.21
  24.2 0.1 maximum_bitcast_fusion.1
  24.3 0.1 maximum_bitcast_fusion
  24.4 0.5 copy.24
  24.9 0.9 %slice.81 = f32[7680]{0:T(1024)S(1)} reshape(f32[2,32,40,3]{3,2,1,0:T(8,128)S(1)} %copy.24) | data formatting | bytes 61440 | tf_op jit(solution)/shard_map/slice | solution.py:182
  25.8 1.3 %collective-permute-start.2 = (f32[7680]{0:T(1024)S(1)}, f32[7680]{0:T(1024)S(1)}, u32[]{:S(2)}, u32[]{:S(2)}) collective-permute-start(f32[7680]{0:T(1024)S(1)} %slice.81), channel_id=1, source_target_pairs={{2,0},{4,2},{6,4},{3,1},{5,3},{7,5},{10,8},{12,10},{14,12},{11,9},... | collective-permute-start | bytes 92168 | tf_op jit(solution)/shard_map/ppermute | solution.py:182
  27.1 0.3 copy.28
  27.3 0.3 copy.26
  27.6 0.1 maximum_bitcast_fusion.3
  27.7 0.1 maximum_bitcast_fusion.2
  27.8 0.5 copy.29
  28.3 0.9 %slice.86 = f32[7680]{0:T(1024)S(1)} reshape(f32[2,32,40,3]{3,2,1,0:T(8,128)S(1)} %copy.29) | data formatting | bytes 61440 | tf_op jit(solution)/shard_map/slice | solution.py:183
  29.2 3.2 %collective-permute-start.3 = (f32[7680]{0:T(1024)S(1)}, f32[7680]{0:T(1024)S(1)}, u32[]{:S(2)}, u32[]{:S(2)}) collective-permute-start(f32[7680]{0:T(1024)S(1)} %slice.86), channel_id=1, source_target_pairs={{0,2},{2,4},{4,6},{1,3},{3,5},{5,7},{8,10},{10,12},{12,14},{9,11},... | collective-permute-start | bytes 92168 | tf_op jit(solution)/shard_map/ppermute | solution.py:183
  32.5 0.8 %pad_maximum_fusion.1.rowh_ref = f32[2,32,8,256]{3,2,1,0:T(8,128)} fusion(f32[1,32,8,256]{3,2,1,0:T(8,128)S(1)} %bitcast.28, f32[1,32,8,256]{3,2,1,0:T(8,128)S(1)} %bitcast.27), kind=kLoop, calls=%fused_computation.13 | loop fusion | flops 131072 | bytes 1048576 | tf_op jit(solution)/shard_map/stack | solution.py:169
  33.3 1.2 %concatenate.43 = f32[2,32,40,3]{3,2,1,0:T(8,128)S(1)} reshape(f32[7680]{0:T(1024)S(1)} %collective-permute-done.2) | data formatting | bytes 61440 | tf_op jit(solution)/shard_map/concatenate | solution.py:184
  34.5 1.2 %concatenate.46 = f32[2,32,40,3]{3,2,1,0:T(8,128)S(1)} reshape(f32[7680]{0:T(1024)S(1)} %collective-permute-done.3) | data formatting | bytes 61440 | tf_op jit(solution)/shard_map/concatenate | solution.py:184
  35.7 1.5 %pad_maximum_fusion.colh_ref = f32[2,32,40,128]{3,2,1,0:T(8,128)} fusion(f32[2,32,40,3]{3,2,1,0:T(8,128)S(1)} %concatenate.46, f32[2,32,40,3]{3,2,1,0:T(8,128)S(1)} %concatenate.43, f32[128]{0:T(128)S(1)} %pad.3.clone), kind=kLoop, calls=%fused_computation.10 | loop fusion | flops 655360 | bytes 1372672 | tf_op jit(solution)/shard_map/concatenate | solution.py:186
  37.2 3.5 %shard_map.91 = (f32[8,16,256]{2,1,0:T(8,128)}, f32[8,16,256]{2,1,0:T(8,128)}) custom-call(s32[1]{0:T(128)} %bitcast.rad_ref.after_ref.recv_ref, f32[32,32,256]{2,1,0:T(8,128)} %lam_ref.7, f32[32,32,256]{2,1,0:T(8,128)} %copy-done, f32[2,32,8,256]{3,2,1,0:T(8,128)} %pad_maximum_fusion.1.rowh_ref, f32[2,32,40,128]{3,2,1,0:T(8,128)} %pad_maximum_fusion.colh_ref, ...), custom_call_target="tpu_custom_call" | custom-call | flops 737280000 | bytes 12800000 | tf_op jit(solution)/shard_map/pallas_call | solution.py:104
  40.7 2.0 %collective-permute-start.4 = (f32[8,16,256]{2,1,0:T(8,128)}, f32[8,16,256]{2,1,0:T(8,128)S(1)}, u32[]{:S(2)}, u32[]{:S(2)}) collective-permute-start(f32[8,16,256]{2,1,0:T(8,128)} %get-tuple-element.15), channel_id=1, source_target_pairs={{0,1},{1,0},{2,3},{3,2},{4,5},{5,4},{6,7},{7,6},{8,9},{9,8},{10,11... | collective-permute-start | bytes 393224 | tf_op jit(solution)/shard_map/ppermute | solution.py:214
  42.7 3.6 %shard_map.92 = (f32[8,16,256]{2,1,0:T(8,128)}, f32[8,16,256]{2,1,0:T(8,128)}) custom-call(s32[1]{0:T(128)} %bitcast.rad_ref.after_ref.recv_ref, f32[32,32,256]{2,1,0:T(8,128)} %lam_ref.7, f32[32,32,256]{2,1,0:T(8,128)} %copy-done, f32[2,32,8,256]{3,2,1,0:T(8,128)} %pad_maximum_fusion.1.rowh_ref, f32[2,32,40,128]{3,2,1,0:T(8,128)} %pad_maximum_fusion.colh_ref, ...), custom_call_target="tpu_custom_call" | custom-call | flops 737280000 | bytes 12800000 | tf_op jit(solution)/shard_map/pallas_call | solution.py:104
  46.2 0.1 collective-permute-start.6
  46.3 0.1 constant_dynamic-slice_fusion.1
  46.4 0.9 %collective-permute-done.4.recv_ref.refs_4_ = f32[8,16,256]{2,1,0:T(8,128)S(1)} collective-permute-done((f32[8,16,256]{2,1,0:T(8,128)}, f32[8,16,256]{2,1,0:T(8,128)S(1)}, u32[]{:S(2)}, u32[]{:S(2)}) %collective-permute-start.4) | collective-permute-done | bytes 131104 | tf_op jit(solution)/shard_map/ppermute | solution.py:214
  47.3 0.6 copy-done.2
  47.9 3.5 %shard_map.93 = (f32[8,16,256]{2,1,0:T(8,128)}, f32[8,16,256]{2,1,0:T(8,128)}) custom-call(s32[1]{0:T(128)} %bitcast.rad_ref.after_ref.recv_ref, f32[32,32,256]{2,1,0:T(8,128)} %lam_ref.7, f32[32,32,256]{2,1,0:T(8,128)} %copy-done, f32[2,32,8,256]{3,2,1,0:T(8,128)} %pad_maximum_fusion.1.rowh_ref, f32[2,32,40,128]{3,2,1,0:T(8,128)} %pad_maximum_fusion.colh_ref, ...), custom_call_target="tpu_custom_call" | custom-call | flops 737280000 | bytes 12800000 | tf_op jit(solution)/shard_map/pallas_call | solution.py:104
  51.4 1.7 %collective-permute-start.5 = (f32[8,16,256]{2,1,0:T(8,128)}, f32[8,16,256]{2,1,0:T(8,128)S(1)}, u32[]{:S(2)}, u32[]{:S(2)}) collective-permute-start(f32[8,16,256]{2,1,0:T(8,128)} %get-tuple-element.16), channel_id=1, source_target_pairs={{0,1},{1,0},{2,3},{3,2},{4,5},{5,4},{6,7},{7,6},{8,9},{9,8},{10,11... | collective-permute-start | bytes 393224 | tf_op jit(solution)/shard_map/ppermute | solution.py:214
  53.2 0.6 copy-done.3
  53.8 3.5 %shard_map.94 = (f32[8,16,256]{2,1,0:T(8,128)}, f32[8,16,256]{2,1,0:T(8,128)}) custom-call(s32[1]{0:T(128)} %bitcast.rad_ref.after_ref.recv_ref, f32[32,32,256]{2,1,0:T(8,128)} %lam_ref.7, f32[32,32,256]{2,1,0:T(8,128)} %copy-done, f32[2,32,8,256]{3,2,1,0:T(8,128)} %pad_maximum_fusion.1.rowh_ref, f32[2,32,40,128]{3,2,1,0:T(8,128)} %pad_maximum_fusion.colh_ref, ...), custom_call_target="tpu_custom_call" | custom-call | flops 737280000 | bytes 12800000 | tf_op jit(solution)/shard_map/pallas_call | solution.py:104
  57.4 0.3 collective-permute-start.7
  57.7 0.7 %constant_dynamic-slice_fusion.r_ref = f32[64,16]{1,0:T(8,128)} fusion(f32[64,64]{1,0:T(8,128)S(1)} %copy-done.5, s32[]{:T(128)S(6)} %add.54), kind=kLoop, calls=%fused_computation.48 | loop fusion | bytes 8196 | tf_op jit(solution)/shard_map/slice | solution.py:224
  58.3 0.7 %pad_maximum_fusion.8.r_ref = f32[64,48]{1,0:T(8,128)} fusion(f32[64,32]{1,0:T(8,128)S(1)} %get-tuple-element.38, f32[64,32]{1,0:T(8,128)S(1)} %get-tuple-element.37), kind=kLoop, calls=%fused_computation.28 | loop fusion | flops 3072 | bytes 28672 | tf_op jit(solution)/shard_map/concatenate | solution.py:219
  59.0 0.6 copy-done.4
  59.7 3.1 %shard_map.95.refs_2_ = f32[64,16,256]{2,1,0:T(8,128)} custom-call(f32[64,48]{1,0:T(8,128)} %pad_maximum_fusion.8.r_ref, f32[8,16,256]{2,1,0:T(8,128)} %get-tuple-element.13.after_ref.refs_0_, f32[8,16,256]{2,1,0:T(8,128)} %get-tuple-element.14.after_ref.refs_1_, f32[8,16,256]{2,1,0:T(8,128)} %get-tuple-element.17.after_ref.refs_2_, ...), custom_call_target="tpu_custom_call" | custom-call | tf_op jit(solution)/shard_map/pallas_call | solution.py:251
  62.8 0.7 copy-done.6
  63.4 3.3 %shard_map.96 = f32[64,16,256]{2,1,0:T(8,128)} custom-call(f32[64,16]{1,0:T(8,128)} %constant_dynamic-slice_fusion.r_ref, f32[8,16,256]{2,1,0:T(8,128)} %copy-done.4, f32[8,16,256]{2,1,0:T(8,128)} %copy-done.6, f32[64,16,256]{2,1,0:T(8,128)} %shard_map.95.refs_2_), custom_call_target="tpu_custom_call" | custom-call | tf_op jit(solution)/shard_map/pallas_call | solution.py:251
  (30 shorter events, 0.1 us)
Async XLA Ops:
  0.0 1.9 %copy-start.1 = (f32[32,32,256]{2,1,0:T(8,128)S(1)}, f32[32,32,256]{2,1,0:T(8,128)}, u32[]{:S(2)}) copy-start(f32[32,32,256]{2,1,0:T(8,128)} %lam_ref.7) | copy-start | bytes 3145732
  1.9 13.2 %copy-start = (f32[32,32,256]{2,1,0:T(8,128)}, f32[32,32,256]{2,1,0:T(8,128)S(1)}, u32[]{:S(2)}) copy-start(f32[32,32,256]{2,1,0:T(8,128)S(1)} %convert_select_fusion.eta_ref) | copy-start | bytes 3145732
  1.9 9.2 %copy-start.7 = (bf16[32,2048]{1,0:T(8,128)(2,1)S(1)}, bf16[32,2048]{1,0:T(8,128)(2,1)}, u32[]{:S(2)}) copy-start(bf16[32,2048]{1,0:T(8,128)(2,1)} %param.15) | copy-start | bytes 393220
  2.8 19.3 %collective-permute-start = (f32[32,6,256]{2,1,0:T(8,128)}, f32[32,6,256]{2,1,0:T(8,128)S(1)}, u32[]{:S(2)}, u32[]{:S(2)}) collective-permute-start(f32[32,6,256]{2,1,0:T(8,128)} %pad_maximum_fusion.2), channel_id=1, source_target_pairs={{8,0},{16,8},{24,16},{9,1},{17,9},{25,17},{10,2},{18,10},{26,18},{... | collective-permute-start | bytes 589832 | tf_op jit(solution)/shard_map/ppermute | solution.py:167
  4.9 17.3 %collective-permute-start.1 = (f32[32,6,256]{2,1,0:T(8,128)}, f32[32,6,256]{2,1,0:T(8,128)}, u32[]{:S(2)}, u32[]{:S(2)}) collective-permute-start(f32[32,6,256]{2,1,0:T(8,128)} %pad_maximum_fusion.3), channel_id=1, source_target_pairs={{0,8},{8,16},{16,24},{1,9},{9,17},{17,25},{2,10},{10,18},{18,26},{... | collective-permute-start | bytes 589832 | tf_op jit(solution)/shard_map/ppermute | solution.py:166
  11.8 7.9 %all-to-all-start = ((bf16[32,4,512]{2,0,1:T(8,128)(2,1)}), bf16[32,4,512]{2,0,1:T(8,128)(2,1)S(1)}, u32[]{:S(2)}, u32[]{:S(2)}) async-start(bf16[32,4,512]{2,0,1:T(8,128)(2,1)} %bitcast.26), calls=%async_computation | async-start | bytes 262144 | tf_op jit(solution)/shard_map/all_to_all | solution.py:155
  15.3 0.7 %copy-start.8 = (s32[2048]{0:T(1024)S(1)}, s32[2048]{0:T(1024)}, u32[]{:S(2)}) copy-start(s32[2048]{0:T(1024)} %param.16) | copy-start | bytes 24580
  15.4 0.7 %copy-start.9 = (s32[4]{0:T(128)S(1)}, s32[4]{0:T(128)}, u32[]{:S(2)}) copy-start(s32[4]{0:T(128)} %param.17) | copy-start | bytes 52
  25.8 7.5 %collective-permute-start.2 = (f32[7680]{0:T(1024)S(1)}, f32[7680]{0:T(1024)S(1)}, u32[]{:S(2)}, u32[]{:S(2)}) collective-permute-start(f32[7680]{0:T(1024)S(1)} %slice.81), channel_id=1, source_target_pairs={{2,0},{4,2},{6,4},{3,1},{5,3},{7,5},{10,8},{12,10},{14,12},{11,9},... | collective-permute-start | bytes 92168 | tf_op jit(solution)/shard_map/ppermute | solution.py:182
  29.2 5.3 %collective-permute-start.3 = (f32[7680]{0:T(1024)S(1)}, f32[7680]{0:T(1024)S(1)}, u32[]{:S(2)}, u32[]{:S(2)}) collective-permute-start(f32[7680]{0:T(1024)S(1)} %slice.86), channel_id=1, source_target_pairs={{0,2},{2,4},{4,6},{1,3},{3,5},{5,7},{8,10},{10,12},{12,14},{9,11},... | collective-permute-start | bytes 92168 | tf_op jit(solution)/shard_map/ppermute | solution.py:183
  40.7 6.5 %collective-permute-start.4 = (f32[8,16,256]{2,1,0:T(8,128)}, f32[8,16,256]{2,1,0:T(8,128)S(1)}, u32[]{:S(2)}, u32[]{:S(2)}) collective-permute-start(f32[8,16,256]{2,1,0:T(8,128)} %get-tuple-element.15), channel_id=1, source_target_pairs={{0,1},{1,0},{2,3},{3,2},{4,5},{5,4},{6,7},{7,6},{8,9},{9,8},{10,11... | collective-permute-start | bytes 393224 | tf_op jit(solution)/shard_map/ppermute | solution.py:214
  42.7 3.6 %copy-start.5 = (f32[64,64]{1,0:T(8,128)S(1)}, f32[64,64]{1,0:T(8,128)}, u32[]{:S(2)}) copy-start(f32[64,64]{1,0:T(8,128)} %param.14) | copy-start | bytes 49156
  46.2 6.9 %collective-permute-start.6 = (f32[8,16,256]{2,1,0:T(8,128)}, f32[8,16,256]{2,1,0:T(8,128)S(1)}, u32[]{:S(2)}, u32[]{:S(2)}) collective-permute-start(f32[8,16,256]{2,1,0:T(8,128)} %get-tuple-element.18), channel_id=1, source_target_pairs={{0,1},{1,0},{2,3},{3,2},{4,5},{5,4},{6,7},{7,6},{8,9},{9,8},{10,11... | collective-permute-start | bytes 393224 | tf_op jit(solution)/shard_map/ppermute | solution.py:214
  47.2 0.6 copy-start.2
  51.4 7.6 %collective-permute-start.5 = (f32[8,16,256]{2,1,0:T(8,128)}, f32[8,16,256]{2,1,0:T(8,128)S(1)}, u32[]{:S(2)}, u32[]{:S(2)}) collective-permute-start(f32[8,16,256]{2,1,0:T(8,128)} %get-tuple-element.16), channel_id=1, source_target_pairs={{0,1},{1,0},{2,3},{3,2},{4,5},{5,4},{6,7},{7,6},{8,9},{9,8},{10,11... | collective-permute-start | bytes 393224 | tf_op jit(solution)/shard_map/ppermute | solution.py:214
  53.2 0.6 copy-start.3
  57.4 5.4 %collective-permute-start.7 = (f32[8,16,256]{2,1,0:T(8,128)}, f32[8,16,256]{2,1,0:T(8,128)S(1)}, u32[]{:S(2)}, u32[]{:S(2)}) collective-permute-start(f32[8,16,256]{2,1,0:T(8,128)} %get-tuple-element.19), channel_id=1, source_target_pairs={{0,1},{1,0},{2,3},{3,2},{4,5},{5,4},{6,7},{7,6},{8,9},{9,8},{10,11... | collective-permute-start | bytes 393224 | tf_op jit(solution)/shard_map/ppermute | solution.py:214
  59.0 0.7 copy-start.4
  62.8 0.7 copy-start.6

commit v7 on v5

--- a/solution.py
+++ b/solution.py
@@ -152,8 +152,6 @@
     d = lax.axis_index("lat")
     r = lax.axis_index("rad")
 
-    received = lax.all_to_all(marker_rows, "lat", split_axis=1, concat_axis=1, tiled=True)
-
     flow = visc_flow.astype(jnp.float32)
     plast = visc_yield.astype(jnp.float32)
     eta = jnp.where(yield_mask == 1, flow * plast / (flow + plast), flow)
@@ -179,6 +177,8 @@
 
     flat = jnp.stack([col_piece(slice(0, g)), col_piece(slice(cols - g, cols))]).reshape(-1)
     piece = flat.shape[0] // 2
+    flat, markers = lax.optimization_barrier((flat, marker_rows))
+    received = lax.all_to_all(markers, "lat", split_axis=1, concat_axis=1, tiled=True)
     from_right = lax.ppermute(flat[:piece], "lat", _pairs(n_lat, -1))
     from_left = lax.ppermute(flat[piece:], "lat", _pairs(n_lat, 1))
     got = jnp.concatenate([from_right, from_left]).reshape(2, 2, layers, ext_rows, g)

time: 67.7 us -> 65.3 us (0.965)
  local copies, waits for them, and re-layouts: 13.9 us -> 12.5 us
  other arithmetic: 7.83 us -> 6.44 us
  waiting for transfers between devices: 2.4 us -> 3.42 us
  starting transfers between devices: 19.4 us -> 18.7 us
    reshape x0 -> x1, local copies, waits for them, and re-layouts: none -> 1.87 us  [per_device(): jnp.stack([col_piece(slice(0, g)), col_piece(slice(cols - g, cols))])]
    ppermute x1, waiting for transfers between devices: 0.01 us -> 1.6 us  [per_device(): bot = lax.ppermute(bot_send, 'cap', _pairs(n_cap, -1))]
    all_to_all x1, waiting for transfers between devices: 1.52 us -> 0.01 us  [per_device(): lax.all_to_all(markers, 'lat', split_axis=1, concat_axis=1, tiled=True)]
    ppermute x1, waiting for transfers between devices: 0.01 us -> 1.19 us  [per_device(): top = lax.ppermute(top_send, 'cap', _pairs(n_cap, 1))]
    slice x1, local copies, waits for them, and re-layouts: 1.09 us -> 0.05 us  [per_device(): top[:, :g]]
    slice x1 -> x0, local copies, waits for them, and re-layouts: 0.88 us -> none  [per_device(): from_left = lax.ppermute(flat[piece:], 'lat', _pairs(n_lat, 1))]
    slice x1, local copies, waits for them, and re-layouts: 0.88 us -> 0.01 us  [per_device(): from_right = lax.ppermute(flat[:piece], 'lat', _pairs(n_lat, -1))]
    concatenate x1, other arithmetic: 0.78 us -> 0.06 us  [per_device(): bot_send = jnp.concatenate([adjoint_temp[:, :g], eta[:, :g]], axis=1)]
  transfers between devices with their start and end apart: 9 -> 9, of which waited for: 2 -> 3; matrix products, arithmetic and copies ran while one was open for 18% -> 15% of each run, Pallas kernels for 21% -> 22%
where the time goes in v7:
time: 65.3 us; the launch traced here: 64.9 us
  Pallas kernels  21.1 us (32%)
  starting transfers between devices  18.7 us (29%)
  local copies, waits for them, and re-layouts  12.5 us (19%)
  other arithmetic  6.44 us (10%)
  waiting for transfers between devices  3.42 us (5%)
  matrix products  2.37 us (4%)
    pallas_call x4, Pallas kernels, _sweeps(): pl.pallas_call(_sweep_kernel, out_shape=out_shape, grid=grid, in_specs=[p...  14.2 us
    pallas_call x2, Pallas kernels, _radial(): pl.pallas_call(functools.partial(_radial_kernel, len(pieces), partial is...  6.9 us
    ppermute x1, starting transfers between devices, per_device(): top = lax.ppermute(top_send, 'cap', _pairs(n_cap, 1))  5.57 us
    ppermute x4, starting transfers between devices, per_device(): lax.ppermute(send, 'rad', _pairs(n_rad, 1) + _pairs(n_rad, -1))  4.05 us
    all_to_all x1, starting transfers between devices, per_device(): lax.all_to_all(markers, 'lat', split_axis=1, concat_axis=1, tiled=True)  3.5 us
    unnamed x23, local copies, waits for them, and re-layouts  3.23 us
    ppermute x1, starting transfers between devices, per_device(): from_left = lax.ppermute(flat[piece:], 'lat', _pairs(n_lat, 1))  3.03 us
    concatenate x2, local copies, waits for them, and re-layouts, per_device(): jnp.concatenate([from_right, from_left]).reshape(2, 2, layers, ext_rows, g)  2.37 us
  transfers between devices with their start and end apart: 9, of which 3 were waited for; matrix products, arithmetic and copies ran while one was open for 15% of the time, Pallas kernels for 22%

profile of v7, /device:TPU:0, one launch (start us, length us, event | category | flops | bytes accessed | tf_op | source)
XLA Modules:
  0.0 64.9 jit_solution(14145661264216783376)
XLA Ops:
  0.0 1.9 %convert_select_fusion.eta_ref = f32[32,32,256]{2,1,0:T(8,128)S(1)} fusion(bf16[32,32,256]{2,1,0:T(8,128)(2,1)} %param.11, bf16[32,32,256]{2,1,0:T(8,128)(2,1)} %param.12, s32[32,32,256]{2,1,0:T(8,128)} %param.13), kind=kLoop, calls=%fused_computation.7 | loop fusion | flops 1835008 | bytes 3145728 | tf_op jit(solution)/shard_map/jit(_where)/select_n | solution.py:157
  1.9 0.0 copy-start
  1.9 0.1 fusion.17
  2.0 0.1 pad_maximum_fusion.2
  2.1 1.3 %collective-permute-start = (f32[32,6,256]{2,1,0:T(8,128)S(1)}, f32[32,6,256]{2,1,0:T(8,128)S(1)}, u32[]{:S(2)}, u32[]{:S(2)}) collective-permute-start(f32[32,6,256]{2,1,0:T(8,128)S(1)} %pad_maximum_fusion.2), channel_id=1, source_target_pairs={{8,0},{16,8},{24,16},{9,1},{17,9},{25,17},{10,2},{18,10},{26,18},{... | collective-permute-start | bytes 589832 | tf_op jit(solution)/shard_map/ppermute | solution.py:165
  3.4 0.1 pad_maximum_fusion.3
  3.5 5.6 %collective-permute-start.1 = (f32[32,6,256]{2,1,0:T(8,128)S(1)}, f32[32,6,256]{2,1,0:T(8,128)S(1)}, u32[]{:S(2)}, u32[]{:S(2)}) collective-permute-start(f32[32,6,256]{2,1,0:T(8,128)S(1)} %pad_maximum_fusion.3), channel_id=1, source_target_pairs={{0,8},{8,16},{16,24},{1,9},{9,17},{17,25},{2,10},{10,18},{18,26},{... | collective-permute-start | bytes 589832 | tf_op jit(solution)/shard_map/ppermute | solution.py:164
  9.1 0.2 fusion.16
  9.3 0.2 fusion.15
  9.5 0.0 copy-start.8
  9.5 0.3 copy.21
  9.8 0.3 copy.30
  10.1 0.3 copy.25
  10.4 0.3 copy.31
  10.7 0.1 pad.25.clone
  10.7 0.1 pad.3.clone
  10.8 0.1 fusion.11
  11.0 0.1 fusion.9
  11.0 0.7 %and_convert_fusion.mask_ref = f32[40,384]{1,0:T(8,128)} fusion(pred[384]{0:T(512)(128)(4,1)S(1)} %compare_and_fusion, pred[40]{0:T(512)(128)(4,1)S(1)} %compare_and_fusion.1), kind=kLoop, calls=%fused_computation.24 | loop fusion | flops 30720 | bytes 61864 | tf_op jit(solution)/shard_map/convert_element_type | solution.py:28
  11.7 1.6 %collective-permute-done = f32[32,6,256]{2,1,0:T(8,128)S(1)} collective-permute-done((f32[32,6,256]{2,1,0:T(8,128)S(1)}, f32[32,6,256]{2,1,0:T(8,128)S(1)}, u32[]{:S(2)}, u32[]{:S(2)}) %collective-permute-start) | collective-permute-done | bytes 196640 | tf_op jit(solution)/shard_map/ppermute | solution.py:165
  13.3 0.1 fusion.21
  13.4 1.2 %collective-permute-done.1 = f32[32,6,256]{2,1,0:T(8,128)S(1)} collective-permute-done((f32[32,6,256]{2,1,0:T(8,128)S(1)}, f32[32,6,256]{2,1,0:T(8,128)S(1)}, u32[]{:S(2)}, u32[]{:S(2)}) %collective-permute-start.1) | collective-permute-done | bytes 196640 | tf_op jit(solution)/shard_map/ppermute | solution.py:164
  14.6 0.1 fusion.22
  14.6 0.1 pad_maximum_fusion.4
  14.8 0.1 fusion.20
  14.9 0.3 copy.22
  15.2 0.1 fusion.19
  15.3 0.3 copy.20
  15.5 0.3 copy.26
  15.8 0.3 copy.24
  16.1 0.1 maximum_bitcast_fusion.3
  16.2 0.1 maximum_bitcast_fusion.2
  16.3 0.1 maximum_bitcast_fusion.5
  16.4 0.1 maximum_bitcast_fusion.4
  16.5 0.9 %copy.27 = f32[2,2,32,40,3]{4,3,2,1,0:T(8,128)S(1)} copy(f32[2,2,32,40,3]{3,2,4,1,0:T(8,128)S(1)} %pad_maximum_fusion.6) | data formatting | bytes 122880 | tf_op jit(solution)/shard_map/stack | solution.py:178
  17.5 0.0 copy-start.7
  17.5 1.9 %reshape.108 = f32[15360]{0:T(1024)S(1)} reshape(f32[2,2,32,40,3]{4,3,2,1,0:T(8,128)S(1)} %copy.27) | data formatting | bytes 122880 | tf_op jit(solution)/shard_map/reshape | solution.py:178
  19.4 1.3 %collective-permute-start.2 = (f32[7680]{0:T(1024)S(1)}, f32[7680]{0:T(1024)S(1)}, u32[]{:S(2)}, u32[]{:S(2)}) collective-permute-start(f32[7680]{0:T(1024)S(1)} %get-tuple-element.41), channel_id=1, source_target_pairs={{2,0},{4,2},{6,4},{3,1},{5,3},{7,5},{10,8},{12,10},{14,12},{11,9},... | collective-permute-start | bytes 92168 | tf_op jit(solution)/shard_map/ppermute | solution.py:182
  20.7 3.0 %collective-permute-start.3 = (f32[7680]{0:T(1024)S(1)}, f32[7680]{0:T(1024)S(1)}, u32[]{:S(2)}, u32[]{:S(2)}) collective-permute-start(f32[7680]{0:T(1024)S(1)} %get-tuple-element.42), channel_id=1, source_target_pairs={{0,2},{2,4},{4,6},{1,3},{3,5},{5,7},{8,10},{10,12},{12,14},{9,11},... | collective-permute-start | bytes 92168 | tf_op jit(solution)/shard_map/ppermute | solution.py:183
  23.7 0.7 %copy.36 = bf16[4,4,8,512]{3,2,0,1:T(8,128)(2,1)} copy(bf16[4,4,8,512]{3,2,1,0:T(8,128)(2,1)S(1)} %bitcast.32) | data formatting | bytes 262144 | tf_op jit(solution)/shard_map/all_to_all | solution.py:181
  24.4 3.5 %all-to-all-start = ((bf16[32,4,512]{2,0,1:T(8,128)(2,1)}), bf16[32,4,512]{2,0,1:T(8,128)(2,1)S(1)}, u32[]{:S(2)}, u32[]{:S(2)}) async-start(bf16[32,4,512]{2,0,1:T(8,128)(2,1)} %bitcast.28), calls=%async_computation | async-start | bytes 262144 | tf_op jit(solution)/shard_map/all_to_all | solution.py:181
  27.9 0.8 %pad_maximum_fusion.1.rowh_ref = f32[2,32,8,256]{3,2,1,0:T(8,128)} fusion(f32[1,32,8,256]{3,2,1,0:T(8,128)S(1)} %bitcast.30, f32[1,32,8,256]{3,2,1,0:T(8,128)S(1)} %bitcast.29), kind=kLoop, calls=%fused_computation.13 | loop fusion | flops 131072 | bytes 1048576 | tf_op jit(solution)/shard_map/stack | solution.py:167
  28.7 1.2 %concatenate.45 = f32[2,32,40,3]{3,2,1,0:T(8,128)S(1)} reshape(f32[7680]{0:T(1024)S(1)} %collective-permute-done.2) | data formatting | bytes 61440 | tf_op jit(solution)/shard_map/concatenate | solution.py:184
  29.9 1.2 %concatenate.46 = f32[2,32,40,3]{3,2,1,0:T(8,128)S(1)} reshape(f32[7680]{0:T(1024)S(1)} %collective-permute-done.3) | data formatting | bytes 61440 | tf_op jit(solution)/shard_map/concatenate | solution.py:184
  31.1 1.5 %pad_maximum_fusion.colh_ref = f32[2,32,40,128]{3,2,1,0:T(8,128)} fusion(f32[2,32,40,3]{3,2,1,0:T(8,128)S(1)} %concatenate.46, f32[2,32,40,3]{3,2,1,0:T(8,128)S(1)} %concatenate.45, f32[128]{0:T(128)S(1)} %pad.3.clone), kind=kLoop, calls=%fused_computation.10 | loop fusion | flops 655360 | bytes 1372672 | tf_op jit(solution)/shard_map/concatenate | solution.py:186
  32.6 2.4 %fusion.dep_ref = f32[32,32,256]{2,1,0:T(8,128)} fusion(pred[32,2048]{1,0:T(8,128)(4,1)S(1)} %fusion.9, bf16[32,2048]{1,0:T(8,128)(2,1)S(1)} %bitcast.33, s32[2048]{0:T(1024)S(1)} %get-tuple-element.45), kind=kOutput, calls=%fused_computation | convolution fusion | flops 1076363264 | bytes 1253376 | tf_op jit(solution)/shard_map/las,sb->lab/dot_general | solution.py:198
  35.0 3.6 %shard_map.91 = (f32[8,16,256]{2,1,0:T(8,128)}, f32[8,16,256]{2,1,0:T(8,128)}) custom-call(s32[1]{0:T(128)} %bitcast.rad_ref.after_ref.recv_ref, f32[32,32,256]{2,1,0:T(8,128)} %lam_ref.7, f32[32,32,256]{2,1,0:T(8,128)} %copy-done, f32[2,32,8,256]{3,2,1,0:T(8,128)} %pad_maximum_fusion.1.rowh_ref, f32[2,32,40,128]{3,2,1,0:T(8,128)} %pad_maximum_fusion.colh_ref, ...), custom_call_target="tpu_custom_call" | custom-call | flops 737280000 | bytes 12800000 | tf_op jit(solution)/shard_map/pallas_call | solution.py:104
  38.5 1.7 %collective-permute-start.4 = (f32[8,16,256]{2,1,0:T(8,128)}, f32[8,16,256]{2,1,0:T(8,128)S(1)}, u32[]{:S(2)}, u32[]{:S(2)}) collective-permute-start(f32[8,16,256]{2,1,0:T(8,128)} %get-tuple-element.19), channel_id=1, source_target_pairs={{0,1},{1,0},{2,3},{3,2},{4,5},{5,4},{6,7},{7,6},{8,9},{9,8},{10,11... | collective-permute-start | bytes 393224 | tf_op jit(solution)/shard_map/ppermute | solution.py:214
  40.2 3.6 %shard_map.92 = (f32[8,16,256]{2,1,0:T(8,128)}, f32[8,16,256]{2,1,0:T(8,128)}) custom-call(s32[1]{0:T(128)} %bitcast.rad_ref.after_ref.recv_ref, f32[32,32,256]{2,1,0:T(8,128)} %lam_ref.7, f32[32,32,256]{2,1,0:T(8,128)} %copy-done, f32[2,32,8,256]{3,2,1,0:T(8,128)} %pad_maximum_fusion.1.rowh_ref, f32[2,32,40,128]{3,2,1,0:T(8,128)} %pad_maximum_fusion.colh_ref, ...), custom_call_target="tpu_custom_call" | custom-call | flops 737280000 | bytes 12800000 | tf_op jit(solution)/shard_map/pallas_call | solution.py:104
  43.8 0.4 collective-permute-start.6
  44.1 0.1 constant_dynamic-slice_fusion.1
  44.2 0.6 collective-permute-done.4.recv_ref.refs_4_
  44.8 0.7 %copy-done.2 = f32[8,16,256]{2,1,0:T(8,128)} copy-done((f32[8,16,256]{2,1,0:T(8,128)}, f32[8,16,256]{2,1,0:T(8,128)S(1)}, u32[]{:S(2)}) %copy-start.2) | copy-done | bytes 131096
  45.5 3.6 %shard_map.93 = (f32[8,16,256]{2,1,0:T(8,128)}, f32[8,16,256]{2,1,0:T(8,128)}) custom-call(s32[1]{0:T(128)} %bitcast.rad_ref.after_ref.recv_ref, f32[32,32,256]{2,1,0:T(8,128)} %lam_ref.7, f32[32,32,256]{2,1,0:T(8,128)} %copy-done, f32[2,32,8,256]{3,2,1,0:T(8,128)} %pad_maximum_fusion.1.rowh_ref, f32[2,32,40,128]{3,2,1,0:T(8,128)} %pad_maximum_fusion.colh_ref, ...), custom_call_target="tpu_custom_call" | custom-call | flops 737280000 | bytes 12800000 | tf_op jit(solution)/shard_map/pallas_call | solution.py:104
  49.0 1.8 %collective-permute-start.5 = (f32[8,16,256]{2,1,0:T(8,128)}, f32[8,16,256]{2,1,0:T(8,128)S(1)}, u32[]{:S(2)}, u32[]{:S(2)}) collective-permute-start(f32[8,16,256]{2,1,0:T(8,128)} %get-tuple-element.20), channel_id=1, source_target_pairs={{0,1},{1,0},{2,3},{3,2},{4,5},{5,4},{6,7},{7,6},{8,9},{9,8},{10,11... | collective-permute-start | bytes 393224 | tf_op jit(solution)/shard_map/ppermute | solution.py:214
  50.9 0.7 %copy-done.3 = f32[8,16,256]{2,1,0:T(8,128)} copy-done((f32[8,16,256]{2,1,0:T(8,128)}, f32[8,16,256]{2,1,0:T(8,128)S(1)}, u32[]{:S(2)}) %copy-start.3) | copy-done | bytes 131096
  51.6 3.6 %shard_map.94 = (f32[8,16,256]{2,1,0:T(8,128)}, f32[8,16,256]{2,1,0:T(8,128)}) custom-call(s32[1]{0:T(128)} %bitcast.rad_ref.after_ref.recv_ref, f32[32,32,256]{2,1,0:T(8,128)} %lam_ref.7, f32[32,32,256]{2,1,0:T(8,128)} %copy-done, f32[2,32,8,256]{3,2,1,0:T(8,128)} %pad_maximum_fusion.1.rowh_ref, f32[2,32,40,128]{3,2,1,0:T(8,128)} %pad_maximum_fusion.colh_ref, ...), custom_call_target="tpu_custom_call" | custom-call | flops 737280000 | bytes 12800000 | tf_op jit(solution)/shard_map/pallas_call | solution.py:104
  55.1 0.2 collective-permute-start.7
  55.3 0.7 %constant_dynamic-slice_fusion.r_ref = f32[64,16]{1,0:T(8,128)} fusion(f32[64,64]{1,0:T(8,128)S(1)} %copy-done.5, s32[]{:T(128)S(6)} %add.54), kind=kLoop, calls=%fused_computation.49 | loop fusion | bytes 8196 | tf_op jit(solution)/shard_map/slice | solution.py:224
  56.0 0.7 %pad_maximum_fusion.7.r_ref = f32[64,48]{1,0:T(8,128)} fusion(f32[64,32]{1,0:T(8,128)S(1)} %get-tuple-element.44, f32[64,32]{1,0:T(8,128)S(1)} %get-tuple-element.43), kind=kLoop, calls=%fused_computation.29 | loop fusion | flops 3072 | bytes 28672 | tf_op jit(solution)/shard_map/concatenate | solution.py:219
  56.7 0.7 %copy-done.4 = f32[8,16,256]{2,1,0:T(8,128)} copy-done((f32[8,16,256]{2,1,0:T(8,128)}, f32[8,16,256]{2,1,0:T(8,128)S(1)}, u32[]{:S(2)}) %copy-start.4) | copy-done | bytes 131096
  57.3 3.4 %shard_map.95.refs_2_ = f32[64,16,256]{2,1,0:T(8,128)} custom-call(f32[64,48]{1,0:T(8,128)} %pad_maximum_fusion.7.r_ref, f32[8,16,256]{2,1,0:T(8,128)} %get-tuple-element.17.after_ref.refs_0_, f32[8,16,256]{2,1,0:T(8,128)} %get-tuple-element.18.after_ref.refs_1_, f32[8,16,256]{2,1,0:T(8,128)} %get-tuple-element.21.after_ref.refs_2_, ...), custom_call_target="tpu_custom_call" | custom-call | tf_op jit(solution)/shard_map/pallas_call | solution.py:251
  60.8 0.7 %copy-done.6 = f32[8,16,256]{2,1,0:T(8,128)} copy-done((f32[8,16,256]{2,1,0:T(8,128)}, f32[8,16,256]{2,1,0:T(8,128)S(1)}, u32[]{:S(2)}) %copy-start.6) | copy-done | bytes 131096
  61.4 3.5 %shard_map.96 = f32[64,16,256]{2,1,0:T(8,128)} custom-call(f32[64,16]{1,0:T(8,128)} %constant_dynamic-slice_fusion.r_ref, f32[8,16,256]{2,1,0:T(8,128)} %copy-done.4, f32[8,16,256]{2,1,0:T(8,128)} %copy-done.6, f32[64,16,256]{2,1,0:T(8,128)} %shard_map.95.refs_2_), custom_call_target="tpu_custom_call" | custom-call | tf_op jit(solution)/shard_map/pallas_call | solution.py:251
  (30 shorter events, 0.2 us)
Async XLA Ops:
  0.0 1.9 %copy-start.1 = (f32[32,32,256]{2,1,0:T(8,128)S(1)}, f32[32,32,256]{2,1,0:T(8,128)}, u32[]{:S(2)}) copy-start(f32[32,32,256]{2,1,0:T(8,128)} %lam_ref.7) | copy-start | bytes 3145732
  1.9 7.3 %copy-start = (f32[32,32,256]{2,1,0:T(8,128)}, f32[32,32,256]{2,1,0:T(8,128)S(1)}, u32[]{:S(2)}) copy-start(f32[32,32,256]{2,1,0:T(8,128)S(1)} %convert_select_fusion.eta_ref) | copy-start | bytes 3145732
  2.1 11.2 %collective-permute-start = (f32[32,6,256]{2,1,0:T(8,128)S(1)}, f32[32,6,256]{2,1,0:T(8,128)S(1)}, u32[]{:S(2)}, u32[]{:S(2)}) collective-permute-start(f32[32,6,256]{2,1,0:T(8,128)S(1)} %pad_maximum_fusion.2), channel_id=1, source_target_pairs={{8,0},{16,8},{24,16},{9,1},{17,9},{25,17},{10,2},{18,10},{26,18},{... | collective-permute-start | bytes 589832 | tf_op jit(solution)/shard_map/ppermute | solution.py:165
  3.5 11.1 %collective-permute-start.1 = (f32[32,6,256]{2,1,0:T(8,128)S(1)}, f32[32,6,256]{2,1,0:T(8,128)S(1)}, u32[]{:S(2)}, u32[]{:S(2)}) collective-permute-start(f32[32,6,256]{2,1,0:T(8,128)S(1)} %pad_maximum_fusion.3), channel_id=1, source_target_pairs={{0,8},{8,16},{16,24},{1,9},{9,17},{17,25},{2,10},{10,18},{18,26},{... | collective-permute-start | bytes 589832 | tf_op jit(solution)/shard_map/ppermute | solution.py:164
  9.5 1.3 %copy-start.8 = (s32[2048]{0:T(1024)S(1)}, s32[2048]{0:T(1024)}, u32[]{:S(2)}) copy-start(s32[2048]{0:T(1024)} %param.16) | copy-start | bytes 24580
  9.5 1.3 %copy-start.9 = (s32[4]{0:T(128)S(1)}, s32[4]{0:T(128)}, u32[]{:S(2)}) copy-start(s32[4]{0:T(128)} %param.17) | copy-start | bytes 52
  17.5 6.2 %copy-start.7 = (bf16[32,2048]{1,0:T(8,128)(2,1)S(1)}, bf16[32,2048]{1,0:T(8,128)(2,1)}, u32[]{:S(2)}) copy-start(bf16[32,2048]{1,0:T(8,128)(2,1)} %param.15) | copy-start | bytes 393220
  19.4 9.4 %collective-permute-start.2 = (f32[7680]{0:T(1024)S(1)}, f32[7680]{0:T(1024)S(1)}, u32[]{:S(2)}, u32[]{:S(2)}) collective-permute-start(f32[7680]{0:T(1024)S(1)} %get-tuple-element.41), channel_id=1, source_target_pairs={{2,0},{4,2},{6,4},{3,1},{5,3},{7,5},{10,8},{12,10},{14,12},{11,9},... | collective-permute-start | bytes 92168 | tf_op jit(solution)/shard_map/ppermute | solution.py:182
  20.7 9.3 %collective-permute-start.3 = (f32[7680]{0:T(1024)S(1)}, f32[7680]{0:T(1024)S(1)}, u32[]{:S(2)}, u32[]{:S(2)}) collective-permute-start(f32[7680]{0:T(1024)S(1)} %get-tuple-element.42), channel_id=1, source_target_pairs={{0,2},{2,4},{4,6},{1,3},{3,5},{5,7},{8,10},{10,12},{12,14},{9,11},... | collective-permute-start | bytes 92168 | tf_op jit(solution)/shard_map/ppermute | solution.py:183
  24.4 8.2 %all-to-all-start = ((bf16[32,4,512]{2,0,1:T(8,128)(2,1)}), bf16[32,4,512]{2,0,1:T(8,128)(2,1)S(1)}, u32[]{:S(2)}, u32[]{:S(2)}) async-start(bf16[32,4,512]{2,0,1:T(8,128)(2,1)} %bitcast.28), calls=%async_computation | async-start | bytes 262144 | tf_op jit(solution)/shard_map/all_to_all | solution.py:181
  38.5 6.3 %collective-permute-start.4 = (f32[8,16,256]{2,1,0:T(8,128)}, f32[8,16,256]{2,1,0:T(8,128)S(1)}, u32[]{:S(2)}, u32[]{:S(2)}) collective-permute-start(f32[8,16,256]{2,1,0:T(8,128)} %get-tuple-element.19), channel_id=1, source_target_pairs={{0,1},{1,0},{2,3},{3,2},{4,5},{5,4},{6,7},{7,6},{8,9},{9,8},{10,11... | collective-permute-start | bytes 393224 | tf_op jit(solution)/shard_map/ppermute | solution.py:214
  40.2 3.9 %copy-start.5 = (f32[64,64]{1,0:T(8,128)S(1)}, f32[64,64]{1,0:T(8,128)}, u32[]{:S(2)}) copy-start(f32[64,64]{1,0:T(8,128)} %param.14) | copy-start | bytes 49156
  43.8 7.1 %collective-permute-start.6 = (f32[8,16,256]{2,1,0:T(8,128)}, f32[8,16,256]{2,1,0:T(8,128)S(1)}, u32[]{:S(2)}, u32[]{:S(2)}) collective-permute-start(f32[8,16,256]{2,1,0:T(8,128)} %get-tuple-element.22), channel_id=1, source_target_pairs={{0,1},{1,0},{2,3},{3,2},{4,5},{5,4},{6,7},{7,6},{8,9},{9,8},{10,11... | collective-permute-start | bytes 393224 | tf_op jit(solution)/shard_map/ppermute | solution.py:214
  44.8 0.7 %copy-start.2 = (f32[8,16,256]{2,1,0:T(8,128)}, f32[8,16,256]{2,1,0:T(8,128)S(1)}, u32[]{:S(2)}) copy-start(f32[8,16,256]{2,1,0:T(8,128)S(1)} %collective-permute-done.4.recv_ref.refs_4_) | copy-start | bytes 393220
  49.0 7.6 %collective-permute-start.5 = (f32[8,16,256]{2,1,0:T(8,128)}, f32[8,16,256]{2,1,0:T(8,128)S(1)}, u32[]{:S(2)}, u32[]{:S(2)}) collective-permute-start(f32[8,16,256]{2,1,0:T(8,128)} %get-tuple-element.20), channel_id=1, source_target_pairs={{0,1},{1,0},{2,3},{3,2},{4,5},{5,4},{6,7},{7,6},{8,9},{9,8},{10,11... | collective-permute-start | bytes 393224 | tf_op jit(solution)/shard_map/ppermute | solution.py:214
  50.9 0.7 %copy-start.3 = (f32[8,16,256]{2,1,0:T(8,128)}, f32[8,16,256]{2,1,0:T(8,128)S(1)}, u32[]{:S(2)}) copy-start(f32[8,16,256]{2,1,0:T(8,128)S(1)} %collective-permute-done.6.recv_ref.refs_5_) | copy-start | bytes 393220
  55.1 5.6 %collective-permute-start.7 = (f32[8,16,256]{2,1,0:T(8,128)}, f32[8,16,256]{2,1,0:T(8,128)S(1)}, u32[]{:S(2)}, u32[]{:S(2)}) collective-permute-start(f32[8,16,256]{2,1,0:T(8,128)} %get-tuple-element.23), channel_id=1, source_target_pairs={{0,1},{1,0},{2,3},{3,2},{4,5},{5,4},{6,7},{7,6},{8,9},{9,8},{10,11... | collective-permute-start | bytes 393224 | tf_op jit(solution)/shard_map/ppermute | solution.py:214
  56.7 0.7 %copy-start.4 = (f32[8,16,256]{2,1,0:T(8,128)}, f32[8,16,256]{2,1,0:T(8,128)S(1)}, u32[]{:S(2)}) copy-start(f32[8,16,256]{2,1,0:T(8,128)S(1)} %collective-permute-done.5.refs_6_.refs_0_) | copy-start | bytes 393220
  60.8 0.7 %copy-start.6 = (f32[8,16,256]{2,1,0:T(8,128)}, f32[8,16,256]{2,1,0:T(8,128)S(1)}, u32[]{:S(2)}) copy-start(f32[8,16,256]{2,1,0:T(8,128)S(1)} %collective-permute-done.7.refs_1_) | copy-start | bytes 393220

commit v8 on v7

--- a/solution.py
+++ b/solution.py
@@ -152,15 +152,18 @@
     d = lax.axis_index("lat")
     r = lax.axis_index("rad")
 
-    flow = visc_flow.astype(jnp.float32)
-    plast = visc_yield.astype(jnp.float32)
-    eta = jnp.where(yield_mask == 1, flow * plast / (flow + plast), flow)
+    def eta_of(sl):
+        flow = visc_flow[:, sl].astype(jnp.float32)
+        plast = visc_yield[:, sl].astype(jnp.float32)
+        return jnp.where(yield_mask[:, sl] == 1, flow * plast / (flow + plast), flow)
+
+    eta = eta_of(slice(None))
 
     g = GHOST
     ext_rows = ((rows + 2 * g + 7) // 8) * 8
     ext_cols = ((cols + 2 * g + 127) // 128) * 128
-    top_send = jnp.concatenate([adjoint_temp[:, rows - g:], eta[:, rows - g:]], axis=1)
-    bot_send = jnp.concatenate([adjoint_temp[:, :g], eta[:, :g]], axis=1)
+    top_send = jnp.concatenate([adjoint_temp[:, rows - g:], eta_of(slice(rows - g, rows))], axis=1)
+    bot_send = jnp.concatenate([adjoint_temp[:, :g], eta_of(slice(0, g))], axis=1)
     top = lax.ppermute(top_send, "cap", _pairs(n_cap, 1))
     bot = lax.ppermute(bot_send, "cap", _pairs(n_cap, -1))
     zr = jnp.zeros((layers, ext_rows - rows - 2 * g, cols), jnp.float32)

time: 65.3 us -> 67.8 us (1.038)
  other arithmetic: 6.44 us -> 7.93 us
  local copies, waits for them, and re-layouts: 12.5 us -> 13.9 us
  waiting for transfers between devices: 3.42 us -> 2.25 us
  starting transfers between devices: 18.7 us -> 19.6 us
    ppermute x1, waiting for transfers between devices: 1.6 us -> 0.01 us  [per_device(): bot = lax.ppermute(bot_send, 'cap', _pairs(n_cap, -1))]
    concatenate x2, other arithmetic: 0.11 us -> 1.49 us  [the longest x1 0.75 us: per_device(): jnp.concatenate([adjoint_temp[:, :g], eta_of(slice(0, g))], axis=1)]
    slice x1, local copies, waits for them, and re-layouts: 0.05 us -> 1.09 us  [per_device(): top[:, :g]]
    ppermute x1, starting transfers between devices: 5.57 us -> 6.39 us  [per_device(): top = lax.ppermute(top_send, 'cap', _pairs(n_cap, 1))]
    unnamed x23 -> x29, local copies, waits for them, and re-layouts: 3.23 us -> 3.74 us
    select_n x1 -> x2, other arithmetic: 1.92 us -> 2.06 us  [eta_of(): jnp.where(yield_mask[:, sl] == 1, flow * plast / (flow + plast), flow)]
  transfers between devices with their start and end apart: 9 -> 9, of which waited for: 3 -> 2; matrix products, arithmetic and copies ran while one was open for 15% -> 16% of each run, Pallas kernels for 22% -> 21%
where the time goes in v8:
time: 67.8 us; the launch traced here: 67.3 us
  Pallas kernels  21.1 us (31%)
  starting transfers between devices  19.6 us (29%)
  local copies, waits for them, and re-layouts  13.9 us (21%)
  other arithmetic  7.93 us (12%)
  matrix products  2.35 us (3%)
  waiting for transfers between devices  2.25 us (3%)
    pallas_call x4, Pallas kernels, _sweeps(): pl.pallas_call(_sweep_kernel, out_shape=out_shape, grid=grid, in_specs=[p...  14.2 us
    pallas_call x2, Pallas kernels, _radial(): pl.pallas_call(functools.partial(_radial_kernel, len(pieces), partial is...  6.88 us
    ppermute x1, starting transfers between devices, per_device(): top = lax.ppermute(top_send, 'cap', _pairs(n_cap, 1))  6.39 us
    ppermute x4, starting transfers between devices, per_device(): lax.ppermute(send, 'rad', _pairs(n_rad, 1) + _pairs(n_rad, -1))  4.05 us
    unnamed x29, local copies, waits for them, and re-layouts  3.74 us
    all_to_all x1, starting transfers between devices, per_device(): lax.all_to_all(markers, 'lat', split_axis=1, concat_axis=1, tiled=True)  3.5 us
    ppermute x1, starting transfers between devices, per_device(): from_left = lax.ppermute(flat[piece:], 'lat', _pairs(n_lat, 1))  3.03 us
    concatenate x2, local copies, waits for them, and re-layouts, per_device(): jnp.concatenate([from_right, from_left]).reshape(2, 2, layers, ext_rows, g)  2.37 us
  transfers between devices with their start and end apart: 9, of which 2 were waited for; matrix products, arithmetic and copies ran while one was open for 16% of the time, Pallas kernels for 21%

profile of v8, /device:TPU:0, one launch (start us, length us, event | category | flops | bytes accessed | tf_op | source)
XLA Modules:
  0.0 67.3 jit_solution(17997817954021204266)
XLA Ops:
  0.0 1.8 %convert_select_fusion.2 = (f32[32,3,256]{2,1,0:T(4,128)S(1)}, f32[32,3,256]{2,1,0:T(4,128)S(1)}, f32[32,3,256]{2,1,0:T(4,128)S(1)}, f32[32,3,256]{2,1,0:T(4,128)S(1)}) fusion(s32[32,32,256]{2,1,0:T(8,128)} %param.13, bf16[32,32,256]{2,1,0:T(8,128)(2,1)} %param.12, bf16[32,32,256]{2,1,0:T(8,128)(2,1)} %param.11, f32[32,32,256]{2,1,0:T(8,128)} %lam_ref.7), kind=kLoop, calls=%fused_computation.24 | loop fusion | flops 344064 | bytes 983040 | tf_op jit(solution)/shard_map/jit(_where)/select_n | solution.py:158
  1.8 0.7 %pad_maximum_fusion.2 = f32[32,6,256]{2,1,0:T(8,128)} fusion(f32[32,3,256]{2,1,0:T(4,128)S(1)} %get-tuple-element.25, f32[32,3,256]{2,1,0:T(4,128)S(1)} %get-tuple-element.50), kind=kLoop, calls=%fused_computation.14 | loop fusion | flops 49152 | bytes 393216 | tf_op jit(solution)/shard_map/concatenate | solution.py:166
  2.5 1.3 %collective-permute-start = (f32[32,6,256]{2,1,0:T(8,128)}, f32[32,6,256]{2,1,0:T(8,128)S(1)}, u32[]{:S(2)}, u32[]{:S(2)}) collective-permute-start(f32[32,6,256]{2,1,0:T(8,128)} %pad_maximum_fusion.2), channel_id=1, source_target_pairs={{8,0},{16,8},{24,16},{9,1},{17,9},{25,17},{10,2},{18,10},{26,18},{... | collective-permute-start | bytes 589832 | tf_op jit(solution)/shard_map/ppermute | solution.py:168
  3.8 0.7 %pad_maximum_fusion.3 = f32[32,6,256]{2,1,0:T(8,128)} fusion(f32[32,3,256]{2,1,0:T(4,128)S(1)} %get-tuple-element.26, f32[32,3,256]{2,1,0:T(4,128)S(1)} %get-tuple-element.49), kind=kLoop, calls=%fused_computation.15 | loop fusion | flops 49152 | bytes 393216 | tf_op jit(solution)/shard_map/concatenate | solution.py:165
  4.6 6.4 %collective-permute-start.1 = (f32[32,6,256]{2,1,0:T(8,128)}, f32[32,6,256]{2,1,0:T(8,128)}, u32[]{:S(2)}, u32[]{:S(2)}) collective-permute-start(f32[32,6,256]{2,1,0:T(8,128)} %pad_maximum_fusion.3), channel_id=1, source_target_pairs={{0,8},{8,16},{16,24},{1,9},{9,17},{17,25},{2,10},{10,18},{18,26},{... | collective-permute-start | bytes 589832 | tf_op jit(solution)/shard_map/ppermute | solution.py:167
  11.0 0.3 convert_select_fusion.eta_ref
  11.3 0.0 copy-start
  11.3 0.2 fusion.17
  11.5 0.2 fusion.18
  11.7 0.5 copy-done
  12.2 0.3 copy.21
  12.5 0.3 copy.30
  12.8 0.3 copy.25
  13.1 0.3 copy.31
  13.4 0.1 pad.25.clone
  13.5 0.1 pad.3.clone
  13.6 0.1 fusion.13
  13.7 0.1 fusion.9
  13.7 0.7 %and_convert_fusion.mask_ref = f32[40,384]{1,0:T(8,128)} fusion(pred[384]{0:T(512)(128)(4,1)S(1)} %compare_and_fusion, pred[40]{0:T(512)(128)(4,1)S(1)} %compare_and_fusion.1), kind=kLoop, calls=%fused_computation.34 | loop fusion | flops 30720 | bytes 61864 | tf_op jit(solution)/shard_map/convert_element_type | solution.py:28
  14.4 0.0 collective-permute-done
  14.4 0.1 fusion.22
  14.5 1.6 %collective-permute-done.1 = f32[32,6,256]{2,1,0:T(8,128)} collective-permute-done((f32[32,6,256]{2,1,0:T(8,128)}, f32[32,6,256]{2,1,0:T(8,128)}, u32[]{:S(2)}, u32[]{:S(2)}) %collective-permute-start.1) | collective-permute-done | bytes 196640 | tf_op jit(solution)/shard_map/ppermute | solution.py:167
  16.1 1.1 %fusion.23 = (f32[32,3,256]{2,1,0:T(4,128)S(1)}, f32[32,3,256]{2,1,0:T(4,128)S(1)}) fusion(f32[32,6,256]{2,1,0:T(8,128)} %collective-permute-done.1), kind=kLoop, calls=%fused_computation.69 | loop fusion | bytes 393216 | tf_op jit(solution)/shard_map/slice | solution.py:171
  17.2 0.1 pad_maximum_fusion.4
  17.3 0.1 fusion.21
  17.4 0.3 copy.22
  17.7 0.1 fusion.20
  17.8 0.3 copy.20
  18.1 0.3 copy.26
  18.4 0.3 copy.24
  18.7 0.1 maximum_bitcast_fusion.3
  18.8 0.1 maximum_bitcast_fusion.2
  18.9 0.1 maximum_bitcast_fusion.5
  19.0 0.1 maximum_bitcast_fusion.4
  19.1 0.9 %copy.27 = f32[2,2,32,40,3]{4,3,2,1,0:T(8,128)S(1)} copy(f32[2,2,32,40,3]{3,2,4,1,0:T(8,128)S(1)} %pad_maximum_fusion.6) | data formatting | bytes 122880 | tf_op jit(solution)/shard_map/stack | solution.py:181
  20.0 0.0 copy-start.10
  20.0 1.9 %reshape.108 = f32[15360]{0:T(1024)S(1)} reshape(f32[2,2,32,40,3]{4,3,2,1,0:T(8,128)S(1)} %copy.27) | data formatting | bytes 122880 | tf_op jit(solution)/shard_map/reshape | solution.py:181
  21.9 1.3 %collective-permute-start.2 = (f32[7680]{0:T(1024)S(1)}, f32[7680]{0:T(1024)S(1)}, u32[]{:S(2)}, u32[]{:S(2)}) collective-permute-start(f32[7680]{0:T(1024)S(1)} %get-tuple-element.41), channel_id=1, source_target_pairs={{2,0},{4,2},{6,4},{3,1},{5,3},{7,5},{10,8},{12,10},{14,12},{11,9},... | collective-permute-start | bytes 92168 | tf_op jit(solution)/shard_map/ppermute | solution.py:185
  23.2 3.0 %collective-permute-start.3 = (f32[7680]{0:T(1024)S(1)}, f32[7680]{0:T(1024)S(1)}, u32[]{:S(2)}, u32[]{:S(2)}) collective-permute-start(f32[7680]{0:T(1024)S(1)} %get-tuple-element.42), channel_id=1, source_target_pairs={{0,2},{2,4},{4,6},{1,3},{3,5},{5,7},{8,10},{10,12},{12,14},{9,11},... | collective-permute-start | bytes 92168 | tf_op jit(solution)/shard_map/ppermute | solution.py:186
  26.3 0.7 copy.36
  26.9 3.5 %all-to-all-start = ((bf16[32,4,512]{2,0,1:T(8,128)(2,1)}), bf16[32,4,512]{2,0,1:T(8,128)(2,1)S(1)}, u32[]{:S(2)}, u32[]{:S(2)}) async-start(bf16[32,4,512]{2,0,1:T(8,128)(2,1)} %bitcast.28), calls=%async_computation | async-start | bytes 262144 | tf_op jit(solution)/shard_map/all_to_all | solution.py:184
  30.4 0.8 %pad_maximum_fusion.1.rowh_ref = f32[2,32,8,256]{3,2,1,0:T(8,128)} fusion(f32[1,32,8,256]{3,2,1,0:T(8,128)S(1)} %bitcast.30, f32[1,32,8,256]{3,2,1,0:T(8,128)S(1)} %bitcast.29), kind=kLoop, calls=%fused_computation.13 | loop fusion | flops 131072 | bytes 1048576 | tf_op jit(solution)/shard_map/stack | solution.py:170
  31.3 1.2 %concatenate.45 = f32[2,32,40,3]{3,2,1,0:T(8,128)S(1)} reshape(f32[7680]{0:T(1024)S(1)} %collective-permute-done.2) | data formatting | bytes 61440 | tf_op jit(solution)/shard_map/concatenate | solution.py:187
  32.5 1.2 %concatenate.46 = f32[2,32,40,3]{3,2,1,0:T(8,128)S(1)} reshape(f32[7680]{0:T(1024)S(1)} %collective-permute-done.3) | data formatting | bytes 61440 | tf_op jit(solution)/shard_map/concatenate | solution.py:187
  33.7 1.5 %pad_maximum_fusion.colh_ref = f32[2,32,40,128]{3,2,1,0:T(8,128)} fusion(f32[2,32,40,3]{3,2,1,0:T(8,128)S(1)} %concatenate.46, f32[2,32,40,3]{3,2,1,0:T(8,128)S(1)} %concatenate.45, f32[128]{0:T(128)S(1)} %pad.3.clone), kind=kLoop, calls=%fused_computation.10 | loop fusion | flops 655360 | bytes 1372672 | tf_op jit(solution)/shard_map/concatenate | solution.py:189
  35.2 2.3 %fusion.dep_ref = f32[32,32,256]{2,1,0:T(8,128)} fusion(pred[32,2048]{1,0:T(8,128)(4,1)S(1)} %fusion.9, bf16[32,2048]{1,0:T(8,128)(2,1)S(1)} %bitcast.33, s32[2048]{0:T(1024)S(1)} %get-tuple-element.45), kind=kOutput, calls=%fused_computation | convolution fusion | flops 1076363264 | bytes 1253376 | tf_op jit(solution)/shard_map/las,sb->lab/dot_general | solution.py:201
  37.5 3.5 %shard_map.91 = (f32[8,16,256]{2,1,0:T(8,128)}, f32[8,16,256]{2,1,0:T(8,128)}) custom-call(s32[1]{0:T(128)} %bitcast.rad_ref.after_ref.recv_ref, f32[32,32,256]{2,1,0:T(8,128)} %lam_ref.7, f32[32,32,256]{2,1,0:T(8,128)} %copy-done, f32[2,32,8,256]{3,2,1,0:T(8,128)} %pad_maximum_fusion.1.rowh_ref, f32[2,32,40,128]{3,2,1,0:T(8,128)} %pad_maximum_fusion.colh_ref, ...), custom_call_target="tpu_custom_call" | custom-call | flops 737280000 | bytes 12800000 | tf_op jit(solution)/shard_map/pallas_call | solution.py:104
  41.1 1.7 %collective-permute-start.4 = (f32[8,16,256]{2,1,0:T(8,128)}, f32[8,16,256]{2,1,0:T(8,128)S(1)}, u32[]{:S(2)}, u32[]{:S(2)}) collective-permute-start(f32[8,16,256]{2,1,0:T(8,128)} %get-tuple-element.19), channel_id=1, source_target_pairs={{0,1},{1,0},{2,3},{3,2},{4,5},{5,4},{6,7},{7,6},{8,9},{9,8},{10,11... | collective-permute-start | bytes 393224 | tf_op jit(solution)/shard_map/ppermute | solution.py:217
  42.7 3.6 %shard_map.92 = (f32[8,16,256]{2,1,0:T(8,128)}, f32[8,16,256]{2,1,0:T(8,128)}) custom-call(s32[1]{0:T(128)} %bitcast.rad_ref.after_ref.recv_ref, f32[32,32,256]{2,1,0:T(8,128)} %lam_ref.7, f32[32,32,256]{2,1,0:T(8,128)} %copy-done, f32[2,32,8,256]{3,2,1,0:T(8,128)} %pad_maximum_fusion.1.rowh_ref, f32[2,32,40,128]{3,2,1,0:T(8,128)} %pad_maximum_fusion.colh_ref, ...), custom_call_target="tpu_custom_call" | custom-call | flops 737280000 | bytes 12800000 | tf_op jit(solution)/shard_map/pallas_call | solution.py:104
  46.3 0.3 collective-permute-start.6
  46.6 0.1 constant_dynamic-slice_fusion.1
  46.7 0.6 collective-permute-done.4.recv_ref.refs_4_
  47.4 0.6 copy-done.5
  48.0 3.5 %shard_map.93 = (f32[8,16,256]{2,1,0:T(8,128)}, f32[8,16,256]{2,1,0:T(8,128)}) custom-call(s32[1]{0:T(128)} %bitcast.rad_ref.after_ref.recv_ref, f32[32,32,256]{2,1,0:T(8,128)} %lam_ref.7, f32[32,32,256]{2,1,0:T(8,128)} %copy-done, f32[2,32,8,256]{3,2,1,0:T(8,128)} %pad_maximum_fusion.1.rowh_ref, f32[2,32,40,128]{3,2,1,0:T(8,128)} %pad_maximum_fusion.colh_ref, ...), custom_call_target="tpu_custom_call" | custom-call | flops 737280000 | bytes 12800000 | tf_op jit(solution)/shard_map/pallas_call | solution.py:104
  51.5 1.8 %collective-permute-start.5 = (f32[8,16,256]{2,1,0:T(8,128)}, f32[8,16,256]{2,1,0:T(8,128)S(1)}, u32[]{:S(2)}, u32[]{:S(2)}) collective-permute-start(f32[8,16,256]{2,1,0:T(8,128)} %get-tuple-element.20), channel_id=1, source_target_pairs={{0,1},{1,0},{2,3},{3,2},{4,5},{5,4},{6,7},{7,6},{8,9},{9,8},{10,11... | collective-permute-start | bytes 393224 | tf_op jit(solution)/shard_map/ppermute | solution.py:217
  53.4 0.7 copy-done.6
  54.0 3.5 %shard_map.94 = (f32[8,16,256]{2,1,0:T(8,128)}, f32[8,16,256]{2,1,0:T(8,128)}) custom-call(s32[1]{0:T(128)} %bitcast.rad_ref.after_ref.recv_ref, f32[32,32,256]{2,1,0:T(8,128)} %lam_ref.7, f32[32,32,256]{2,1,0:T(8,128)} %copy-done, f32[2,32,8,256]{3,2,1,0:T(8,128)} %pad_maximum_fusion.1.rowh_ref, f32[2,32,40,128]{3,2,1,0:T(8,128)} %pad_maximum_fusion.colh_ref, ...), custom_call_target="tpu_custom_call" | custom-call | flops 737280000 | bytes 12800000 | tf_op jit(solution)/shard_map/pallas_call | solution.py:104
  57.6 0.2 collective-permute-start.7
  57.8 0.7 %constant_dynamic-slice_fusion.r_ref = f32[64,16]{1,0:T(8,128)} fusion(f32[64,64]{1,0:T(8,128)S(1)} %copy-done.8, s32[]{:T(128)S(6)} %add.62), kind=kLoop, calls=%fused_computation.59 | loop fusion | bytes 8196 | tf_op jit(solution)/shard_map/slice | solution.py:227
  58.5 0.7 %pad_maximum_fusion.7.r_ref = f32[64,48]{1,0:T(8,128)} fusion(f32[64,32]{1,0:T(8,128)S(1)} %get-tuple-element.44, f32[64,32]{1,0:T(8,128)S(1)} %get-tuple-element.43), kind=kLoop, calls=%fused_computation.39 | loop fusion | flops 3072 | bytes 28672 | tf_op jit(solution)/shard_map/concatenate | solution.py:222
  59.2 0.6 copy-done.7
  59.8 3.4 %shard_map.95.refs_2_ = f32[64,16,256]{2,1,0:T(8,128)} custom-call(f32[64,48]{1,0:T(8,128)} %pad_maximum_fusion.7.r_ref, f32[8,16,256]{2,1,0:T(8,128)} %get-tuple-element.17.after_ref.refs_0_, f32[8,16,256]{2,1,0:T(8,128)} %get-tuple-element.18.after_ref.refs_1_, f32[8,16,256]{2,1,0:T(8,128)} %get-tuple-element.21.after_ref.refs_2_, ...), custom_call_target="tpu_custom_call" | custom-call | tf_op jit(solution)/shard_map/pallas_call | solution.py:254
  63.2 0.6 copy-done.9
  63.9 3.5 %shard_map.96 = f32[64,16,256]{2,1,0:T(8,128)} custom-call(f32[64,16]{1,0:T(8,128)} %constant_dynamic-slice_fusion.r_ref, f32[8,16,256]{2,1,0:T(8,128)} %copy-done.7, f32[8,16,256]{2,1,0:T(8,128)} %copy-done.9, f32[64,16,256]{2,1,0:T(8,128)} %shard_map.95.refs_2_), custom_call_target="tpu_custom_call" | custom-call | tf_op jit(solution)/shard_map/pallas_call | solution.py:254
  (36 shorter events, 0.2 us)
Async XLA Ops:
  0.0 11.0 %copy-start.3 = (bf16[32,32,256]{2,1,0:T(8,128)(2,1)S(1)}, bf16[32,32,256]{2,1,0:T(8,128)(2,1)}, u32[]{:S(2)}) copy-start(bf16[32,32,256]{2,1,0:T(8,128)(2,1)} %param.11) | copy-start | bytes 1572868
  0.0 11.0 %copy-start.4 = (bf16[32,32,256]{2,1,0:T(8,128)(2,1)S(1)}, bf16[32,32,256]{2,1,0:T(8,128)(2,1)}, u32[]{:S(2)}) copy-start(bf16[32,32,256]{2,1,0:T(8,128)(2,1)} %param.12) | copy-start | bytes 1572868
  0.0 11.0 %copy-start.2 = (s32[32,32,256]{2,1,0:T(8,128)S(1)}, s32[32,32,256]{2,1,0:T(8,128)}, u32[]{:S(2)}) copy-start(s32[32,32,256]{2,1,0:T(8,128)} %param.13) | copy-start | bytes 3145732
  2.5 11.9 %collective-permute-start = (f32[32,6,256]{2,1,0:T(8,128)}, f32[32,6,256]{2,1,0:T(8,128)S(1)}, u32[]{:S(2)}, u32[]{:S(2)}) collective-permute-start(f32[32,6,256]{2,1,0:T(8,128)} %pad_maximum_fusion.2), channel_id=1, source_target_pairs={{8,0},{16,8},{24,16},{9,1},{17,9},{25,17},{10,2},{18,10},{26,18},{... | collective-permute-start | bytes 589832 | tf_op jit(solution)/shard_map/ppermute | solution.py:168
  4.6 6.7 %copy-start.1 = (f32[32,32,256]{2,1,0:T(8,128)S(1)}, f32[32,32,256]{2,1,0:T(8,128)}, u32[]{:S(2)}) copy-start(f32[32,32,256]{2,1,0:T(8,128)} %lam_ref.7) | copy-start | bytes 3145732
  4.6 11.6 %collective-permute-start.1 = (f32[32,6,256]{2,1,0:T(8,128)}, f32[32,6,256]{2,1,0:T(8,128)}, u32[]{:S(2)}, u32[]{:S(2)}) collective-permute-start(f32[32,6,256]{2,1,0:T(8,128)} %pad_maximum_fusion.3), channel_id=1, source_target_pairs={{0,8},{8,16},{16,24},{1,9},{9,17},{17,25},{2,10},{10,18},{18,26},{... | collective-permute-start | bytes 589832 | tf_op jit(solution)/shard_map/ppermute | solution.py:167
  11.3 1.0 %copy-start = (f32[32,32,256]{2,1,0:T(8,128)}, f32[32,32,256]{2,1,0:T(8,128)S(1)}, u32[]{:S(2)}) copy-start(f32[32,32,256]{2,1,0:T(8,128)S(1)} %convert_select_fusion.eta_ref) | copy-start | bytes 3145732
  12.2 1.3 %copy-start.11 = (s32[2048]{0:T(1024)S(1)}, s32[2048]{0:T(1024)}, u32[]{:S(2)}) copy-start(s32[2048]{0:T(1024)} %param.16) | copy-start | bytes 24580
  12.2 1.3 %copy-start.12 = (s32[4]{0:T(128)S(1)}, s32[4]{0:T(128)}, u32[]{:S(2)}) copy-start(s32[4]{0:T(128)} %param.17) | copy-start | bytes 52
  20.0 6.2 %copy-start.10 = (bf16[32,2048]{1,0:T(8,128)(2,1)S(1)}, bf16[32,2048]{1,0:T(8,128)(2,1)}, u32[]{:S(2)}) copy-start(bf16[32,2048]{1,0:T(8,128)(2,1)} %param.15) | copy-start | bytes 393220
  21.9 9.4 %collective-permute-start.2 = (f32[7680]{0:T(1024)S(1)}, f32[7680]{0:T(1024)S(1)}, u32[]{:S(2)}, u32[]{:S(2)}) collective-permute-start(f32[7680]{0:T(1024)S(1)} %get-tuple-element.41), channel_id=1, source_target_pairs={{2,0},{4,2},{6,4},{3,1},{5,3},{7,5},{10,8},{12,10},{14,12},{11,9},... | collective-permute-start | bytes 92168 | tf_op jit(solution)/shard_map/ppermute | solution.py:185
  23.2 9.3 %collective-permute-start.3 = (f32[7680]{0:T(1024)S(1)}, f32[7680]{0:T(1024)S(1)}, u32[]{:S(2)}, u32[]{:S(2)}) collective-permute-start(f32[7680]{0:T(1024)S(1)} %get-tuple-element.42), channel_id=1, source_target_pairs={{0,2},{2,4},{4,6},{1,3},{3,5},{5,7},{8,10},{10,12},{12,14},{9,11},... | collective-permute-start | bytes 92168 | tf_op jit(solution)/shard_map/ppermute | solution.py:186
  26.9 8.2 %all-to-all-start = ((bf16[32,4,512]{2,0,1:T(8,128)(2,1)}), bf16[32,4,512]{2,0,1:T(8,128)(2,1)S(1)}, u32[]{:S(2)}, u32[]{:S(2)}) async-start(bf16[32,4,512]{2,0,1:T(8,128)(2,1)} %bitcast.28), calls=%async_computation | async-start | bytes 262144 | tf_op jit(solution)/shard_map/all_to_all | solution.py:184
  41.1 6.3 %collective-permute-start.4 = (f32[8,16,256]{2,1,0:T(8,128)}, f32[8,16,256]{2,1,0:T(8,128)S(1)}, u32[]{:S(2)}, u32[]{:S(2)}) collective-permute-start(f32[8,16,256]{2,1,0:T(8,128)} %get-tuple-element.19), channel_id=1, source_target_pairs={{0,1},{1,0},{2,3},{3,2},{4,5},{5,4},{6,7},{7,6},{8,9},{9,8},{10,11... | collective-permute-start | bytes 393224 | tf_op jit(solution)/shard_map/ppermute | solution.py:217
  42.7 3.9 %copy-start.8 = (f32[64,64]{1,0:T(8,128)S(1)}, f32[64,64]{1,0:T(8,128)}, u32[]{:S(2)}) copy-start(f32[64,64]{1,0:T(8,128)} %param.14) | copy-start | bytes 49156
  46.3 7.1 %collective-permute-start.6 = (f32[8,16,256]{2,1,0:T(8,128)}, f32[8,16,256]{2,1,0:T(8,128)S(1)}, u32[]{:S(2)}, u32[]{:S(2)}) collective-permute-start(f32[8,16,256]{2,1,0:T(8,128)} %get-tuple-element.22), channel_id=1, source_target_pairs={{0,1},{1,0},{2,3},{3,2},{4,5},{5,4},{6,7},{7,6},{8,9},{9,8},{10,11... | collective-permute-start | bytes 393224 | tf_op jit(solution)/shard_map/ppermute | solution.py:217
  47.3 0.7 copy-start.5
  51.5 7.6 %collective-permute-start.5 = (f32[8,16,256]{2,1,0:T(8,128)}, f32[8,16,256]{2,1,0:T(8,128)S(1)}, u32[]{:S(2)}, u32[]{:S(2)}) collective-permute-start(f32[8,16,256]{2,1,0:T(8,128)} %get-tuple-element.20), channel_id=1, source_target_pairs={{0,1},{1,0},{2,3},{3,2},{4,5},{5,4},{6,7},{7,6},{8,9},{9,8},{10,11... | collective-permute-start | bytes 393224 | tf_op jit(solution)/shard_map/ppermute | solution.py:217
  53.4 0.7 copy-start.6
  57.6 5.6 %collective-permute-start.7 = (f32[8,16,256]{2,1,0:T(8,128)}, f32[8,16,256]{2,1,0:T(8,128)S(1)}, u32[]{:S(2)}, u32[]{:S(2)}) collective-permute-start(f32[8,16,256]{2,1,0:T(8,128)} %get-tuple-element.23), channel_id=1, source_target_pairs={{0,1},{1,0},{2,3},{3,2},{4,5},{5,4},{6,7},{7,6},{8,9},{9,8},{10,11... | collective-permute-start | bytes 393224 | tf_op jit(solution)/shard_map/ppermute | solution.py:217
  59.2 0.6 copy-start.7
  63.2 0.6 copy-start.9

commit v9 on v7

--- a/solution.py
+++ b/solution.py
@@ -63,23 +63,18 @@
     cd = dn(ca_raw) * mq
     cb = cb_raw * mq
     cl = lf(cb_raw) * mq
+    csum = (ca + cd) + (cb + cl)
     w = lam
     for _ in range(PICARD - 1):
-        total = ca * (up(w) - w)
-        total = total + cd * (dn(w) - w)
-        total = total + cb * (rt(w) - w)
-        total = total + cl * (lf(w) - w)
-        w = lam + total
+        near = (ca * up(w) + cd * dn(w)) + (cb * rt(w) + cl * lf(w))
+        w = lam + (near - csum * w)
 
     def main(x):
         return x[:, :rows, :cols]
 
-    wm = main(w)
-    total = main(ca) * (main(up(w)) - wm)
-    total = total + main(cd) * (main(dn(w)) - wm)
-    total = total + main(cb) * (main(rt(w)) - wm)
-    total = total + main(cl) * (main(lf(w)) - wm)
-    w3 = main(lam) + total
+    near = (main(ca) * main(up(w)) + main(cd) * main(dn(w))) + (
+        main(cb) * main(rt(w)) + main(cl) * main(lf(w)))
+    w3 = main(lam) + (near - main(csum) * main(w))
     v0 = vel_ref[0].astype(jnp.float32)
     v1 = vel_ref[1].astype(jnp.float32)
     adv = v0 * main(up(lam) - dn(lam)) + v1 * main(rt(lam) - lf(lam))

time: 65.3 us -> 65.7 us (level)
  no operation moved by 1% of the time
where the time goes in v9:
time: 65.7 us; the launch traced here: 65.2 us
  Pallas kernels  21.6 us (33%)
  starting transfers between devices  18.7 us (28%)
  local copies, waits for them, and re-layouts  12.5 us (19%)
  other arithmetic  6.44 us (10%)
  waiting for transfers between devices  3.31 us (5%)
  matrix products  2.37 us (4%)
    pallas_call x4, Pallas kernels, _sweeps(): pl.pallas_call(_sweep_kernel, out_shape=out_shape, grid=grid, in_specs=[p...  14.7 us
    pallas_call x2, Pallas kernels, _radial(): pl.pallas_call(functools.partial(_radial_kernel, len(pieces), partial is...  6.89 us
    ppermute x1, starting transfers between devices, per_device(): top = lax.ppermute(top_send, 'cap', _pairs(n_cap, 1))  5.57 us
    ppermute x4, starting transfers between devices, per_device(): lax.ppermute(send, 'rad', _pairs(n_rad, 1) + _pairs(n_rad, -1))  4.05 us
    all_to_all x1, starting transfers between devices, per_device(): lax.all_to_all(markers, 'lat', split_axis=1, concat_axis=1, tiled=True)  3.5 us
    unnamed x23, local copies, waits for them, and re-layouts  3.23 us
    ppermute x1, starting transfers between devices, per_device(): from_left = lax.ppermute(flat[piece:], 'lat', _pairs(n_lat, 1))  3.03 us
    concatenate x2, local copies, waits for them, and re-layouts, per_device(): jnp.concatenate([from_right, from_left]).reshape(2, 2, layers, ext_rows, g)  2.37 us
  transfers between devices with their start and end apart: 9, of which 3 were waited for; matrix products, arithmetic and copies ran while one was open for 15% of the time, Pallas kernels for 22%

profile of v9, /device:TPU:0, one launch (start us, length us, event | category | flops | bytes accessed | tf_op | source)
XLA Modules:
  0.0 65.2 jit_solution(1957504106927499585)
XLA Ops:
  0.0 1.9 %convert_select_fusion.eta_ref = f32[32,32,256]{2,1,0:T(8,128)S(1)} fusion(bf16[32,32,256]{2,1,0:T(8,128)(2,1)} %param.11, bf16[32,32,256]{2,1,0:T(8,128)(2,1)} %param.12, s32[32,32,256]{2,1,0:T(8,128)} %param.13), kind=kLoop, calls=%fused_computation.7 | loop fusion | flops 1835008 | bytes 3145728 | tf_op jit(solution)/shard_map/jit(_where)/select_n | solution.py:152
  1.9 0.0 copy-start
  1.9 0.1 fusion.17
  2.0 0.1 pad_maximum_fusion.2
  2.1 1.3 %collective-permute-start = (f32[32,6,256]{2,1,0:T(8,128)S(1)}, f32[32,6,256]{2,1,0:T(8,128)S(1)}, u32[]{:S(2)}, u32[]{:S(2)}) collective-permute-start(f32[32,6,256]{2,1,0:T(8,128)S(1)} %pad_maximum_fusion.2), channel_id=1, source_target_pairs={{8,0},{16,8},{24,16},{9,1},{17,9},{25,17},{10,2},{18,10},{26,18},{... | collective-permute-start | bytes 589832 | tf_op jit(solution)/shard_map/ppermute | solution.py:160
  3.4 0.1 pad_maximum_fusion.3
  3.5 5.6 %collective-permute-start.1 = (f32[32,6,256]{2,1,0:T(8,128)S(1)}, f32[32,6,256]{2,1,0:T(8,128)S(1)}, u32[]{:S(2)}, u32[]{:S(2)}) collective-permute-start(f32[32,6,256]{2,1,0:T(8,128)S(1)} %pad_maximum_fusion.3), channel_id=1, source_target_pairs={{0,8},{8,16},{16,24},{1,9},{9,17},{17,25},{2,10},{10,18},{18,26},{... | collective-permute-start | bytes 589832 | tf_op jit(solution)/shard_map/ppermute | solution.py:159
  9.1 0.2 fusion.16
  9.3 0.2 fusion.15
  9.5 0.0 copy-start.8
  9.5 0.0 copy-start.9
  9.5 0.3 copy.21
  9.8 0.3 copy.30
  10.1 0.3 copy.25
  10.4 0.3 copy.31
  10.7 0.1 pad.25.clone
  10.7 0.1 pad.3.clone
  10.8 0.1 fusion.11
  11.0 0.1 fusion.9
  11.0 0.7 %and_convert_fusion.mask_ref = f32[40,384]{1,0:T(8,128)} fusion(pred[384]{0:T(512)(128)(4,1)S(1)} %compare_and_fusion, pred[40]{0:T(512)(128)(4,1)S(1)} %compare_and_fusion.1), kind=kLoop, calls=%fused_computation.24 | loop fusion | flops 30720 | bytes 61864 | tf_op jit(solution)/shard_map/convert_element_type | solution.py:28
  11.7 1.6 %collective-permute-done = f32[32,6,256]{2,1,0:T(8,128)S(1)} collective-permute-done((f32[32,6,256]{2,1,0:T(8,128)S(1)}, f32[32,6,256]{2,1,0:T(8,128)S(1)}, u32[]{:S(2)}, u32[]{:S(2)}) %collective-permute-start) | collective-permute-done | bytes 196640 | tf_op jit(solution)/shard_map/ppermute | solution.py:160
  13.3 0.1 fusion.21
  13.4 1.2 %collective-permute-done.1 = f32[32,6,256]{2,1,0:T(8,128)S(1)} collective-permute-done((f32[32,6,256]{2,1,0:T(8,128)S(1)}, f32[32,6,256]{2,1,0:T(8,128)S(1)}, u32[]{:S(2)}, u32[]{:S(2)}) %collective-permute-start.1) | collective-permute-done | bytes 196640 | tf_op jit(solution)/shard_map/ppermute | solution.py:159
  14.6 0.1 fusion.22
  14.6 0.1 pad_maximum_fusion.4
  14.8 0.1 fusion.20
  14.9 0.3 copy.22
  15.2 0.1 fusion.19
  15.3 0.3 copy.20
  15.5 0.3 copy.26
  15.8 0.3 copy.24
  16.1 0.1 maximum_bitcast_fusion.3
  16.2 0.1 maximum_bitcast_fusion.2
  16.3 0.1 maximum_bitcast_fusion.5
  16.4 0.1 maximum_bitcast_fusion.4
  16.5 0.9 %copy.27 = f32[2,2,32,40,3]{4,3,2,1,0:T(8,128)S(1)} copy(f32[2,2,32,40,3]{3,2,4,1,0:T(8,128)S(1)} %pad_maximum_fusion.6) | data formatting | bytes 122880 | tf_op jit(solution)/shard_map/stack | solution.py:173
  17.5 1.9 %reshape.108 = f32[15360]{0:T(1024)S(1)} reshape(f32[2,2,32,40,3]{4,3,2,1,0:T(8,128)S(1)} %copy.27) | data formatting | bytes 122880 | tf_op jit(solution)/shard_map/reshape | solution.py:173
  19.4 1.3 %collective-permute-start.2 = (f32[7680]{0:T(1024)S(1)}, f32[7680]{0:T(1024)S(1)}, u32[]{:S(2)}, u32[]{:S(2)}) collective-permute-start(f32[7680]{0:T(1024)S(1)} %get-tuple-element.41), channel_id=1, source_target_pairs={{2,0},{4,2},{6,4},{3,1},{5,3},{7,5},{10,8},{12,10},{14,12},{11,9},... | collective-permute-start | bytes 92168 | tf_op jit(solution)/shard_map/ppermute | solution.py:177
  20.7 3.0 %collective-permute-start.3 = (f32[7680]{0:T(1024)S(1)}, f32[7680]{0:T(1024)S(1)}, u32[]{:S(2)}, u32[]{:S(2)}) collective-permute-start(f32[7680]{0:T(1024)S(1)} %get-tuple-element.42), channel_id=1, source_target_pairs={{0,2},{2,4},{4,6},{1,3},{3,5},{5,7},{8,10},{10,12},{12,14},{9,11},... | collective-permute-start | bytes 92168 | tf_op jit(solution)/shard_map/ppermute | solution.py:178
  23.7 0.7 %copy.36 = bf16[4,4,8,512]{3,2,0,1:T(8,128)(2,1)} copy(bf16[4,4,8,512]{3,2,1,0:T(8,128)(2,1)S(1)} %bitcast.32) | data formatting | bytes 262144 | tf_op jit(solution)/shard_map/all_to_all | solution.py:176
  24.4 3.5 %all-to-all-start = ((bf16[32,4,512]{2,0,1:T(8,128)(2,1)}), bf16[32,4,512]{2,0,1:T(8,128)(2,1)S(1)}, u32[]{:S(2)}, u32[]{:S(2)}) async-start(bf16[32,4,512]{2,0,1:T(8,128)(2,1)} %bitcast.28), calls=%async_computation | async-start | bytes 262144 | tf_op jit(solution)/shard_map/all_to_all | solution.py:176
  27.9 0.8 %pad_maximum_fusion.1.rowh_ref = f32[2,32,8,256]{3,2,1,0:T(8,128)} fusion(f32[1,32,8,256]{3,2,1,0:T(8,128)S(1)} %bitcast.30, f32[1,32,8,256]{3,2,1,0:T(8,128)S(1)} %bitcast.29), kind=kLoop, calls=%fused_computation.13 | loop fusion | flops 131072 | bytes 1048576 | tf_op jit(solution)/shard_map/stack | solution.py:162
  28.7 1.2 %concatenate.45 = f32[2,32,40,3]{3,2,1,0:T(8,128)S(1)} reshape(f32[7680]{0:T(1024)S(1)} %collective-permute-done.2) | data formatting | bytes 61440 | tf_op jit(solution)/shard_map/concatenate | solution.py:179
  29.9 1.2 %concatenate.46 = f32[2,32,40,3]{3,2,1,0:T(8,128)S(1)} reshape(f32[7680]{0:T(1024)S(1)} %collective-permute-done.3) | data formatting | bytes 61440 | tf_op jit(solution)/shard_map/concatenate | solution.py:179
  31.1 1.5 %pad_maximum_fusion.colh_ref = f32[2,32,40,128]{3,2,1,0:T(8,128)} fusion(f32[2,32,40,3]{3,2,1,0:T(8,128)S(1)} %concatenate.46, f32[2,32,40,3]{3,2,1,0:T(8,128)S(1)} %concatenate.45, f32[128]{0:T(128)S(1)} %pad.3.clone), kind=kLoop, calls=%fused_computation.10 | loop fusion | flops 655360 | bytes 1372672 | tf_op jit(solution)/shard_map/concatenate | solution.py:181
  32.6 2.4 %fusion.dep_ref = f32[32,32,256]{2,1,0:T(8,128)} fusion(pred[32,2048]{1,0:T(8,128)(4,1)S(1)} %fusion.9, bf16[32,2048]{1,0:T(8,128)(2,1)S(1)} %bitcast.33, s32[2048]{0:T(1024)S(1)} %get-tuple-element.45), kind=kOutput, calls=%fused_computation | convolution fusion | flops 1076363264 | bytes 1253376 | tf_op jit(solution)/shard_map/las,sb->lab/dot_general | solution.py:193
  35.0 3.7 %shard_map.91 = (f32[8,16,256]{2,1,0:T(8,128)}, f32[8,16,256]{2,1,0:T(8,128)}) custom-call(s32[1]{0:T(128)} %bitcast.rad_ref.after_ref.recv_ref, f32[32,32,256]{2,1,0:T(8,128)} %lam_ref.7, f32[32,32,256]{2,1,0:T(8,128)} %copy-done, f32[2,32,8,256]{3,2,1,0:T(8,128)} %pad_maximum_fusion.1.rowh_ref, f32[2,32,40,128]{3,2,1,0:T(8,128)} %pad_maximum_fusion.colh_ref, ...), custom_call_target="tpu_custom_call" | custom-call | flops 737280000 | bytes 12800000 | tf_op jit(solution)/shard_map/pallas_call | solution.py:99
  38.7 1.7 %collective-permute-start.4 = (f32[8,16,256]{2,1,0:T(8,128)}, f32[8,16,256]{2,1,0:T(8,128)S(1)}, u32[]{:S(2)}, u32[]{:S(2)}) collective-permute-start(f32[8,16,256]{2,1,0:T(8,128)} %get-tuple-element.19), channel_id=1, source_target_pairs={{0,1},{1,0},{2,3},{3,2},{4,5},{5,4},{6,7},{7,6},{8,9},{9,8},{10,11... | collective-permute-start | bytes 393224 | tf_op jit(solution)/shard_map/ppermute | solution.py:209
  40.3 3.7 %shard_map.92 = (f32[8,16,256]{2,1,0:T(8,128)}, f32[8,16,256]{2,1,0:T(8,128)}) custom-call(s32[1]{0:T(128)} %bitcast.rad_ref.after_ref.recv_ref, f32[32,32,256]{2,1,0:T(8,128)} %lam_ref.7, f32[32,32,256]{2,1,0:T(8,128)} %copy-done, f32[2,32,8,256]{3,2,1,0:T(8,128)} %pad_maximum_fusion.1.rowh_ref, f32[2,32,40,128]{3,2,1,0:T(8,128)} %pad_maximum_fusion.colh_ref, ...), custom_call_target="tpu_custom_call" | custom-call | flops 737280000 | bytes 12800000 | tf_op jit(solution)/shard_map/pallas_call | solution.py:99
  44.0 0.4 collective-permute-start.6
  44.4 0.1 constant_dynamic-slice_fusion.1
  44.5 0.5 collective-permute-done.4.recv_ref.refs_4_
  45.0 0.7 %copy-done.2 = f32[8,16,256]{2,1,0:T(8,128)} copy-done((f32[8,16,256]{2,1,0:T(8,128)}, f32[8,16,256]{2,1,0:T(8,128)S(1)}, u32[]{:S(2)}) %copy-start.2) | copy-done | bytes 131096
  45.6 3.7 %shard_map.93 = (f32[8,16,256]{2,1,0:T(8,128)}, f32[8,16,256]{2,1,0:T(8,128)}) custom-call(s32[1]{0:T(128)} %bitcast.rad_ref.after_ref.recv_ref, f32[32,32,256]{2,1,0:T(8,128)} %lam_ref.7, f32[32,32,256]{2,1,0:T(8,128)} %copy-done, f32[2,32,8,256]{3,2,1,0:T(8,128)} %pad_maximum_fusion.1.rowh_ref, f32[2,32,40,128]{3,2,1,0:T(8,128)} %pad_maximum_fusion.colh_ref, ...), custom_call_target="tpu_custom_call" | custom-call | flops 737280000 | bytes 12800000 | tf_op jit(solution)/shard_map/pallas_call | solution.py:99
  49.3 1.8 %collective-permute-start.5 = (f32[8,16,256]{2,1,0:T(8,128)}, f32[8,16,256]{2,1,0:T(8,128)S(1)}, u32[]{:S(2)}, u32[]{:S(2)}) collective-permute-start(f32[8,16,256]{2,1,0:T(8,128)} %get-tuple-element.20), channel_id=1, source_target_pairs={{0,1},{1,0},{2,3},{3,2},{4,5},{5,4},{6,7},{7,6},{8,9},{9,8},{10,11... | collective-permute-start | bytes 393224 | tf_op jit(solution)/shard_map/ppermute | solution.py:209
  51.1 0.7 %copy-done.3 = f32[8,16,256]{2,1,0:T(8,128)} copy-done((f32[8,16,256]{2,1,0:T(8,128)}, f32[8,16,256]{2,1,0:T(8,128)S(1)}, u32[]{:S(2)}) %copy-start.3) | copy-done | bytes 131096
  51.8 3.7 %shard_map.94 = (f32[8,16,256]{2,1,0:T(8,128)}, f32[8,16,256]{2,1,0:T(8,128)}) custom-call(s32[1]{0:T(128)} %bitcast.rad_ref.after_ref.recv_ref, f32[32,32,256]{2,1,0:T(8,128)} %lam_ref.7, f32[32,32,256]{2,1,0:T(8,128)} %copy-done, f32[2,32,8,256]{3,2,1,0:T(8,128)} %pad_maximum_fusion.1.rowh_ref, f32[2,32,40,128]{3,2,1,0:T(8,128)} %pad_maximum_fusion.colh_ref, ...), custom_call_target="tpu_custom_call" | custom-call | flops 737280000 | bytes 12800000 | tf_op jit(solution)/shard_map/pallas_call | solution.py:99
  55.5 0.2 collective-permute-start.7
  55.7 0.7 %constant_dynamic-slice_fusion.r_ref = f32[64,16]{1,0:T(8,128)} fusion(f32[64,64]{1,0:T(8,128)S(1)} %copy-done.5, s32[]{:T(128)S(6)} %add.54), kind=kLoop, calls=%fused_computation.49 | loop fusion | bytes 8196 | tf_op jit(solution)/shard_map/slice | solution.py:219
  56.3 0.7 %pad_maximum_fusion.7.r_ref = f32[64,48]{1,0:T(8,128)} fusion(f32[64,32]{1,0:T(8,128)S(1)} %get-tuple-element.44, f32[64,32]{1,0:T(8,128)S(1)} %get-tuple-element.43), kind=kLoop, calls=%fused_computation.29 | loop fusion | flops 3072 | bytes 28672 | tf_op jit(solution)/shard_map/concatenate | solution.py:214
  57.0 0.7 copy-done.4
  57.7 3.4 %shard_map.95.refs_2_ = f32[64,16,256]{2,1,0:T(8,128)} custom-call(f32[64,48]{1,0:T(8,128)} %pad_maximum_fusion.7.r_ref, f32[8,16,256]{2,1,0:T(8,128)} %get-tuple-element.17.after_ref.refs_0_, f32[8,16,256]{2,1,0:T(8,128)} %get-tuple-element.18.after_ref.refs_1_, f32[8,16,256]{2,1,0:T(8,128)} %get-tuple-element.21.after_ref.refs_2_, ...), custom_call_target="tpu_custom_call" | custom-call | tf_op jit(solution)/shard_map/pallas_call | solution.py:246
  61.1 0.7 copy-done.6
  61.8 3.5 %shard_map.96 = f32[64,16,256]{2,1,0:T(8,128)} custom-call(f32[64,16]{1,0:T(8,128)} %constant_dynamic-slice_fusion.r_ref, f32[8,16,256]{2,1,0:T(8,128)} %copy-done.4, f32[8,16,256]{2,1,0:T(8,128)} %copy-done.6, f32[64,16,256]{2,1,0:T(8,128)} %shard_map.95.refs_2_), custom_call_target="tpu_custom_call" | custom-call | tf_op jit(solution)/shard_map/pallas_call | solution.py:246
  (30 shorter events, 0.2 us)
Async XLA Ops:
  0.0 1.9 %copy-start.1 = (f32[32,32,256]{2,1,0:T(8,128)S(1)}, f32[32,32,256]{2,1,0:T(8,128)}, u32[]{:S(2)}) copy-start(f32[32,32,256]{2,1,0:T(8,128)} %lam_ref.7) | copy-start | bytes 3145732
  1.9 7.3 %copy-start = (f32[32,32,256]{2,1,0:T(8,128)}, f32[32,32,256]{2,1,0:T(8,128)S(1)}, u32[]{:S(2)}) copy-start(f32[32,32,256]{2,1,0:T(8,128)S(1)} %convert_select_fusion.eta_ref) | copy-start | bytes 3145732
  2.1 11.2 %collective-permute-start = (f32[32,6,256]{2,1,0:T(8,128)S(1)}, f32[32,6,256]{2,1,0:T(8,128)S(1)}, u32[]{:S(2)}, u32[]{:S(2)}) collective-permute-start(f32[32,6,256]{2,1,0:T(8,128)S(1)} %pad_maximum_fusion.2), channel_id=1, source_target_pairs={{8,0},{16,8},{24,16},{9,1},{17,9},{25,17},{10,2},{18,10},{26,18},{... | collective-permute-start | bytes 589832 | tf_op jit(solution)/shard_map/ppermute | solution.py:160
  3.5 11.1 %collective-permute-start.1 = (f32[32,6,256]{2,1,0:T(8,128)S(1)}, f32[32,6,256]{2,1,0:T(8,128)S(1)}, u32[]{:S(2)}, u32[]{:S(2)}) collective-permute-start(f32[32,6,256]{2,1,0:T(8,128)S(1)} %pad_maximum_fusion.3), channel_id=1, source_target_pairs={{0,8},{8,16},{16,24},{1,9},{9,17},{17,25},{2,10},{10,18},{18,26},{... | collective-permute-start | bytes 589832 | tf_op jit(solution)/shard_map/ppermute | solution.py:159
  9.5 1.3 %copy-start.8 = (s32[2048]{0:T(1024)S(1)}, s32[2048]{0:T(1024)}, u32[]{:S(2)}) copy-start(s32[2048]{0:T(1024)} %param.16) | copy-start | bytes 24580
  9.5 1.3 %copy-start.9 = (s32[4]{0:T(128)S(1)}, s32[4]{0:T(128)}, u32[]{:S(2)}) copy-start(s32[4]{0:T(128)} %param.17) | copy-start | bytes 52
  17.5 6.2 %copy-start.7 = (bf16[32,2048]{1,0:T(8,128)(2,1)S(1)}, bf16[32,2048]{1,0:T(8,128)(2,1)}, u32[]{:S(2)}) copy-start(bf16[32,2048]{1,0:T(8,128)(2,1)} %param.15) | copy-start | bytes 393220
  19.4 9.4 %collective-permute-start.2 = (f32[7680]{0:T(1024)S(1)}, f32[7680]{0:T(1024)S(1)}, u32[]{:S(2)}, u32[]{:S(2)}) collective-permute-start(f32[7680]{0:T(1024)S(1)} %get-tuple-element.41), channel_id=1, source_target_pairs={{2,0},{4,2},{6,4},{3,1},{5,3},{7,5},{10,8},{12,10},{14,12},{11,9},... | collective-permute-start | bytes 92168 | tf_op jit(solution)/shard_map/ppermute | solution.py:177
  20.7 9.3 %collective-permute-start.3 = (f32[7680]{0:T(1024)S(1)}, f32[7680]{0:T(1024)S(1)}, u32[]{:S(2)}, u32[]{:S(2)}) collective-permute-start(f32[7680]{0:T(1024)S(1)} %get-tuple-element.42), channel_id=1, source_target_pairs={{0,2},{2,4},{4,6},{1,3},{3,5},{5,7},{8,10},{10,12},{12,14},{9,11},... | collective-permute-start | bytes 92168 | tf_op jit(solution)/shard_map/ppermute | solution.py:178
  24.4 8.2 %all-to-all-start = ((bf16[32,4,512]{2,0,1:T(8,128)(2,1)}), bf16[32,4,512]{2,0,1:T(8,128)(2,1)S(1)}, u32[]{:S(2)}, u32[]{:S(2)}) async-start(bf16[32,4,512]{2,0,1:T(8,128)(2,1)} %bitcast.28), calls=%async_computation | async-start | bytes 262144 | tf_op jit(solution)/shard_map/all_to_all | solution.py:176
  38.7 6.3 %collective-permute-start.4 = (f32[8,16,256]{2,1,0:T(8,128)}, f32[8,16,256]{2,1,0:T(8,128)S(1)}, u32[]{:S(2)}, u32[]{:S(2)}) collective-permute-start(f32[8,16,256]{2,1,0:T(8,128)} %get-tuple-element.19), channel_id=1, source_target_pairs={{0,1},{1,0},{2,3},{3,2},{4,5},{5,4},{6,7},{7,6},{8,9},{9,8},{10,11... | collective-permute-start | bytes 393224 | tf_op jit(solution)/shard_map/ppermute | solution.py:209
  40.3 4.0 %copy-start.5 = (f32[64,64]{1,0:T(8,128)S(1)}, f32[64,64]{1,0:T(8,128)}, u32[]{:S(2)}) copy-start(f32[64,64]{1,0:T(8,128)} %param.14) | copy-start | bytes 49156
  44.0 7.1 %collective-permute-start.6 = (f32[8,16,256]{2,1,0:T(8,128)}, f32[8,16,256]{2,1,0:T(8,128)S(1)}, u32[]{:S(2)}, u32[]{:S(2)}) collective-permute-start(f32[8,16,256]{2,1,0:T(8,128)} %get-tuple-element.22), channel_id=1, source_target_pairs={{0,1},{1,0},{2,3},{3,2},{4,5},{5,4},{6,7},{7,6},{8,9},{9,8},{10,11... | collective-permute-start | bytes 393224 | tf_op jit(solution)/shard_map/ppermute | solution.py:209
  45.0 0.7 %copy-start.2 = (f32[8,16,256]{2,1,0:T(8,128)}, f32[8,16,256]{2,1,0:T(8,128)S(1)}, u32[]{:S(2)}) copy-start(f32[8,16,256]{2,1,0:T(8,128)S(1)} %collective-permute-done.4.recv_ref.refs_4_) | copy-start | bytes 393220
  49.3 7.8 %collective-permute-start.5 = (f32[8,16,256]{2,1,0:T(8,128)}, f32[8,16,256]{2,1,0:T(8,128)S(1)}, u32[]{:S(2)}, u32[]{:S(2)}) collective-permute-start(f32[8,16,256]{2,1,0:T(8,128)} %get-tuple-element.20), channel_id=1, source_target_pairs={{0,1},{1,0},{2,3},{3,2},{4,5},{5,4},{6,7},{7,6},{8,9},{9,8},{10,11... | collective-permute-start | bytes 393224 | tf_op jit(solution)/shard_map/ppermute | solution.py:209
  51.1 0.7 %copy-start.3 = (f32[8,16,256]{2,1,0:T(8,128)}, f32[8,16,256]{2,1,0:T(8,128)S(1)}, u32[]{:S(2)}) copy-start(f32[8,16,256]{2,1,0:T(8,128)S(1)} %collective-permute-done.6.recv_ref.refs_5_) | copy-start | bytes 393220
  55.5 5.6 %collective-permute-start.7 = (f32[8,16,256]{2,1,0:T(8,128)}, f32[8,16,256]{2,1,0:T(8,128)S(1)}, u32[]{:S(2)}, u32[]{:S(2)}) collective-permute-start(f32[8,16,256]{2,1,0:T(8,128)} %get-tuple-element.23), channel_id=1, source_target_pairs={{0,1},{1,0},{2,3},{3,2},{4,5},{5,4},{6,7},{7,6},{8,9},{9,8},{10,11... | collective-permute-start | bytes 393224 | tf_op jit(solution)/shard_map/ppermute | solution.py:209
  57.0 0.7 %copy-start.4 = (f32[8,16,256]{2,1,0:T(8,128)}, f32[8,16,256]{2,1,0:T(8,128)S(1)}, u32[]{:S(2)}) copy-start(f32[8,16,256]{2,1,0:T(8,128)S(1)} %collective-permute-done.5.refs_6_.refs_0_) | copy-start | bytes 393220
  61.1 0.7 %copy-start.6 = (f32[8,16,256]{2,1,0:T(8,128)}, f32[8,16,256]{2,1,0:T(8,128)S(1)}, u32[]{:S(2)}) copy-start(f32[8,16,256]{2,1,0:T(8,128)S(1)} %collective-permute-done.7.refs_1_) | copy-start | bytes 393220

commit v10 on v7

--- a/solution.py
+++ b/solution.py
@@ -200,7 +200,7 @@
     rad_idx = r.astype(jnp.int32).reshape(1)
     n_chunks = 4
     chunk = layers // n_chunks
-    block_layers = 4
+    block_layers = 2
     keeps = []
     recvs = []
     after = rad_idx

time: 65.3 us -> 68.4 us (1.047)
  Pallas kernels: 21.1 us -> 24.3 us
    pallas_call x4, Pallas kernels: 14.2 us -> 17.4 us  [_sweeps(): pl.pallas_call(_sweep_kernel, out_shape=out_shape, grid=grid, in_specs=[p...]
  transfers between devices with their start and end apart: 9 -> 9, of which waited for: 3 -> 3; matrix products, arithmetic and copies ran while one was open for 15% -> 14% of each run, Pallas kernels for 22% -> 24%
where the time goes in v10:
time: 68.4 us; the launch traced here: 67.5 us
  Pallas kernels  24.3 us (36%)
  starting transfers between devices  18.7 us (27%)
  local copies, waits for them, and re-layouts  12.5 us (18%)
  other arithmetic  6.44 us (9%)
  waiting for transfers between devices  2.88 us (4%)
  matrix products  2.37 us (3%)
    pallas_call x4, Pallas kernels, _sweeps(): pl.pallas_call(_sweep_kernel, out_shape=out_shape, grid=grid, in_specs=[p...  17.4 us
    pallas_call x2, Pallas kernels, _radial(): pl.pallas_call(functools.partial(_radial_kernel, len(pieces), partial is...  6.9 us
    ppermute x1, starting transfers between devices, per_device(): top = lax.ppermute(top_send, 'cap', _pairs(n_cap, 1))  5.57 us
    ppermute x4, starting transfers between devices, per_device(): lax.ppermute(send, 'rad', _pairs(n_rad, 1) + _pairs(n_rad, -1))  4.05 us
    all_to_all x1, starting transfers between devices, per_device(): lax.all_to_all(markers, 'lat', split_axis=1, concat_axis=1, tiled=True)  3.5 us
    unnamed x23, local copies, waits for them, and re-layouts  3.23 us
    ppermute x1, starting transfers between devices, per_device(): from_left = lax.ppermute(flat[piece:], 'lat', _pairs(n_lat, 1))  3.03 us
    concatenate x2, local copies, waits for them, and re-layouts, per_device(): jnp.concatenate([from_right, from_left]).reshape(2, 2, layers, ext_rows, g)  2.37 us
  transfers between devices with their start and end apart: 9, of which 3 were waited for; matrix products, arithmetic and copies ran while one was open for 14% of the time, Pallas kernels for 24%

profile of v10, /device:TPU:0, one launch (start us, length us, event | category | flops | bytes accessed | tf_op | source)
XLA Modules:
  0.0 67.5 jit_solution(8229453656634143797)
XLA Ops:
  0.0 1.9 %convert_select_fusion.eta_ref = f32[32,32,256]{2,1,0:T(8,128)S(1)} fusion(bf16[32,32,256]{2,1,0:T(8,128)(2,1)} %param.11, bf16[32,32,256]{2,1,0:T(8,128)(2,1)} %param.12, s32[32,32,256]{2,1,0:T(8,128)} %param.13), kind=kLoop, calls=%fused_computation.7 | loop fusion | flops 1835008 | bytes 3145728 | tf_op jit(solution)/shard_map/jit(_where)/select_n | solution.py:157
  1.9 0.0 copy-start
  1.9 0.1 fusion.17
  2.0 0.1 pad_maximum_fusion.2
  2.1 1.3 %collective-permute-start = (f32[32,6,256]{2,1,0:T(8,128)S(1)}, f32[32,6,256]{2,1,0:T(8,128)S(1)}, u32[]{:S(2)}, u32[]{:S(2)}) collective-permute-start(f32[32,6,256]{2,1,0:T(8,128)S(1)} %pad_maximum_fusion.2), channel_id=1, source_target_pairs={{8,0},{16,8},{24,16},{9,1},{17,9},{25,17},{10,2},{18,10},{26,18},{... | collective-permute-start | bytes 589832 | tf_op jit(solution)/shard_map/ppermute | solution.py:165
  3.4 0.1 pad_maximum_fusion.3
  3.5 5.6 %collective-permute-start.1 = (f32[32,6,256]{2,1,0:T(8,128)S(1)}, f32[32,6,256]{2,1,0:T(8,128)S(1)}, u32[]{:S(2)}, u32[]{:S(2)}) collective-permute-start(f32[32,6,256]{2,1,0:T(8,128)S(1)} %pad_maximum_fusion.3), channel_id=1, source_target_pairs={{0,8},{8,16},{16,24},{1,9},{9,17},{17,25},{2,10},{10,18},{18,26},{... | collective-permute-start | bytes 589832 | tf_op jit(solution)/shard_map/ppermute | solution.py:164
  9.1 0.2 fusion.16
  9.3 0.2 fusion.15
  9.5 0.0 copy-start.8
  9.5 0.3 copy.21
  9.8 0.3 copy.30
  10.1 0.3 copy.25
  10.4 0.3 copy.31
  10.7 0.1 pad.25.clone
  10.7 0.1 pad.3.clone
  10.8 0.1 fusion.11
  11.0 0.1 fusion.9
  11.0 0.7 %and_convert_fusion.mask_ref = f32[40,384]{1,0:T(8,128)} fusion(pred[384]{0:T(512)(128)(4,1)S(1)} %compare_and_fusion, pred[40]{0:T(512)(128)(4,1)S(1)} %compare_and_fusion.1), kind=kLoop, calls=%fused_computation.24 | loop fusion | flops 30720 | bytes 61864 | tf_op jit(solution)/shard_map/convert_element_type | solution.py:28
  11.7 1.6 %collective-permute-done = f32[32,6,256]{2,1,0:T(8,128)S(1)} collective-permute-done((f32[32,6,256]{2,1,0:T(8,128)S(1)}, f32[32,6,256]{2,1,0:T(8,128)S(1)}, u32[]{:S(2)}, u32[]{:S(2)}) %collective-permute-start) | collective-permute-done | bytes 196640 | tf_op jit(solution)/shard_map/ppermute | solution.py:165
  13.3 0.1 fusion.21
  13.4 1.2 %collective-permute-done.1 = f32[32,6,256]{2,1,0:T(8,128)S(1)} collective-permute-done((f32[32,6,256]{2,1,0:T(8,128)S(1)}, f32[32,6,256]{2,1,0:T(8,128)S(1)}, u32[]{:S(2)}, u32[]{:S(2)}) %collective-permute-start.1) | collective-permute-done | bytes 196640 | tf_op jit(solution)/shard_map/ppermute | solution.py:164
  14.6 0.1 fusion.22
  14.6 0.1 pad_maximum_fusion.4
  14.8 0.1 fusion.20
  14.9 0.3 copy.22
  15.2 0.1 fusion.19
  15.3 0.3 copy.20
  15.5 0.3 copy.26
  15.8 0.3 copy.24
  16.1 0.1 maximum_bitcast_fusion.3
  16.2 0.1 maximum_bitcast_fusion.2
  16.3 0.1 maximum_bitcast_fusion.5
  16.4 0.1 maximum_bitcast_fusion.4
  16.5 0.9 %copy.27 = f32[2,2,32,40,3]{4,3,2,1,0:T(8,128)S(1)} copy(f32[2,2,32,40,3]{3,2,4,1,0:T(8,128)S(1)} %pad_maximum_fusion.6) | data formatting | bytes 122880 | tf_op jit(solution)/shard_map/stack | solution.py:178
  17.5 0.0 copy-start.7
  17.5 1.9 %reshape.108 = f32[15360]{0:T(1024)S(1)} reshape(f32[2,2,32,40,3]{4,3,2,1,0:T(8,128)S(1)} %copy.27) | data formatting | bytes 122880 | tf_op jit(solution)/shard_map/reshape | solution.py:178
  19.4 1.3 %collective-permute-start.2 = (f32[7680]{0:T(1024)S(1)}, f32[7680]{0:T(1024)S(1)}, u32[]{:S(2)}, u32[]{:S(2)}) collective-permute-start(f32[7680]{0:T(1024)S(1)} %get-tuple-element.41), channel_id=1, source_target_pairs={{2,0},{4,2},{6,4},{3,1},{5,3},{7,5},{10,8},{12,10},{14,12},{11,9},... | collective-permute-start | bytes 92168 | tf_op jit(solution)/shard_map/ppermute | solution.py:182
  20.7 3.0 %collective-permute-start.3 = (f32[7680]{0:T(1024)S(1)}, f32[7680]{0:T(1024)S(1)}, u32[]{:S(2)}, u32[]{:S(2)}) collective-permute-start(f32[7680]{0:T(1024)S(1)} %get-tuple-element.42), channel_id=1, source_target_pairs={{0,2},{2,4},{4,6},{1,3},{3,5},{5,7},{8,10},{10,12},{12,14},{9,11},... | collective-permute-start | bytes 92168 | tf_op jit(solution)/shard_map/ppermute | solution.py:183
  23.7 0.7 copy.36
  24.4 3.5 %all-to-all-start = ((bf16[32,4,512]{2,0,1:T(8,128)(2,1)}), bf16[32,4,512]{2,0,1:T(8,128)(2,1)S(1)}, u32[]{:S(2)}, u32[]{:S(2)}) async-start(bf16[32,4,512]{2,0,1:T(8,128)(2,1)} %bitcast.28), calls=%async_computation | async-start | bytes 262144 | tf_op jit(solution)/shard_map/all_to_all | solution.py:181
  27.9 0.8 %pad_maximum_fusion.1.rowh_ref = f32[2,32,8,256]{3,2,1,0:T(8,128)} fusion(f32[1,32,8,256]{3,2,1,0:T(8,128)S(1)} %bitcast.30, f32[1,32,8,256]{3,2,1,0:T(8,128)S(1)} %bitcast.29), kind=kLoop, calls=%fused_computation.13 | loop fusion | flops 131072 | bytes 1048576 | tf_op jit(solution)/shard_map/stack | solution.py:167
  28.7 1.2 %concatenate.45 = f32[2,32,40,3]{3,2,1,0:T(8,128)S(1)} reshape(f32[7680]{0:T(1024)S(1)} %collective-permute-done.2) | data formatting | bytes 61440 | tf_op jit(solution)/shard_map/concatenate | solution.py:184
  29.9 1.2 %concatenate.46 = f32[2,32,40,3]{3,2,1,0:T(8,128)S(1)} reshape(f32[7680]{0:T(1024)S(1)} %collective-permute-done.3) | data formatting | bytes 61440 | tf_op jit(solution)/shard_map/concatenate | solution.py:184
  31.1 1.5 %pad_maximum_fusion.colh_ref = f32[2,32,40,128]{3,2,1,0:T(8,128)} fusion(f32[2,32,40,3]{3,2,1,0:T(8,128)S(1)} %concatenate.46, f32[2,32,40,3]{3,2,1,0:T(8,128)S(1)} %concatenate.45, f32[128]{0:T(128)S(1)} %pad.3.clone), kind=kLoop, calls=%fused_computation.10 | loop fusion | flops 655360 | bytes 1372672 | tf_op jit(solution)/shard_map/concatenate | solution.py:186
  32.6 2.4 %fusion.dep_ref = f32[32,32,256]{2,1,0:T(8,128)} fusion(pred[32,2048]{1,0:T(8,128)(4,1)S(1)} %fusion.9, bf16[32,2048]{1,0:T(8,128)(2,1)S(1)} %bitcast.33, s32[2048]{0:T(1024)S(1)} %get-tuple-element.45), kind=kOutput, calls=%fused_computation | convolution fusion | flops 1076363264 | bytes 1253376 | tf_op jit(solution)/shard_map/las,sb->lab/dot_general | solution.py:198
  35.0 4.3 %shard_map.91 = (f32[8,16,256]{2,1,0:T(8,128)}, f32[8,16,256]{2,1,0:T(8,128)}) custom-call(s32[1]{0:T(128)} %bitcast.rad_ref.after_ref.recv_ref, f32[32,32,256]{2,1,0:T(8,128)} %lam_ref.7, f32[32,32,256]{2,1,0:T(8,128)} %copy-done, f32[2,32,8,256]{3,2,1,0:T(8,128)} %pad_maximum_fusion.1.rowh_ref, f32[2,32,40,128]{3,2,1,0:T(8,128)} %pad_maximum_fusion.colh_ref, ...), custom_call_target="tpu_custom_call" | custom-call | flops 737280000 | bytes 12800000 | tf_op jit(solution)/shard_map/pallas_call | solution.py:104
  39.3 1.7 %collective-permute-start.4 = (f32[8,16,256]{2,1,0:T(8,128)}, f32[8,16,256]{2,1,0:T(8,128)S(1)}, u32[]{:S(2)}, u32[]{:S(2)}) collective-permute-start(f32[8,16,256]{2,1,0:T(8,128)} %get-tuple-element.19), channel_id=1, source_target_pairs={{0,1},{1,0},{2,3},{3,2},{4,5},{5,4},{6,7},{7,6},{8,9},{9,8},{10,11... | collective-permute-start | bytes 393224 | tf_op jit(solution)/shard_map/ppermute | solution.py:214
  41.0 4.4 %shard_map.92 = (f32[8,16,256]{2,1,0:T(8,128)}, f32[8,16,256]{2,1,0:T(8,128)}) custom-call(s32[1]{0:T(128)} %bitcast.rad_ref.after_ref.recv_ref, f32[32,32,256]{2,1,0:T(8,128)} %lam_ref.7, f32[32,32,256]{2,1,0:T(8,128)} %copy-done, f32[2,32,8,256]{3,2,1,0:T(8,128)} %pad_maximum_fusion.1.rowh_ref, f32[2,32,40,128]{3,2,1,0:T(8,128)} %pad_maximum_fusion.colh_ref, ...), custom_call_target="tpu_custom_call" | custom-call | flops 737280000 | bytes 12800000 | tf_op jit(solution)/shard_map/pallas_call | solution.py:104
  45.4 0.4 collective-permute-start.6
  45.7 0.1 constant_dynamic-slice_fusion.1
  45.8 0.7 copy-done.2
  46.5 4.3 %shard_map.93 = (f32[8,16,256]{2,1,0:T(8,128)}, f32[8,16,256]{2,1,0:T(8,128)}) custom-call(s32[1]{0:T(128)} %bitcast.rad_ref.after_ref.recv_ref, f32[32,32,256]{2,1,0:T(8,128)} %lam_ref.7, f32[32,32,256]{2,1,0:T(8,128)} %copy-done, f32[2,32,8,256]{3,2,1,0:T(8,128)} %pad_maximum_fusion.1.rowh_ref, f32[2,32,40,128]{3,2,1,0:T(8,128)} %pad_maximum_fusion.colh_ref, ...), custom_call_target="tpu_custom_call" | custom-call | flops 737280000 | bytes 12800000 | tf_op jit(solution)/shard_map/pallas_call | solution.py:104
  50.8 1.7 %collective-permute-start.5 = (f32[8,16,256]{2,1,0:T(8,128)}, f32[8,16,256]{2,1,0:T(8,128)S(1)}, u32[]{:S(2)}, u32[]{:S(2)}) collective-permute-start(f32[8,16,256]{2,1,0:T(8,128)} %get-tuple-element.20), channel_id=1, source_target_pairs={{0,1},{1,0},{2,3},{3,2},{4,5},{5,4},{6,7},{7,6},{8,9},{9,8},{10,11... | collective-permute-start | bytes 393224 | tf_op jit(solution)/shard_map/ppermute | solution.py:214
  52.5 0.7 copy-done.3
  53.2 4.4 %shard_map.94 = (f32[8,16,256]{2,1,0:T(8,128)}, f32[8,16,256]{2,1,0:T(8,128)}) custom-call(s32[1]{0:T(128)} %bitcast.rad_ref.after_ref.recv_ref, f32[32,32,256]{2,1,0:T(8,128)} %lam_ref.7, f32[32,32,256]{2,1,0:T(8,128)} %copy-done, f32[2,32,8,256]{3,2,1,0:T(8,128)} %pad_maximum_fusion.1.rowh_ref, f32[2,32,40,128]{3,2,1,0:T(8,128)} %pad_maximum_fusion.colh_ref, ...), custom_call_target="tpu_custom_call" | custom-call | flops 737280000 | bytes 12800000 | tf_op jit(solution)/shard_map/pallas_call | solution.py:104
  57.5 0.4 collective-permute-start.7
  57.9 0.7 %constant_dynamic-slice_fusion.r_ref = f32[64,16]{1,0:T(8,128)} fusion(f32[64,64]{1,0:T(8,128)S(1)} %copy-done.5, s32[]{:T(128)S(6)} %add.54), kind=kLoop, calls=%fused_computation.49 | loop fusion | bytes 8196 | tf_op jit(solution)/shard_map/slice | solution.py:224
  58.6 0.7 %pad_maximum_fusion.7.r_ref = f32[64,48]{1,0:T(8,128)} fusion(f32[64,32]{1,0:T(8,128)S(1)} %get-tuple-element.44, f32[64,32]{1,0:T(8,128)S(1)} %get-tuple-element.43), kind=kLoop, calls=%fused_computation.29 | loop fusion | flops 3072 | bytes 28672 | tf_op jit(solution)/shard_map/concatenate | solution.py:219
  59.3 0.7 copy-done.4
  59.9 3.4 %shard_map.95.refs_2_ = f32[64,16,256]{2,1,0:T(8,128)} custom-call(f32[64,48]{1,0:T(8,128)} %pad_maximum_fusion.7.r_ref, f32[8,16,256]{2,1,0:T(8,128)} %get-tuple-element.17.after_ref.refs_0_, f32[8,16,256]{2,1,0:T(8,128)} %get-tuple-element.18.after_ref.refs_1_, f32[8,16,256]{2,1,0:T(8,128)} %get-tuple-element.21.after_ref.refs_2_, ...), custom_call_target="tpu_custom_call" | custom-call | tf_op jit(solution)/shard_map/pallas_call | solution.py:251
  63.3 0.1 collective-permute-done.7.refs_1_
  63.4 0.7 copy-done.6
  64.1 3.5 %shard_map.96 = f32[64,16,256]{2,1,0:T(8,128)} custom-call(f32[64,16]{1,0:T(8,128)} %constant_dynamic-slice_fusion.r_ref, f32[8,16,256]{2,1,0:T(8,128)} %copy-done.4, f32[8,16,256]{2,1,0:T(8,128)} %copy-done.6, f32[64,16,256]{2,1,0:T(8,128)} %shard_map.95.refs_2_), custom_call_target="tpu_custom_call" | custom-call | tf_op jit(solution)/shard_map/pallas_call | solution.py:251
  (30 shorter events, 0.2 us)
Async XLA Ops:
  0.0 1.9 %copy-start.1 = (f32[32,32,256]{2,1,0:T(8,128)S(1)}, f32[32,32,256]{2,1,0:T(8,128)}, u32[]{:S(2)}) copy-start(f32[32,32,256]{2,1,0:T(8,128)} %lam_ref.7) | copy-start | bytes 3145732
  1.9 7.3 %copy-start = (f32[32,32,256]{2,1,0:T(8,128)}, f32[32,32,256]{2,1,0:T(8,128)S(1)}, u32[]{:S(2)}) copy-start(f32[32,32,256]{2,1,0:T(8,128)S(1)} %convert_select_fusion.eta_ref) | copy-start | bytes 3145732
  2.1 11.2 %collective-permute-start = (f32[32,6,256]{2,1,0:T(8,128)S(1)}, f32[32,6,256]{2,1,0:T(8,128)S(1)}, u32[]{:S(2)}, u32[]{:S(2)}) collective-permute-start(f32[32,6,256]{2,1,0:T(8,128)S(1)} %pad_maximum_fusion.2), channel_id=1, source_target_pairs={{8,0},{16,8},{24,16},{9,1},{17,9},{25,17},{10,2},{18,10},{26,18},{... | collective-permute-start | bytes 589832 | tf_op jit(solution)/shard_map/ppermute | solution.py:165
  3.5 11.1 %collective-permute-start.1 = (f32[32,6,256]{2,1,0:T(8,128)S(1)}, f32[32,6,256]{2,1,0:T(8,128)S(1)}, u32[]{:S(2)}, u32[]{:S(2)}) collective-permute-start(f32[32,6,256]{2,1,0:T(8,128)S(1)} %pad_maximum_fusion.3), channel_id=1, source_target_pairs={{0,8},{8,16},{16,24},{1,9},{9,17},{17,25},{2,10},{10,18},{18,26},{... | collective-permute-start | bytes 589832 | tf_op jit(solution)/shard_map/ppermute | solution.py:164
  9.5 1.3 %copy-start.8 = (s32[2048]{0:T(1024)S(1)}, s32[2048]{0:T(1024)}, u32[]{:S(2)}) copy-start(s32[2048]{0:T(1024)} %param.16) | copy-start | bytes 24580
  9.5 1.3 %copy-start.9 = (s32[4]{0:T(128)S(1)}, s32[4]{0:T(128)}, u32[]{:S(2)}) copy-start(s32[4]{0:T(128)} %param.17) | copy-start | bytes 52
  17.5 6.2 %copy-start.7 = (bf16[32,2048]{1,0:T(8,128)(2,1)S(1)}, bf16[32,2048]{1,0:T(8,128)(2,1)}, u32[]{:S(2)}) copy-start(bf16[32,2048]{1,0:T(8,128)(2,1)} %param.15) | copy-start | bytes 393220
  19.4 9.4 %collective-permute-start.2 = (f32[7680]{0:T(1024)S(1)}, f32[7680]{0:T(1024)S(1)}, u32[]{:S(2)}, u32[]{:S(2)}) collective-permute-start(f32[7680]{0:T(1024)S(1)} %get-tuple-element.41), channel_id=1, source_target_pairs={{2,0},{4,2},{6,4},{3,1},{5,3},{7,5},{10,8},{12,10},{14,12},{11,9},... | collective-permute-start | bytes 92168 | tf_op jit(solution)/shard_map/ppermute | solution.py:182
  20.7 9.3 %collective-permute-start.3 = (f32[7680]{0:T(1024)S(1)}, f32[7680]{0:T(1024)S(1)}, u32[]{:S(2)}, u32[]{:S(2)}) collective-permute-start(f32[7680]{0:T(1024)S(1)} %get-tuple-element.42), channel_id=1, source_target_pairs={{0,2},{2,4},{4,6},{1,3},{3,5},{5,7},{8,10},{10,12},{12,14},{9,11},... | collective-permute-start | bytes 92168 | tf_op jit(solution)/shard_map/ppermute | solution.py:183
  24.4 8.2 %all-to-all-start = ((bf16[32,4,512]{2,0,1:T(8,128)(2,1)}), bf16[32,4,512]{2,0,1:T(8,128)(2,1)S(1)}, u32[]{:S(2)}, u32[]{:S(2)}) async-start(bf16[32,4,512]{2,0,1:T(8,128)(2,1)} %bitcast.28), calls=%async_computation | async-start | bytes 262144 | tf_op jit(solution)/shard_map/all_to_all | solution.py:181
  39.3 6.5 %collective-permute-start.4 = (f32[8,16,256]{2,1,0:T(8,128)}, f32[8,16,256]{2,1,0:T(8,128)S(1)}, u32[]{:S(2)}, u32[]{:S(2)}) collective-permute-start(f32[8,16,256]{2,1,0:T(8,128)} %get-tuple-element.19), channel_id=1, source_target_pairs={{0,1},{1,0},{2,3},{3,2},{4,5},{5,4},{6,7},{7,6},{8,9},{9,8},{10,11... | collective-permute-start | bytes 393224 | tf_op jit(solution)/shard_map/ppermute | solution.py:214
  41.0 4.7 %copy-start.5 = (f32[64,64]{1,0:T(8,128)S(1)}, f32[64,64]{1,0:T(8,128)}, u32[]{:S(2)}) copy-start(f32[64,64]{1,0:T(8,128)} %param.14) | copy-start | bytes 49156
  45.4 7.1 %collective-permute-start.6 = (f32[8,16,256]{2,1,0:T(8,128)}, f32[8,16,256]{2,1,0:T(8,128)S(1)}, u32[]{:S(2)}, u32[]{:S(2)}) collective-permute-start(f32[8,16,256]{2,1,0:T(8,128)} %get-tuple-element.22), channel_id=1, source_target_pairs={{0,1},{1,0},{2,3},{3,2},{4,5},{5,4},{6,7},{7,6},{8,9},{9,8},{10,11... | collective-permute-start | bytes 393224 | tf_op jit(solution)/shard_map/ppermute | solution.py:214
  45.8 0.7 copy-start.2
  50.8 8.4 %collective-permute-start.5 = (f32[8,16,256]{2,1,0:T(8,128)}, f32[8,16,256]{2,1,0:T(8,128)S(1)}, u32[]{:S(2)}, u32[]{:S(2)}) collective-permute-start(f32[8,16,256]{2,1,0:T(8,128)} %get-tuple-element.20), channel_id=1, source_target_pairs={{0,1},{1,0},{2,3},{3,2},{4,5},{5,4},{6,7},{7,6},{8,9},{9,8},{10,11... | collective-permute-start | bytes 393224 | tf_op jit(solution)/shard_map/ppermute | solution.py:214
  52.5 0.7 copy-start.3
  57.5 5.9 %collective-permute-start.7 = (f32[8,16,256]{2,1,0:T(8,128)}, f32[8,16,256]{2,1,0:T(8,128)S(1)}, u32[]{:S(2)}, u32[]{:S(2)}) collective-permute-start(f32[8,16,256]{2,1,0:T(8,128)} %get-tuple-element.23), channel_id=1, source_target_pairs={{0,1},{1,0},{2,3},{3,2},{4,5},{5,4},{6,7},{7,6},{8,9},{9,8},{10,11... | collective-permute-start | bytes 393224 | tf_op jit(solution)/shard_map/ppermute | solution.py:214
  59.3 0.7 copy-start.4
  63.4 0.7 copy-start.6

commit v11 on v10

--- a/solution.py
+++ b/solution.py
@@ -200,7 +200,7 @@
     rad_idx = r.astype(jnp.int32).reshape(1)
     n_chunks = 4
     chunk = layers // n_chunks
-    block_layers = 2
+    block_layers = 8
     keeps = []
     recvs = []
     after = rad_idx

time: 68.4 us -> 65.1 us (0.952)
  Pallas kernels: 24.3 us -> 20.8 us
    pallas_call x4, Pallas kernels: 17.4 us -> 13.9 us  [_sweeps(): pl.pallas_call(_sweep_kernel, out_shape=out_shape, grid=grid, in_specs=[p...]
  transfers between devices with their start and end apart: 9 -> 9, of which waited for: 3 -> 3; matrix products, arithmetic and copies ran while one was open for 14% -> 15% of each run, Pallas kernels for 24% -> 21%
where the time goes in v11:
time: 65.1 us; the launch traced here: 64.7 us
  Pallas kernels  20.8 us (32%)
  starting transfers between devices  18.7 us (29%)
  local copies, waits for them, and re-layouts  12.5 us (19%)
  other arithmetic  6.44 us (10%)
  waiting for transfers between devices  3.49 us (5%)
  matrix products  2.37 us (4%)
    pallas_call x4, Pallas kernels, _sweeps(): pl.pallas_call(_sweep_kernel, out_shape=out_shape, grid=grid, in_specs=[p...  13.9 us
    pallas_call x2, Pallas kernels, _radial(): pl.pallas_call(functools.partial(_radial_kernel, len(pieces), partial is...  6.9 us
    ppermute x1, starting transfers between devices, per_device(): top = lax.ppermute(top_send, 'cap', _pairs(n_cap, 1))  5.57 us
    ppermute x4, starting transfers between devices, per_device(): lax.ppermute(send, 'rad', _pairs(n_rad, 1) + _pairs(n_rad, -1))  4.05 us
    all_to_all x1, starting transfers between devices, per_device(): lax.all_to_all(markers, 'lat', split_axis=1, concat_axis=1, tiled=True)  3.5 us
    unnamed x23, local copies, waits for them, and re-layouts  3.23 us
    ppermute x1, starting transfers between devices, per_device(): from_left = lax.ppermute(flat[piece:], 'lat', _pairs(n_lat, 1))  3.03 us
    concatenate x2, local copies, waits for them, and re-layouts, per_device(): jnp.concatenate([from_right, from_left]).reshape(2, 2, layers, ext_rows, g)  2.37 us
  transfers between devices with their start and end apart: 9, of which 3 were waited for; matrix products, arithmetic and copies ran while one was open for 15% of the time, Pallas kernels for 21%

profile of v11, /device:TPU:0, one launch (start us, length us, event | category | flops | bytes accessed | tf_op | source)
XLA Modules:
  0.0 64.7 jit_solution(15969856212156841076)
XLA Ops:
  0.0 1.9 %convert_select_fusion.eta_ref = f32[32,32,256]{2,1,0:T(8,128)S(1)} fusion(bf16[32,32,256]{2,1,0:T(8,128)(2,1)} %param.11, bf16[32,32,256]{2,1,0:T(8,128)(2,1)} %param.12, s32[32,32,256]{2,1,0:T(8,128)} %param.13), kind=kLoop, calls=%fused_computation.7 | loop fusion | flops 1835008 | bytes 3145728 | tf_op jit(solution)/shard_map/jit(_where)/select_n | solution.py:157
  1.9 0.0 copy-start
  1.9 0.1 fusion.17
  2.0 0.1 pad_maximum_fusion.2
  2.1 1.3 %collective-permute-start = (f32[32,6,256]{2,1,0:T(8,128)S(1)}, f32[32,6,256]{2,1,0:T(8,128)S(1)}, u32[]{:S(2)}, u32[]{:S(2)}) collective-permute-start(f32[32,6,256]{2,1,0:T(8,128)S(1)} %pad_maximum_fusion.2), channel_id=1, source_target_pairs={{8,0},{16,8},{24,16},{9,1},{17,9},{25,17},{10,2},{18,10},{26,18},{... | collective-permute-start | bytes 589832 | tf_op jit(solution)/shard_map/ppermute | solution.py:165
  3.4 0.1 pad_maximum_fusion.3
  3.5 5.6 %collective-permute-start.1 = (f32[32,6,256]{2,1,0:T(8,128)S(1)}, f32[32,6,256]{2,1,0:T(8,128)S(1)}, u32[]{:S(2)}, u32[]{:S(2)}) collective-permute-start(f32[32,6,256]{2,1,0:T(8,128)S(1)} %pad_maximum_fusion.3), channel_id=1, source_target_pairs={{0,8},{8,16},{16,24},{1,9},{9,17},{17,25},{2,10},{10,18},{18,26},{... | collective-permute-start | bytes 589832 | tf_op jit(solution)/shard_map/ppermute | solution.py:164
  9.1 0.2 fusion.16
  9.3 0.2 fusion.15
  9.5 0.0 copy-start.8
  9.5 0.3 copy.21
  9.8 0.3 copy.30
  10.1 0.3 copy.25
  10.4 0.3 copy.31
  10.7 0.1 pad.25.clone
  10.7 0.1 pad.3.clone
  10.8 0.1 fusion.11
  11.0 0.1 fusion.9
  11.0 0.7 %and_convert_fusion.mask_ref = f32[40,384]{1,0:T(8,128)} fusion(pred[384]{0:T(512)(128)(4,1)S(1)} %compare_and_fusion, pred[40]{0:T(512)(128)(4,1)S(1)} %compare_and_fusion.1), kind=kLoop, calls=%fused_computation.24 | loop fusion | flops 30720 | bytes 61864 | tf_op jit(solution)/shard_map/convert_element_type | solution.py:28
  11.7 1.6 %collective-permute-done = f32[32,6,256]{2,1,0:T(8,128)S(1)} collective-permute-done((f32[32,6,256]{2,1,0:T(8,128)S(1)}, f32[32,6,256]{2,1,0:T(8,128)S(1)}, u32[]{:S(2)}, u32[]{:S(2)}) %collective-permute-start) | collective-permute-done | bytes 196640 | tf_op jit(solution)/shard_map/ppermute | solution.py:165
  13.3 0.1 fusion.21
  13.4 1.2 %collective-permute-done.1 = f32[32,6,256]{2,1,0:T(8,128)S(1)} collective-permute-done((f32[32,6,256]{2,1,0:T(8,128)S(1)}, f32[32,6,256]{2,1,0:T(8,128)S(1)}, u32[]{:S(2)}, u32[]{:S(2)}) %collective-permute-start.1) | collective-permute-done | bytes 196640 | tf_op jit(solution)/shard_map/ppermute | solution.py:164
  14.6 0.1 fusion.22
  14.6 0.1 pad_maximum_fusion.4
  14.8 0.1 fusion.20
  14.9 0.3 copy.22
  15.2 0.1 fusion.19
  15.3 0.3 copy.20
  15.5 0.3 copy.26
  15.8 0.3 copy.24
  16.1 0.1 maximum_bitcast_fusion.3
  16.2 0.1 maximum_bitcast_fusion.2
  16.3 0.1 maximum_bitcast_fusion.5
  16.4 0.1 maximum_bitcast_fusion.4
  16.5 0.9 %copy.27 = f32[2,2,32,40,3]{4,3,2,1,0:T(8,128)S(1)} copy(f32[2,2,32,40,3]{3,2,4,1,0:T(8,128)S(1)} %pad_maximum_fusion.6) | data formatting | bytes 122880 | tf_op jit(solution)/shard_map/stack | solution.py:178
  17.5 0.0 copy-start.7
  17.5 1.9 %reshape.108 = f32[15360]{0:T(1024)S(1)} reshape(f32[2,2,32,40,3]{4,3,2,1,0:T(8,128)S(1)} %copy.27) | data formatting | bytes 122880 | tf_op jit(solution)/shard_map/reshape | solution.py:178
  19.4 1.3 %collective-permute-start.2 = (f32[7680]{0:T(1024)S(1)}, f32[7680]{0:T(1024)S(1)}, u32[]{:S(2)}, u32[]{:S(2)}) collective-permute-start(f32[7680]{0:T(1024)S(1)} %get-tuple-element.41), channel_id=1, source_target_pairs={{2,0},{4,2},{6,4},{3,1},{5,3},{7,5},{10,8},{12,10},{14,12},{11,9},... | collective-permute-start | bytes 92168 | tf_op jit(solution)/shard_map/ppermute | solution.py:182
  20.7 3.0 %collective-permute-start.3 = (f32[7680]{0:T(1024)S(1)}, f32[7680]{0:T(1024)S(1)}, u32[]{:S(2)}, u32[]{:S(2)}) collective-permute-start(f32[7680]{0:T(1024)S(1)} %get-tuple-element.42), channel_id=1, source_target_pairs={{0,2},{2,4},{4,6},{1,3},{3,5},{5,7},{8,10},{10,12},{12,14},{9,11},... | collective-permute-start | bytes 92168 | tf_op jit(solution)/shard_map/ppermute | solution.py:183
  23.7 0.7 %copy.36 = bf16[4,4,8,512]{3,2,0,1:T(8,128)(2,1)} copy(bf16[4,4,8,512]{3,2,1,0:T(8,128)(2,1)S(1)} %bitcast.32) | data formatting | bytes 262144 | tf_op jit(solution)/shard_map/all_to_all | solution.py:181
  24.4 3.5 %all-to-all-start = ((bf16[32,4,512]{2,0,1:T(8,128)(2,1)}), bf16[32,4,512]{2,0,1:T(8,128)(2,1)S(1)}, u32[]{:S(2)}, u32[]{:S(2)}) async-start(bf16[32,4,512]{2,0,1:T(8,128)(2,1)} %bitcast.28), calls=%async_computation | async-start | bytes 262144 | tf_op jit(solution)/shard_map/all_to_all | solution.py:181
  27.9 0.8 %pad_maximum_fusion.1.rowh_ref = f32[2,32,8,256]{3,2,1,0:T(8,128)} fusion(f32[1,32,8,256]{3,2,1,0:T(8,128)S(1)} %bitcast.30, f32[1,32,8,256]{3,2,1,0:T(8,128)S(1)} %bitcast.29), kind=kLoop, calls=%fused_computation.13 | loop fusion | flops 131072 | bytes 1048576 | tf_op jit(solution)/shard_map/stack | solution.py:167
  28.7 1.2 %concatenate.45 = f32[2,32,40,3]{3,2,1,0:T(8,128)S(1)} reshape(f32[7680]{0:T(1024)S(1)} %collective-permute-done.2) | data formatting | bytes 61440 | tf_op jit(solution)/shard_map/concatenate | solution.py:184
  29.9 1.2 %concatenate.46 = f32[2,32,40,3]{3,2,1,0:T(8,128)S(1)} reshape(f32[7680]{0:T(1024)S(1)} %collective-permute-done.3) | data formatting | bytes 61440 | tf_op jit(solution)/shard_map/concatenate | solution.py:184
  31.1 1.5 %pad_maximum_fusion.colh_ref = f32[2,32,40,128]{3,2,1,0:T(8,128)} fusion(f32[2,32,40,3]{3,2,1,0:T(8,128)S(1)} %concatenate.46, f32[2,32,40,3]{3,2,1,0:T(8,128)S(1)} %concatenate.45, f32[128]{0:T(128)S(1)} %pad.3.clone), kind=kLoop, calls=%fused_computation.10 | loop fusion | flops 655360 | bytes 1372672 | tf_op jit(solution)/shard_map/concatenate | solution.py:186
  32.6 2.4 %fusion.dep_ref = f32[32,32,256]{2,1,0:T(8,128)} fusion(pred[32,2048]{1,0:T(8,128)(4,1)S(1)} %fusion.9, bf16[32,2048]{1,0:T(8,128)(2,1)S(1)} %bitcast.33, s32[2048]{0:T(1024)S(1)} %get-tuple-element.45), kind=kOutput, calls=%fused_computation | convolution fusion | flops 1076363264 | bytes 1253376 | tf_op jit(solution)/shard_map/las,sb->lab/dot_general | solution.py:198
  35.0 3.5 %shard_map.91 = (f32[8,16,256]{2,1,0:T(8,128)}, f32[8,16,256]{2,1,0:T(8,128)}) custom-call(s32[1]{0:T(128)} %bitcast.rad_ref.after_ref.recv_ref, f32[32,32,256]{2,1,0:T(8,128)} %lam_ref.7, f32[32,32,256]{2,1,0:T(8,128)} %copy-done, f32[2,32,8,256]{3,2,1,0:T(8,128)} %pad_maximum_fusion.1.rowh_ref, f32[2,32,40,128]{3,2,1,0:T(8,128)} %pad_maximum_fusion.colh_ref, ...), custom_call_target="tpu_custom_call" | custom-call | flops 737280000 | bytes 12800000 | tf_op jit(solution)/shard_map/pallas_call | solution.py:104
  38.5 1.7 %collective-permute-start.4 = (f32[8,16,256]{2,1,0:T(8,128)}, f32[8,16,256]{2,1,0:T(8,128)S(1)}, u32[]{:S(2)}, u32[]{:S(2)}) collective-permute-start(f32[8,16,256]{2,1,0:T(8,128)} %get-tuple-element.19), channel_id=1, source_target_pairs={{0,1},{1,0},{2,3},{3,2},{4,5},{5,4},{6,7},{7,6},{8,9},{9,8},{10,11... | collective-permute-start | bytes 393224 | tf_op jit(solution)/shard_map/ppermute | solution.py:214
  40.2 3.5 %shard_map.92 = (f32[8,16,256]{2,1,0:T(8,128)}, f32[8,16,256]{2,1,0:T(8,128)}) custom-call(s32[1]{0:T(128)} %bitcast.rad_ref.after_ref.recv_ref, f32[32,32,256]{2,1,0:T(8,128)} %lam_ref.7, f32[32,32,256]{2,1,0:T(8,128)} %copy-done, f32[2,32,8,256]{3,2,1,0:T(8,128)} %pad_maximum_fusion.1.rowh_ref, f32[2,32,40,128]{3,2,1,0:T(8,128)} %pad_maximum_fusion.colh_ref, ...), custom_call_target="tpu_custom_call" | custom-call | flops 737280000 | bytes 12800000 | tf_op jit(solution)/shard_map/pallas_call | solution.py:104
  43.7 0.4 collective-permute-start.6
  44.0 0.1 constant_dynamic-slice_fusion.1
  44.1 0.7 %collective-permute-done.4.recv_ref.refs_4_ = f32[8,16,256]{2,1,0:T(8,128)S(1)} collective-permute-done((f32[8,16,256]{2,1,0:T(8,128)}, f32[8,16,256]{2,1,0:T(8,128)S(1)}, u32[]{:S(2)}, u32[]{:S(2)}) %collective-permute-start.4) | collective-permute-done | bytes 131104 | tf_op jit(solution)/shard_map/ppermute | solution.py:214
  44.8 0.7 %copy-done.2 = f32[8,16,256]{2,1,0:T(8,128)} copy-done((f32[8,16,256]{2,1,0:T(8,128)}, f32[8,16,256]{2,1,0:T(8,128)S(1)}, u32[]{:S(2)}) %copy-start.2) | copy-done | bytes 131096
  45.4 3.5 %shard_map.93 = (f32[8,16,256]{2,1,0:T(8,128)}, f32[8,16,256]{2,1,0:T(8,128)}) custom-call(s32[1]{0:T(128)} %bitcast.rad_ref.after_ref.recv_ref, f32[32,32,256]{2,1,0:T(8,128)} %lam_ref.7, f32[32,32,256]{2,1,0:T(8,128)} %copy-done, f32[2,32,8,256]{3,2,1,0:T(8,128)} %pad_maximum_fusion.1.rowh_ref, f32[2,32,40,128]{3,2,1,0:T(8,128)} %pad_maximum_fusion.colh_ref, ...), custom_call_target="tpu_custom_call" | custom-call | flops 737280000 | bytes 12800000 | tf_op jit(solution)/shard_map/pallas_call | solution.py:104
  48.9 1.8 %collective-permute-start.5 = (f32[8,16,256]{2,1,0:T(8,128)}, f32[8,16,256]{2,1,0:T(8,128)S(1)}, u32[]{:S(2)}, u32[]{:S(2)}) collective-permute-start(f32[8,16,256]{2,1,0:T(8,128)} %get-tuple-element.20), channel_id=1, source_target_pairs={{0,1},{1,0},{2,3},{3,2},{4,5},{5,4},{6,7},{7,6},{8,9},{9,8},{10,11... | collective-permute-start | bytes 393224 | tf_op jit(solution)/shard_map/ppermute | solution.py:214
  50.8 0.7 %copy-done.3 = f32[8,16,256]{2,1,0:T(8,128)} copy-done((f32[8,16,256]{2,1,0:T(8,128)}, f32[8,16,256]{2,1,0:T(8,128)S(1)}, u32[]{:S(2)}) %copy-start.3) | copy-done | bytes 131096
  51.4 3.5 %shard_map.94 = (f32[8,16,256]{2,1,0:T(8,128)}, f32[8,16,256]{2,1,0:T(8,128)}) custom-call(s32[1]{0:T(128)} %bitcast.rad_ref.after_ref.recv_ref, f32[32,32,256]{2,1,0:T(8,128)} %lam_ref.7, f32[32,32,256]{2,1,0:T(8,128)} %copy-done, f32[2,32,8,256]{3,2,1,0:T(8,128)} %pad_maximum_fusion.1.rowh_ref, f32[2,32,40,128]{3,2,1,0:T(8,128)} %pad_maximum_fusion.colh_ref, ...), custom_call_target="tpu_custom_call" | custom-call | flops 737280000 | bytes 12800000 | tf_op jit(solution)/shard_map/pallas_call | solution.py:104
  54.9 0.2 collective-permute-start.7
  55.1 0.7 %constant_dynamic-slice_fusion.r_ref = f32[64,16]{1,0:T(8,128)} fusion(f32[64,64]{1,0:T(8,128)S(1)} %copy-done.5, s32[]{:T(128)S(6)} %add.54), kind=kLoop, calls=%fused_computation.49 | loop fusion | bytes 8196 | tf_op jit(solution)/shard_map/slice | solution.py:224
  55.8 0.7 %pad_maximum_fusion.7.r_ref = f32[64,48]{1,0:T(8,128)} fusion(f32[64,32]{1,0:T(8,128)S(1)} %get-tuple-element.44, f32[64,32]{1,0:T(8,128)S(1)} %get-tuple-element.43), kind=kLoop, calls=%fused_computation.29 | loop fusion | flops 3072 | bytes 28672 | tf_op jit(solution)/shard_map/concatenate | solution.py:219
  56.5 0.7 %copy-done.4 = f32[8,16,256]{2,1,0:T(8,128)} copy-done((f32[8,16,256]{2,1,0:T(8,128)}, f32[8,16,256]{2,1,0:T(8,128)S(1)}, u32[]{:S(2)}) %copy-start.4) | copy-done | bytes 131096
  57.1 3.4 %shard_map.95.refs_2_ = f32[64,16,256]{2,1,0:T(8,128)} custom-call(f32[64,48]{1,0:T(8,128)} %pad_maximum_fusion.7.r_ref, f32[8,16,256]{2,1,0:T(8,128)} %get-tuple-element.17.after_ref.refs_0_, f32[8,16,256]{2,1,0:T(8,128)} %get-tuple-element.18.after_ref.refs_1_, f32[8,16,256]{2,1,0:T(8,128)} %get-tuple-element.21.after_ref.refs_2_, ...), custom_call_target="tpu_custom_call" | custom-call | tf_op jit(solution)/shard_map/pallas_call | solution.py:251
  60.5 0.7 %copy-done.6 = f32[8,16,256]{2,1,0:T(8,128)} copy-done((f32[8,16,256]{2,1,0:T(8,128)}, f32[8,16,256]{2,1,0:T(8,128)S(1)}, u32[]{:S(2)}) %copy-start.6) | copy-done | bytes 131096
  61.2 3.5 %shard_map.96 = f32[64,16,256]{2,1,0:T(8,128)} custom-call(f32[64,16]{1,0:T(8,128)} %constant_dynamic-slice_fusion.r_ref, f32[8,16,256]{2,1,0:T(8,128)} %copy-done.4, f32[8,16,256]{2,1,0:T(8,128)} %copy-done.6, f32[64,16,256]{2,1,0:T(8,128)} %shard_map.95.refs_2_), custom_call_target="tpu_custom_call" | custom-call | tf_op jit(solution)/shard_map/pallas_call | solution.py:251
  (30 shorter events, 0.2 us)
Async XLA Ops:
  0.0 1.9 %copy-start.1 = (f32[32,32,256]{2,1,0:T(8,128)S(1)}, f32[32,32,256]{2,1,0:T(8,128)}, u32[]{:S(2)}) copy-start(f32[32,32,256]{2,1,0:T(8,128)} %lam_ref.7) | copy-start | bytes 3145732
  1.9 7.3 %copy-start = (f32[32,32,256]{2,1,0:T(8,128)}, f32[32,32,256]{2,1,0:T(8,128)S(1)}, u32[]{:S(2)}) copy-start(f32[32,32,256]{2,1,0:T(8,128)S(1)} %convert_select_fusion.eta_ref) | copy-start | bytes 3145732
  2.1 11.2 %collective-permute-start = (f32[32,6,256]{2,1,0:T(8,128)S(1)}, f32[32,6,256]{2,1,0:T(8,128)S(1)}, u32[]{:S(2)}, u32[]{:S(2)}) collective-permute-start(f32[32,6,256]{2,1,0:T(8,128)S(1)} %pad_maximum_fusion.2), channel_id=1, source_target_pairs={{8,0},{16,8},{24,16},{9,1},{17,9},{25,17},{10,2},{18,10},{26,18},{... | collective-permute-start | bytes 589832 | tf_op jit(solution)/shard_map/ppermute | solution.py:165
  3.5 11.1 %collective-permute-start.1 = (f32[32,6,256]{2,1,0:T(8,128)S(1)}, f32[32,6,256]{2,1,0:T(8,128)S(1)}, u32[]{:S(2)}, u32[]{:S(2)}) collective-permute-start(f32[32,6,256]{2,1,0:T(8,128)S(1)} %pad_maximum_fusion.3), channel_id=1, source_target_pairs={{0,8},{8,16},{16,24},{1,9},{9,17},{17,25},{2,10},{10,18},{18,26},{... | collective-permute-start | bytes 589832 | tf_op jit(solution)/shard_map/ppermute | solution.py:164
  9.5 1.3 %copy-start.8 = (s32[2048]{0:T(1024)S(1)}, s32[2048]{0:T(1024)}, u32[]{:S(2)}) copy-start(s32[2048]{0:T(1024)} %param.16) | copy-start | bytes 24580
  9.5 1.3 %copy-start.9 = (s32[4]{0:T(128)S(1)}, s32[4]{0:T(128)}, u32[]{:S(2)}) copy-start(s32[4]{0:T(128)} %param.17) | copy-start | bytes 52
  17.5 6.2 %copy-start.7 = (bf16[32,2048]{1,0:T(8,128)(2,1)S(1)}, bf16[32,2048]{1,0:T(8,128)(2,1)}, u32[]{:S(2)}) copy-start(bf16[32,2048]{1,0:T(8,128)(2,1)} %param.15) | copy-start | bytes 393220
  19.4 9.4 %collective-permute-start.2 = (f32[7680]{0:T(1024)S(1)}, f32[7680]{0:T(1024)S(1)}, u32[]{:S(2)}, u32[]{:S(2)}) collective-permute-start(f32[7680]{0:T(1024)S(1)} %get-tuple-element.41), channel_id=1, source_target_pairs={{2,0},{4,2},{6,4},{3,1},{5,3},{7,5},{10,8},{12,10},{14,12},{11,9},... | collective-permute-start | bytes 92168 | tf_op jit(solution)/shard_map/ppermute | solution.py:182
  20.7 9.3 %collective-permute-start.3 = (f32[7680]{0:T(1024)S(1)}, f32[7680]{0:T(1024)S(1)}, u32[]{:S(2)}, u32[]{:S(2)}) collective-permute-start(f32[7680]{0:T(1024)S(1)} %get-tuple-element.42), channel_id=1, source_target_pairs={{0,2},{2,4},{4,6},{1,3},{3,5},{5,7},{8,10},{10,12},{12,14},{9,11},... | collective-permute-start | bytes 92168 | tf_op jit(solution)/shard_map/ppermute | solution.py:183
  24.4 8.2 %all-to-all-start = ((bf16[32,4,512]{2,0,1:T(8,128)(2,1)}), bf16[32,4,512]{2,0,1:T(8,128)(2,1)S(1)}, u32[]{:S(2)}, u32[]{:S(2)}) async-start(bf16[32,4,512]{2,0,1:T(8,128)(2,1)} %bitcast.28), calls=%async_computation | async-start | bytes 262144 | tf_op jit(solution)/shard_map/all_to_all | solution.py:181
  38.5 6.3 %collective-permute-start.4 = (f32[8,16,256]{2,1,0:T(8,128)}, f32[8,16,256]{2,1,0:T(8,128)S(1)}, u32[]{:S(2)}, u32[]{:S(2)}) collective-permute-start(f32[8,16,256]{2,1,0:T(8,128)} %get-tuple-element.19), channel_id=1, source_target_pairs={{0,1},{1,0},{2,3},{3,2},{4,5},{5,4},{6,7},{7,6},{8,9},{9,8},{10,11... | collective-permute-start | bytes 393224 | tf_op jit(solution)/shard_map/ppermute | solution.py:214
  40.2 3.9 %copy-start.5 = (f32[64,64]{1,0:T(8,128)S(1)}, f32[64,64]{1,0:T(8,128)}, u32[]{:S(2)}) copy-start(f32[64,64]{1,0:T(8,128)} %param.14) | copy-start | bytes 49156
  43.7 7.1 %collective-permute-start.6 = (f32[8,16,256]{2,1,0:T(8,128)}, f32[8,16,256]{2,1,0:T(8,128)S(1)}, u32[]{:S(2)}, u32[]{:S(2)}) collective-permute-start(f32[8,16,256]{2,1,0:T(8,128)} %get-tuple-element.22), channel_id=1, source_target_pairs={{0,1},{1,0},{2,3},{3,2},{4,5},{5,4},{6,7},{7,6},{8,9},{9,8},{10,11... | collective-permute-start | bytes 393224 | tf_op jit(solution)/shard_map/ppermute | solution.py:214
  44.8 0.7 %copy-start.2 = (f32[8,16,256]{2,1,0:T(8,128)}, f32[8,16,256]{2,1,0:T(8,128)S(1)}, u32[]{:S(2)}) copy-start(f32[8,16,256]{2,1,0:T(8,128)S(1)} %collective-permute-done.4.recv_ref.refs_4_) | copy-start | bytes 393220
  48.9 7.5 %collective-permute-start.5 = (f32[8,16,256]{2,1,0:T(8,128)}, f32[8,16,256]{2,1,0:T(8,128)S(1)}, u32[]{:S(2)}, u32[]{:S(2)}) collective-permute-start(f32[8,16,256]{2,1,0:T(8,128)} %get-tuple-element.20), channel_id=1, source_target_pairs={{0,1},{1,0},{2,3},{3,2},{4,5},{5,4},{6,7},{7,6},{8,9},{9,8},{10,11... | collective-permute-start | bytes 393224 | tf_op jit(solution)/shard_map/ppermute | solution.py:214
  50.8 0.7 %copy-start.3 = (f32[8,16,256]{2,1,0:T(8,128)}, f32[8,16,256]{2,1,0:T(8,128)S(1)}, u32[]{:S(2)}) copy-start(f32[8,16,256]{2,1,0:T(8,128)S(1)} %collective-permute-done.6.recv_ref.refs_5_) | copy-start | bytes 393220
  54.9 5.6 %collective-permute-start.7 = (f32[8,16,256]{2,1,0:T(8,128)}, f32[8,16,256]{2,1,0:T(8,128)S(1)}, u32[]{:S(2)}, u32[]{:S(2)}) collective-permute-start(f32[8,16,256]{2,1,0:T(8,128)} %get-tuple-element.23), channel_id=1, source_target_pairs={{0,1},{1,0},{2,3},{3,2},{4,5},{5,4},{6,7},{7,6},{8,9},{9,8},{10,11... | collective-permute-start | bytes 393224 | tf_op jit(solution)/shard_map/ppermute | solution.py:214
  56.5 0.7 %copy-start.4 = (f32[8,16,256]{2,1,0:T(8,128)}, f32[8,16,256]{2,1,0:T(8,128)S(1)}, u32[]{:S(2)}) copy-start(f32[8,16,256]{2,1,0:T(8,128)S(1)} %collective-permute-done.5.refs_6_.refs_0_) | copy-start | bytes 393220
  60.5 0.7 %copy-start.6 = (f32[8,16,256]{2,1,0:T(8,128)}, f32[8,16,256]{2,1,0:T(8,128)S(1)}, u32[]{:S(2)}) copy-start(f32[8,16,256]{2,1,0:T(8,128)S(1)} %collective-permute-done.7.refs_1_) | copy-start | bytes 393220

commit v12 on v11

--- a/solution.py
+++ b/solution.py
@@ -232,13 +232,12 @@
     step = pieces[0].shape[0]
     for i, p in enumerate(pieces):
         xs[i * step:(i + 1) * step] = p[...]
-    rmat = r_ref[...]
-    for a in range(xs.shape[1]):
-        y = jnp.dot(rmat, xs[:, a, :], precision=lax.Precision.HIGHEST,
-                    preferred_element_type=jnp.float32)
-        if has_partial:
-            y = partial_ref[:, a, :] + y
-        out_ref[:, a, :] = y
+    n_l, n_a, n_b = xs.shape
+    y = jnp.dot(r_ref[...], xs[...].reshape(n_l, n_a * n_b), precision=lax.Precision.HIGHEST,
+                preferred_element_type=jnp.float32).reshape(out_ref.shape)
+    if has_partial:
+        y = partial_ref[...] + y
+    out_ref[...] = y
 
 
 def _radial(r_cols, pieces, partial=None, after=None):

time: 65.1 us -> 65 us (level)
  no operation moved by 1% of the time
where the time goes in v12:
time: 65 us; the launch traced here: 64.6 us
  Pallas kernels  20.7 us (32%)
  starting transfers between devices  18.7 us (29%)
  local copies, waits for them, and re-layouts  12.5 us (19%)
  other arithmetic  6.44 us (10%)
  waiting for transfers between devices  3.49 us (5%)
  matrix products  2.37 us (4%)
    pallas_call x4, Pallas kernels, _sweeps(): pl.pallas_call(_sweep_kernel, out_shape=out_shape, grid=grid, in_specs=[p...  13.9 us
    pallas_call x2, Pallas kernels, _radial(): pl.pallas_call(functools.partial(_radial_kernel, len(pieces), partial is...  6.78 us
    ppermute x1, starting transfers between devices, per_device(): top = lax.ppermute(top_send, 'cap', _pairs(n_cap, 1))  5.57 us
    ppermute x4, starting transfers between devices, per_device(): lax.ppermute(send, 'rad', _pairs(n_rad, 1) + _pairs(n_rad, -1))  4.05 us
    all_to_all x1, starting transfers between devices, per_device(): lax.all_to_all(markers, 'lat', split_axis=1, concat_axis=1, tiled=True)  3.5 us
    unnamed x23, local copies, waits for them, and re-layouts  3.23 us
    ppermute x1, starting transfers between devices, per_device(): from_left = lax.ppermute(flat[piece:], 'lat', _pairs(n_lat, 1))  3.03 us
    concatenate x2, local copies, waits for them, and re-layouts, per_device(): jnp.concatenate([from_right, from_left]).reshape(2, 2, layers, ext_rows, g)  2.37 us
  transfers between devices with their start and end apart: 9, of which 3 were waited for; matrix products, arithmetic and copies ran while one was open for 15% of the time, Pallas kernels for 21%

profile of v12, /device:TPU:0, one launch (start us, length us, event | category | flops | bytes accessed | tf_op | source)
XLA Modules:
  0.0 64.6 jit_solution(4373836463677865482)
XLA Ops:
  0.0 1.9 %convert_select_fusion.eta_ref = f32[32,32,256]{2,1,0:T(8,128)S(1)} fusion(bf16[32,32,256]{2,1,0:T(8,128)(2,1)} %param.11, bf16[32,32,256]{2,1,0:T(8,128)(2,1)} %param.12, s32[32,32,256]{2,1,0:T(8,128)} %param.13), kind=kLoop, calls=%fused_computation.7 | loop fusion | flops 1835008 | bytes 3145728 | tf_op jit(solution)/shard_map/jit(_where)/select_n | solution.py:157
  1.9 0.0 copy-start
  1.9 0.1 fusion.17
  2.0 0.1 pad_maximum_fusion.2
  2.1 1.3 %collective-permute-start = (f32[32,6,256]{2,1,0:T(8,128)S(1)}, f32[32,6,256]{2,1,0:T(8,128)S(1)}, u32[]{:S(2)}, u32[]{:S(2)}) collective-permute-start(f32[32,6,256]{2,1,0:T(8,128)S(1)} %pad_maximum_fusion.2), channel_id=1, source_target_pairs={{8,0},{16,8},{24,16},{9,1},{17,9},{25,17},{10,2},{18,10},{26,18},{... | collective-permute-start | bytes 589832 | tf_op jit(solution)/shard_map/ppermute | solution.py:165
  3.4 0.1 pad_maximum_fusion.3
  3.5 5.6 %collective-permute-start.1 = (f32[32,6,256]{2,1,0:T(8,128)S(1)}, f32[32,6,256]{2,1,0:T(8,128)S(1)}, u32[]{:S(2)}, u32[]{:S(2)}) collective-permute-start(f32[32,6,256]{2,1,0:T(8,128)S(1)} %pad_maximum_fusion.3), channel_id=1, source_target_pairs={{0,8},{8,16},{16,24},{1,9},{9,17},{17,25},{2,10},{10,18},{18,26},{... | collective-permute-start | bytes 589832 | tf_op jit(solution)/shard_map/ppermute | solution.py:164
  9.1 0.2 fusion.16
  9.3 0.2 fusion.15
  9.5 0.0 copy-start.8
  9.5 0.3 copy.21
  9.8 0.3 copy.30
  10.1 0.3 copy.25
  10.4 0.3 copy.31
  10.7 0.1 pad.25.clone
  10.7 0.1 pad.3.clone
  10.8 0.1 fusion.11
  11.0 0.1 fusion.9
  11.0 0.7 %and_convert_fusion.mask_ref = f32[40,384]{1,0:T(8,128)} fusion(pred[384]{0:T(512)(128)(4,1)S(1)} %compare_and_fusion, pred[40]{0:T(512)(128)(4,1)S(1)} %compare_and_fusion.1), kind=kLoop, calls=%fused_computation.24 | loop fusion | flops 30720 | bytes 61864 | tf_op jit(solution)/shard_map/convert_element_type | solution.py:28
  11.7 1.6 %collective-permute-done = f32[32,6,256]{2,1,0:T(8,128)S(1)} collective-permute-done((f32[32,6,256]{2,1,0:T(8,128)S(1)}, f32[32,6,256]{2,1,0:T(8,128)S(1)}, u32[]{:S(2)}, u32[]{:S(2)}) %collective-permute-start) | collective-permute-done | bytes 196640 | tf_op jit(solution)/shard_map/ppermute | solution.py:165
  13.3 0.1 fusion.21
  13.4 1.2 %collective-permute-done.1 = f32[32,6,256]{2,1,0:T(8,128)S(1)} collective-permute-done((f32[32,6,256]{2,1,0:T(8,128)S(1)}, f32[32,6,256]{2,1,0:T(8,128)S(1)}, u32[]{:S(2)}, u32[]{:S(2)}) %collective-permute-start.1) | collective-permute-done | bytes 196640 | tf_op jit(solution)/shard_map/ppermute | solution.py:164
  14.6 0.1 fusion.22
  14.6 0.1 pad_maximum_fusion.4
  14.8 0.1 fusion.20
  14.9 0.3 copy.22
  15.2 0.1 fusion.19
  15.3 0.3 copy.20
  15.5 0.3 copy.26
  15.8 0.3 copy.24
  16.1 0.1 maximum_bitcast_fusion.3
  16.2 0.1 maximum_bitcast_fusion.2
  16.3 0.1 maximum_bitcast_fusion.5
  16.4 0.1 maximum_bitcast_fusion.4
  16.5 0.9 %copy.27 = f32[2,2,32,40,3]{4,3,2,1,0:T(8,128)S(1)} copy(f32[2,2,32,40,3]{3,2,4,1,0:T(8,128)S(1)} %pad_maximum_fusion.6) | data formatting | bytes 122880 | tf_op jit(solution)/shard_map/stack | solution.py:178
  17.5 0.0 copy-start.7
  17.5 1.9 %reshape.108 = f32[15360]{0:T(1024)S(1)} reshape(f32[2,2,32,40,3]{4,3,2,1,0:T(8,128)S(1)} %copy.27) | data formatting | bytes 122880 | tf_op jit(solution)/shard_map/reshape | solution.py:178
  19.4 1.3 %collective-permute-start.2 = (f32[7680]{0:T(1024)S(1)}, f32[7680]{0:T(1024)S(1)}, u32[]{:S(2)}, u32[]{:S(2)}) collective-permute-start(f32[7680]{0:T(1024)S(1)} %get-tuple-element.41), channel_id=1, source_target_pairs={{2,0},{4,2},{6,4},{3,1},{5,3},{7,5},{10,8},{12,10},{14,12},{11,9},... | collective-permute-start | bytes 92168 | tf_op jit(solution)/shard_map/ppermute | solution.py:182
  20.7 3.0 %collective-permute-start.3 = (f32[7680]{0:T(1024)S(1)}, f32[7680]{0:T(1024)S(1)}, u32[]{:S(2)}, u32[]{:S(2)}) collective-permute-start(f32[7680]{0:T(1024)S(1)} %get-tuple-element.42), channel_id=1, source_target_pairs={{0,2},{2,4},{4,6},{1,3},{3,5},{5,7},{8,10},{10,12},{12,14},{9,11},... | collective-permute-start | bytes 92168 | tf_op jit(solution)/shard_map/ppermute | solution.py:183
  23.7 0.7 %copy.36 = bf16[4,4,8,512]{3,2,0,1:T(8,128)(2,1)} copy(bf16[4,4,8,512]{3,2,1,0:T(8,128)(2,1)S(1)} %bitcast.32) | data formatting | bytes 262144 | tf_op jit(solution)/shard_map/all_to_all | solution.py:181
  24.4 3.5 %all-to-all-start = ((bf16[32,4,512]{2,0,1:T(8,128)(2,1)}), bf16[32,4,512]{2,0,1:T(8,128)(2,1)S(1)}, u32[]{:S(2)}, u32[]{:S(2)}) async-start(bf16[32,4,512]{2,0,1:T(8,128)(2,1)} %bitcast.28), calls=%async_computation | async-start | bytes 262144 | tf_op jit(solution)/shard_map/all_to_all | solution.py:181
  27.9 0.8 %pad_maximum_fusion.1.rowh_ref = f32[2,32,8,256]{3,2,1,0:T(8,128)} fusion(f32[1,32,8,256]{3,2,1,0:T(8,128)S(1)} %bitcast.30, f32[1,32,8,256]{3,2,1,0:T(8,128)S(1)} %bitcast.29), kind=kLoop, calls=%fused_computation.13 | loop fusion | flops 131072 | bytes 1048576 | tf_op jit(solution)/shard_map/stack | solution.py:167
  28.7 1.2 %concatenate.45 = f32[2,32,40,3]{3,2,1,0:T(8,128)S(1)} reshape(f32[7680]{0:T(1024)S(1)} %collective-permute-done.2) | data formatting | bytes 61440 | tf_op jit(solution)/shard_map/concatenate | solution.py:184
  29.9 1.2 %concatenate.46 = f32[2,32,40,3]{3,2,1,0:T(8,128)S(1)} reshape(f32[7680]{0:T(1024)S(1)} %collective-permute-done.3) | data formatting | bytes 61440 | tf_op jit(solution)/shard_map/concatenate | solution.py:184
  31.1 1.5 %pad_maximum_fusion.colh_ref = f32[2,32,40,128]{3,2,1,0:T(8,128)} fusion(f32[2,32,40,3]{3,2,1,0:T(8,128)S(1)} %concatenate.46, f32[2,32,40,3]{3,2,1,0:T(8,128)S(1)} %concatenate.45, f32[128]{0:T(128)S(1)} %pad.3.clone), kind=kLoop, calls=%fused_computation.10 | loop fusion | flops 655360 | bytes 1372672 | tf_op jit(solution)/shard_map/concatenate | solution.py:186
  32.6 2.4 %fusion.dep_ref = f32[32,32,256]{2,1,0:T(8,128)} fusion(pred[32,2048]{1,0:T(8,128)(4,1)S(1)} %fusion.9, bf16[32,2048]{1,0:T(8,128)(2,1)S(1)} %bitcast.33, s32[2048]{0:T(1024)S(1)} %get-tuple-element.45), kind=kOutput, calls=%fused_computation | convolution fusion | flops 1076363264 | bytes 1253376 | tf_op jit(solution)/shard_map/las,sb->lab/dot_general | solution.py:198
  35.0 3.5 %shard_map.91 = (f32[8,16,256]{2,1,0:T(8,128)}, f32[8,16,256]{2,1,0:T(8,128)}) custom-call(s32[1]{0:T(128)} %bitcast.rad_ref.after_ref.recv_ref, f32[32,32,256]{2,1,0:T(8,128)} %lam_ref.7, f32[32,32,256]{2,1,0:T(8,128)} %copy-done, f32[2,32,8,256]{3,2,1,0:T(8,128)} %pad_maximum_fusion.1.rowh_ref, f32[2,32,40,128]{3,2,1,0:T(8,128)} %pad_maximum_fusion.colh_ref, ...), custom_call_target="tpu_custom_call" | custom-call | flops 737280000 | bytes 12800000 | tf_op jit(solution)/shard_map/pallas_call | solution.py:104
  38.5 1.7 %collective-permute-start.4 = (f32[8,16,256]{2,1,0:T(8,128)}, f32[8,16,256]{2,1,0:T(8,128)S(1)}, u32[]{:S(2)}, u32[]{:S(2)}) collective-permute-start(f32[8,16,256]{2,1,0:T(8,128)} %get-tuple-element.19), channel_id=1, source_target_pairs={{0,1},{1,0},{2,3},{3,2},{4,5},{5,4},{6,7},{7,6},{8,9},{9,8},{10,11... | collective-permute-start | bytes 393224 | tf_op jit(solution)/shard_map/ppermute | solution.py:214
  40.2 3.5 %shard_map.92 = (f32[8,16,256]{2,1,0:T(8,128)}, f32[8,16,256]{2,1,0:T(8,128)}) custom-call(s32[1]{0:T(128)} %bitcast.rad_ref.after_ref.recv_ref, f32[32,32,256]{2,1,0:T(8,128)} %lam_ref.7, f32[32,32,256]{2,1,0:T(8,128)} %copy-done, f32[2,32,8,256]{3,2,1,0:T(8,128)} %pad_maximum_fusion.1.rowh_ref, f32[2,32,40,128]{3,2,1,0:T(8,128)} %pad_maximum_fusion.colh_ref, ...), custom_call_target="tpu_custom_call" | custom-call | flops 737280000 | bytes 12800000 | tf_op jit(solution)/shard_map/pallas_call | solution.py:104
  43.7 0.4 collective-permute-start.6
  44.0 0.1 constant_dynamic-slice_fusion.1
  44.1 0.7 %collective-permute-done.4.recv_ref.refs_4_ = f32[8,16,256]{2,1,0:T(8,128)S(1)} collective-permute-done((f32[8,16,256]{2,1,0:T(8,128)}, f32[8,16,256]{2,1,0:T(8,128)S(1)}, u32[]{:S(2)}, u32[]{:S(2)}) %collective-permute-start.4) | collective-permute-done | bytes 131104 | tf_op jit(solution)/shard_map/ppermute | solution.py:214
  44.8 0.7 %copy-done.2 = f32[8,16,256]{2,1,0:T(8,128)} copy-done((f32[8,16,256]{2,1,0:T(8,128)}, f32[8,16,256]{2,1,0:T(8,128)S(1)}, u32[]{:S(2)}) %copy-start.2) | copy-done | bytes 131096
  45.4 3.5 %shard_map.93 = (f32[8,16,256]{2,1,0:T(8,128)}, f32[8,16,256]{2,1,0:T(8,128)}) custom-call(s32[1]{0:T(128)} %bitcast.rad_ref.after_ref.recv_ref, f32[32,32,256]{2,1,0:T(8,128)} %lam_ref.7, f32[32,32,256]{2,1,0:T(8,128)} %copy-done, f32[2,32,8,256]{3,2,1,0:T(8,128)} %pad_maximum_fusion.1.rowh_ref, f32[2,32,40,128]{3,2,1,0:T(8,128)} %pad_maximum_fusion.colh_ref, ...), custom_call_target="tpu_custom_call" | custom-call | flops 737280000 | bytes 12800000 | tf_op jit(solution)/shard_map/pallas_call | solution.py:104
  48.9 1.8 %collective-permute-start.5 = (f32[8,16,256]{2,1,0:T(8,128)}, f32[8,16,256]{2,1,0:T(8,128)S(1)}, u32[]{:S(2)}, u32[]{:S(2)}) collective-permute-start(f32[8,16,256]{2,1,0:T(8,128)} %get-tuple-element.20), channel_id=1, source_target_pairs={{0,1},{1,0},{2,3},{3,2},{4,5},{5,4},{6,7},{7,6},{8,9},{9,8},{10,11... | collective-permute-start | bytes 393224 | tf_op jit(solution)/shard_map/ppermute | solution.py:214
  50.8 0.7 %copy-done.3 = f32[8,16,256]{2,1,0:T(8,128)} copy-done((f32[8,16,256]{2,1,0:T(8,128)}, f32[8,16,256]{2,1,0:T(8,128)S(1)}, u32[]{:S(2)}) %copy-start.3) | copy-done | bytes 131096
  51.4 3.5 %shard_map.94 = (f32[8,16,256]{2,1,0:T(8,128)}, f32[8,16,256]{2,1,0:T(8,128)}) custom-call(s32[1]{0:T(128)} %bitcast.rad_ref.after_ref.recv_ref, f32[32,32,256]{2,1,0:T(8,128)} %lam_ref.7, f32[32,32,256]{2,1,0:T(8,128)} %copy-done, f32[2,32,8,256]{3,2,1,0:T(8,128)} %pad_maximum_fusion.1.rowh_ref, f32[2,32,40,128]{3,2,1,0:T(8,128)} %pad_maximum_fusion.colh_ref, ...), custom_call_target="tpu_custom_call" | custom-call | flops 737280000 | bytes 12800000 | tf_op jit(solution)/shard_map/pallas_call | solution.py:104
  54.9 0.2 collective-permute-start.7
  55.1 0.7 %constant_dynamic-slice_fusion.r_ref = f32[64,16]{1,0:T(8,128)} fusion(f32[64,64]{1,0:T(8,128)S(1)} %copy-done.5, s32[]{:T(128)S(6)} %add.54), kind=kLoop, calls=%fused_computation.49 | loop fusion | bytes 8196 | tf_op jit(solution)/shard_map/slice | solution.py:224
  55.8 0.7 %pad_maximum_fusion.7.r_ref = f32[64,48]{1,0:T(8,128)} fusion(f32[64,32]{1,0:T(8,128)S(1)} %get-tuple-element.44, f32[64,32]{1,0:T(8,128)S(1)} %get-tuple-element.43), kind=kLoop, calls=%fused_computation.29 | loop fusion | flops 3072 | bytes 28672 | tf_op jit(solution)/shard_map/concatenate | solution.py:219
  56.5 0.7 %copy-done.4 = f32[8,16,256]{2,1,0:T(8,128)} copy-done((f32[8,16,256]{2,1,0:T(8,128)}, f32[8,16,256]{2,1,0:T(8,128)S(1)}, u32[]{:S(2)}) %copy-start.4) | copy-done | bytes 131096
  57.1 3.3 %shard_map.95.refs_2_ = f32[64,16,256]{2,1,0:T(8,128)} custom-call(f32[64,48]{1,0:T(8,128)} %pad_maximum_fusion.7.r_ref, f32[8,16,256]{2,1,0:T(8,128)} %get-tuple-element.17.after_ref.refs_0_, f32[8,16,256]{2,1,0:T(8,128)} %get-tuple-element.18.after_ref.refs_1_, f32[8,16,256]{2,1,0:T(8,128)} %get-tuple-element.21.after_ref.refs_2_, ...), custom_call_target="tpu_custom_call" | custom-call | tf_op jit(solution)/shard_map/pallas_call | solution.py:250
  60.4 0.7 %copy-done.6 = f32[8,16,256]{2,1,0:T(8,128)} copy-done((f32[8,16,256]{2,1,0:T(8,128)}, f32[8,16,256]{2,1,0:T(8,128)S(1)}, u32[]{:S(2)}) %copy-start.6) | copy-done | bytes 131096
  61.1 3.5 %shard_map.96 = f32[64,16,256]{2,1,0:T(8,128)} custom-call(f32[64,16]{1,0:T(8,128)} %constant_dynamic-slice_fusion.r_ref, f32[8,16,256]{2,1,0:T(8,128)} %copy-done.4, f32[8,16,256]{2,1,0:T(8,128)} %copy-done.6, f32[64,16,256]{2,1,0:T(8,128)} %shard_map.95.refs_2_), custom_call_target="tpu_custom_call" | custom-call | tf_op jit(solution)/shard_map/pallas_call | solution.py:250
  (30 shorter events, 0.2 us)
Async XLA Ops:
  0.0 1.9 %copy-start.1 = (f32[32,32,256]{2,1,0:T(8,128)S(1)}, f32[32,32,256]{2,1,0:T(8,128)}, u32[]{:S(2)}) copy-start(f32[32,32,256]{2,1,0:T(8,128)} %lam_ref.7) | copy-start | bytes 3145732
  1.9 7.3 %copy-start = (f32[32,32,256]{2,1,0:T(8,128)}, f32[32,32,256]{2,1,0:T(8,128)S(1)}, u32[]{:S(2)}) copy-start(f32[32,32,256]{2,1,0:T(8,128)S(1)} %convert_select_fusion.eta_ref) | copy-start | bytes 3145732
  2.1 11.2 %collective-permute-start = (f32[32,6,256]{2,1,0:T(8,128)S(1)}, f32[32,6,256]{2,1,0:T(8,128)S(1)}, u32[]{:S(2)}, u32[]{:S(2)}) collective-permute-start(f32[32,6,256]{2,1,0:T(8,128)S(1)} %pad_maximum_fusion.2), channel_id=1, source_target_pairs={{8,0},{16,8},{24,16},{9,1},{17,9},{25,17},{10,2},{18,10},{26,18},{... | collective-permute-start | bytes 589832 | tf_op jit(solution)/shard_map/ppermute | solution.py:165
  3.5 11.1 %collective-permute-start.1 = (f32[32,6,256]{2,1,0:T(8,128)S(1)}, f32[32,6,256]{2,1,0:T(8,128)S(1)}, u32[]{:S(2)}, u32[]{:S(2)}) collective-permute-start(f32[32,6,256]{2,1,0:T(8,128)S(1)} %pad_maximum_fusion.3), channel_id=1, source_target_pairs={{0,8},{8,16},{16,24},{1,9},{9,17},{17,25},{2,10},{10,18},{18,26},{... | collective-permute-start | bytes 589832 | tf_op jit(solution)/shard_map/ppermute | solution.py:164
  9.5 1.3 %copy-start.8 = (s32[2048]{0:T(1024)S(1)}, s32[2048]{0:T(1024)}, u32[]{:S(2)}) copy-start(s32[2048]{0:T(1024)} %param.16) | copy-start | bytes 24580
  9.5 1.3 %copy-start.9 = (s32[4]{0:T(128)S(1)}, s32[4]{0:T(128)}, u32[]{:S(2)}) copy-start(s32[4]{0:T(128)} %param.17) | copy-start | bytes 52
  17.5 6.2 %copy-start.7 = (bf16[32,2048]{1,0:T(8,128)(2,1)S(1)}, bf16[32,2048]{1,0:T(8,128)(2,1)}, u32[]{:S(2)}) copy-start(bf16[32,2048]{1,0:T(8,128)(2,1)} %param.15) | copy-start | bytes 393220
  19.4 9.4 %collective-permute-start.2 = (f32[7680]{0:T(1024)S(1)}, f32[7680]{0:T(1024)S(1)}, u32[]{:S(2)}, u32[]{:S(2)}) collective-permute-start(f32[7680]{0:T(1024)S(1)} %get-tuple-element.41), channel_id=1, source_target_pairs={{2,0},{4,2},{6,4},{3,1},{5,3},{7,5},{10,8},{12,10},{14,12},{11,9},... | collective-permute-start | bytes 92168 | tf_op jit(solution)/shard_map/ppermute | solution.py:182
  20.7 9.3 %collective-permute-start.3 = (f32[7680]{0:T(1024)S(1)}, f32[7680]{0:T(1024)S(1)}, u32[]{:S(2)}, u32[]{:S(2)}) collective-permute-start(f32[7680]{0:T(1024)S(1)} %get-tuple-element.42), channel_id=1, source_target_pairs={{0,2},{2,4},{4,6},{1,3},{3,5},{5,7},{8,10},{10,12},{12,14},{9,11},... | collective-permute-start | bytes 92168 | tf_op jit(solution)/shard_map/ppermute | solution.py:183
  24.4 8.2 %all-to-all-start = ((bf16[32,4,512]{2,0,1:T(8,128)(2,1)}), bf16[32,4,512]{2,0,1:T(8,128)(2,1)S(1)}, u32[]{:S(2)}, u32[]{:S(2)}) async-start(bf16[32,4,512]{2,0,1:T(8,128)(2,1)} %bitcast.28), calls=%async_computation | async-start | bytes 262144 | tf_op jit(solution)/shard_map/all_to_all | solution.py:181
  38.5 6.3 %collective-permute-start.4 = (f32[8,16,256]{2,1,0:T(8,128)}, f32[8,16,256]{2,1,0:T(8,128)S(1)}, u32[]{:S(2)}, u32[]{:S(2)}) collective-permute-start(f32[8,16,256]{2,1,0:T(8,128)} %get-tuple-element.19), channel_id=1, source_target_pairs={{0,1},{1,0},{2,3},{3,2},{4,5},{5,4},{6,7},{7,6},{8,9},{9,8},{10,11... | collective-permute-start | bytes 393224 | tf_op jit(solution)/shard_map/ppermute | solution.py:214
  40.2 3.9 %copy-start.5 = (f32[64,64]{1,0:T(8,128)S(1)}, f32[64,64]{1,0:T(8,128)}, u32[]{:S(2)}) copy-start(f32[64,64]{1,0:T(8,128)} %param.14) | copy-start | bytes 49156
  43.7 7.1 %collective-permute-start.6 = (f32[8,16,256]{2,1,0:T(8,128)}, f32[8,16,256]{2,1,0:T(8,128)S(1)}, u32[]{:S(2)}, u32[]{:S(2)}) collective-permute-start(f32[8,16,256]{2,1,0:T(8,128)} %get-tuple-element.22), channel_id=1, source_target_pairs={{0,1},{1,0},{2,3},{3,2},{4,5},{5,4},{6,7},{7,6},{8,9},{9,8},{10,11... | collective-permute-start | bytes 393224 | tf_op jit(solution)/shard_map/ppermute | solution.py:214
  44.8 0.7 %copy-start.2 = (f32[8,16,256]{2,1,0:T(8,128)}, f32[8,16,256]{2,1,0:T(8,128)S(1)}, u32[]{:S(2)}) copy-start(f32[8,16,256]{2,1,0:T(8,128)S(1)} %collective-permute-done.4.recv_ref.refs_4_) | copy-start | bytes 393220
  48.9 7.5 %collective-permute-start.5 = (f32[8,16,256]{2,1,0:T(8,128)}, f32[8,16,256]{2,1,0:T(8,128)S(1)}, u32[]{:S(2)}, u32[]{:S(2)}) collective-permute-start(f32[8,16,256]{2,1,0:T(8,128)} %get-tuple-element.20), channel_id=1, source_target_pairs={{0,1},{1,0},{2,3},{3,2},{4,5},{5,4},{6,7},{7,6},{8,9},{9,8},{10,11... | collective-permute-start | bytes 393224 | tf_op jit(solution)/shard_map/ppermute | solution.py:214
  50.8 0.7 %copy-start.3 = (f32[8,16,256]{2,1,0:T(8,128)}, f32[8,16,256]{2,1,0:T(8,128)S(1)}, u32[]{:S(2)}) copy-start(f32[8,16,256]{2,1,0:T(8,128)S(1)} %collective-permute-done.6.recv_ref.refs_5_) | copy-start | bytes 393220
  54.9 5.5 %collective-permute-start.7 = (f32[8,16,256]{2,1,0:T(8,128)}, f32[8,16,256]{2,1,0:T(8,128)S(1)}, u32[]{:S(2)}, u32[]{:S(2)}) collective-permute-start(f32[8,16,256]{2,1,0:T(8,128)} %get-tuple-element.23), channel_id=1, source_target_pairs={{0,1},{1,0},{2,3},{3,2},{4,5},{5,4},{6,7},{7,6},{8,9},{9,8},{10,11... | collective-permute-start | bytes 393224 | tf_op jit(solution)/shard_map/ppermute | solution.py:214
  56.5 0.7 %copy-start.4 = (f32[8,16,256]{2,1,0:T(8,128)}, f32[8,16,256]{2,1,0:T(8,128)S(1)}, u32[]{:S(2)}) copy-start(f32[8,16,256]{2,1,0:T(8,128)S(1)} %collective-permute-done.5.refs_6_.refs_0_) | copy-start | bytes 393220
  60.4 0.7 %copy-start.6 = (f32[8,16,256]{2,1,0:T(8,128)}, f32[8,16,256]{2,1,0:T(8,128)S(1)}, u32[]{:S(2)}) copy-start(f32[8,16,256]{2,1,0:T(8,128)S(1)} %collective-permute-done.7.refs_1_) | copy-start | bytes 393220

commit v13 on v12

--- a/solution.py
+++ b/solution.py
@@ -242,17 +242,21 @@
 
 def _radial(r_cols, pieces, partial=None, after=None):
     n_k, n_l = r_cols.shape
-    _, n_a, n_b = pieces[0].shape
+    step, n_a, n_b = pieces[0].shape
+    tile = 8
     extra = [] if partial is None else [partial]
     fake = [] if after is None else [after]
-    in_specs = [pl.BlockSpec(memory_space=pltpu.VMEM)] * (1 + len(pieces) + len(extra))
+    in_specs = [pl.BlockSpec((n_k, n_l), lambda t: (0, 0))]
+    in_specs += [pl.BlockSpec((step, tile, n_b), lambda t: (0, t, 0))] * len(pieces)
+    in_specs += [pl.BlockSpec((n_k, tile, n_b), lambda t: (0, t, 0))] * len(extra)
     in_specs += [pl.BlockSpec(memory_space=pl.ANY)] * len(fake)
     return pl.pallas_call(
         functools.partial(_radial_kernel, len(pieces), partial is not None),
         out_shape=jax.ShapeDtypeStruct((n_k, n_a, n_b), jnp.float32),
+        grid=(n_a // tile,),
         in_specs=in_specs,
-        out_specs=pl.BlockSpec(memory_space=pltpu.VMEM),
-        scratch_shapes=[pltpu.VMEM((n_l, n_a, n_b), jnp.float32)],
+        out_specs=pl.BlockSpec((n_k, tile, n_b), lambda t: (0, t, 0)),
+        scratch_shapes=[pltpu.VMEM((n_l, tile, n_b), jnp.float32)],
     )(r_cols, *pieces, *extra, *fake)
 
 

time: 65 us -> 64.7 us (level)
  transfers between devices with their start and end apart: 9 -> 9, of which waited for: 3 -> 4; matrix products, arithmetic and copies ran while one was open for 15% -> 15% of each run, Pallas kernels for 21% -> 21%
where the time goes in v13:
time: 64.7 us; the launch traced here: 64.2 us
  Pallas kernels  20.3 us (31%)
  starting transfers between devices  18.7 us (29%)
  local copies, waits for them, and re-layouts  12.5 us (19%)
  other arithmetic  6.44 us (10%)
  waiting for transfers between devices  3.55 us (5%)
  matrix products  2.37 us (4%)
    pallas_call x4, Pallas kernels, _sweeps(): pl.pallas_call(_sweep_kernel, out_shape=out_shape, grid=grid, in_specs=[p...  13.9 us
    pallas_call x2, Pallas kernels, _radial(): pl.pallas_call(functools.partial(_radial_kernel, len(pieces), partial is...  6.34 us
    ppermute x1, starting transfers between devices, per_device(): top = lax.ppermute(top_send, 'cap', _pairs(n_cap, 1))  5.57 us
    ppermute x4, starting transfers between devices, per_device(): lax.ppermute(send, 'rad', _pairs(n_rad, 1) + _pairs(n_rad, -1))  4.05 us
    all_to_all x1, starting transfers between devices, per_device(): lax.all_to_all(markers, 'lat', split_axis=1, concat_axis=1, tiled=True)  3.5 us
    unnamed x23, local copies, waits for them, and re-layouts  3.23 us
    ppermute x1, starting transfers between devices, per_device(): from_left = lax.ppermute(flat[piece:], 'lat', _pairs(n_lat, 1))  3.03 us
    concatenate x2, local copies, waits for them, and re-layouts, per_device(): jnp.concatenate([from_right, from_left]).reshape(2, 2, layers, ext_rows, g)  2.37 us
  transfers between devices with their start and end apart: 9, of which 4 were waited for; matrix products, arithmetic and copies ran while one was open for 15% of the time, Pallas kernels for 21%

profile of v13, /device:TPU:0, one launch (start us, length us, event | category | flops | bytes accessed | tf_op | source)
XLA Modules:
  0.0 64.2 jit_solution(5524557324826259115)
XLA Ops:
  0.0 1.9 %convert_select_fusion.eta_ref = f32[32,32,256]{2,1,0:T(8,128)S(1)} fusion(bf16[32,32,256]{2,1,0:T(8,128)(2,1)} %param.11, bf16[32,32,256]{2,1,0:T(8,128)(2,1)} %param.12, s32[32,32,256]{2,1,0:T(8,128)} %param.13), kind=kLoop, calls=%fused_computation.7 | loop fusion | flops 1835008 | bytes 3145728 | tf_op jit(solution)/shard_map/jit(_where)/select_n | solution.py:157
  1.9 0.1 fusion.17
  2.0 0.1 pad_maximum_fusion.2
  2.1 1.3 %collective-permute-start = (f32[32,6,256]{2,1,0:T(8,128)S(1)}, f32[32,6,256]{2,1,0:T(8,128)S(1)}, u32[]{:S(2)}, u32[]{:S(2)}) collective-permute-start(f32[32,6,256]{2,1,0:T(8,128)S(1)} %pad_maximum_fusion.2), channel_id=1, source_target_pairs={{8,0},{16,8},{24,16},{9,1},{17,9},{25,17},{10,2},{18,10},{26,18},{... | collective-permute-start | bytes 589832 | tf_op jit(solution)/shard_map/ppermute | solution.py:165
  3.4 0.1 pad_maximum_fusion.3
  3.5 5.6 %collective-permute-start.1 = (f32[32,6,256]{2,1,0:T(8,128)S(1)}, f32[32,6,256]{2,1,0:T(8,128)S(1)}, u32[]{:S(2)}, u32[]{:S(2)}) collective-permute-start(f32[32,6,256]{2,1,0:T(8,128)S(1)} %pad_maximum_fusion.3), channel_id=1, source_target_pairs={{0,8},{8,16},{16,24},{1,9},{9,17},{17,25},{2,10},{10,18},{18,26},{... | collective-permute-start | bytes 589832 | tf_op jit(solution)/shard_map/ppermute | solution.py:164
  9.1 0.2 fusion.16
  9.3 0.2 fusion.15
  9.5 0.0 copy-start.8
  9.5 0.3 copy.21
  9.8 0.3 copy.30
  10.1 0.3 copy.25
  10.4 0.3 copy.31
  10.7 0.1 pad.25.clone
  10.7 0.1 pad.3.clone
  10.8 0.1 fusion.11
  11.0 0.1 fusion.9
  11.0 0.7 %and_convert_fusion.mask_ref = f32[40,384]{1,0:T(8,128)} fusion(pred[384]{0:T(512)(128)(4,1)S(1)} %compare_and_fusion, pred[40]{0:T(512)(128)(4,1)S(1)} %compare_and_fusion.1), kind=kLoop, calls=%fused_computation.24 | loop fusion | flops 30720 | bytes 61864 | tf_op jit(solution)/shard_map/convert_element_type | solution.py:28
  11.7 1.6 %collective-permute-done = f32[32,6,256]{2,1,0:T(8,128)S(1)} collective-permute-done((f32[32,6,256]{2,1,0:T(8,128)S(1)}, f32[32,6,256]{2,1,0:T(8,128)S(1)}, u32[]{:S(2)}, u32[]{:S(2)}) %collective-permute-start) | collective-permute-done | bytes 196640 | tf_op jit(solution)/shard_map/ppermute | solution.py:165
  13.3 0.1 fusion.21
  13.4 1.2 %collective-permute-done.1 = f32[32,6,256]{2,1,0:T(8,128)S(1)} collective-permute-done((f32[32,6,256]{2,1,0:T(8,128)S(1)}, f32[32,6,256]{2,1,0:T(8,128)S(1)}, u32[]{:S(2)}, u32[]{:S(2)}) %collective-permute-start.1) | collective-permute-done | bytes 196640 | tf_op jit(solution)/shard_map/ppermute | solution.py:164
  14.6 0.1 fusion.22
  14.6 0.1 pad_maximum_fusion.4
  14.8 0.1 fusion.20
  14.9 0.3 copy.22
  15.2 0.1 fusion.19
  15.3 0.3 copy.20
  15.5 0.3 copy.26
  15.8 0.3 copy.24
  16.1 0.1 maximum_bitcast_fusion.3
  16.2 0.1 maximum_bitcast_fusion.2
  16.3 0.1 maximum_bitcast_fusion.5
  16.4 0.1 maximum_bitcast_fusion.4
  16.5 0.9 %copy.27 = f32[2,2,32,40,3]{4,3,2,1,0:T(8,128)S(1)} copy(f32[2,2,32,40,3]{3,2,4,1,0:T(8,128)S(1)} %pad_maximum_fusion.6) | data formatting | bytes 122880 | tf_op jit(solution)/shard_map/stack | solution.py:178
  17.5 0.0 copy-start.7
  17.5 1.9 %reshape.108 = f32[15360]{0:T(1024)S(1)} reshape(f32[2,2,32,40,3]{4,3,2,1,0:T(8,128)S(1)} %copy.27) | data formatting | bytes 122880 | tf_op jit(solution)/shard_map/reshape | solution.py:178
  19.4 1.3 %collective-permute-start.2 = (f32[7680]{0:T(1024)S(1)}, f32[7680]{0:T(1024)S(1)}, u32[]{:S(2)}, u32[]{:S(2)}) collective-permute-start(f32[7680]{0:T(1024)S(1)} %get-tuple-element.41), channel_id=1, source_target_pairs={{2,0},{4,2},{6,4},{3,1},{5,3},{7,5},{10,8},{12,10},{14,12},{11,9},... | collective-permute-start | bytes 92168 | tf_op jit(solution)/shard_map/ppermute | solution.py:182
  20.7 3.0 %collective-permute-start.3 = (f32[7680]{0:T(1024)S(1)}, f32[7680]{0:T(1024)S(1)}, u32[]{:S(2)}, u32[]{:S(2)}) collective-permute-start(f32[7680]{0:T(1024)S(1)} %get-tuple-element.42), channel_id=1, source_target_pairs={{0,2},{2,4},{4,6},{1,3},{3,5},{5,7},{8,10},{10,12},{12,14},{9,11},... | collective-permute-start | bytes 92168 | tf_op jit(solution)/shard_map/ppermute | solution.py:183
  23.7 0.7 %copy.36 = bf16[4,4,8,512]{3,2,0,1:T(8,128)(2,1)} copy(bf16[4,4,8,512]{3,2,1,0:T(8,128)(2,1)S(1)} %bitcast.32) | data formatting | bytes 262144 | tf_op jit(solution)/shard_map/all_to_all | solution.py:181
  24.4 3.5 %all-to-all-start = ((bf16[32,4,512]{2,0,1:T(8,128)(2,1)}), bf16[32,4,512]{2,0,1:T(8,128)(2,1)S(1)}, u32[]{:S(2)}, u32[]{:S(2)}) async-start(bf16[32,4,512]{2,0,1:T(8,128)(2,1)} %bitcast.28), calls=%async_computation | async-start | bytes 262144 | tf_op jit(solution)/shard_map/all_to_all | solution.py:181
  27.9 0.8 %pad_maximum_fusion.1.rowh_ref = f32[2,32,8,256]{3,2,1,0:T(8,128)} fusion(f32[1,32,8,256]{3,2,1,0:T(8,128)S(1)} %bitcast.30, f32[1,32,8,256]{3,2,1,0:T(8,128)S(1)} %bitcast.29), kind=kLoop, calls=%fused_computation.13 | loop fusion | flops 131072 | bytes 1048576 | tf_op jit(solution)/shard_map/stack | solution.py:167
  28.7 1.2 %concatenate.45 = f32[2,32,40,3]{3,2,1,0:T(8,128)S(1)} reshape(f32[7680]{0:T(1024)S(1)} %collective-permute-done.2) | data formatting | bytes 61440 | tf_op jit(solution)/shard_map/concatenate | solution.py:184
  29.9 1.2 %concatenate.46 = f32[2,32,40,3]{3,2,1,0:T(8,128)S(1)} reshape(f32[7680]{0:T(1024)S(1)} %collective-permute-done.3) | data formatting | bytes 61440 | tf_op jit(solution)/shard_map/concatenate | solution.py:184
  31.1 1.5 %pad_maximum_fusion.colh_ref = f32[2,32,40,128]{3,2,1,0:T(8,128)} fusion(f32[2,32,40,3]{3,2,1,0:T(8,128)S(1)} %concatenate.46, f32[2,32,40,3]{3,2,1,0:T(8,128)S(1)} %concatenate.45, f32[128]{0:T(128)S(1)} %pad.3.clone), kind=kLoop, calls=%fused_computation.10 | loop fusion | flops 655360 | bytes 1372672 | tf_op jit(solution)/shard_map/concatenate | solution.py:186
  32.6 2.4 %fusion.dep_ref = f32[32,32,256]{2,1,0:T(8,128)} fusion(pred[32,2048]{1,0:T(8,128)(4,1)S(1)} %fusion.9, bf16[32,2048]{1,0:T(8,128)(2,1)S(1)} %bitcast.33, s32[2048]{0:T(1024)S(1)} %get-tuple-element.45), kind=kOutput, calls=%fused_computation | convolution fusion | flops 1076363264 | bytes 1253376 | tf_op jit(solution)/shard_map/las,sb->lab/dot_general | solution.py:198
  35.0 3.5 %shard_map.91 = (f32[8,16,256]{2,1,0:T(8,128)}, f32[8,16,256]{2,1,0:T(8,128)}) custom-call(s32[1]{0:T(128)} %bitcast.rad_ref.after_ref.recv_ref, f32[32,32,256]{2,1,0:T(8,128)} %lam_ref.7, f32[32,32,256]{2,1,0:T(8,128)} %copy-done, f32[2,32,8,256]{3,2,1,0:T(8,128)} %pad_maximum_fusion.1.rowh_ref, f32[2,32,40,128]{3,2,1,0:T(8,128)} %pad_maximum_fusion.colh_ref, ...), custom_call_target="tpu_custom_call" | custom-call | flops 737280000 | bytes 12800000 | tf_op jit(solution)/shard_map/pallas_call | solution.py:104
  38.5 1.7 %collective-permute-start.4 = (f32[8,16,256]{2,1,0:T(8,128)}, f32[8,16,256]{2,1,0:T(8,128)S(1)}, u32[]{:S(2)}, u32[]{:S(2)}) collective-permute-start(f32[8,16,256]{2,1,0:T(8,128)} %get-tuple-element.19), channel_id=1, source_target_pairs={{0,1},{1,0},{2,3},{3,2},{4,5},{5,4},{6,7},{7,6},{8,9},{9,8},{10,11... | collective-permute-start | bytes 393224 | tf_op jit(solution)/shard_map/ppermute | solution.py:214
  40.2 3.5 %shard_map.92 = (f32[8,16,256]{2,1,0:T(8,128)}, f32[8,16,256]{2,1,0:T(8,128)}) custom-call(s32[1]{0:T(128)} %bitcast.rad_ref.after_ref.recv_ref, f32[32,32,256]{2,1,0:T(8,128)} %lam_ref.7, f32[32,32,256]{2,1,0:T(8,128)} %copy-done, f32[2,32,8,256]{3,2,1,0:T(8,128)} %pad_maximum_fusion.1.rowh_ref, f32[2,32,40,128]{3,2,1,0:T(8,128)} %pad_maximum_fusion.colh_ref, ...), custom_call_target="tpu_custom_call" | custom-call | flops 737280000 | bytes 12800000 | tf_op jit(solution)/shard_map/pallas_call | solution.py:104
  43.7 0.4 collective-permute-start.6
  44.0 0.1 constant_dynamic-slice_fusion.1
  44.1 0.7 %collective-permute-done.4.recv_ref.refs_4_ = f32[8,16,256]{2,1,0:T(8,128)S(1)} collective-permute-done((f32[8,16,256]{2,1,0:T(8,128)}, f32[8,16,256]{2,1,0:T(8,128)S(1)}, u32[]{:S(2)}, u32[]{:S(2)}) %collective-permute-start.4) | collective-permute-done | bytes 131104 | tf_op jit(solution)/shard_map/ppermute | solution.py:214
  44.8 0.7 %copy-done.2 = f32[8,16,256]{2,1,0:T(8,128)} copy-done((f32[8,16,256]{2,1,0:T(8,128)}, f32[8,16,256]{2,1,0:T(8,128)S(1)}, u32[]{:S(2)}) %copy-start.2) | copy-done | bytes 131096
  45.4 3.5 %shard_map.93 = (f32[8,16,256]{2,1,0:T(8,128)}, f32[8,16,256]{2,1,0:T(8,128)}) custom-call(s32[1]{0:T(128)} %bitcast.rad_ref.after_ref.recv_ref, f32[32,32,256]{2,1,0:T(8,128)} %lam_ref.7, f32[32,32,256]{2,1,0:T(8,128)} %copy-done, f32[2,32,8,256]{3,2,1,0:T(8,128)} %pad_maximum_fusion.1.rowh_ref, f32[2,32,40,128]{3,2,1,0:T(8,128)} %pad_maximum_fusion.colh_ref, ...), custom_call_target="tpu_custom_call" | custom-call | flops 737280000 | bytes 12800000 | tf_op jit(solution)/shard_map/pallas_call | solution.py:104
  48.9 1.8 %collective-permute-start.5 = (f32[8,16,256]{2,1,0:T(8,128)}, f32[8,16,256]{2,1,0:T(8,128)S(1)}, u32[]{:S(2)}, u32[]{:S(2)}) collective-permute-start(f32[8,16,256]{2,1,0:T(8,128)} %get-tuple-element.20), channel_id=1, source_target_pairs={{0,1},{1,0},{2,3},{3,2},{4,5},{5,4},{6,7},{7,6},{8,9},{9,8},{10,11... | collective-permute-start | bytes 393224 | tf_op jit(solution)/shard_map/ppermute | solution.py:214
  50.8 0.7 %copy-done.3 = f32[8,16,256]{2,1,0:T(8,128)} copy-done((f32[8,16,256]{2,1,0:T(8,128)}, f32[8,16,256]{2,1,0:T(8,128)S(1)}, u32[]{:S(2)}) %copy-start.3) | copy-done | bytes 131096
  51.4 3.5 %shard_map.94 = (f32[8,16,256]{2,1,0:T(8,128)}, f32[8,16,256]{2,1,0:T(8,128)}) custom-call(s32[1]{0:T(128)} %bitcast.rad_ref.after_ref.recv_ref, f32[32,32,256]{2,1,0:T(8,128)} %lam_ref.7, f32[32,32,256]{2,1,0:T(8,128)} %copy-done, f32[2,32,8,256]{3,2,1,0:T(8,128)} %pad_maximum_fusion.1.rowh_ref, f32[2,32,40,128]{3,2,1,0:T(8,128)} %pad_maximum_fusion.colh_ref, ...), custom_call_target="tpu_custom_call" | custom-call | flops 737280000 | bytes 12800000 | tf_op jit(solution)/shard_map/pallas_call | solution.py:104
  54.9 0.2 collective-permute-start.7
  55.1 0.7 %constant_dynamic-slice_fusion.r_ref = f32[64,16]{1,0:T(8,128)} fusion(f32[64,64]{1,0:T(8,128)S(1)} %copy-done.5, s32[]{:T(128)S(6)} %add.54), kind=kLoop, calls=%fused_computation.49 | loop fusion | bytes 8196 | tf_op jit(solution)/shard_map/slice | solution.py:224
  55.8 0.7 %pad_maximum_fusion.7.r_ref = f32[64,48]{1,0:T(8,128)} fusion(f32[64,32]{1,0:T(8,128)S(1)} %get-tuple-element.44, f32[64,32]{1,0:T(8,128)S(1)} %get-tuple-element.43), kind=kLoop, calls=%fused_computation.29 | loop fusion | flops 3072 | bytes 28672 | tf_op jit(solution)/shard_map/concatenate | solution.py:219
  56.5 0.7 %copy-done.4 = f32[8,16,256]{2,1,0:T(8,128)} copy-done((f32[8,16,256]{2,1,0:T(8,128)}, f32[8,16,256]{2,1,0:T(8,128)S(1)}, u32[]{:S(2)}) %copy-start.4) | copy-done | bytes 131096
  57.1 3.2 %shard_map.95.refs_2_ = f32[64,16,256]{2,1,0:T(8,128)} custom-call(f32[64,48]{1,0:T(8,128)} %pad_maximum_fusion.7.r_ref, f32[8,16,256]{2,1,0:T(8,128)} %get-tuple-element.17.after_ref.refs_0_, f32[8,16,256]{2,1,0:T(8,128)} %get-tuple-element.18.after_ref.refs_1_, f32[8,16,256]{2,1,0:T(8,128)} %get-tuple-element.21.after_ref.refs_2_, ...), custom_call_target="tpu_custom_call" | custom-call | tf_op jit(solution)/shard_map/pallas_call | solution.py:253
  60.3 0.1 collective-permute-done.7.refs_1_
  60.3 0.7 %copy-done.6 = f32[8,16,256]{2,1,0:T(8,128)} copy-done((f32[8,16,256]{2,1,0:T(8,128)}, f32[8,16,256]{2,1,0:T(8,128)S(1)}, u32[]{:S(2)}) %copy-start.6) | copy-done | bytes 131096
  61.0 3.2 %shard_map.96 = f32[64,16,256]{2,1,0:T(8,128)} custom-call(f32[64,16]{1,0:T(8,128)} %constant_dynamic-slice_fusion.r_ref, f32[8,16,256]{2,1,0:T(8,128)} %copy-done.4, f32[8,16,256]{2,1,0:T(8,128)} %copy-done.6, f32[64,16,256]{2,1,0:T(8,128)} %shard_map.95.refs_2_), custom_call_target="tpu_custom_call" | custom-call | tf_op jit(solution)/shard_map/pallas_call | solution.py:253
  (30 shorter events, 0.2 us)
Async XLA Ops:
  0.0 1.9 %copy-start.1 = (f32[32,32,256]{2,1,0:T(8,128)S(1)}, f32[32,32,256]{2,1,0:T(8,128)}, u32[]{:S(2)}) copy-start(f32[32,32,256]{2,1,0:T(8,128)} %lam_ref.7) | copy-start | bytes 3145732
  1.9 7.3 %copy-start = (f32[32,32,256]{2,1,0:T(8,128)}, f32[32,32,256]{2,1,0:T(8,128)S(1)}, u32[]{:S(2)}) copy-start(f32[32,32,256]{2,1,0:T(8,128)S(1)} %convert_select_fusion.eta_ref) | copy-start | bytes 3145732
  2.1 11.2 %collective-permute-start = (f32[32,6,256]{2,1,0:T(8,128)S(1)}, f32[32,6,256]{2,1,0:T(8,128)S(1)}, u32[]{:S(2)}, u32[]{:S(2)}) collective-permute-start(f32[32,6,256]{2,1,0:T(8,128)S(1)} %pad_maximum_fusion.2), channel_id=1, source_target_pairs={{8,0},{16,8},{24,16},{9,1},{17,9},{25,17},{10,2},{18,10},{26,18},{... | collective-permute-start | bytes 589832 | tf_op jit(solution)/shard_map/ppermute | solution.py:165
  3.5 11.1 %collective-permute-start.1 = (f32[32,6,256]{2,1,0:T(8,128)S(1)}, f32[32,6,256]{2,1,0:T(8,128)S(1)}, u32[]{:S(2)}, u32[]{:S(2)}) collective-permute-start(f32[32,6,256]{2,1,0:T(8,128)S(1)} %pad_maximum_fusion.3), channel_id=1, source_target_pairs={{0,8},{8,16},{16,24},{1,9},{9,17},{17,25},{2,10},{10,18},{18,26},{... | collective-permute-start | bytes 589832 | tf_op jit(solution)/shard_map/ppermute | solution.py:164
  9.5 1.3 %copy-start.8 = (s32[2048]{0:T(1024)S(1)}, s32[2048]{0:T(1024)}, u32[]{:S(2)}) copy-start(s32[2048]{0:T(1024)} %param.16) | copy-start | bytes 24580
  9.5 1.3 %copy-start.9 = (s32[4]{0:T(128)S(1)}, s32[4]{0:T(128)}, u32[]{:S(2)}) copy-start(s32[4]{0:T(128)} %param.17) | copy-start | bytes 52
  17.5 6.2 %copy-start.7 = (bf16[32,2048]{1,0:T(8,128)(2,1)S(1)}, bf16[32,2048]{1,0:T(8,128)(2,1)}, u32[]{:S(2)}) copy-start(bf16[32,2048]{1,0:T(8,128)(2,1)} %param.15) | copy-start | bytes 393220
  19.4 9.4 %collective-permute-start.2 = (f32[7680]{0:T(1024)S(1)}, f32[7680]{0:T(1024)S(1)}, u32[]{:S(2)}, u32[]{:S(2)}) collective-permute-start(f32[7680]{0:T(1024)S(1)} %get-tuple-element.41), channel_id=1, source_target_pairs={{2,0},{4,2},{6,4},{3,1},{5,3},{7,5},{10,8},{12,10},{14,12},{11,9},... | collective-permute-start | bytes 92168 | tf_op jit(solution)/shard_map/ppermute | solution.py:182
  20.7 9.3 %collective-permute-start.3 = (f32[7680]{0:T(1024)S(1)}, f32[7680]{0:T(1024)S(1)}, u32[]{:S(2)}, u32[]{:S(2)}) collective-permute-start(f32[7680]{0:T(1024)S(1)} %get-tuple-element.42), channel_id=1, source_target_pairs={{0,2},{2,4},{4,6},{1,3},{3,5},{5,7},{8,10},{10,12},{12,14},{9,11},... | collective-permute-start | bytes 92168 | tf_op jit(solution)/shard_map/ppermute | solution.py:183
  24.4 8.2 %all-to-all-start = ((bf16[32,4,512]{2,0,1:T(8,128)(2,1)}), bf16[32,4,512]{2,0,1:T(8,128)(2,1)S(1)}, u32[]{:S(2)}, u32[]{:S(2)}) async-start(bf16[32,4,512]{2,0,1:T(8,128)(2,1)} %bitcast.28), calls=%async_computation | async-start | bytes 262144 | tf_op jit(solution)/shard_map/all_to_all | solution.py:181
  38.5 6.3 %collective-permute-start.4 = (f32[8,16,256]{2,1,0:T(8,128)}, f32[8,16,256]{2,1,0:T(8,128)S(1)}, u32[]{:S(2)}, u32[]{:S(2)}) collective-permute-start(f32[8,16,256]{2,1,0:T(8,128)} %get-tuple-element.19), channel_id=1, source_target_pairs={{0,1},{1,0},{2,3},{3,2},{4,5},{5,4},{6,7},{7,6},{8,9},{9,8},{10,11... | collective-permute-start | bytes 393224 | tf_op jit(solution)/shard_map/ppermute | solution.py:214
  40.2 3.9 %copy-start.5 = (f32[64,64]{1,0:T(8,128)S(1)}, f32[64,64]{1,0:T(8,128)}, u32[]{:S(2)}) copy-start(f32[64,64]{1,0:T(8,128)} %param.14) | copy-start | bytes 49156
  43.7 7.1 %collective-permute-start.6 = (f32[8,16,256]{2,1,0:T(8,128)}, f32[8,16,256]{2,1,0:T(8,128)S(1)}, u32[]{:S(2)}, u32[]{:S(2)}) collective-permute-start(f32[8,16,256]{2,1,0:T(8,128)} %get-tuple-element.22), channel_id=1, source_target_pairs={{0,1},{1,0},{2,3},{3,2},{4,5},{5,4},{6,7},{7,6},{8,9},{9,8},{10,11... | collective-permute-start | bytes 393224 | tf_op jit(solution)/shard_map/ppermute | solution.py:214
  44.8 0.7 %copy-start.2 = (f32[8,16,256]{2,1,0:T(8,128)}, f32[8,16,256]{2,1,0:T(8,128)S(1)}, u32[]{:S(2)}) copy-start(f32[8,16,256]{2,1,0:T(8,128)S(1)} %collective-permute-done.4.recv_ref.refs_4_) | copy-start | bytes 393220
  48.9 7.5 %collective-permute-start.5 = (f32[8,16,256]{2,1,0:T(8,128)}, f32[8,16,256]{2,1,0:T(8,128)S(1)}, u32[]{:S(2)}, u32[]{:S(2)}) collective-permute-start(f32[8,16,256]{2,1,0:T(8,128)} %get-tuple-element.20), channel_id=1, source_target_pairs={{0,1},{1,0},{2,3},{3,2},{4,5},{5,4},{6,7},{7,6},{8,9},{9,8},{10,11... | collective-permute-start | bytes 393224 | tf_op jit(solution)/shard_map/ppermute | solution.py:214
  50.8 0.7 %copy-start.3 = (f32[8,16,256]{2,1,0:T(8,128)}, f32[8,16,256]{2,1,0:T(8,128)S(1)}, u32[]{:S(2)}) copy-start(f32[8,16,256]{2,1,0:T(8,128)S(1)} %collective-permute-done.6.recv_ref.refs_5_) | copy-start | bytes 393220
  54.9 5.4 %collective-permute-start.7 = (f32[8,16,256]{2,1,0:T(8,128)}, f32[8,16,256]{2,1,0:T(8,128)S(1)}, u32[]{:S(2)}, u32[]{:S(2)}) collective-permute-start(f32[8,16,256]{2,1,0:T(8,128)} %get-tuple-element.23), channel_id=1, source_target_pairs={{0,1},{1,0},{2,3},{3,2},{4,5},{5,4},{6,7},{7,6},{8,9},{9,8},{10,11... | collective-permute-start | bytes 393224 | tf_op jit(solution)/shard_map/ppermute | solution.py:214
  56.5 0.7 %copy-start.4 = (f32[8,16,256]{2,1,0:T(8,128)}, f32[8,16,256]{2,1,0:T(8,128)S(1)}, u32[]{:S(2)}) copy-start(f32[8,16,256]{2,1,0:T(8,128)S(1)} %collective-permute-done.5.refs_6_.refs_0_) | copy-start | bytes 393220
  60.3 0.7 %copy-start.6 = (f32[8,16,256]{2,1,0:T(8,128)}, f32[8,16,256]{2,1,0:T(8,128)S(1)}, u32[]{:S(2)}) copy-start(f32[8,16,256]{2,1,0:T(8,128)S(1)} %collective-permute-done.7.refs_1_) | copy-start | bytes 393220

commit v14 on v13

--- a/solution.py
+++ b/solution.py
@@ -228,12 +228,31 @@
     pieces = refs[:n_pieces]
     rest = refs[n_pieces:]
     partial_ref = rest[0] if has_partial else None
-    out_ref, xs = rest[-2], rest[-1]
+    out_ref, xs, kr = rest[-3], rest[-2], rest[-1]
+    n_k, n_l = r_ref.shape
+    tile = out_ref.shape[1]
+    hi = lax.Precision.HIGHEST
+
+    @pl.when(pl.program_id(0) == 0)
+    def _():
+        shift = tile.bit_length() - 1
+        p = lax.broadcasted_iota(jnp.int32, (n_k * tile, n_k), 0)
+        q = lax.broadcasted_iota(jnp.int32, (n_k * tile, n_k), 1)
+        rep_rows = jnp.where(lax.shift_right_logical(p, shift) == q, 1.0, 0.0)
+        rows_r = jnp.dot(rep_rows, r_ref[...], precision=hi, preferred_element_type=jnp.float32)
+        p = lax.broadcasted_iota(jnp.int32, (n_l, n_l * tile), 0)
+        q = lax.broadcasted_iota(jnp.int32, (n_l, n_l * tile), 1)
+        rep_cols = jnp.where(p == lax.shift_right_logical(q, shift), 1.0, 0.0)
+        full = jnp.dot(rows_r, rep_cols, precision=hi, preferred_element_type=jnp.float32)
+        i = lax.broadcasted_iota(jnp.int32, full.shape, 0) & (tile - 1)
+        j = lax.broadcasted_iota(jnp.int32, full.shape, 1) & (tile - 1)
+        kr[...] = jnp.where(i == j, full, 0.0)
+
     step = pieces[0].shape[0]
-    for i, p in enumerate(pieces):
-        xs[i * step:(i + 1) * step] = p[...]
-    n_l, n_a, n_b = xs.shape
-    y = jnp.dot(r_ref[...], xs[...].reshape(n_l, n_a * n_b), precision=lax.Precision.HIGHEST,
+    for n, piece in enumerate(pieces):
+        xs[n * step:(n + 1) * step] = piece[...]
+    n_b = xs.shape[2]
+    y = jnp.dot(kr[...], xs[...].reshape(n_l * tile, n_b), precision=hi,
                 preferred_element_type=jnp.float32).reshape(out_ref.shape)
     if has_partial:
         y = partial_ref[...] + y
@@ -256,7 +275,10 @@
         grid=(n_a // tile,),
         in_specs=in_specs,
         out_specs=pl.BlockSpec((n_k, tile, n_b), lambda t: (0, t, 0)),
-        scratch_shapes=[pltpu.VMEM((n_l, tile, n_b), jnp.float32)],
+        scratch_shapes=[
+            pltpu.VMEM((n_l, tile, n_b), jnp.float32),
+            pltpu.VMEM((n_k * tile, n_l * tile), jnp.float32),
+        ],
     )(r_cols, *pieces, *extra, *fake)
 
 

time: 64.7 us -> 67.7 us (1.046)
  Pallas kernels: 20.3 us -> 23.4 us
    pallas_call x2, Pallas kernels: 6.34 us -> 9.41 us  [_radial(): pl.pallas_call(functools.partial(_radial_kernel, len(pieces), partial is...]
  transfers between devices with their start and end apart: 9 -> 9, of which waited for: 4 -> 3; matrix products, arithmetic and copies ran while one was open for 15% -> 14% of each run, Pallas kernels for 21% -> 23%
where the time goes in v14:
time: 67.7 us; the launch traced here: 67.2 us
  Pallas kernels  23.4 us (35%)
  starting transfers between devices  18.7 us (28%)
  local copies, waits for them, and re-layouts  12.5 us (18%)
  other arithmetic  6.44 us (10%)
  waiting for transfers between devices  3.49 us (5%)
  matrix products  2.37 us (4%)
    pallas_call x4, Pallas kernels, _sweeps(): pl.pallas_call(_sweep_kernel, out_shape=out_shape, grid=grid, in_specs=[p...  13.9 us
    pallas_call x2, Pallas kernels, _radial(): pl.pallas_call(functools.partial(_radial_kernel, len(pieces), partial is...  9.41 us
    ppermute x1, starting transfers between devices, per_device(): top = lax.ppermute(top_send, 'cap', _pairs(n_cap, 1))  5.57 us
    ppermute x4, starting transfers between devices, per_device(): lax.ppermute(send, 'rad', _pairs(n_rad, 1) + _pairs(n_rad, -1))  4.05 us
    all_to_all x1, starting transfers between devices, per_device(): lax.all_to_all(markers, 'lat', split_axis=1, concat_axis=1, tiled=True)  3.5 us
    unnamed x23, local copies, waits for them, and re-layouts  3.23 us
    ppermute x1, starting transfers between devices, per_device(): from_left = lax.ppermute(flat[piece:], 'lat', _pairs(n_lat, 1))  3.03 us
    concatenate x2, local copies, waits for them, and re-layouts, per_device(): jnp.concatenate([from_right, from_left]).reshape(2, 2, layers, ext_rows, g)  2.37 us
  transfers between devices with their start and end apart: 9, of which 3 were waited for; matrix products, arithmetic and copies ran while one was open for 14% of the time, Pallas kernels for 23%

profile of v14, /device:TPU:0, one launch (start us, length us, event | category | flops | bytes accessed | tf_op | source)
XLA Modules:
  0.0 67.2 jit_solution(13034134918441497669)
XLA Ops:
  0.0 1.9 %convert_select_fusion.eta_ref = f32[32,32,256]{2,1,0:T(8,128)S(1)} fusion(bf16[32,32,256]{2,1,0:T(8,128)(2,1)} %param.11, bf16[32,32,256]{2,1,0:T(8,128)(2,1)} %param.12, s32[32,32,256]{2,1,0:T(8,128)} %param.13), kind=kLoop, calls=%fused_computation.7 | loop fusion | flops 1835008 | bytes 3145728 | tf_op jit(solution)/shard_map/jit(_where)/select_n | solution.py:157
  1.9 0.0 copy-start
  1.9 0.1 fusion.17
  2.0 0.1 pad_maximum_fusion.2
  2.1 1.3 %collective-permute-start = (f32[32,6,256]{2,1,0:T(8,128)S(1)}, f32[32,6,256]{2,1,0:T(8,128)S(1)}, u32[]{:S(2)}, u32[]{:S(2)}) collective-permute-start(f32[32,6,256]{2,1,0:T(8,128)S(1)} %pad_maximum_fusion.2), channel_id=1, source_target_pairs={{8,0},{16,8},{24,16},{9,1},{17,9},{25,17},{10,2},{18,10},{26,18},{... | collective-permute-start | bytes 589832 | tf_op jit(solution)/shard_map/ppermute | solution.py:165
  3.4 0.1 pad_maximum_fusion.3
  3.5 5.6 %collective-permute-start.1 = (f32[32,6,256]{2,1,0:T(8,128)S(1)}, f32[32,6,256]{2,1,0:T(8,128)S(1)}, u32[]{:S(2)}, u32[]{:S(2)}) collective-permute-start(f32[32,6,256]{2,1,0:T(8,128)S(1)} %pad_maximum_fusion.3), channel_id=1, source_target_pairs={{0,8},{8,16},{16,24},{1,9},{9,17},{17,25},{2,10},{10,18},{18,26},{... | collective-permute-start | bytes 589832 | tf_op jit(solution)/shard_map/ppermute | solution.py:164
  9.1 0.2 fusion.16
  9.3 0.2 fusion.15
  9.5 0.0 copy-start.8
  9.5 0.0 copy-start.9
  9.5 0.3 copy.21
  9.8 0.3 copy.30
  10.1 0.3 copy.25
  10.4 0.3 copy.31
  10.7 0.1 pad.25.clone
  10.7 0.1 pad.3.clone
  10.8 0.1 fusion.11
  11.0 0.1 fusion.9
  11.0 0.7 %and_convert_fusion.mask_ref = f32[40,384]{1,0:T(8,128)} fusion(pred[384]{0:T(512)(128)(4,1)S(1)} %compare_and_fusion, pred[40]{0:T(512)(128)(4,1)S(1)} %compare_and_fusion.1), kind=kLoop, calls=%fused_computation.24 | loop fusion | flops 30720 | bytes 61864 | tf_op jit(solution)/shard_map/convert_element_type | solution.py:28
  11.7 1.6 %collective-permute-done = f32[32,6,256]{2,1,0:T(8,128)S(1)} collective-permute-done((f32[32,6,256]{2,1,0:T(8,128)S(1)}, f32[32,6,256]{2,1,0:T(8,128)S(1)}, u32[]{:S(2)}, u32[]{:S(2)}) %collective-permute-start) | collective-permute-done | bytes 196640 | tf_op jit(solution)/shard_map/ppermute | solution.py:165
  13.3 0.1 fusion.21
  13.4 1.2 %collective-permute-done.1 = f32[32,6,256]{2,1,0:T(8,128)S(1)} collective-permute-done((f32[32,6,256]{2,1,0:T(8,128)S(1)}, f32[32,6,256]{2,1,0:T(8,128)S(1)}, u32[]{:S(2)}, u32[]{:S(2)}) %collective-permute-start.1) | collective-permute-done | bytes 196640 | tf_op jit(solution)/shard_map/ppermute | solution.py:164
  14.6 0.1 fusion.22
  14.6 0.1 pad_maximum_fusion.4
  14.8 0.1 fusion.20
  14.9 0.3 copy.22
  15.2 0.1 fusion.19
  15.3 0.3 copy.20
  15.5 0.3 copy.26
  15.8 0.3 copy.24
  16.1 0.1 maximum_bitcast_fusion.3
  16.2 0.1 maximum_bitcast_fusion.2
  16.3 0.1 maximum_bitcast_fusion.5
  16.4 0.1 maximum_bitcast_fusion.4
  16.5 0.9 %copy.27 = f32[2,2,32,40,3]{4,3,2,1,0:T(8,128)S(1)} copy(f32[2,2,32,40,3]{3,2,4,1,0:T(8,128)S(1)} %pad_maximum_fusion.6) | data formatting | bytes 122880 | tf_op jit(solution)/shard_map/stack | solution.py:178
  17.5 1.9 %reshape.108 = f32[15360]{0:T(1024)S(1)} reshape(f32[2,2,32,40,3]{4,3,2,1,0:T(8,128)S(1)} %copy.27) | data formatting | bytes 122880 | tf_op jit(solution)/shard_map/reshape | solution.py:178
  19.4 1.3 %collective-permute-start.2 = (f32[7680]{0:T(1024)S(1)}, f32[7680]{0:T(1024)S(1)}, u32[]{:S(2)}, u32[]{:S(2)}) collective-permute-start(f32[7680]{0:T(1024)S(1)} %get-tuple-element.41), channel_id=1, source_target_pairs={{2,0},{4,2},{6,4},{3,1},{5,3},{7,5},{10,8},{12,10},{14,12},{11,9},... | collective-permute-start | bytes 92168 | tf_op jit(solution)/shard_map/ppermute | solution.py:182
  20.7 3.0 %collective-permute-start.3 = (f32[7680]{0:T(1024)S(1)}, f32[7680]{0:T(1024)S(1)}, u32[]{:S(2)}, u32[]{:S(2)}) collective-permute-start(f32[7680]{0:T(1024)S(1)} %get-tuple-element.42), channel_id=1, source_target_pairs={{0,2},{2,4},{4,6},{1,3},{3,5},{5,7},{8,10},{10,12},{12,14},{9,11},... | collective-permute-start | bytes 92168 | tf_op jit(solution)/shard_map/ppermute | solution.py:183
  23.7 0.7 copy.36
  24.4 3.5 %all-to-all-start = ((bf16[32,4,512]{2,0,1:T(8,128)(2,1)}), bf16[32,4,512]{2,0,1:T(8,128)(2,1)S(1)}, u32[]{:S(2)}, u32[]{:S(2)}) async-start(bf16[32,4,512]{2,0,1:T(8,128)(2,1)} %bitcast.28), calls=%async_computation | async-start | bytes 262144 | tf_op jit(solution)/shard_map/all_to_all | solution.py:181
  27.9 0.8 %pad_maximum_fusion.1.rowh_ref = f32[2,32,8,256]{3,2,1,0:T(8,128)} fusion(f32[1,32,8,256]{3,2,1,0:T(8,128)S(1)} %bitcast.30, f32[1,32,8,256]{3,2,1,0:T(8,128)S(1)} %bitcast.29), kind=kLoop, calls=%fused_computation.13 | loop fusion | flops 131072 | bytes 1048576 | tf_op jit(solution)/shard_map/stack | solution.py:167
  28.7 1.2 %concatenate.45 = f32[2,32,40,3]{3,2,1,0:T(8,128)S(1)} reshape(f32[7680]{0:T(1024)S(1)} %collective-permute-done.2) | data formatting | bytes 61440 | tf_op jit(solution)/shard_map/concatenate | solution.py:184
  29.9 1.2 %concatenate.46 = f32[2,32,40,3]{3,2,1,0:T(8,128)S(1)} reshape(f32[7680]{0:T(1024)S(1)} %collective-permute-done.3) | data formatting | bytes 61440 | tf_op jit(solution)/shard_map/concatenate | solution.py:184
  31.1 1.5 %pad_maximum_fusion.colh_ref = f32[2,32,40,128]{3,2,1,0:T(8,128)} fusion(f32[2,32,40,3]{3,2,1,0:T(8,128)S(1)} %concatenate.46, f32[2,32,40,3]{3,2,1,0:T(8,128)S(1)} %concatenate.45, f32[128]{0:T(128)S(1)} %pad.3.clone), kind=kLoop, calls=%fused_computation.10 | loop fusion | flops 655360 | bytes 1372672 | tf_op jit(solution)/shard_map/concatenate | solution.py:186
  32.6 2.4 %fusion.dep_ref = f32[32,32,256]{2,1,0:T(8,128)} fusion(pred[32,2048]{1,0:T(8,128)(4,1)S(1)} %fusion.9, bf16[32,2048]{1,0:T(8,128)(2,1)S(1)} %bitcast.33, s32[2048]{0:T(1024)S(1)} %get-tuple-element.45), kind=kOutput, calls=%fused_computation | convolution fusion | flops 1076363264 | bytes 1253376 | tf_op jit(solution)/shard_map/las,sb->lab/dot_general | solution.py:198
  35.0 3.5 %shard_map.91 = (f32[8,16,256]{2,1,0:T(8,128)}, f32[8,16,256]{2,1,0:T(8,128)}) custom-call(s32[1]{0:T(128)} %bitcast.rad_ref.after_ref.recv_ref, f32[32,32,256]{2,1,0:T(8,128)} %lam_ref.7, f32[32,32,256]{2,1,0:T(8,128)} %copy-done, f32[2,32,8,256]{3,2,1,0:T(8,128)} %pad_maximum_fusion.1.rowh_ref, f32[2,32,40,128]{3,2,1,0:T(8,128)} %pad_maximum_fusion.colh_ref, ...), custom_call_target="tpu_custom_call" | custom-call | flops 737280000 | bytes 12800000 | tf_op jit(solution)/shard_map/pallas_call | solution.py:104
  38.5 1.7 %collective-permute-start.4 = (f32[8,16,256]{2,1,0:T(8,128)}, f32[8,16,256]{2,1,0:T(8,128)S(1)}, u32[]{:S(2)}, u32[]{:S(2)}) collective-permute-start(f32[8,16,256]{2,1,0:T(8,128)} %get-tuple-element.19), channel_id=1, source_target_pairs={{0,1},{1,0},{2,3},{3,2},{4,5},{5,4},{6,7},{7,6},{8,9},{9,8},{10,11... | collective-permute-start | bytes 393224 | tf_op jit(solution)/shard_map/ppermute | solution.py:214
  40.2 3.5 %shard_map.92 = (f32[8,16,256]{2,1,0:T(8,128)}, f32[8,16,256]{2,1,0:T(8,128)}) custom-call(s32[1]{0:T(128)} %bitcast.rad_ref.after_ref.recv_ref, f32[32,32,256]{2,1,0:T(8,128)} %lam_ref.7, f32[32,32,256]{2,1,0:T(8,128)} %copy-done, f32[2,32,8,256]{3,2,1,0:T(8,128)} %pad_maximum_fusion.1.rowh_ref, f32[2,32,40,128]{3,2,1,0:T(8,128)} %pad_maximum_fusion.colh_ref, ...), custom_call_target="tpu_custom_call" | custom-call | flops 737280000 | bytes 12800000 | tf_op jit(solution)/shard_map/pallas_call | solution.py:104
  43.7 0.4 collective-permute-start.6
  44.0 0.1 constant_dynamic-slice_fusion.1
  44.1 0.7 %collective-permute-done.4.recv_ref.refs_4_ = f32[8,16,256]{2,1,0:T(8,128)S(1)} collective-permute-done((f32[8,16,256]{2,1,0:T(8,128)}, f32[8,16,256]{2,1,0:T(8,128)S(1)}, u32[]{:S(2)}, u32[]{:S(2)}) %collective-permute-start.4) | collective-permute-done | bytes 131104 | tf_op jit(solution)/shard_map/ppermute | solution.py:214
  44.8 0.7 copy-done.2
  45.4 3.5 %shard_map.93 = (f32[8,16,256]{2,1,0:T(8,128)}, f32[8,16,256]{2,1,0:T(8,128)}) custom-call(s32[1]{0:T(128)} %bitcast.rad_ref.after_ref.recv_ref, f32[32,32,256]{2,1,0:T(8,128)} %lam_ref.7, f32[32,32,256]{2,1,0:T(8,128)} %copy-done, f32[2,32,8,256]{3,2,1,0:T(8,128)} %pad_maximum_fusion.1.rowh_ref, f32[2,32,40,128]{3,2,1,0:T(8,128)} %pad_maximum_fusion.colh_ref, ...), custom_call_target="tpu_custom_call" | custom-call | flops 737280000 | bytes 12800000 | tf_op jit(solution)/shard_map/pallas_call | solution.py:104
  48.9 1.8 %collective-permute-start.5 = (f32[8,16,256]{2,1,0:T(8,128)}, f32[8,16,256]{2,1,0:T(8,128)S(1)}, u32[]{:S(2)}, u32[]{:S(2)}) collective-permute-start(f32[8,16,256]{2,1,0:T(8,128)} %get-tuple-element.20), channel_id=1, source_target_pairs={{0,1},{1,0},{2,3},{3,2},{4,5},{5,4},{6,7},{7,6},{8,9},{9,8},{10,11... | collective-permute-start | bytes 393224 | tf_op jit(solution)/shard_map/ppermute | solution.py:214
  50.8 0.7 copy-done.3
  51.4 3.5 %shard_map.94 = (f32[8,16,256]{2,1,0:T(8,128)}, f32[8,16,256]{2,1,0:T(8,128)}) custom-call(s32[1]{0:T(128)} %bitcast.rad_ref.after_ref.recv_ref, f32[32,32,256]{2,1,0:T(8,128)} %lam_ref.7, f32[32,32,256]{2,1,0:T(8,128)} %copy-done, f32[2,32,8,256]{3,2,1,0:T(8,128)} %pad_maximum_fusion.1.rowh_ref, f32[2,32,40,128]{3,2,1,0:T(8,128)} %pad_maximum_fusion.colh_ref, ...), custom_call_target="tpu_custom_call" | custom-call | flops 737280000 | bytes 12800000 | tf_op jit(solution)/shard_map/pallas_call | solution.py:104
  54.9 0.2 collective-permute-start.7
  55.1 0.7 %constant_dynamic-slice_fusion.r_ref = f32[64,16]{1,0:T(8,128)} fusion(f32[64,64]{1,0:T(8,128)S(1)} %copy-done.5, s32[]{:T(128)S(6)} %add.54), kind=kLoop, calls=%fused_computation.49 | loop fusion | bytes 8196 | tf_op jit(solution)/shard_map/slice | solution.py:224
  55.8 0.7 %pad_maximum_fusion.7.r_ref = f32[64,48]{1,0:T(8,128)} fusion(f32[64,32]{1,0:T(8,128)S(1)} %get-tuple-element.44, f32[64,32]{1,0:T(8,128)S(1)} %get-tuple-element.43), kind=kLoop, calls=%fused_computation.29 | loop fusion | flops 3072 | bytes 28672 | tf_op jit(solution)/shard_map/concatenate | solution.py:219
  56.5 0.7 copy-done.4
  57.1 5.3 %shard_map.95.refs_2_ = f32[64,16,256]{2,1,0:T(8,128)} custom-call(f32[64,48]{1,0:T(8,128)} %pad_maximum_fusion.7.r_ref, f32[8,16,256]{2,1,0:T(8,128)} %get-tuple-element.17.after_ref.refs_0_, f32[8,16,256]{2,1,0:T(8,128)} %get-tuple-element.18.after_ref.refs_1_, f32[8,16,256]{2,1,0:T(8,128)} %get-tuple-element.21.after_ref.refs_2_, ...), custom_call_target="tpu_custom_call" | custom-call | tf_op jit(solution)/shard_map/pallas_call | solution.py:272
  62.5 0.6 copy-done.6
  63.1 4.1 %shard_map.96 = f32[64,16,256]{2,1,0:T(8,128)} custom-call(f32[64,16]{1,0:T(8,128)} %constant_dynamic-slice_fusion.r_ref, f32[8,16,256]{2,1,0:T(8,128)} %copy-done.4, f32[8,16,256]{2,1,0:T(8,128)} %copy-done.6, f32[64,16,256]{2,1,0:T(8,128)} %shard_map.95.refs_2_), custom_call_target="tpu_custom_call" | custom-call | tf_op jit(solution)/shard_map/pallas_call | solution.py:272
  (30 shorter events, 0.2 us)
Async XLA Ops:
  0.0 1.9 %copy-start.1 = (f32[32,32,256]{2,1,0:T(8,128)S(1)}, f32[32,32,256]{2,1,0:T(8,128)}, u32[]{:S(2)}) copy-start(f32[32,32,256]{2,1,0:T(8,128)} %lam_ref.7) | copy-start | bytes 3145732
  1.9 7.3 %copy-start = (f32[32,32,256]{2,1,0:T(8,128)}, f32[32,32,256]{2,1,0:T(8,128)S(1)}, u32[]{:S(2)}) copy-start(f32[32,32,256]{2,1,0:T(8,128)S(1)} %convert_select_fusion.eta_ref) | copy-start | bytes 3145732
  2.1 11.2 %collective-permute-start = (f32[32,6,256]{2,1,0:T(8,128)S(1)}, f32[32,6,256]{2,1,0:T(8,128)S(1)}, u32[]{:S(2)}, u32[]{:S(2)}) collective-permute-start(f32[32,6,256]{2,1,0:T(8,128)S(1)} %pad_maximum_fusion.2), channel_id=1, source_target_pairs={{8,0},{16,8},{24,16},{9,1},{17,9},{25,17},{10,2},{18,10},{26,18},{... | collective-permute-start | bytes 589832 | tf_op jit(solution)/shard_map/ppermute | solution.py:165
  3.5 11.1 %collective-permute-start.1 = (f32[32,6,256]{2,1,0:T(8,128)S(1)}, f32[32,6,256]{2,1,0:T(8,128)S(1)}, u32[]{:S(2)}, u32[]{:S(2)}) collective-permute-start(f32[32,6,256]{2,1,0:T(8,128)S(1)} %pad_maximum_fusion.3), channel_id=1, source_target_pairs={{0,8},{8,16},{16,24},{1,9},{9,17},{17,25},{2,10},{10,18},{18,26},{... | collective-permute-start | bytes 589832 | tf_op jit(solution)/shard_map/ppermute | solution.py:164
  9.5 1.3 %copy-start.8 = (s32[2048]{0:T(1024)S(1)}, s32[2048]{0:T(1024)}, u32[]{:S(2)}) copy-start(s32[2048]{0:T(1024)} %param.16) | copy-start | bytes 24580
  9.5 1.3 %copy-start.9 = (s32[4]{0:T(128)S(1)}, s32[4]{0:T(128)}, u32[]{:S(2)}) copy-start(s32[4]{0:T(128)} %param.17) | copy-start | bytes 52
  17.5 6.2 %copy-start.7 = (bf16[32,2048]{1,0:T(8,128)(2,1)S(1)}, bf16[32,2048]{1,0:T(8,128)(2,1)}, u32[]{:S(2)}) copy-start(bf16[32,2048]{1,0:T(8,128)(2,1)} %param.15) | copy-start | bytes 393220
  19.4 9.4 %collective-permute-start.2 = (f32[7680]{0:T(1024)S(1)}, f32[7680]{0:T(1024)S(1)}, u32[]{:S(2)}, u32[]{:S(2)}) collective-permute-start(f32[7680]{0:T(1024)S(1)} %get-tuple-element.41), channel_id=1, source_target_pairs={{2,0},{4,2},{6,4},{3,1},{5,3},{7,5},{10,8},{12,10},{14,12},{11,9},... | collective-permute-start | bytes 92168 | tf_op jit(solution)/shard_map/ppermute | solution.py:182
  20.7 9.3 %collective-permute-start.3 = (f32[7680]{0:T(1024)S(1)}, f32[7680]{0:T(1024)S(1)}, u32[]{:S(2)}, u32[]{:S(2)}) collective-permute-start(f32[7680]{0:T(1024)S(1)} %get-tuple-element.42), channel_id=1, source_target_pairs={{0,2},{2,4},{4,6},{1,3},{3,5},{5,7},{8,10},{10,12},{12,14},{9,11},... | collective-permute-start | bytes 92168 | tf_op jit(solution)/shard_map/ppermute | solution.py:183
  24.4 8.2 %all-to-all-start = ((bf16[32,4,512]{2,0,1:T(8,128)(2,1)}), bf16[32,4,512]{2,0,1:T(8,128)(2,1)S(1)}, u32[]{:S(2)}, u32[]{:S(2)}) async-start(bf16[32,4,512]{2,0,1:T(8,128)(2,1)} %bitcast.28), calls=%async_computation | async-start | bytes 262144 | tf_op jit(solution)/shard_map/all_to_all | solution.py:181
  38.5 6.3 %collective-permute-start.4 = (f32[8,16,256]{2,1,0:T(8,128)}, f32[8,16,256]{2,1,0:T(8,128)S(1)}, u32[]{:S(2)}, u32[]{:S(2)}) collective-permute-start(f32[8,16,256]{2,1,0:T(8,128)} %get-tuple-element.19), channel_id=1, source_target_pairs={{0,1},{1,0},{2,3},{3,2},{4,5},{5,4},{6,7},{7,6},{8,9},{9,8},{10,11... | collective-permute-start | bytes 393224 | tf_op jit(solution)/shard_map/ppermute | solution.py:214
  40.2 3.9 %copy-start.5 = (f32[64,64]{1,0:T(8,128)S(1)}, f32[64,64]{1,0:T(8,128)}, u32[]{:S(2)}) copy-start(f32[64,64]{1,0:T(8,128)} %param.14) | copy-start | bytes 49156
  43.7 7.1 %collective-permute-start.6 = (f32[8,16,256]{2,1,0:T(8,128)}, f32[8,16,256]{2,1,0:T(8,128)S(1)}, u32[]{:S(2)}, u32[]{:S(2)}) collective-permute-start(f32[8,16,256]{2,1,0:T(8,128)} %get-tuple-element.22), channel_id=1, source_target_pairs={{0,1},{1,0},{2,3},{3,2},{4,5},{5,4},{6,7},{7,6},{8,9},{9,8},{10,11... | collective-permute-start | bytes 393224 | tf_op jit(solution)/shard_map/ppermute | solution.py:214
  44.8 0.7 copy-start.2
  48.9 7.5 %collective-permute-start.5 = (f32[8,16,256]{2,1,0:T(8,128)}, f32[8,16,256]{2,1,0:T(8,128)S(1)}, u32[]{:S(2)}, u32[]{:S(2)}) collective-permute-start(f32[8,16,256]{2,1,0:T(8,128)} %get-tuple-element.20), channel_id=1, source_target_pairs={{0,1},{1,0},{2,3},{3,2},{4,5},{5,4},{6,7},{7,6},{8,9},{9,8},{10,11... | collective-permute-start | bytes 393224 | tf_op jit(solution)/shard_map/ppermute | solution.py:214
  50.8 0.7 copy-start.3
  54.9 7.6 %collective-permute-start.7 = (f32[8,16,256]{2,1,0:T(8,128)}, f32[8,16,256]{2,1,0:T(8,128)S(1)}, u32[]{:S(2)}, u32[]{:S(2)}) collective-permute-start(f32[8,16,256]{2,1,0:T(8,128)} %get-tuple-element.23), channel_id=1, source_target_pairs={{0,1},{1,0},{2,3},{3,2},{4,5},{5,4},{6,7},{7,6},{8,9},{9,8},{10,11... | collective-permute-start | bytes 393224 | tf_op jit(solution)/shard_map/ppermute | solution.py:214
  56.5 0.7 copy-start.4
  62.4 0.7 copy-start.6

commit v15 on v13

--- a/solution.py
+++ b/solution.py
@@ -175,7 +175,8 @@
             parts.append(jnp.concatenate([src[:, :, sl], rowh[k][:, :, sl]], axis=1))
         return jnp.stack(parts)
 
-    flat = jnp.stack([col_piece(slice(0, g)), col_piece(slice(cols - g, cols))]).reshape(-1)
+    both_sides = jnp.stack([col_piece(slice(0, g)), col_piece(slice(cols - g, cols))])
+    flat = both_sides.reshape(-1, 128) if both_sides.size % 256 == 0 else both_sides.reshape(-1)
     piece = flat.shape[0] // 2
     flat, markers = lax.optimization_barrier((flat, marker_rows))
     received = lax.all_to_all(markers, "lat", split_axis=1, concat_axis=1, tiled=True)

time: 64.7 us -> 64.7 us (level)
    concatenate x2 -> x0, local copies, waits for them, and re-layouts: 2.37 us -> none  [per_device(): jnp.concatenate([from_right, from_left]).reshape(2, 2, layers, ext_rows, g)]
    squeeze x0 -> x2, local copies, waits for them, and re-layouts: none -> 2.37 us  [per_device(): colh = jnp.concatenate([got[0], zc, got[1]], axis=3)]
where the time goes in v15:
time: 64.7 us; the launch traced here: 64.2 us
  Pallas kernels  20.3 us (31%)
  starting transfers between devices  18.7 us (29%)
  local copies, waits for them, and re-layouts  12.5 us (19%)
  other arithmetic  6.44 us (10%)
  waiting for transfers between devices  3.55 us (5%)
  matrix products  2.37 us (4%)
    pallas_call x4, Pallas kernels, _sweeps(): pl.pallas_call(_sweep_kernel, out_shape=out_shape, grid=grid, in_specs=[p...  13.9 us
    pallas_call x2, Pallas kernels, _radial(): pl.pallas_call(functools.partial(_radial_kernel, len(pieces), partial is...  6.34 us
    ppermute x1, starting transfers between devices, per_device(): top = lax.ppermute(top_send, 'cap', _pairs(n_cap, 1))  5.57 us
    ppermute x4, starting transfers between devices, per_device(): lax.ppermute(send, 'rad', _pairs(n_rad, 1) + _pairs(n_rad, -1))  4.05 us
    all_to_all x1, starting transfers between devices, per_device(): lax.all_to_all(markers, 'lat', split_axis=1, concat_axis=1, tiled=True)  3.5 us
    unnamed x23, local copies, waits for them, and re-layouts  3.23 us
    ppermute x1, starting transfers between devices, per_device(): from_left = lax.ppermute(flat[piece:], 'lat', _pairs(n_lat, 1))  3.03 us
    squeeze x2, local copies, waits for them, and re-layouts, per_device(): colh = jnp.concatenate([got[0], zc, got[1]], axis=3)  2.37 us
  transfers between devices with their start and end apart: 9, of which 4 were waited for; matrix products, arithmetic and copies ran while one was open for 15% of the time, Pallas kernels for 21%

profile of v15, /device:TPU:0, one launch (start us, length us, event | category | flops | bytes accessed | tf_op | source)
XLA Modules:
  0.0 64.2 jit_solution(5524557324826259115)
XLA Ops:
  0.0 1.9 %convert_select_fusion.eta_ref = f32[32,32,256]{2,1,0:T(8,128)S(1)} fusion(bf16[32,32,256]{2,1,0:T(8,128)(2,1)} %param.11, bf16[32,32,256]{2,1,0:T(8,128)(2,1)} %param.12, s32[32,32,256]{2,1,0:T(8,128)} %param.13), kind=kLoop, calls=%fused_computation.7 | loop fusion | flops 1835008 | bytes 3145728 | tf_op jit(solution)/shard_map/jit(_where)/select_n | solution.py:157
  1.9 0.1 fusion.17
  2.0 0.1 pad_maximum_fusion.2
  2.1 1.3 %collective-permute-start = (f32[32,6,256]{2,1,0:T(8,128)S(1)}, f32[32,6,256]{2,1,0:T(8,128)S(1)}, u32[]{:S(2)}, u32[]{:S(2)}) collective-permute-start(f32[32,6,256]{2,1,0:T(8,128)S(1)} %pad_maximum_fusion.2), channel_id=1, source_target_pairs={{8,0},{16,8},{24,16},{9,1},{17,9},{25,17},{10,2},{18,10},{26,18},{... | collective-permute-start | bytes 589832 | tf_op jit(solution)/shard_map/ppermute | solution.py:165
  3.4 0.1 pad_maximum_fusion.3
  3.5 5.6 %collective-permute-start.1 = (f32[32,6,256]{2,1,0:T(8,128)S(1)}, f32[32,6,256]{2,1,0:T(8,128)S(1)}, u32[]{:S(2)}, u32[]{:S(2)}) collective-permute-start(f32[32,6,256]{2,1,0:T(8,128)S(1)} %pad_maximum_fusion.3), channel_id=1, source_target_pairs={{0,8},{8,16},{16,24},{1,9},{9,17},{17,25},{2,10},{10,18},{18,26},{... | collective-permute-start | bytes 589832 | tf_op jit(solution)/shard_map/ppermute | solution.py:164
  9.1 0.2 fusion.16
  9.3 0.2 fusion.15
  9.5 0.0 copy-start.8
  9.5 0.3 copy.21
  9.8 0.3 copy.30
  10.1 0.3 copy.25
  10.4 0.3 copy.31
  10.7 0.1 pad.25.clone
  10.7 0.1 pad.3.clone
  10.8 0.1 fusion.11
  11.0 0.1 fusion.9
  11.0 0.7 %and_convert_fusion.mask_ref = f32[40,384]{1,0:T(8,128)} fusion(pred[384]{0:T(512)(128)(4,1)S(1)} %compare_and_fusion, pred[40]{0:T(512)(128)(4,1)S(1)} %compare_and_fusion.1), kind=kLoop, calls=%fused_computation.24 | loop fusion | flops 30720 | bytes 61864 | tf_op jit(solution)/shard_map/convert_element_type | solution.py:28
  11.7 1.6 %collective-permute-done = f32[32,6,256]{2,1,0:T(8,128)S(1)} collective-permute-done((f32[32,6,256]{2,1,0:T(8,128)S(1)}, f32[32,6,256]{2,1,0:T(8,128)S(1)}, u32[]{:S(2)}, u32[]{:S(2)}) %collective-permute-start) | collective-permute-done | bytes 196640 | tf_op jit(solution)/shard_map/ppermute | solution.py:165
  13.3 0.1 fusion.21
  13.4 1.2 %collective-permute-done.1 = f32[32,6,256]{2,1,0:T(8,128)S(1)} collective-permute-done((f32[32,6,256]{2,1,0:T(8,128)S(1)}, f32[32,6,256]{2,1,0:T(8,128)S(1)}, u32[]{:S(2)}, u32[]{:S(2)}) %collective-permute-start.1) | collective-permute-done | bytes 196640 | tf_op jit(solution)/shard_map/ppermute | solution.py:164
  14.6 0.1 fusion.22
  14.6 0.1 pad_maximum_fusion.4
  14.8 0.1 fusion.20
  14.9 0.3 copy.22
  15.2 0.1 fusion.19
  15.3 0.3 copy.20
  15.5 0.3 copy.26
  15.8 0.3 copy.24
  16.1 0.1 maximum_bitcast_fusion.3
  16.2 0.1 maximum_bitcast_fusion.2
  16.3 0.1 maximum_bitcast_fusion.5
  16.4 0.1 maximum_bitcast_fusion.4
  16.5 0.9 %copy.27 = f32[2,2,32,40,3]{4,3,2,1,0:T(8,128)S(1)} copy(f32[2,2,32,40,3]{3,2,4,1,0:T(8,128)S(1)} %pad_maximum_fusion.6) | data formatting | bytes 122880 | tf_op jit(solution)/shard_map/stack | solution.py:178
  17.5 0.0 copy-start.7
  17.5 1.9 %reshape.102 = f32[120,128]{1,0:T(8,128)S(1)} reshape(f32[2,2,32,40,3]{4,3,2,1,0:T(8,128)S(1)} %copy.27) | data formatting | bytes 122880 | tf_op jit(solution)/shard_map/reshape | solution.py:179
  19.4 1.3 %collective-permute-start.2 = (f32[60,128]{1,0:T(8,128)S(1)}, f32[60,128]{1,0:T(8,128)S(1)}, u32[]{:S(2)}, u32[]{:S(2)}) collective-permute-start(f32[60,128]{1,0:T(8,128)S(1)} %get-tuple-element.41), channel_id=1, source_target_pairs={{2,0},{4,2},{6,4},{3,1},{5,3},{7,5},{10,8},{12,10},{14,12},{11,9},... | collective-permute-start | bytes 92168 | tf_op jit(solution)/shard_map/ppermute | solution.py:183
  20.7 3.0 %collective-permute-start.3 = (f32[60,128]{1,0:T(8,128)S(1)}, f32[60,128]{1,0:T(8,128)S(1)}, u32[]{:S(2)}, u32[]{:S(2)}) collective-permute-start(f32[60,128]{1,0:T(8,128)S(1)} %get-tuple-element.42), channel_id=1, source_target_pairs={{0,2},{2,4},{4,6},{1,3},{3,5},{5,7},{8,10},{10,12},{12,14},{9,11},... | collective-permute-start | bytes 92168 | tf_op jit(solution)/shard_map/ppermute | solution.py:184
  23.7 0.7 %copy.36 = bf16[4,4,8,512]{3,2,0,1:T(8,128)(2,1)} copy(bf16[4,4,8,512]{3,2,1,0:T(8,128)(2,1)S(1)} %bitcast.32) | data formatting | bytes 262144 | tf_op jit(solution)/shard_map/all_to_all | solution.py:182
  24.4 3.5 %all-to-all-start = ((bf16[32,4,512]{2,0,1:T(8,128)(2,1)}), bf16[32,4,512]{2,0,1:T(8,128)(2,1)S(1)}, u32[]{:S(2)}, u32[]{:S(2)}) async-start(bf16[32,4,512]{2,0,1:T(8,128)(2,1)} %bitcast.28), calls=%async_computation | async-start | bytes 262144 | tf_op jit(solution)/shard_map/all_to_all | solution.py:182
  27.9 0.8 %pad_maximum_fusion.1.rowh_ref = f32[2,32,8,256]{3,2,1,0:T(8,128)} fusion(f32[1,32,8,256]{3,2,1,0:T(8,128)S(1)} %bitcast.30, f32[1,32,8,256]{3,2,1,0:T(8,128)S(1)} %bitcast.29), kind=kLoop, calls=%fused_computation.13 | loop fusion | flops 131072 | bytes 1048576 | tf_op jit(solution)/shard_map/stack | solution.py:167
  28.7 1.2 %squeeze.6 = f32[2,32,40,3]{3,2,1,0:T(8,128)S(1)} reshape(f32[60,128]{1,0:T(8,128)S(1)} %collective-permute-done.2) | data formatting | bytes 61440 | tf_op jit(solution)/shard_map/squeeze | solution.py:187
  29.9 1.2 %squeeze.7 = f32[2,32,40,3]{3,2,1,0:T(8,128)S(1)} reshape(f32[60,128]{1,0:T(8,128)S(1)} %collective-permute-done.3) | data formatting | bytes 61440 | tf_op jit(solution)/shard_map/squeeze | solution.py:187
  31.1 1.5 %pad_maximum_fusion.colh_ref = f32[2,32,40,128]{3,2,1,0:T(8,128)} fusion(f32[2,32,40,3]{3,2,1,0:T(8,128)S(1)} %squeeze.7, f32[2,32,40,3]{3,2,1,0:T(8,128)S(1)} %squeeze.6, f32[128]{0:T(128)S(1)} %pad.3.clone), kind=kLoop, calls=%fused_computation.10 | loop fusion | flops 655360 | bytes 1372672 | tf_op jit(solution)/shard_map/concatenate | solution.py:187
  32.6 2.4 %fusion.dep_ref = f32[32,32,256]{2,1,0:T(8,128)} fusion(pred[32,2048]{1,0:T(8,128)(4,1)S(1)} %fusion.9, bf16[32,2048]{1,0:T(8,128)(2,1)S(1)} %bitcast.33, s32[2048]{0:T(1024)S(1)} %get-tuple-element.45), kind=kOutput, calls=%fused_computation | convolution fusion | flops 1076363264 | bytes 1253376 | tf_op jit(solution)/shard_map/las,sb->lab/dot_general | solution.py:199
  35.0 3.5 %shard_map.91 = (f32[8,16,256]{2,1,0:T(8,128)}, f32[8,16,256]{2,1,0:T(8,128)}) custom-call(s32[1]{0:T(128)} %bitcast.rad_ref.after_ref.recv_ref, f32[32,32,256]{2,1,0:T(8,128)} %lam_ref.7, f32[32,32,256]{2,1,0:T(8,128)} %copy-done, f32[2,32,8,256]{3,2,1,0:T(8,128)} %pad_maximum_fusion.1.rowh_ref, f32[2,32,40,128]{3,2,1,0:T(8,128)} %pad_maximum_fusion.colh_ref, ...), custom_call_target="tpu_custom_call" | custom-call | flops 737280000 | bytes 12800000 | tf_op jit(solution)/shard_map/pallas_call | solution.py:104
  38.5 1.7 %collective-permute-start.4 = (f32[8,16,256]{2,1,0:T(8,128)}, f32[8,16,256]{2,1,0:T(8,128)S(1)}, u32[]{:S(2)}, u32[]{:S(2)}) collective-permute-start(f32[8,16,256]{2,1,0:T(8,128)} %get-tuple-element.19), channel_id=1, source_target_pairs={{0,1},{1,0},{2,3},{3,2},{4,5},{5,4},{6,7},{7,6},{8,9},{9,8},{10,11... | collective-permute-start | bytes 393224 | tf_op jit(solution)/shard_map/ppermute | solution.py:215
  40.2 3.5 %shard_map.92 = (f32[8,16,256]{2,1,0:T(8,128)}, f32[8,16,256]{2,1,0:T(8,128)}) custom-call(s32[1]{0:T(128)} %bitcast.rad_ref.after_ref.recv_ref, f32[32,32,256]{2,1,0:T(8,128)} %lam_ref.7, f32[32,32,256]{2,1,0:T(8,128)} %copy-done, f32[2,32,8,256]{3,2,1,0:T(8,128)} %pad_maximum_fusion.1.rowh_ref, f32[2,32,40,128]{3,2,1,0:T(8,128)} %pad_maximum_fusion.colh_ref, ...), custom_call_target="tpu_custom_call" | custom-call | flops 737280000 | bytes 12800000 | tf_op jit(solution)/shard_map/pallas_call | solution.py:104
  43.7 0.4 collective-permute-start.6
  44.0 0.1 constant_dynamic-slice_fusion.1
  44.1 0.7 %collective-permute-done.4.recv_ref.refs_4_ = f32[8,16,256]{2,1,0:T(8,128)S(1)} collective-permute-done((f32[8,16,256]{2,1,0:T(8,128)}, f32[8,16,256]{2,1,0:T(8,128)S(1)}, u32[]{:S(2)}, u32[]{:S(2)}) %collective-permute-start.4) | collective-permute-done | bytes 131104 | tf_op jit(solution)/shard_map/ppermute | solution.py:215
  44.8 0.7 %copy-done.2 = f32[8,16,256]{2,1,0:T(8,128)} copy-done((f32[8,16,256]{2,1,0:T(8,128)}, f32[8,16,256]{2,1,0:T(8,128)S(1)}, u32[]{:S(2)}) %copy-start.2) | copy-done | bytes 131096
  45.4 3.5 %shard_map.93 = (f32[8,16,256]{2,1,0:T(8,128)}, f32[8,16,256]{2,1,0:T(8,128)}) custom-call(s32[1]{0:T(128)} %bitcast.rad_ref.after_ref.recv_ref, f32[32,32,256]{2,1,0:T(8,128)} %lam_ref.7, f32[32,32,256]{2,1,0:T(8,128)} %copy-done, f32[2,32,8,256]{3,2,1,0:T(8,128)} %pad_maximum_fusion.1.rowh_ref, f32[2,32,40,128]{3,2,1,0:T(8,128)} %pad_maximum_fusion.colh_ref, ...), custom_call_target="tpu_custom_call" | custom-call | flops 737280000 | bytes 12800000 | tf_op jit(solution)/shard_map/pallas_call | solution.py:104
  48.9 1.8 %collective-permute-start.5 = (f32[8,16,256]{2,1,0:T(8,128)}, f32[8,16,256]{2,1,0:T(8,128)S(1)}, u32[]{:S(2)}, u32[]{:S(2)}) collective-permute-start(f32[8,16,256]{2,1,0:T(8,128)} %get-tuple-element.20), channel_id=1, source_target_pairs={{0,1},{1,0},{2,3},{3,2},{4,5},{5,4},{6,7},{7,6},{8,9},{9,8},{10,11... | collective-permute-start | bytes 393224 | tf_op jit(solution)/shard_map/ppermute | solution.py:215
  50.8 0.7 %copy-done.3 = f32[8,16,256]{2,1,0:T(8,128)} copy-done((f32[8,16,256]{2,1,0:T(8,128)}, f32[8,16,256]{2,1,0:T(8,128)S(1)}, u32[]{:S(2)}) %copy-start.3) | copy-done | bytes 131096
  51.4 3.5 %shard_map.94 = (f32[8,16,256]{2,1,0:T(8,128)}, f32[8,16,256]{2,1,0:T(8,128)}) custom-call(s32[1]{0:T(128)} %bitcast.rad_ref.after_ref.recv_ref, f32[32,32,256]{2,1,0:T(8,128)} %lam_ref.7, f32[32,32,256]{2,1,0:T(8,128)} %copy-done, f32[2,32,8,256]{3,2,1,0:T(8,128)} %pad_maximum_fusion.1.rowh_ref, f32[2,32,40,128]{3,2,1,0:T(8,128)} %pad_maximum_fusion.colh_ref, ...), custom_call_target="tpu_custom_call" | custom-call | flops 737280000 | bytes 12800000 | tf_op jit(solution)/shard_map/pallas_call | solution.py:104
  54.9 0.2 collective-permute-start.7
  55.1 0.7 %constant_dynamic-slice_fusion.r_ref = f32[64,16]{1,0:T(8,128)} fusion(f32[64,64]{1,0:T(8,128)S(1)} %copy-done.5, s32[]{:T(128)S(6)} %add.54), kind=kLoop, calls=%fused_computation.49 | loop fusion | bytes 8196 | tf_op jit(solution)/shard_map/slice | solution.py:225
  55.8 0.7 %pad_maximum_fusion.7.r_ref = f32[64,48]{1,0:T(8,128)} fusion(f32[64,32]{1,0:T(8,128)S(1)} %get-tuple-element.44, f32[64,32]{1,0:T(8,128)S(1)} %get-tuple-element.43), kind=kLoop, calls=%fused_computation.29 | loop fusion | flops 3072 | bytes 28672 | tf_op jit(solution)/shard_map/concatenate | solution.py:220
  56.5 0.7 %copy-done.4 = f32[8,16,256]{2,1,0:T(8,128)} copy-done((f32[8,16,256]{2,1,0:T(8,128)}, f32[8,16,256]{2,1,0:T(8,128)S(1)}, u32[]{:S(2)}) %copy-start.4) | copy-done | bytes 131096
  57.1 3.2 %shard_map.95.refs_2_ = f32[64,16,256]{2,1,0:T(8,128)} custom-call(f32[64,48]{1,0:T(8,128)} %pad_maximum_fusion.7.r_ref, f32[8,16,256]{2,1,0:T(8,128)} %get-tuple-element.17.after_ref.refs_0_, f32[8,16,256]{2,1,0:T(8,128)} %get-tuple-element.18.after_ref.refs_1_, f32[8,16,256]{2,1,0:T(8,128)} %get-tuple-element.21.after_ref.refs_2_, ...), custom_call_target="tpu_custom_call" | custom-call | tf_op jit(solution)/shard_map/pallas_call | solution.py:254
  60.3 0.1 collective-permute-done.7.refs_1_
  60.3 0.7 %copy-done.6 = f32[8,16,256]{2,1,0:T(8,128)} copy-done((f32[8,16,256]{2,1,0:T(8,128)}, f32[8,16,256]{2,1,0:T(8,128)S(1)}, u32[]{:S(2)}) %copy-start.6) | copy-done | bytes 131096
  61.0 3.2 %shard_map.96 = f32[64,16,256]{2,1,0:T(8,128)} custom-call(f32[64,16]{1,0:T(8,128)} %constant_dynamic-slice_fusion.r_ref, f32[8,16,256]{2,1,0:T(8,128)} %copy-done.4, f32[8,16,256]{2,1,0:T(8,128)} %copy-done.6, f32[64,16,256]{2,1,0:T(8,128)} %shard_map.95.refs_2_), custom_call_target="tpu_custom_call" | custom-call | tf_op jit(solution)/shard_map/pallas_call | solution.py:254
  (30 shorter events, 0.2 us)
Async XLA Ops:
  0.0 1.9 %copy-start.1 = (f32[32,32,256]{2,1,0:T(8,128)S(1)}, f32[32,32,256]{2,1,0:T(8,128)}, u32[]{:S(2)}) copy-start(f32[32,32,256]{2,1,0:T(8,128)} %lam_ref.7) | copy-start | bytes 3145732
  1.9 7.3 %copy-start = (f32[32,32,256]{2,1,0:T(8,128)}, f32[32,32,256]{2,1,0:T(8,128)S(1)}, u32[]{:S(2)}) copy-start(f32[32,32,256]{2,1,0:T(8,128)S(1)} %convert_select_fusion.eta_ref) | copy-start | bytes 3145732
  2.1 11.2 %collective-permute-start = (f32[32,6,256]{2,1,0:T(8,128)S(1)}, f32[32,6,256]{2,1,0:T(8,128)S(1)}, u32[]{:S(2)}, u32[]{:S(2)}) collective-permute-start(f32[32,6,256]{2,1,0:T(8,128)S(1)} %pad_maximum_fusion.2), channel_id=1, source_target_pairs={{8,0},{16,8},{24,16},{9,1},{17,9},{25,17},{10,2},{18,10},{26,18},{... | collective-permute-start | bytes 589832 | tf_op jit(solution)/shard_map/ppermute | solution.py:165
  3.5 11.1 %collective-permute-start.1 = (f32[32,6,256]{2,1,0:T(8,128)S(1)}, f32[32,6,256]{2,1,0:T(8,128)S(1)}, u32[]{:S(2)}, u32[]{:S(2)}) collective-permute-start(f32[32,6,256]{2,1,0:T(8,128)S(1)} %pad_maximum_fusion.3), channel_id=1, source_target_pairs={{0,8},{8,16},{16,24},{1,9},{9,17},{17,25},{2,10},{10,18},{18,26},{... | collective-permute-start | bytes 589832 | tf_op jit(solution)/shard_map/ppermute | solution.py:164
  9.5 1.3 %copy-start.8 = (s32[2048]{0:T(1024)S(1)}, s32[2048]{0:T(1024)}, u32[]{:S(2)}) copy-start(s32[2048]{0:T(1024)} %param.16) | copy-start | bytes 24580
  9.5 1.3 %copy-start.9 = (s32[4]{0:T(128)S(1)}, s32[4]{0:T(128)}, u32[]{:S(2)}) copy-start(s32[4]{0:T(128)} %param.17) | copy-start | bytes 52
  17.5 6.2 %copy-start.7 = (bf16[32,2048]{1,0:T(8,128)(2,1)S(1)}, bf16[32,2048]{1,0:T(8,128)(2,1)}, u32[]{:S(2)}) copy-start(bf16[32,2048]{1,0:T(8,128)(2,1)} %param.15) | copy-start | bytes 393220
  19.4 9.4 %collective-permute-start.2 = (f32[60,128]{1,0:T(8,128)S(1)}, f32[60,128]{1,0:T(8,128)S(1)}, u32[]{:S(2)}, u32[]{:S(2)}) collective-permute-start(f32[60,128]{1,0:T(8,128)S(1)} %get-tuple-element.41), channel_id=1, source_target_pairs={{2,0},{4,2},{6,4},{3,1},{5,3},{7,5},{10,8},{12,10},{14,12},{11,9},... | collective-permute-start | bytes 92168 | tf_op jit(solution)/shard_map/ppermute | solution.py:183
  20.7 9.3 %collective-permute-start.3 = (f32[60,128]{1,0:T(8,128)S(1)}, f32[60,128]{1,0:T(8,128)S(1)}, u32[]{:S(2)}, u32[]{:S(2)}) collective-permute-start(f32[60,128]{1,0:T(8,128)S(1)} %get-tuple-element.42), channel_id=1, source_target_pairs={{0,2},{2,4},{4,6},{1,3},{3,5},{5,7},{8,10},{10,12},{12,14},{9,11},... | collective-permute-start | bytes 92168 | tf_op jit(solution)/shard_map/ppermute | solution.py:184
  24.4 8.2 %all-to-all-start = ((bf16[32,4,512]{2,0,1:T(8,128)(2,1)}), bf16[32,4,512]{2,0,1:T(8,128)(2,1)S(1)}, u32[]{:S(2)}, u32[]{:S(2)}) async-start(bf16[32,4,512]{2,0,1:T(8,128)(2,1)} %bitcast.28), calls=%async_computation | async-start | bytes 262144 | tf_op jit(solution)/shard_map/all_to_all | solution.py:182
  38.5 6.3 %collective-permute-start.4 = (f32[8,16,256]{2,1,0:T(8,128)}, f32[8,16,256]{2,1,0:T(8,128)S(1)}, u32[]{:S(2)}, u32[]{:S(2)}) collective-permute-start(f32[8,16,256]{2,1,0:T(8,128)} %get-tuple-element.19), channel_id=1, source_target_pairs={{0,1},{1,0},{2,3},{3,2},{4,5},{5,4},{6,7},{7,6},{8,9},{9,8},{10,11... | collective-permute-start | bytes 393224 | tf_op jit(solution)/shard_map/ppermute | solution.py:215
  40.2 3.9 %copy-start.5 = (f32[64,64]{1,0:T(8,128)S(1)}, f32[64,64]{1,0:T(8,128)}, u32[]{:S(2)}) copy-start(f32[64,64]{1,0:T(8,128)} %param.14) | copy-start | bytes 49156
  43.7 7.1 %collective-permute-start.6 = (f32[8,16,256]{2,1,0:T(8,128)}, f32[8,16,256]{2,1,0:T(8,128)S(1)}, u32[]{:S(2)}, u32[]{:S(2)}) collective-permute-start(f32[8,16,256]{2,1,0:T(8,128)} %get-tuple-element.22), channel_id=1, source_target_pairs={{0,1},{1,0},{2,3},{3,2},{4,5},{5,4},{6,7},{7,6},{8,9},{9,8},{10,11... | collective-permute-start | bytes 393224 | tf_op jit(solution)/shard_map/ppermute | solution.py:215
  44.8 0.7 %copy-start.2 = (f32[8,16,256]{2,1,0:T(8,128)}, f32[8,16,256]{2,1,0:T(8,128)S(1)}, u32[]{:S(2)}) copy-start(f32[8,16,256]{2,1,0:T(8,128)S(1)} %collective-permute-done.4.recv_ref.refs_4_) | copy-start | bytes 393220
  48.9 7.5 %collective-permute-start.5 = (f32[8,16,256]{2,1,0:T(8,128)}, f32[8,16,256]{2,1,0:T(8,128)S(1)}, u32[]{:S(2)}, u32[]{:S(2)}) collective-permute-start(f32[8,16,256]{2,1,0:T(8,128)} %get-tuple-element.20), channel_id=1, source_target_pairs={{0,1},{1,0},{2,3},{3,2},{4,5},{5,4},{6,7},{7,6},{8,9},{9,8},{10,11... | collective-permute-start | bytes 393224 | tf_op jit(solution)/shard_map/ppermute | solution.py:215
  50.8 0.7 %copy-start.3 = (f32[8,16,256]{2,1,0:T(8,128)}, f32[8,16,256]{2,1,0:T(8,128)S(1)}, u32[]{:S(2)}) copy-start(f32[8,16,256]{2,1,0:T(8,128)S(1)} %collective-permute-done.6.recv_ref.refs_5_) | copy-start | bytes 393220
  54.9 5.4 %collective-permute-start.7 = (f32[8,16,256]{2,1,0:T(8,128)}, f32[8,16,256]{2,1,0:T(8,128)S(1)}, u32[]{:S(2)}, u32[]{:S(2)}) collective-permute-start(f32[8,16,256]{2,1,0:T(8,128)} %get-tuple-element.23), channel_id=1, source_target_pairs={{0,1},{1,0},{2,3},{3,2},{4,5},{5,4},{6,7},{7,6},{8,9},{9,8},{10,11... | collective-permute-start | bytes 393224 | tf_op jit(solution)/shard_map/ppermute | solution.py:215
  56.5 0.7 %copy-start.4 = (f32[8,16,256]{2,1,0:T(8,128)}, f32[8,16,256]{2,1,0:T(8,128)S(1)}, u32[]{:S(2)}) copy-start(f32[8,16,256]{2,1,0:T(8,128)S(1)} %collective-permute-done.5.refs_6_.refs_0_) | copy-start | bytes 393220
  60.3 0.7 %copy-start.6 = (f32[8,16,256]{2,1,0:T(8,128)}, f32[8,16,256]{2,1,0:T(8,128)S(1)}, u32[]{:S(2)}) copy-start(f32[8,16,256]{2,1,0:T(8,128)S(1)} %collective-permute-done.7.refs_1_) | copy-start | bytes 393220

commit v16 on v13

--- a/solution.py
+++ b/solution.py
@@ -177,13 +177,13 @@
 
     flat = jnp.stack([col_piece(slice(0, g)), col_piece(slice(cols - g, cols))]).reshape(-1)
     piece = flat.shape[0] // 2
-    flat, markers = lax.optimization_barrier((flat, marker_rows))
-    received = lax.all_to_all(markers, "lat", split_axis=1, concat_axis=1, tiled=True)
     from_right = lax.ppermute(flat[:piece], "lat", _pairs(n_lat, -1))
     from_left = lax.ppermute(flat[piece:], "lat", _pairs(n_lat, 1))
     got = jnp.concatenate([from_right, from_left]).reshape(2, 2, layers, ext_rows, g)
     zc = jnp.zeros((2, layers, ext_rows, ext_cols - cols - 2 * g), jnp.float32)
     colh = jnp.concatenate([got[0], zc, got[1]], axis=3)
+    colh, markers = lax.optimization_barrier((colh, marker_rows))
+    received = lax.all_to_all(markers, "lat", split_axis=1, concat_axis=1, tiled=True)
     mask = _inside_mask(rows, cols, ext_rows, ext_cols, c, d, n_cap, n_lat)
 
     senders = n_lat

time: 64.7 us -> 68.7 us (1.062)
  waiting for transfers between devices: 3.55 us -> 7.43 us
    all_to_all x1, waiting for transfers between devices: 0.01 us -> 3.83 us  [per_device(): lax.all_to_all(markers, 'lat', split_axis=1, concat_axis=1, tiled=True)]
    reshape x1 -> x0, local copies, waits for them, and re-layouts: 1.87 us -> none  [per_device(): jnp.stack([col_piece(slice(0, g)), col_piece(slice(cols - g, cols))])]
    slice x0 -> x1, local copies, waits for them, and re-layouts: none -> 0.88 us  [per_device(): from_left = lax.ppermute(flat[piece:], 'lat', _pairs(n_lat, 1))]
    slice x1, local copies, waits for them, and re-layouts: 0.01 us -> 0.88 us  [per_device(): from_right = lax.ppermute(flat[:piece], 'lat', _pairs(n_lat, -1))]
    ppermute x1, waiting for transfers between devices: 1.6 us -> 2.4 us  [per_device(): bot = lax.ppermute(bot_send, 'cap', _pairs(n_cap, -1))]
    ppermute x4, waiting for transfers between devices: 0.74 us -> 0.01 us  [per_device(): lax.ppermute(send, 'rad', _pairs(n_rad, 1) + _pairs(n_rad, -1))]
  transfers between devices with their start and end apart: 9 -> 9, of which waited for: 4 -> 3; matrix products, arithmetic and copies ran while one was open for 15% -> 12% of each run, Pallas kernels for 21% -> 20%
where the time goes in v16:
time: 68.7 us; the launch traced here: 68.2 us
  Pallas kernels  20.3 us (30%)
  starting transfers between devices  19 us (28%)
  local copies, waits for them, and re-layouts  12.4 us (18%)
  waiting for transfers between devices  7.43 us (11%)
  other arithmetic  6.43 us (9%)
  matrix products  2.37 us (3%)
    pallas_call x4, Pallas kernels, _sweeps(): pl.pallas_call(_sweep_kernel, out_shape=out_shape, grid=grid, in_specs=[p...  13.9 us
    pallas_call x2, Pallas kernels, _radial(): pl.pallas_call(functools.partial(_radial_kernel, len(pieces), partial is...  6.35 us
    ppermute x1, starting transfers between devices, per_device(): top = lax.ppermute(top_send, 'cap', _pairs(n_cap, 1))  5.57 us
    ppermute x4, starting transfers between devices, per_device(): lax.ppermute(send, 'rad', _pairs(n_rad, 1) + _pairs(n_rad, -1))  4.05 us
    all_to_all x1, waiting for transfers between devices, per_device(): lax.all_to_all(markers, 'lat', split_axis=1, concat_axis=1, tiled=True)  3.83 us
    all_to_all x1, starting transfers between devices, per_device(): lax.all_to_all(markers, 'lat', split_axis=1, concat_axis=1, tiled=True)  3.76 us
    unnamed x23, local copies, waits for them, and re-layouts  3.19 us
    ppermute x1, starting transfers between devices, per_device(): from_left = lax.ppermute(flat[piece:], 'lat', _pairs(n_lat, 1))  3.03 us
  transfers between devices with their start and end apart: 9, of which 3 were waited for; matrix products, arithmetic and copies ran while one was open for 12% of the time, Pallas kernels for 20%

profile of v16, /device:TPU:0, one launch (start us, length us, event | category | flops | bytes accessed | tf_op | source)
XLA Modules:
  0.0 68.2 jit_solution(1062550902357571697)
XLA Ops:
  0.0 1.9 %convert_select_fusion.eta_ref = f32[32,32,256]{2,1,0:T(8,128)S(1)} fusion(bf16[32,32,256]{2,1,0:T(8,128)(2,1)} %param.11, bf16[32,32,256]{2,1,0:T(8,128)(2,1)} %param.12, s32[32,32,256]{2,1,0:T(8,128)} %param.13), kind=kLoop, calls=%fused_computation.7 | loop fusion | flops 1835008 | bytes 3145728 | tf_op jit(solution)/shard_map/jit(_where)/select_n | solution.py:157
  1.9 0.0 copy-start
  1.9 0.1 fusion.17
  2.0 0.1 pad_maximum_fusion.2
  2.1 1.3 %collective-permute-start = (f32[32,6,256]{2,1,0:T(8,128)S(1)}, f32[32,6,256]{2,1,0:T(8,128)S(1)}, u32[]{:S(2)}, u32[]{:S(2)}) collective-permute-start(f32[32,6,256]{2,1,0:T(8,128)S(1)} %pad_maximum_fusion.2), channel_id=1, source_target_pairs={{8,0},{16,8},{24,16},{9,1},{17,9},{25,17},{10,2},{18,10},{26,18},{... | collective-permute-start | bytes 589832 | tf_op jit(solution)/shard_map/ppermute | solution.py:165
  3.4 0.1 pad_maximum_fusion.3
  3.5 5.6 %collective-permute-start.1 = (f32[32,6,256]{2,1,0:T(8,128)S(1)}, f32[32,6,256]{2,1,0:T(8,128)S(1)}, u32[]{:S(2)}, u32[]{:S(2)}) collective-permute-start(f32[32,6,256]{2,1,0:T(8,128)S(1)} %pad_maximum_fusion.3), channel_id=1, source_target_pairs={{0,8},{8,16},{16,24},{1,9},{9,17},{17,25},{2,10},{10,18},{18,26},{... | collective-permute-start | bytes 589832 | tf_op jit(solution)/shard_map/ppermute | solution.py:164
  9.1 0.2 fusion.16
  9.3 0.2 fusion.15
  9.5 0.3 copy.22
  9.8 0.3 copy.32
  10.1 0.3 copy.27
  10.4 0.3 copy.33
  10.7 0.1 fusion.11
  10.8 0.1 pad.23.clone
  10.8 0.1 fusion.9
  10.9 2.4 %collective-permute-done = f32[32,6,256]{2,1,0:T(8,128)S(1)} collective-permute-done((f32[32,6,256]{2,1,0:T(8,128)S(1)}, f32[32,6,256]{2,1,0:T(8,128)S(1)}, u32[]{:S(2)}, u32[]{:S(2)}) %collective-permute-start) | collective-permute-done | bytes 196640 | tf_op jit(solution)/shard_map/ppermute | solution.py:165
  13.3 0.1 fusion.21
  13.4 1.2 %collective-permute-done.1 = f32[32,6,256]{2,1,0:T(8,128)S(1)} collective-permute-done((f32[32,6,256]{2,1,0:T(8,128)S(1)}, f32[32,6,256]{2,1,0:T(8,128)S(1)}, u32[]{:S(2)}, u32[]{:S(2)}) %collective-permute-start.1) | collective-permute-done | bytes 196640 | tf_op jit(solution)/shard_map/ppermute | solution.py:164
  14.6 0.1 fusion.22
  14.6 0.1 pad_maximum_fusion.4
  14.8 0.1 fusion.20
  14.9 0.3 copy.23
  15.2 0.1 fusion.19
  15.3 0.3 copy.21
  15.5 0.1 maximum_bitcast_fusion.1
  15.6 0.1 maximum_bitcast_fusion
  15.7 0.5 copy.24
  16.3 0.9 %slice.81 = f32[7680]{0:T(1024)S(1)} reshape(f32[2,32,40,3]{3,2,1,0:T(8,128)S(1)} %copy.24) | data formatting | bytes 61440 | tf_op jit(solution)/shard_map/slice | solution.py:180
  17.2 1.3 %collective-permute-start.2 = (f32[7680]{0:T(1024)S(1)}, f32[7680]{0:T(1024)S(1)}, u32[]{:S(2)}, u32[]{:S(2)}) collective-permute-start(f32[7680]{0:T(1024)S(1)} %slice.81), channel_id=1, source_target_pairs={{2,0},{4,2},{6,4},{3,1},{5,3},{7,5},{10,8},{12,10},{14,12},{11,9},... | collective-permute-start | bytes 92168 | tf_op jit(solution)/shard_map/ppermute | solution.py:180
  18.5 0.3 copy.28
  18.7 0.3 copy.26
  19.0 0.1 maximum_bitcast_fusion.3
  19.1 0.1 maximum_bitcast_fusion.2
  19.2 0.5 copy.29
  19.7 0.9 %slice.86 = f32[7680]{0:T(1024)S(1)} reshape(f32[2,32,40,3]{3,2,1,0:T(8,128)S(1)} %copy.29) | data formatting | bytes 61440 | tf_op jit(solution)/shard_map/slice | solution.py:181
  20.6 3.0 %collective-permute-start.3 = (f32[7680]{0:T(1024)S(1)}, f32[7680]{0:T(1024)S(1)}, u32[]{:S(2)}, u32[]{:S(2)}) collective-permute-start(f32[7680]{0:T(1024)S(1)} %slice.86), channel_id=1, source_target_pairs={{0,2},{2,4},{4,6},{1,3},{3,5},{5,7},{8,10},{10,12},{12,14},{9,11},... | collective-permute-start | bytes 92168 | tf_op jit(solution)/shard_map/ppermute | solution.py:181
  23.7 0.7 %and_convert_fusion.mask_ref = f32[40,384]{1,0:T(8,128)} fusion(pred[384]{0:T(512)(128)(4,1)S(1)} %compare_and_fusion, pred[40]{0:T(512)(128)(4,1)S(1)} %compare_and_fusion.1), kind=kLoop, calls=%fused_computation.23 | loop fusion | flops 30720 | bytes 61864 | tf_op jit(solution)/shard_map/convert_element_type | solution.py:28
  24.3 0.1 pad.3.clone
  24.4 1.2 %concatenate.43 = f32[2,32,40,3]{3,2,1,0:T(8,128)S(1)} reshape(f32[7680]{0:T(1024)S(1)} %collective-permute-done.2) | data formatting | bytes 61440 | tf_op jit(solution)/shard_map/concatenate | solution.py:182
  25.6 1.2 %concatenate.46 = f32[2,32,40,3]{3,2,1,0:T(8,128)S(1)} reshape(f32[7680]{0:T(1024)S(1)} %collective-permute-done.3) | data formatting | bytes 61440 | tf_op jit(solution)/shard_map/concatenate | solution.py:182
  26.8 1.5 %pad_maximum_fusion.colh_ref = f32[2,32,40,128]{3,2,1,0:T(8,128)} fusion(f32[2,32,40,3]{3,2,1,0:T(8,128)S(1)} %concatenate.46, f32[2,32,40,3]{3,2,1,0:T(8,128)S(1)} %concatenate.43, f32[128]{0:T(128)S(1)} %pad.3.clone), kind=kLoop, calls=%fused_computation.10 | loop fusion | flops 655360 | bytes 1372672 | tf_op jit(solution)/shard_map/concatenate | solution.py:184
  28.3 0.7 copy.38
  29.0 3.8 %all-to-all-start = ((bf16[32,4,512]{2,0,1:T(8,128)(2,1)}), bf16[32,4,512]{2,0,1:T(8,128)(2,1)S(1)}, u32[]{:S(2)}, u32[]{:S(2)}) async-start(bf16[32,4,512]{2,0,1:T(8,128)(2,1)} %bitcast.26), calls=%async_computation | async-start | bytes 262144 | tf_op jit(solution)/shard_map/all_to_all | solution.py:186
  32.7 0.8 %pad_maximum_fusion.1.rowh_ref = f32[2,32,8,256]{3,2,1,0:T(8,128)} fusion(f32[1,32,8,256]{3,2,1,0:T(8,128)S(1)} %bitcast.28, f32[1,32,8,256]{3,2,1,0:T(8,128)S(1)} %bitcast.27), kind=kLoop, calls=%fused_computation.13 | loop fusion | flops 131072 | bytes 1048576 | tf_op jit(solution)/shard_map/stack | solution.py:167
  33.6 3.8 %all-to-all-done = bf16[32,4,512]{2,0,1:T(8,128)(2,1)S(1)} async-done(((bf16[32,4,512]{2,0,1:T(8,128)(2,1)}), bf16[32,4,512]{2,0,1:T(8,128)(2,1)S(1)}, u32[]{:S(2)}, u32[]{:S(2)}) %all-to-all-start) | async-done | bytes 131104 | tf_op jit(solution)/shard_map/all_to_all | solution.py:186
  37.4 2.4 %fusion.dep_ref = f32[32,32,256]{2,1,0:T(8,128)} fusion(pred[32,2048]{1,0:T(8,128)(4,1)S(1)} %fusion.9, bf16[32,2048]{1,0:T(8,128)(2,1)S(1)} %bitcast.31, s32[2048]{0:T(1024)S(1)} %get-tuple-element.43), kind=kOutput, calls=%fused_computation | convolution fusion | flops 1076363264 | bytes 1253376 | tf_op jit(solution)/shard_map/las,sb->lab/dot_general | solution.py:198
  39.8 3.5 %shard_map.91 = (f32[8,16,256]{2,1,0:T(8,128)}, f32[8,16,256]{2,1,0:T(8,128)}) custom-call(s32[1]{0:T(128)} %bitcast.rad_ref.after_ref.recv_ref, f32[32,32,256]{2,1,0:T(8,128)} %lam_ref.7, f32[32,32,256]{2,1,0:T(8,128)} %copy-done, f32[2,32,8,256]{3,2,1,0:T(8,128)} %pad_maximum_fusion.1.rowh_ref, f32[2,32,40,128]{3,2,1,0:T(8,128)} %pad_maximum_fusion.colh_ref, ...), custom_call_target="tpu_custom_call" | custom-call | flops 737280000 | bytes 12800000 | tf_op jit(solution)/shard_map/pallas_call | solution.py:104
  43.3 1.5 %collective-permute-start.4 = (f32[8,16,256]{2,1,0:T(8,128)}, f32[8,16,256]{2,1,0:T(8,128)S(1)}, u32[]{:S(2)}, u32[]{:S(2)}) collective-permute-start(f32[8,16,256]{2,1,0:T(8,128)} %get-tuple-element.19), channel_id=1, source_target_pairs={{0,1},{1,0},{2,3},{3,2},{4,5},{5,4},{6,7},{7,6},{8,9},{9,8},{10,11... | collective-permute-start | bytes 393224 | tf_op jit(solution)/shard_map/ppermute | solution.py:214
  44.8 3.5 %shard_map.92 = (f32[8,16,256]{2,1,0:T(8,128)}, f32[8,16,256]{2,1,0:T(8,128)}) custom-call(s32[1]{0:T(128)} %bitcast.rad_ref.after_ref.recv_ref, f32[32,32,256]{2,1,0:T(8,128)} %lam_ref.7, f32[32,32,256]{2,1,0:T(8,128)} %copy-done, f32[2,32,8,256]{3,2,1,0:T(8,128)} %pad_maximum_fusion.1.rowh_ref, f32[2,32,40,128]{3,2,1,0:T(8,128)} %pad_maximum_fusion.colh_ref, ...), custom_call_target="tpu_custom_call" | custom-call | flops 737280000 | bytes 12800000 | tf_op jit(solution)/shard_map/pallas_call | solution.py:104
  48.3 0.5 collective-permute-start.6
  48.8 0.1 constant_dynamic-slice_fusion.1
  48.9 0.6 copy-done.2
  49.5 3.5 %shard_map.93 = (f32[8,16,256]{2,1,0:T(8,128)}, f32[8,16,256]{2,1,0:T(8,128)}) custom-call(s32[1]{0:T(128)} %bitcast.rad_ref.after_ref.recv_ref, f32[32,32,256]{2,1,0:T(8,128)} %lam_ref.7, f32[32,32,256]{2,1,0:T(8,128)} %copy-done, f32[2,32,8,256]{3,2,1,0:T(8,128)} %pad_maximum_fusion.1.rowh_ref, f32[2,32,40,128]{3,2,1,0:T(8,128)} %pad_maximum_fusion.colh_ref, ...), custom_call_target="tpu_custom_call" | custom-call | flops 737280000 | bytes 12800000 | tf_op jit(solution)/shard_map/pallas_call | solution.py:104
  53.0 1.5 %collective-permute-start.5 = (f32[8,16,256]{2,1,0:T(8,128)}, f32[8,16,256]{2,1,0:T(8,128)S(1)}, u32[]{:S(2)}, u32[]{:S(2)}) collective-permute-start(f32[8,16,256]{2,1,0:T(8,128)} %get-tuple-element.20), channel_id=1, source_target_pairs={{0,1},{1,0},{2,3},{3,2},{4,5},{5,4},{6,7},{7,6},{8,9},{9,8},{10,11... | collective-permute-start | bytes 393224 | tf_op jit(solution)/shard_map/ppermute | solution.py:214
  54.5 0.6 copy-done.3
  55.2 3.5 %shard_map.94 = (f32[8,16,256]{2,1,0:T(8,128)}, f32[8,16,256]{2,1,0:T(8,128)}) custom-call(s32[1]{0:T(128)} %bitcast.rad_ref.after_ref.recv_ref, f32[32,32,256]{2,1,0:T(8,128)} %lam_ref.7, f32[32,32,256]{2,1,0:T(8,128)} %copy-done, f32[2,32,8,256]{3,2,1,0:T(8,128)} %pad_maximum_fusion.1.rowh_ref, f32[2,32,40,128]{3,2,1,0:T(8,128)} %pad_maximum_fusion.colh_ref, ...), custom_call_target="tpu_custom_call" | custom-call | flops 737280000 | bytes 12800000 | tf_op jit(solution)/shard_map/pallas_call | solution.py:104
  58.6 0.5 collective-permute-start.7
  59.1 0.7 constant_dynamic-slice_fusion.r_ref
  59.8 0.7 %pad_maximum_fusion.8.r_ref = f32[64,48]{1,0:T(8,128)} fusion(f32[64,32]{1,0:T(8,128)S(1)} %get-tuple-element.42, f32[64,32]{1,0:T(8,128)S(1)} %get-tuple-element.41), kind=kLoop, calls=%fused_computation.28 | loop fusion | flops 3072 | bytes 28672 | tf_op jit(solution)/shard_map/concatenate | solution.py:219
  60.5 0.6 copy-done.4
  61.2 3.2 %shard_map.95.refs_2_ = f32[64,16,256]{2,1,0:T(8,128)} custom-call(f32[64,48]{1,0:T(8,128)} %pad_maximum_fusion.8.r_ref, f32[8,16,256]{2,1,0:T(8,128)} %get-tuple-element.17.after_ref.refs_0_, f32[8,16,256]{2,1,0:T(8,128)} %get-tuple-element.18.after_ref.refs_1_, f32[8,16,256]{2,1,0:T(8,128)} %get-tuple-element.21.after_ref.refs_2_, ...), custom_call_target="tpu_custom_call" | custom-call | tf_op jit(solution)/shard_map/pallas_call | solution.py:253
  64.3 0.6 copy-done.6
  65.0 3.2 %shard_map.96 = f32[64,16,256]{2,1,0:T(8,128)} custom-call(f32[64,16]{1,0:T(8,128)} %constant_dynamic-slice_fusion.r_ref, f32[8,16,256]{2,1,0:T(8,128)} %copy-done.4, f32[8,16,256]{2,1,0:T(8,128)} %copy-done.6, f32[64,16,256]{2,1,0:T(8,128)} %shard_map.95.refs_2_), custom_call_target="tpu_custom_call" | custom-call | tf_op jit(solution)/shard_map/pallas_call | solution.py:253
  (30 shorter events, 0.1 us)
Async XLA Ops:
  0.0 1.9 %copy-start.1 = (f32[32,32,256]{2,1,0:T(8,128)S(1)}, f32[32,32,256]{2,1,0:T(8,128)}, u32[]{:S(2)}) copy-start(f32[32,32,256]{2,1,0:T(8,128)} %lam_ref.7) | copy-start | bytes 3145732
  1.9 7.3 %copy-start = (f32[32,32,256]{2,1,0:T(8,128)}, f32[32,32,256]{2,1,0:T(8,128)S(1)}, u32[]{:S(2)}) copy-start(f32[32,32,256]{2,1,0:T(8,128)S(1)} %convert_select_fusion.eta_ref) | copy-start | bytes 3145732
  2.1 11.2 %collective-permute-start = (f32[32,6,256]{2,1,0:T(8,128)S(1)}, f32[32,6,256]{2,1,0:T(8,128)S(1)}, u32[]{:S(2)}, u32[]{:S(2)}) collective-permute-start(f32[32,6,256]{2,1,0:T(8,128)S(1)} %pad_maximum_fusion.2), channel_id=1, source_target_pairs={{8,0},{16,8},{24,16},{9,1},{17,9},{25,17},{10,2},{18,10},{26,18},{... | collective-permute-start | bytes 589832 | tf_op jit(solution)/shard_map/ppermute | solution.py:165
  3.5 11.1 %collective-permute-start.1 = (f32[32,6,256]{2,1,0:T(8,128)S(1)}, f32[32,6,256]{2,1,0:T(8,128)S(1)}, u32[]{:S(2)}, u32[]{:S(2)}) collective-permute-start(f32[32,6,256]{2,1,0:T(8,128)S(1)} %pad_maximum_fusion.3), channel_id=1, source_target_pairs={{0,8},{8,16},{16,24},{1,9},{9,17},{17,25},{2,10},{10,18},{18,26},{... | collective-permute-start | bytes 589832 | tf_op jit(solution)/shard_map/ppermute | solution.py:164
  9.5 1.2 %copy-start.8 = (s32[2048]{0:T(1024)S(1)}, s32[2048]{0:T(1024)}, u32[]{:S(2)}) copy-start(s32[2048]{0:T(1024)} %param.16) | copy-start | bytes 24580
  9.5 1.2 %copy-start.9 = (s32[4]{0:T(128)S(1)}, s32[4]{0:T(128)}, u32[]{:S(2)}) copy-start(s32[4]{0:T(128)} %param.17) | copy-start | bytes 52
  17.2 7.3 %collective-permute-start.2 = (f32[7680]{0:T(1024)S(1)}, f32[7680]{0:T(1024)S(1)}, u32[]{:S(2)}, u32[]{:S(2)}) collective-permute-start(f32[7680]{0:T(1024)S(1)} %slice.81), channel_id=1, source_target_pairs={{2,0},{4,2},{6,4},{3,1},{5,3},{7,5},{10,8},{12,10},{14,12},{11,9},... | collective-permute-start | bytes 92168 | tf_op jit(solution)/shard_map/ppermute | solution.py:180
  20.6 5.0 %collective-permute-start.3 = (f32[7680]{0:T(1024)S(1)}, f32[7680]{0:T(1024)S(1)}, u32[]{:S(2)}, u32[]{:S(2)}) collective-permute-start(f32[7680]{0:T(1024)S(1)} %slice.86), channel_id=1, source_target_pairs={{0,2},{2,4},{4,6},{1,3},{3,5},{5,7},{8,10},{10,12},{12,14},{9,11},... | collective-permute-start | bytes 92168 | tf_op jit(solution)/shard_map/ppermute | solution.py:181
  26.8 1.5 %copy-start.7 = (bf16[32,2048]{1,0:T(8,128)(2,1)S(1)}, bf16[32,2048]{1,0:T(8,128)(2,1)}, u32[]{:S(2)}) copy-start(bf16[32,2048]{1,0:T(8,128)(2,1)} %param.15) | copy-start | bytes 393220
  29.0 8.4 %all-to-all-start = ((bf16[32,4,512]{2,0,1:T(8,128)(2,1)}), bf16[32,4,512]{2,0,1:T(8,128)(2,1)S(1)}, u32[]{:S(2)}, u32[]{:S(2)}) async-start(bf16[32,4,512]{2,0,1:T(8,128)(2,1)} %bitcast.26), calls=%async_computation | async-start | bytes 262144 | tf_op jit(solution)/shard_map/all_to_all | solution.py:186
  43.3 5.6 %collective-permute-start.4 = (f32[8,16,256]{2,1,0:T(8,128)}, f32[8,16,256]{2,1,0:T(8,128)S(1)}, u32[]{:S(2)}, u32[]{:S(2)}) collective-permute-start(f32[8,16,256]{2,1,0:T(8,128)} %get-tuple-element.19), channel_id=1, source_target_pairs={{0,1},{1,0},{2,3},{3,2},{4,5},{5,4},{6,7},{7,6},{8,9},{9,8},{10,11... | collective-permute-start | bytes 393224 | tf_op jit(solution)/shard_map/ppermute | solution.py:214
  44.8 4.0 %copy-start.5 = (f32[64,64]{1,0:T(8,128)S(1)}, f32[64,64]{1,0:T(8,128)}, u32[]{:S(2)}) copy-start(f32[64,64]{1,0:T(8,128)} %param.14) | copy-start | bytes 49156
  48.3 6.2 %collective-permute-start.6 = (f32[8,16,256]{2,1,0:T(8,128)}, f32[8,16,256]{2,1,0:T(8,128)S(1)}, u32[]{:S(2)}, u32[]{:S(2)}) collective-permute-start(f32[8,16,256]{2,1,0:T(8,128)} %get-tuple-element.22), channel_id=1, source_target_pairs={{0,1},{1,0},{2,3},{3,2},{4,5},{5,4},{6,7},{7,6},{8,9},{9,8},{10,11... | collective-permute-start | bytes 393224 | tf_op jit(solution)/shard_map/ppermute | solution.py:214
  48.9 0.6 copy-start.2
  53.0 7.5 %collective-permute-start.5 = (f32[8,16,256]{2,1,0:T(8,128)}, f32[8,16,256]{2,1,0:T(8,128)S(1)}, u32[]{:S(2)}, u32[]{:S(2)}) collective-permute-start(f32[8,16,256]{2,1,0:T(8,128)} %get-tuple-element.20), channel_id=1, source_target_pairs={{0,1},{1,0},{2,3},{3,2},{4,5},{5,4},{6,7},{7,6},{8,9},{9,8},{10,11... | collective-permute-start | bytes 393224 | tf_op jit(solution)/shard_map/ppermute | solution.py:214
  54.5 0.6 copy-start.3
  58.6 5.7 %collective-permute-start.7 = (f32[8,16,256]{2,1,0:T(8,128)}, f32[8,16,256]{2,1,0:T(8,128)S(1)}, u32[]{:S(2)}, u32[]{:S(2)}) collective-permute-start(f32[8,16,256]{2,1,0:T(8,128)} %get-tuple-element.23), channel_id=1, source_target_pairs={{0,1},{1,0},{2,3},{3,2},{4,5},{5,4},{6,7},{7,6},{8,9},{9,8},{10,11... | collective-permute-start | bytes 393224 | tf_op jit(solution)/shard_map/ppermute | solution.py:214
  60.5 0.7 copy-start.4
  64.3 0.7 copy-start.6

commit v17 on v13

--- a/solution.py
+++ b/solution.py
@@ -36,10 +36,16 @@
                   after_ref, recv_ref, send_ref, keep_ref, lam_x, eta_x):
     layers, rows, cols = lam_ref.shape
     n_r, n_c = lam_x.shape[1], lam_x.shape[2]
+    g = colh_ref.shape[-1]
     for ref, src, k in ((lam_x, lam_ref, 0), (eta_x, eta_ref, 1)):
         ref[:, :rows, :cols] = src[...]
         ref[:, rows:, :cols] = rowh_ref[k]
-        ref[:, :, cols:] = colh_ref[k]
+        ref[:, :, cols:] = jnp.zeros((layers, n_r, n_c - cols), jnp.float32)
+        ref[:, :, cols:cols + g] = colh_ref[1, k]
+        left = ref[:, :, cols:]
+        ref[:, :, cols:] = jnp.zeros((layers, n_r, n_c - cols), jnp.float32)
+        ref[:, :, cols:cols + g] = colh_ref[0, k]
+        ref[:, :, cols:] = ref[:, :, cols:] + pltpu.roll(left, n_c - cols - g, 2)
     lam = lam_x[...]
     eta = eta_x[...]
     m = mask_ref[...][None]
@@ -110,7 +116,7 @@
             pl.BlockSpec((bl, rows, cols), lambda i: (i + off, 0, 0)),
             pl.BlockSpec((bl, rows, cols), lambda i: (i + off, 0, 0)),
             pl.BlockSpec((2, bl, ext_r - rows, cols), lambda i: (0, i + off, 0, 0)),
-            pl.BlockSpec((2, bl, ext_r, ext_c - cols), lambda i: (0, i + off, 0, 0)),
+            pl.BlockSpec((2, 2, bl, ext_r, GHOST), lambda i: (0, 0, i + off, 0, 0)),
             pl.BlockSpec((ext_r, ext_c), lambda i: (0, 0)),
             pl.BlockSpec((2, bl, rows, cols), lambda i: (0, i + off, 0, 0)),
             pl.BlockSpec((bl, rows, cols), lambda i: (i + off, 0, 0)),
@@ -182,8 +188,7 @@
     from_right = lax.ppermute(flat[:piece], "lat", _pairs(n_lat, -1))
     from_left = lax.ppermute(flat[piece:], "lat", _pairs(n_lat, 1))
     got = jnp.concatenate([from_right, from_left]).reshape(2, 2, layers, ext_rows, g)
-    zc = jnp.zeros((2, layers, ext_rows, ext_cols - cols - 2 * g), jnp.float32)
-    colh = jnp.concatenate([got[0], zc, got[1]], axis=3)
+    colh = got
     mask = _inside_mask(rows, cols, ext_rows, ext_cols, c, d, n_cap, n_lat)
 
     senders = n_lat

time: 64.7 us -> 70.3 us (1.087)
  local copies, waits for them, and re-layouts: 12.5 us -> 18.1 us
  other arithmetic: 6.44 us -> 4.94 us
  Pallas kernels: 20.3 us -> 21.3 us
    concatenate x2 -> x3, local copies, waits for them, and re-layouts: 2.37 us -> 6.69 us  [per_device(): jnp.concatenate([from_right, from_left]).reshape(2, 2, layers, ext_rows, g)]
    concatenate x1 -> x0, other arithmetic: 1.49 us -> none  [per_device(): colh = jnp.concatenate([got[0], zc, got[1]], axis=3)]
    unnamed x23 -> x26, local copies, waits for them, and re-layouts: 3.23 us -> 4.6 us
    pallas_call x4, Pallas kernels: 13.9 us -> 14.9 us  [_sweeps(): pl.pallas_call(_sweep_kernel, out_shape=out_shape, grid=grid, in_specs=[p...]
  transfers between devices with their start and end apart: 9 -> 9, of which waited for: 4 -> 3; matrix products, arithmetic and copies ran while one was open for 15% -> 20% of each run, Pallas kernels for 21% -> 21%
where the time goes in v17:
time: 70.3 us; the launch traced here: 69.6 us
  Pallas kernels  21.3 us (30%)
  starting transfers between devices  19.4 us (28%)
  local copies, waits for them, and re-layouts  18.1 us (26%)
  other arithmetic  4.94 us (7%)
  waiting for transfers between devices  3.31 us (5%)
  matrix products  2.36 us (3%)
    pallas_call x4, Pallas kernels, _sweeps(): pl.pallas_call(_sweep_kernel, out_shape=out_shape, grid=grid, in_specs=[p...  14.9 us
    concatenate x3, local copies, waits for them, and re-layouts, per_device(): jnp.concatenate([from_right, from_left]).reshape(2, 2, layers, ext_rows, g)  6.69 us
    pallas_call x2, Pallas kernels, _radial(): pl.pallas_call(functools.partial(_radial_kernel, len(pieces), partial is...  6.34 us
    ppermute x1, starting transfers between devices, per_device(): top = lax.ppermute(top_send, 'cap', _pairs(n_cap, 1))  5.57 us
    unnamed x26, local copies, waits for them, and re-layouts  4.6 us
    ppermute x4, starting transfers between devices, per_device(): lax.ppermute(send, 'rad', _pairs(n_rad, 1) + _pairs(n_rad, -1))  4.08 us
    ppermute x1, starting transfers between devices, per_device(): from_left = lax.ppermute(flat[piece:], 'lat', _pairs(n_lat, 1))  3.63 us
    all_to_all x1, starting transfers between devices, per_device(): lax.all_to_all(markers, 'lat', split_axis=1, concat_axis=1, tiled=True)  3.5 us
  transfers between devices with their start and end apart: 9, of which 3 were waited for; matrix products, arithmetic and copies ran while one was open for 20% of the time, Pallas kernels for 21%

profile of v17, /device:TPU:0, one launch (start us, length us, event | category | flops | bytes accessed | tf_op | source)
XLA Modules:
  0.0 69.6 jit_solution(2147860946638816855)
XLA Ops:
  0.0 1.9 %convert_select_fusion.eta_ref = f32[32,32,256]{2,1,0:T(8,128)S(1)} fusion(bf16[32,32,256]{2,1,0:T(8,128)(2,1)} %param.11, bf16[32,32,256]{2,1,0:T(8,128)(2,1)} %param.12, s32[32,32,256]{2,1,0:T(8,128)} %param.13), kind=kLoop, calls=%fused_computation.7 | loop fusion | flops 1835008 | bytes 3145728 | tf_op jit(solution)/shard_map/jit(_where)/select_n | solution.py:163
  1.9 0.1 fusion.17
  2.0 0.1 pad_maximum_fusion.1
  2.1 1.3 %collective-permute-start = (f32[32,6,256]{2,1,0:T(8,128)S(1)}, f32[32,6,256]{2,1,0:T(8,128)S(1)}, u32[]{:S(2)}, u32[]{:S(2)}) collective-permute-start(f32[32,6,256]{2,1,0:T(8,128)S(1)} %pad_maximum_fusion.1), channel_id=1, source_target_pairs={{8,0},{16,8},{24,16},{9,1},{17,9},{25,17},{10,2},{18,10},{26,18},{... | collective-permute-start | bytes 589832 | tf_op jit(solution)/shard_map/ppermute | solution.py:171
  3.4 0.1 pad_maximum_fusion.2
  3.5 5.6 %collective-permute-start.1 = (f32[32,6,256]{2,1,0:T(8,128)S(1)}, f32[32,6,256]{2,1,0:T(8,128)S(1)}, u32[]{:S(2)}, u32[]{:S(2)}) collective-permute-start(f32[32,6,256]{2,1,0:T(8,128)S(1)} %pad_maximum_fusion.2), channel_id=1, source_target_pairs={{0,8},{8,16},{16,24},{1,9},{9,17},{17,25},{2,10},{10,18},{18,26},{... | collective-permute-start | bytes 589832 | tf_op jit(solution)/shard_map/ppermute | solution.py:170
  9.1 0.2 fusion.16
  9.3 0.0 copy-start.9
  9.3 0.0 copy-start.10
  9.3 0.2 fusion.15
  9.5 0.3 copy.44
  9.8 0.3 copy.53
  10.1 0.3 copy.48
  10.4 0.3 copy.54
  10.7 0.1 fusion.11
  10.8 0.1 pad.22.clone
  10.9 0.1 fusion.9
  10.9 0.7 and_convert_fusion.mask_ref
  11.6 1.7 %collective-permute-done = f32[32,6,256]{2,1,0:T(8,128)S(1)} collective-permute-done((f32[32,6,256]{2,1,0:T(8,128)S(1)}, f32[32,6,256]{2,1,0:T(8,128)S(1)}, u32[]{:S(2)}, u32[]{:S(2)}) %collective-permute-start) | collective-permute-done | bytes 196640 | tf_op jit(solution)/shard_map/ppermute | solution.py:171
  13.3 0.1 fusion.21
  13.4 1.2 %collective-permute-done.1 = f32[32,6,256]{2,1,0:T(8,128)S(1)} collective-permute-done((f32[32,6,256]{2,1,0:T(8,128)S(1)}, f32[32,6,256]{2,1,0:T(8,128)S(1)}, u32[]{:S(2)}, u32[]{:S(2)}) %collective-permute-start.1) | collective-permute-done | bytes 196640 | tf_op jit(solution)/shard_map/ppermute | solution.py:170
  14.6 0.1 fusion.22
  14.6 0.1 pad_maximum_fusion.3
  14.8 0.1 fusion.20
  14.9 0.3 copy.45
  15.2 0.1 fusion.19
  15.3 0.3 copy.43
  15.5 0.3 copy.49
  15.8 0.3 copy.47
  16.1 0.1 maximum_bitcast_fusion.3
  16.2 0.1 maximum_bitcast_fusion.2
  16.3 0.1 maximum_bitcast_fusion.5
  16.4 0.1 maximum_bitcast_fusion.4
  16.5 0.0 copy-start.8
  16.5 0.9 %copy.50 = f32[2,2,32,40,3]{4,3,2,1,0:T(8,128)S(1)} copy(f32[2,2,32,40,3]{3,2,4,1,0:T(8,128)S(1)} %pad_maximum_fusion.5) | data formatting | bytes 122880 | tf_op jit(solution)/shard_map/stack | solution.py:184
  17.5 1.9 %reshape.100 = f32[15360]{0:T(1024)S(1)} reshape(f32[2,2,32,40,3]{4,3,2,1,0:T(8,128)S(1)} %copy.50) | data formatting | bytes 122880 | tf_op jit(solution)/shard_map/reshape | solution.py:184
  19.4 1.3 %collective-permute-start.2 = (f32[7680]{0:T(1024)S(1)}, f32[7680]{0:T(1024)S(1)}, u32[]{:S(2)}, u32[]{:S(2)}) collective-permute-start(f32[7680]{0:T(1024)S(1)} %get-tuple-element.42), channel_id=1, source_target_pairs={{2,0},{4,2},{6,4},{3,1},{5,3},{7,5},{10,8},{12,10},{14,12},{11,9},... | collective-permute-start | bytes 92168 | tf_op jit(solution)/shard_map/ppermute | solution.py:188
  20.7 3.6 %collective-permute-start.3 = (f32[7680]{0:T(1024)S(1)}, f32[7680]{0:T(1024)}, u32[]{:S(2)}, u32[]{:S(2)}) collective-permute-start(f32[7680]{0:T(1024)S(1)} %get-tuple-element.41), channel_id=1, source_target_pairs={{0,2},{2,4},{4,6},{1,3},{3,5},{5,7},{8,10},{10,12},{12,14},{9,11},... | collective-permute-start | bytes 92168 | tf_op jit(solution)/shard_map/ppermute | solution.py:189
  24.3 0.7 copy.59
  25.0 3.5 %all-to-all-start = ((bf16[32,4,512]{2,0,1:T(8,128)(2,1)}), bf16[32,4,512]{2,0,1:T(8,128)(2,1)S(1)}, u32[]{:S(2)}, u32[]{:S(2)}) async-start(bf16[32,4,512]{2,0,1:T(8,128)(2,1)} %bitcast.28), calls=%async_computation | async-start | bytes 262144 | tf_op jit(solution)/shard_map/all_to_all | solution.py:187
  28.5 0.8 %pad_maximum_fusion.rowh_ref = f32[2,32,8,256]{3,2,1,0:T(8,128)} fusion(f32[1,32,8,256]{3,2,1,0:T(8,128)S(1)} %bitcast.30, f32[1,32,8,256]{3,2,1,0:T(8,128)S(1)} %bitcast.29), kind=kLoop, calls=%fused_computation.12 | loop fusion | flops 131072 | bytes 1048576 | tf_op jit(solution)/shard_map/stack | solution.py:173
  29.3 2.3 %concatenate.43 = f32[1,2,32,40,3]{4,3,2,1,0:T(8,128)} reshape(f32[7680]{0:T(1024)S(1)} %collective-permute-done.2) | data formatting | bytes 61440 | tf_op jit(solution)/shard_map/concatenate | solution.py:190
  31.6 1.4 %constant_dynamic-update-slice_fusion.1 = f32[2,2,32,40,3]{4,3,2,1,0:T(8,128)S(1)} fusion(f32[1,2,32,40,3]{4,3,2,1,0:T(8,128)} %concatenate.43), kind=kLoop, calls=%fused_computation.39 | loop fusion | bytes 1341440
  33.0 3.0 %concatenate.44 = f32[1,2,32,40,3]{4,3,2,1,0:T(8,128)} reshape(f32[7680]{0:T(1024)} %collective-permute-done.3) | data formatting | bytes 61440 | tf_op jit(solution)/shard_map/concatenate | solution.py:190
  36.0 1.4 %constant_dynamic-update-slice_fusion.colh_ref = f32[2,2,32,40,3]{4,3,2,1,0:T(8,128)S(1)} fusion(f32[2,2,32,40,3]{4,3,2,1,0:T(8,128)S(1)} %constant_dynamic-update-slice_fusion.1, f32[1,2,32,40,3]{4,3,2,1,0:T(8,128)} %concatenate.44), kind=kLoop, calls=%fused_computation.38 | loop fusion | bytes 1341440 | tf_op jit(solution)/shard_map/concatenate | solution.py:190
  37.5 2.4 %fusion.dep_ref = f32[32,32,256]{2,1,0:T(8,128)} fusion(pred[32,2048]{1,0:T(8,128)(4,1)S(1)} %fusion.9, bf16[32,2048]{1,0:T(8,128)(2,1)S(1)} %bitcast.33, s32[2048]{0:T(1024)S(1)} %get-tuple-element.45), kind=kOutput, calls=%fused_computation | convolution fusion | flops 1076363264 | bytes 1253376 | tf_op jit(solution)/shard_map/las,sb->lab/dot_general | solution.py:203
  39.8 3.7 %shard_map.91 = (f32[8,16,256]{2,1,0:T(8,128)}, f32[8,16,256]{2,1,0:T(8,128)}) custom-call(s32[1]{0:T(128)} %bitcast.rad_ref.after_ref.recv_ref, f32[32,32,256]{2,1,0:T(8,128)} %lam_ref.7, f32[32,32,256]{2,1,0:T(8,128)} %copy-done.1, f32[2,32,8,256]{3,2,1,0:T(8,128)} %pad_maximum_fusion.rowh_ref, f32[2,2,32,40,3]{4,3,2,1,0:T(8,128)} %copy-done, ...), custom_call_target="tpu_custom_call" | custom-call | flops 737280000 | bytes 12800000 | tf_op jit(solution)/shard_map/pallas_call | solution.py:110
  43.5 1.7 %collective-permute-start.4 = (f32[8,16,256]{2,1,0:T(8,128)}, f32[8,16,256]{2,1,0:T(8,128)S(1)}, u32[]{:S(2)}, u32[]{:S(2)}) collective-permute-start(f32[8,16,256]{2,1,0:T(8,128)} %get-tuple-element.19), channel_id=1, source_target_pairs={{0,1},{1,0},{2,3},{3,2},{4,5},{5,4},{6,7},{7,6},{8,9},{9,8},{10,11... | collective-permute-start | bytes 393224 | tf_op jit(solution)/shard_map/ppermute | solution.py:219
  45.2 3.7 %shard_map.92 = (f32[8,16,256]{2,1,0:T(8,128)}, f32[8,16,256]{2,1,0:T(8,128)}) custom-call(s32[1]{0:T(128)} %bitcast.rad_ref.after_ref.recv_ref, f32[32,32,256]{2,1,0:T(8,128)} %lam_ref.7, f32[32,32,256]{2,1,0:T(8,128)} %copy-done.1, f32[2,32,8,256]{3,2,1,0:T(8,128)} %pad_maximum_fusion.rowh_ref, f32[2,2,32,40,3]{4,3,2,1,0:T(8,128)} %copy-done, ...), custom_call_target="tpu_custom_call" | custom-call | flops 737280000 | bytes 12800000 | tf_op jit(solution)/shard_map/pallas_call | solution.py:110
  49.0 0.4 collective-permute-start.6
  49.3 0.1 constant_dynamic-slice_fusion.1
  49.4 0.4 collective-permute-done.4.recv_ref.refs_4_
  49.8 0.7 copy-done.3
  50.5 3.7 %shard_map.93 = (f32[8,16,256]{2,1,0:T(8,128)}, f32[8,16,256]{2,1,0:T(8,128)}) custom-call(s32[1]{0:T(128)} %bitcast.rad_ref.after_ref.recv_ref, f32[32,32,256]{2,1,0:T(8,128)} %lam_ref.7, f32[32,32,256]{2,1,0:T(8,128)} %copy-done.1, f32[2,32,8,256]{3,2,1,0:T(8,128)} %pad_maximum_fusion.rowh_ref, f32[2,2,32,40,3]{4,3,2,1,0:T(8,128)} %copy-done, ...), custom_call_target="tpu_custom_call" | custom-call | flops 737280000 | bytes 12800000 | tf_op jit(solution)/shard_map/pallas_call | solution.py:110
  54.2 1.5 %collective-permute-start.5 = (f32[8,16,256]{2,1,0:T(8,128)}, f32[8,16,256]{2,1,0:T(8,128)S(1)}, u32[]{:S(2)}, u32[]{:S(2)}) collective-permute-start(f32[8,16,256]{2,1,0:T(8,128)} %get-tuple-element.20), channel_id=1, source_target_pairs={{0,1},{1,0},{2,3},{3,2},{4,5},{5,4},{6,7},{7,6},{8,9},{9,8},{10,11... | collective-permute-start | bytes 393224 | tf_op jit(solution)/shard_map/ppermute | solution.py:219
  55.7 0.6 copy-done.4
  56.4 3.7 %shard_map.94 = (f32[8,16,256]{2,1,0:T(8,128)}, f32[8,16,256]{2,1,0:T(8,128)}) custom-call(s32[1]{0:T(128)} %bitcast.rad_ref.after_ref.recv_ref, f32[32,32,256]{2,1,0:T(8,128)} %lam_ref.7, f32[32,32,256]{2,1,0:T(8,128)} %copy-done.1, f32[2,32,8,256]{3,2,1,0:T(8,128)} %pad_maximum_fusion.rowh_ref, f32[2,2,32,40,3]{4,3,2,1,0:T(8,128)} %copy-done, ...), custom_call_target="tpu_custom_call" | custom-call | flops 737280000 | bytes 12800000 | tf_op jit(solution)/shard_map/pallas_call | solution.py:110
  60.1 0.5 collective-permute-start.7
  60.6 0.7 constant_dynamic-slice_fusion.r_ref
  61.3 0.7 pad_maximum_fusion.6.r_ref
  62.0 0.6 copy-done.5
  62.6 3.2 %shard_map.95.refs_2_ = f32[64,16,256]{2,1,0:T(8,128)} custom-call(f32[64,48]{1,0:T(8,128)} %pad_maximum_fusion.6.r_ref, f32[8,16,256]{2,1,0:T(8,128)} %get-tuple-element.17.after_ref.refs_0_, f32[8,16,256]{2,1,0:T(8,128)} %get-tuple-element.18.after_ref.refs_1_, f32[8,16,256]{2,1,0:T(8,128)} %get-tuple-element.21.after_ref.refs_2_, ...), custom_call_target="tpu_custom_call" | custom-call | tf_op jit(solution)/shard_map/pallas_call | solution.py:258
  65.8 0.7 copy-done.7
  66.5 3.2 %shard_map.96 = f32[64,16,256]{2,1,0:T(8,128)} custom-call(f32[64,16]{1,0:T(8,128)} %constant_dynamic-slice_fusion.r_ref, f32[8,16,256]{2,1,0:T(8,128)} %copy-done.5, f32[8,16,256]{2,1,0:T(8,128)} %copy-done.7, f32[64,16,256]{2,1,0:T(8,128)} %shard_map.95.refs_2_), custom_call_target="tpu_custom_call" | custom-call | tf_op jit(solution)/shard_map/pallas_call | solution.py:258
  (31 shorter events, 0.2 us)
Async XLA Ops:
  0.0 1.9 %copy-start.2 = (f32[32,32,256]{2,1,0:T(8,128)S(1)}, f32[32,32,256]{2,1,0:T(8,128)}, u32[]{:S(2)}) copy-start(f32[32,32,256]{2,1,0:T(8,128)} %lam_ref.7) | copy-start | bytes 3145732
  1.9 7.6 %copy-start.1 = (f32[32,32,256]{2,1,0:T(8,128)}, f32[32,32,256]{2,1,0:T(8,128)S(1)}, u32[]{:S(2)}) copy-start(f32[32,32,256]{2,1,0:T(8,128)S(1)} %convert_select_fusion.eta_ref) | copy-start | bytes 3145732
  2.1 11.2 %collective-permute-start = (f32[32,6,256]{2,1,0:T(8,128)S(1)}, f32[32,6,256]{2,1,0:T(8,128)S(1)}, u32[]{:S(2)}, u32[]{:S(2)}) collective-permute-start(f32[32,6,256]{2,1,0:T(8,128)S(1)} %pad_maximum_fusion.1), channel_id=1, source_target_pairs={{8,0},{16,8},{24,16},{9,1},{17,9},{25,17},{10,2},{18,10},{26,18},{... | collective-permute-start | bytes 589832 | tf_op jit(solution)/shard_map/ppermute | solution.py:171
  3.5 11.1 %collective-permute-start.1 = (f32[32,6,256]{2,1,0:T(8,128)S(1)}, f32[32,6,256]{2,1,0:T(8,128)S(1)}, u32[]{:S(2)}, u32[]{:S(2)}) collective-permute-start(f32[32,6,256]{2,1,0:T(8,128)S(1)} %pad_maximum_fusion.2), channel_id=1, source_target_pairs={{0,8},{8,16},{16,24},{1,9},{9,17},{17,25},{2,10},{10,18},{18,26},{... | collective-permute-start | bytes 589832 | tf_op jit(solution)/shard_map/ppermute | solution.py:170
  9.3 1.4 %copy-start.9 = (s32[2048]{0:T(1024)S(1)}, s32[2048]{0:T(1024)}, u32[]{:S(2)}) copy-start(s32[2048]{0:T(1024)} %param.16) | copy-start | bytes 24580
  9.3 1.4 %copy-start.10 = (s32[4]{0:T(128)S(1)}, s32[4]{0:T(128)}, u32[]{:S(2)}) copy-start(s32[4]{0:T(128)} %param.17) | copy-start | bytes 52
  16.5 7.8 %copy-start.8 = (bf16[32,2048]{1,0:T(8,128)(2,1)S(1)}, bf16[32,2048]{1,0:T(8,128)(2,1)}, u32[]{:S(2)}) copy-start(bf16[32,2048]{1,0:T(8,128)(2,1)} %param.15) | copy-start | bytes 393220
  19.4 9.9 %collective-permute-start.2 = (f32[7680]{0:T(1024)S(1)}, f32[7680]{0:T(1024)S(1)}, u32[]{:S(2)}, u32[]{:S(2)}) collective-permute-start(f32[7680]{0:T(1024)S(1)} %get-tuple-element.42), channel_id=1, source_target_pairs={{2,0},{4,2},{6,4},{3,1},{5,3},{7,5},{10,8},{12,10},{14,12},{11,9},... | collective-permute-start | bytes 92168 | tf_op jit(solution)/shard_map/ppermute | solution.py:188
  20.7 12.3 %collective-permute-start.3 = (f32[7680]{0:T(1024)S(1)}, f32[7680]{0:T(1024)}, u32[]{:S(2)}, u32[]{:S(2)}) collective-permute-start(f32[7680]{0:T(1024)S(1)} %get-tuple-element.41), channel_id=1, source_target_pairs={{0,2},{2,4},{4,6},{1,3},{3,5},{5,7},{8,10},{10,12},{12,14},{9,11},... | collective-permute-start | bytes 92168 | tf_op jit(solution)/shard_map/ppermute | solution.py:189
  25.0 12.5 %all-to-all-start = ((bf16[32,4,512]{2,0,1:T(8,128)(2,1)}), bf16[32,4,512]{2,0,1:T(8,128)(2,1)S(1)}, u32[]{:S(2)}, u32[]{:S(2)}) async-start(bf16[32,4,512]{2,0,1:T(8,128)(2,1)} %bitcast.28), calls=%async_computation | async-start | bytes 262144 | tf_op jit(solution)/shard_map/all_to_all | solution.py:187
  37.4 2.4 %copy-start = (f32[2,2,32,40,3]{4,3,2,1,0:T(8,128)}, f32[2,2,32,40,3]{4,3,2,1,0:T(8,128)S(1)}, u32[]{:S(2)}) copy-start(f32[2,2,32,40,3]{4,3,2,1,0:T(8,128)S(1)} %constant_dynamic-update-slice_fusion.colh_ref) | copy-start | bytes 184324
  43.5 6.3 %collective-permute-start.4 = (f32[8,16,256]{2,1,0:T(8,128)}, f32[8,16,256]{2,1,0:T(8,128)S(1)}, u32[]{:S(2)}, u32[]{:S(2)}) collective-permute-start(f32[8,16,256]{2,1,0:T(8,128)} %get-tuple-element.19), channel_id=1, source_target_pairs={{0,1},{1,0},{2,3},{3,2},{4,5},{5,4},{6,7},{7,6},{8,9},{9,8},{10,11... | collective-permute-start | bytes 393224 | tf_op jit(solution)/shard_map/ppermute | solution.py:219
  45.2 4.1 %copy-start.6 = (f32[64,64]{1,0:T(8,128)S(1)}, f32[64,64]{1,0:T(8,128)}, u32[]{:S(2)}) copy-start(f32[64,64]{1,0:T(8,128)} %param.14) | copy-start | bytes 49156
  49.0 6.8 %collective-permute-start.6 = (f32[8,16,256]{2,1,0:T(8,128)}, f32[8,16,256]{2,1,0:T(8,128)S(1)}, u32[]{:S(2)}, u32[]{:S(2)}) collective-permute-start(f32[8,16,256]{2,1,0:T(8,128)} %get-tuple-element.22), channel_id=1, source_target_pairs={{0,1},{1,0},{2,3},{3,2},{4,5},{5,4},{6,7},{7,6},{8,9},{9,8},{10,11... | collective-permute-start | bytes 393224 | tf_op jit(solution)/shard_map/ppermute | solution.py:219
  49.8 0.7 copy-start.3
  54.2 7.8 %collective-permute-start.5 = (f32[8,16,256]{2,1,0:T(8,128)}, f32[8,16,256]{2,1,0:T(8,128)S(1)}, u32[]{:S(2)}, u32[]{:S(2)}) collective-permute-start(f32[8,16,256]{2,1,0:T(8,128)} %get-tuple-element.20), channel_id=1, source_target_pairs={{0,1},{1,0},{2,3},{3,2},{4,5},{5,4},{6,7},{7,6},{8,9},{9,8},{10,11... | collective-permute-start | bytes 393224 | tf_op jit(solution)/shard_map/ppermute | solution.py:219
  55.7 0.6 copy-start.4
  60.1 5.7 %collective-permute-start.7 = (f32[8,16,256]{2,1,0:T(8,128)}, f32[8,16,256]{2,1,0:T(8,128)S(1)}, u32[]{:S(2)}, u32[]{:S(2)}) collective-permute-start(f32[8,16,256]{2,1,0:T(8,128)} %get-tuple-element.23), channel_id=1, source_target_pairs={{0,1},{1,0},{2,3},{3,2},{4,5},{5,4},{6,7},{7,6},{8,9},{9,8},{10,11... | collective-permute-start | bytes 393224 | tf_op jit(solution)/shard_map/ppermute | solution.py:219
  62.0 0.6 copy-start.5
  65.8 0.7 copy-start.7
